TPU v7x, 32 devices: a whole 2x2x4 slice. The times are simulated.
32 devices in a mesh: east: 4 (over x, core), north: 2 (over y), depth: 4 (over z).
Axes of the slice: x: 2, y: 2, z: 4, core: 2. Of those that a mesh axis runs over, the one named last changes fastest.
Arguments:
- thermal_field: float32 [256, 32, 256], P('depth', 'east', 'north'), may hold values from 0.2 to 1.6, as said below
- liquid_fraction: float32 [256, 32, 256], P('depth', 'east', 'north'), may hold values from 0 to 0.6
- steam_content_grid: float32 [256, 32, 256], P('depth', 'east', 'north'), may hold values from 0 to 1
- carbonic_gas_grid: float32 [256, 32, 256], P('depth', 'east', 'north'), may hold values from 0 to 0.5
- stratum_number_grid: int32 [256, 32, 256], P('depth', 'east', 'north'), may hold values from 0 to 11, as said below
- injection_flags: int32 [256, 32, 256], P('depth', 'east', 'north'), may hold values 0 or 1
- lateral_transmissivity: float32 [2, 12], replicated, may hold values from 0.02 to 0.12
- vertical_transmissivity: float32 [12], replicated, may hold values from 20 to 2000
- stratum_advection_offsets: float32 [2, 12], replicated, may hold values from -0.45 to 0.45
Outputs:
- thermal_field_next: float32 [256, 32, 256], P('depth', 'east', 'north')
- liquid_fraction_next: float32 [256, 32, 256], P('depth', 'east', 'north')
- steam_content_next: float32 [256, 32, 256], P('depth', 'east', 'north')
- carbonic_gas_next: float32 [256, 32, 256], P('depth', 'east', 'north')
Inputs may be any that keep to these rules, and one draw needn't show every extreme that they name: `thermal_field`: drawn per cell. `stratum_number_grid`: every layer number occurs.
All inputs are finite; a program needn't handle non-finite values. No bound on the sum of `injection_flags` on one device may be relied on, other than what follows from the above.
Results may differ from a plain program's by a relative error of at most 0.0003.
Values sent between devices are 32-bit elements; how exact they have to be, the bound alone decides.
No kernel may reach another device: no remote copies, remote signals or barrier semaphores. Data moves between devices by JAX's collectives and lax.ppermute only.
A program may use at most 64 MiB of HBM per device.

v0:
```python
import jax
import jax.numpy as jnp
from jax import lax
from jax.sharding import PartitionSpec as P

SECTIONS = 4


SOFTEN = 0.5
HEAT_CARRY = 0.5
SILL_RATE = 0.3
SILL_HEAT = 2.5
WATER_INPUT = 0.2
CARBON_INPUT = 0.1
MELT_SHARPNESS = 4.0
SOLIDUS = 1.0
DEPRESSION = 0.5
MELT_RATE = 0.5
LATENT = 0.3


def with_halo(block, sides, width):
    for axis, dim in sides:
        count = lax.axis_size(axis)
        forward = [(i, i + 1) for i in range(count - 1)]
        forward.append((count - 1, 0))
        backward = [(target, source) for source, target in forward]
        low = lax.ppermute(
            lax.slice_in_dim(block, block.shape[dim] - width, None, axis=dim), axis, forward
        )
        high = lax.ppermute(lax.slice_in_dim(block, 0, width, axis=dim), axis, backward)
        block = jnp.concatenate([low, block, high], axis=dim)
    return block


def lookup_table(layers, table):
    result = jnp.zeros((table.shape[0],) + layers.shape, jnp.float32)
    for layer_no in range(table.shape[1]):
        result = jnp.where(
            layers[None] == layer_no, table[:, layer_no][:, None, None, None], result
        )
    return result


def lateral_section(padded, coeffs, sill):
    soften = jnp.exp(-SOFTEN * padded[0])
    cond_x = (coeffs[0] * soften)[..., 1:-1]
    cond_y = (coeffs[1] * soften)[..., 1:-1, :]
    drift_x = coeffs[2][..., 1:-1]
    drift_y = coeffs[3][..., 1:-1, :]
    mobile_x = padded[:3, ..., 1:-1]
    mobile_y = padded[:3, ..., 1:-1, :]
    face_cx = 0.5 * (cond_x[..., :-1, :] + cond_x[..., 1:, :])
    face_cy = 0.5 * (cond_y[..., :-1] + cond_y[..., 1:])
    face_vx = 0.5 * (drift_x[..., :-1, :] + drift_x[..., 1:, :])
    face_vy = 0.5 * (drift_y[..., :-1] + drift_y[..., 1:])
    flux_x = face_cx * (mobile_x[0, ..., 1:, :] - mobile_x[0, ..., :-1, :])
    flux_y = face_cy * (mobile_y[0, ..., 1:] - mobile_y[0, ..., :-1])
    diffused = flux_x[..., 1:, :] - flux_x[..., :-1, :] + flux_y[..., 1:] - flux_y[..., :-1]
    carried_x = (
        jnp.maximum(face_vx, 0.0) * mobile_x[..., :-1, :]
        + jnp.minimum(face_vx, 0.0) * mobile_x[..., 1:, :]
    )
    carried_y = (
        jnp.maximum(face_vy, 0.0) * mobile_y[..., :-1]
        + jnp.minimum(face_vy, 0.0) * mobile_y[..., 1:]
    )
    inflow = (
        carried_x[..., :-1, :] - carried_x[..., 1:, :] + carried_y[..., :-1] - carried_y[..., 1:]
    )
    inner = padded[..., 1:-1, 1:-1]
    heat_one = inner[0] + diffused + HEAT_CARRY * inflow[0]
    water_two = inner[1] + inflow[1] + sill * WATER_INPUT
    carbon_two = inner[2] + inflow[2] + sill * CARBON_INPUT
    heat_two = heat_one + sill * SILL_RATE * (SILL_HEAT - heat_one)
    target = jax.nn.sigmoid(MELT_SHARPNESS * (heat_two - SOLIDUS + DEPRESSION * water_two))
    melt_two = inner[3] + MELT_RATE * (target - inner[3])
    heat_three = heat_two - LATENT * (melt_two - inner[3])
    return jnp.stack([heat_three, water_two, carbon_two, melt_two])


def column_faces(cond_col):
    roof_boundary_face = jnp.concatenate([cond_col[:1], 0.5 * (cond_col[:-1] + cond_col[1:])], 0)
    floor_boundary_face = jnp.concatenate([roof_boundary_face[1:], jnp.zeros_like(cond_col[:1])], 0)
    return (roof_boundary_face, floor_boundary_face)


def reduce_solve(lower_band, main_band, upper_band, right_side):
    count = main_band.shape[0]
    if count == 1:
        return right_side / main_band
    half = main_band.shape[0] // 2
    tail = main_band.shape[1:]
    sides = right_side.shape[0]
    lower_pairs = lower_band.reshape((half, 2) + tail)
    main_pairs = main_band.reshape((half, 2) + tail)
    upper_pairs = upper_band.reshape((half, 2) + tail)
    side_pairs = right_side.reshape((sides, half, 2) + tail)
    even_lower, odd_lower = (lower_pairs[:, 0], lower_pairs[:, 1])
    even_main, odd_main = (main_pairs[:, 0], main_pairs[:, 1])
    even_upper, odd_upper = (upper_pairs[:, 0], upper_pairs[:, 1])
    even_side, odd_side = (side_pairs[:, :, 0], side_pairs[:, :, 1])
    blank = jnp.zeros_like(even_main[:1])
    next_lower = jnp.concatenate([even_lower[1:], blank], 0)
    next_main = jnp.concatenate([even_main[1:], blank + 1.0], 0)
    next_upper = jnp.concatenate([even_upper[1:], blank], 0)
    next_side = jnp.concatenate([even_side[:, 1:], jnp.zeros_like(even_side[:, :1])], 1)
    left_factor = -odd_lower / even_main
    right_factor = -odd_upper / next_main
    odd_solution = reduce_solve(
        left_factor * even_lower,
        odd_main + left_factor * even_upper + right_factor * next_lower,
        right_factor * next_upper,
        odd_side + left_factor * even_side + right_factor * next_side,
    )
    prior_solution = jnp.concatenate([jnp.zeros_like(odd_solution[:, :1]), odd_solution[:, :-1]], 1)
    even_solution = (
        even_side - even_lower * prior_solution - even_upper * odd_solution
    ) / even_main
    merged = jnp.stack([even_solution, odd_solution], 2).reshape((sides, 2 * half) + tail)
    return merged


def local(
    thermal_field,
    liquid_fraction,
    steam_content_grid,
    carbonic_gas_grid,
    stratum_number_grid,
    injection_flags,
    lateral_transmissivity,
    vertical_transmissivity,
    stratum_advection_offsets,
):
    table = jnp.concatenate(
        [lateral_transmissivity, stratum_advection_offsets, vertical_transmissivity[None]], 0
    )
    vertical_base = lookup_table(stratum_number_grid, table[4:5])[0]
    sill = injection_flags.astype(jnp.float32)
    packed_marks = stratum_number_grid * 2 + injection_flags
    chamber_state = jnp.stack(
        [thermal_field, steam_content_grid, carbonic_gas_grid, liquid_fraction]
    )
    marks_rim = with_halo(packed_marks, (("east", 1), ("north", 2)), 1)
    lateral_pad = lookup_table(marks_rim // 2, table[:4])
    for section_no in range(SECTIONS):
        mobile_rim = with_halo(chamber_state[:3], (("east", 2), ("north", 3)), 1)
        melt_pad = jnp.pad(chamber_state[3], ((0, 0), (1, 1), (1, 1)))
        rimmed_state = jnp.concatenate([mobile_rim, melt_pad[None]], 0)
        chamber_state = lateral_section(rimmed_state, lateral_pad, sill)
    lateral_thermal_diffusion = chamber_state[0]
    conduct = vertical_base * jnp.exp(-SOFTEN * lateral_thermal_diffusion)
    heat_column = lax.all_to_all(
        lateral_thermal_diffusion, "depth", split_axis=1, concat_axis=0, tiled=True
    )
    cond_column = lax.all_to_all(conduct, "depth", split_axis=1, concat_axis=0, tiled=True)
    roof_boundary_face, floor_boundary_face = column_faces(cond_column)
    lower_band = jnp.concatenate(
        [jnp.zeros_like(roof_boundary_face[:1]), -roof_boundary_face[1:]], 0
    )
    solved = reduce_solve(
        lower_band,
        1.0 + roof_boundary_face + floor_boundary_face,
        -floor_boundary_face,
        heat_column[None],
    )[0]
    heat_next = lax.all_to_all(solved, "depth", split_axis=0, concat_axis=1, tiled=True)
    return (heat_next, chamber_state[3], chamber_state[1], chamber_state[2])


def solution(mesh):
    placed = (
        P("depth", "east", "north"),
        P("depth", "east", "north"),
        P("depth", "east", "north"),
        P("depth", "east", "north"),
        P("depth", "east", "north"),
        P("depth", "east", "north"),
        P(),
        P(),
        P(),
    )
    return jax.shard_map(
        local,
        mesh=mesh,
        in_specs=placed,
        out_specs=(
            P("depth", "east", "north"),
            P("depth", "east", "north"),
            P("depth", "east", "north"),
            P("depth", "east", "north"),
        ),
        check_vma=False,
    )
```

profile of v0, /device:TPU:0, one launch (start us, length us, event | category | flops | bytes accessed | tf_op | source)
XLA Modules:
  0.0 180.4 jit_solution(7017571378439631794)
XLA Ops:
  2.4 2.0 %collective-permute-start.1 = (s32[64,1,128]{2,0,1:T(8,128)S(1)}, s32[64,1,128]{2,0,1:T(8,128)S(1)}, u32[]{:S(2)}, u32[]{:S(2)}) collective-permute-start(s32[64,1,128]{2,0,1:T(8,128)S(1)} %get-tuple-element.124), channel_id=1, source_target_pairs={{8,0},{16,8},{24,16},{0,24},{9,1},{17,9},{25,17},{1,25},{10,2},{18... | collective-permute-start | bytes 98312 | tf_op jit(solution)/shard_map/ppermute | solution.py:31
  9.6 2.3 %collective-permute-start.2 = (s32[64,10,1]{2,0,1:T(8,128)S(1)}, s32[64,10,1]{2,0,1:T(8,128)S(1)}, u32[]{:S(2)}, u32[]{:S(2)}) collective-permute-start(s32[64,10,1]{2,0,1:T(8,128)S(1)} %get-tuple-element.109), channel_id=1, source_target_pairs={{0,4},{4,0},{1,5},{5,1},{2,6},{6,2},{3,7},{7,3},{8,12},{12,8},{9,1... | collective-permute-start | bytes 7688 | tf_op jit(solution)/shard_map/ppermute | solution.py:28
  12.7 7.7 %collective-permute-done.2 = s32[64,10,1]{2,0,1:T(8,128)S(1)} collective-permute-done((s32[64,10,1]{2,0,1:T(8,128)S(1)}, s32[64,10,1]{2,0,1:T(8,128)S(1)}, u32[]{:S(2)}, u32[]{:S(2)}) %collective-permute-start.2) | collective-permute-done | bytes 2592 | tf_op jit(solution)/shard_map/ppermute | solution.py:28
  20.4 6.5 %collective-permute-done.3 = s32[64,10,1]{2,0,1:T(8,128)S(1)} collective-permute-done((s32[64,10,1]{2,0,1:T(8,128)S(1)}, s32[64,10,1]{2,0,1:T(8,128)S(1)}, u32[]{:S(2)}, u32[]{:S(2)}) %collective-permute-start.3) | collective-permute-done | bytes 2592 | tf_op jit(solution)/shard_map/ppermute | solution.py:31
  28.2 2.0 %broadcast_compare_fusion.8 = (pred[64,10,130]{2,0,1:T(8,128)(4,1)}, pred[64,10,130]{2,0,1:T(8,128)(4,1)}, pred[64,10,130]{2,0,1:T(8,128)(4,1)}, pred[64,10,130]...) fusion(s32[64,10,130]{2,0,1:T(8,128)S(1)} %get-tuple-element.57), kind=kLoop, calls=%fused_computation.166 | loop fusion | flops 915200 | bytes 1248000 | tf_op jit(solution)/shard_map/eq | solution.py:40
  31.5 1.6 collective-permute-start.7
  33.6 3.4 %select_select_fusion = f32[4,64,10,130]{3,1,2,0:T(8,128)S(1)} fusion(f32[4]{0:T(128)} %get-tuple-element.13, f32[4]{0:T(128)} %get-tuple-element.14, f32[4]{0:T(128)} %get-tuple-element.15, f32[4]{0:T(128)} %get-tuple-element.16, f32[4]{0:T(128)} %get-tuple-element.17, f32[4]{0:T(128)} %get-tuple-element.18, f32[4]{0:T(128)} %get-tuple-element.19, ...), kind=kLoop, calls=%fused_computation | loop fusion | flops 3993600 | bytes 2329792 | tf_op jit(solution)/shard_map/jit(_where)/select_n | solution.py:39
  37.0 2.0 %copy.286 = f32[3,64,10,1]{3,1,2,0:T(8,128)} copy(f32[3,64,10,1]{1,3,2,0:T(1,128)} %collective-permute-done.6) | data formatting | bytes 15360 | tf_op jit(solution)/shard_map/ppermute | solution.py:28
  39.1 1.3 copy.287
  40.4 1.4 multiply_bitcast_fusion.7
  46.7 2.2 %fusion.125 = (f32[1,64,8,128]{3,1,2,0:T(8,128)S(1)}, f32[64,8,128]{2,0,1:T(8,128)S(1)}, f32[64,8,128]{2,0,1:T(8,128)}, f32[64,8,128]{2,0,1:T(8,128)S(1)}, f32[64,8,128]{2,0,1:T(8,128)S(1)}) fusion(f32[1,64,10,130]{3,1,2,0:T(8,128)} %pad_bitcast_fusion.3, s32[64,8,128]{2,1,0:T(8,128)S(1)} %copy-done.24, f32[3,64,8,128]{3,1,2,0:T(8,128)S(1)} %slice_subtract_fusion.6, ...), kind=kLoop, calls=%fused_computation.432 | loop fusion | flops 1966080 | bytes 4456448 | tf_op jit(solution)/shard_map/stack | solution.py:79
  49.0 1.7 collective-permute-start.9
  51.8 1.5 collective-permute-done.8
  54.1 1.6 fusion.143
  55.7 1.5 copy.295
  57.2 1.6 copy.296
  58.8 1.5 collective-permute-start.11
  60.8 2.8 %pad_maximum_fusion.45 = (f32[3,64,9,128]{3,1,2,0:T(8,128)}, f32[3,64,9,128]{3,1,2,0:T(8,128)}, f32[3,64,9,128]{3,1,2,0:T(8,128)}) fusion(f32[3,64,1,128]{3,1,2,0:T(8,128)} %copy-done.41, f32[1,64,8,128]{3,1,2,0:T(8,128)S(1)} %bitcast.660, f32[1,64,8,128]{3,1,2,0:T(8,128)S(1)} %bitcast.678, f32[1,64,8,128]{3,1,2,0:T(8,128)S(1)} %get-tuple-element.50, ...), kind=kLoop, calls=%fused_computation.63 | loop fusion | flops 1990656 | bytes 4227072 | tf_op jit(solution)/shard_map/concatenate | solution.py:32
  64.1 2.0 %copy.297 = f32[3,64,10,1]{3,1,2,0:T(8,128)} copy(f32[3,64,10,1]{1,3,2,0:T(1,128)} %collective-permute-done.10) | data formatting | bytes 15360 | tf_op jit(solution)/shard_map/ppermute | solution.py:28
  66.1 1.3 copy.298
  67.5 1.5 multiply_bitcast_fusion.5
  72.0 1.6 fusion.42
  74.7 2.4 %fusion.126 = (f32[1,64,8,128]{3,1,2,0:T(8,128)S(1)}, f32[64,8,128]{2,0,1:T(8,128)S(1)}, f32[64,8,128]{2,0,1:T(8,128)}, f32[64,8,128]{2,0,1:T(8,128)S(1)}, f32[1,64,8,128]{3,1,2,0:T(8,128)S(1)}) fusion(f32[1,64,10,130]{3,1,2,0:T(8,128)} %pad_bitcast_fusion.2, s32[64,8,128]{2,1,0:T(8,128)S(1)} %copy-done.25, f32[3,64,8,128]{3,1,2,0:T(8,128)S(1)} %slice_subtract_fusion.4, ...), kind=kLoop, calls=%fused_computation.433 | loop fusion | flops 2162688 | bytes 4980736 | tf_op jit(solution)/shard_map/stack | solution.py:79
  77.1 1.7 collective-permute-start.13
  80.0 1.6 collective-permute-done.12
  82.2 1.6 fusion.142
  83.8 1.6 copy.301
  85.4 1.6 copy.302
  89.1 2.9 %pad_maximum_fusion.46 = (f32[3,64,9,128]{3,1,2,0:T(8,128)}, f32[3,64,9,128]{3,1,2,0:T(8,128)}, f32[3,64,9,128]{3,1,2,0:T(8,128)}) fusion(f32[3,64,1,128]{3,1,2,0:T(8,128)} %copy-done.39, f32[1,64,8,128]{3,1,2,0:T(8,128)} %copy-done.22, f32[1,64,8,128]{3,1,2,0:T(8,128)S(1)} %bitcast.672, f32[1,64,8,128]{3,1,2,0:T(8,128)S(1)} %copy-done.21, ...), kind=kLoop, calls=%fused_computation.65 | loop fusion | flops 1990656 | bytes 4227072 | tf_op jit(solution)/shard_map/concatenate | solution.py:32
  92.0 2.0 %copy.303 = f32[3,64,10,1]{3,1,2,0:T(8,128)} copy(f32[3,64,10,1]{1,3,2,0:T(1,128)} %collective-permute-done.14) | data formatting | bytes 15360 | tf_op jit(solution)/shard_map/ppermute | solution.py:28
  95.4 1.5 multiply_bitcast_fusion.3
  99.9 1.6 fusion.39
  102.6 2.4 %fusion.127 = (f32[1,64,8,128]{3,1,2,0:T(8,128)S(1)}, f32[64,8,128]{2,0,1:T(8,128)S(1)}, f32[64,8,128]{2,0,1:T(8,128)}, f32[64,8,128]{2,0,1:T(8,128)S(1)}, f32[1,64,8,128]{3,1,2,0:T(8,128)S(1)}) fusion(f32[1,64,10,130]{3,1,2,0:T(8,128)} %pad_bitcast_fusion.1, s32[64,8,128]{2,1,0:T(8,128)S(1)} %copy-done.26, f32[3,64,8,128]{3,1,2,0:T(8,128)S(1)} %slice_subtract_fusion.2, ...), kind=kLoop, calls=%fused_computation.434 | loop fusion | flops 2293760 | bytes 5242880 | tf_op jit(solution)/shard_map/stack | solution.py:79
  105.1 1.7 collective-permute-start.17
  108.0 1.9 %collective-permute-done.16 = f32[3,64,1,128]{3,1,2,0:T(8,128)S(1)} collective-permute-done((f32[3,64,1,128]{3,1,2,0:T(8,128)S(1)}, f32[3,64,1,128]{3,1,2,0:T(8,128)S(1)}, u32[]{:S(2)}, u32[]{:S(2)}) %collective-permute-start.16) | collective-permute-done | bytes 98336 | tf_op jit(solution)/shard_map/ppermute | solution.py:28
  110.5 1.6 fusion.141
  112.1 1.6 copy.307
  113.7 1.6 copy.308
  117.3 2.9 %pad_maximum_fusion.47 = (f32[3,64,9,128]{3,1,2,0:T(8,128)}, f32[3,64,9,128]{3,1,2,0:T(8,128)}, f32[3,64,9,128]{3,1,2,0:T(8,128)}) fusion(f32[3,64,1,128]{3,1,2,0:T(8,128)} %copy-done.37, f32[1,64,8,128]{3,1,2,0:T(8,128)} %copy-done.18, f32[1,64,8,128]{3,1,2,0:T(8,128)S(1)} %bitcast.666, f32[1,64,8,128]{3,1,2,0:T(8,128)S(1)} %copy-done.17, ...), kind=kLoop, calls=%fused_computation.67 | loop fusion | flops 1990656 | bytes 4227072 | tf_op jit(solution)/shard_map/concatenate | solution.py:32
  120.3 2.0 %copy.309 = f32[3,64,10,1]{3,1,2,0:T(8,128)} copy(f32[3,64,10,1]{1,3,2,0:T(1,128)} %collective-permute-done.18) | data formatting | bytes 15360 | tf_op jit(solution)/shard_map/ppermute | solution.py:28
  123.6 1.5 multiply_bitcast_fusion.1
  130.6 1.6 fusion.49
  132.2 9.9 %exponential_multiply_fusion = (f32[64,8,128]{2,0,1:T(8,128)S(1)}, f32[64,8,128]{2,0,1:T(8,128)}, f32[64,8,128]{2,0,1:T(8,128)S(1)}, f32[64,8,128]{2,0,1:T(8,128)S(1)}) fusion(s32[64,8,128]{2,1,0:T(8,128)S(1)} %copy-done.49, f32[]{:T(128)} %bitcast.65, f32[]{:T(128)} %bitcast.64, f32[]{:T(128)} %bitcast.63, f32[]{:T(128)} %bitcast.62, f32[]{:T(128)} %bitcast.61, ...), kind=kLoop, calls=%fused_computation.253 | loop fusion | flops 2818048 | bytes 2621488 | tf_op jit(solution)/shard_map/mul | solution.py:152
  142.0 13.3 %all_to_all.51 = f32[64,8,128]{2,0,1:T(8,128)S(1)} all-to-all(f32[64,8,128]{2,0,1:T(8,128)S(1)} %get-tuple-element.32), channel_id=1, replica_groups=mesh['east'=4,'north'=2,'depth'=4] {'depth'}, dimensions={1} | all-to-all | bytes 524288 | tf_op jit(solution)/shard_map/all_to_all | solution.py:156
  155.4 3.4 %all-to-all-start = ((f32[64,8,128]{2,0,1:T(8,128)}), f32[64,8,128]{2,0,1:T(8,128)S(1)}, u32[]{:S(2)}, u32[]{:S(2)}) async-start(f32[64,8,128]{2,0,1:T(8,128)} %get-tuple-element.33), calls=%async_computation | async-start | bytes 524288 | tf_op jit(solution)/shard_map/all_to_all | solution.py:153
  161.7 5.0 %all-to-all-done = f32[64,8,128]{2,0,1:T(8,128)S(1)} async-done(((f32[64,8,128]{2,0,1:T(8,128)}), f32[64,8,128]{2,0,1:T(8,128)S(1)}, u32[]{:S(2)}, u32[]{:S(2)}) %all-to-all-start) | async-done | bytes 262176 | tf_op jit(solution)/shard_map/all_to_all | solution.py:153
  169.3 3.4 %all-to-all-start.2 = ((f32[256,2,128]{2,1,0:T(2,128)}), f32[256,2,128]{2,1,0:T(2,128)S(1)}, u32[]{:S(2)}, u32[]{:S(2)}) async-start(f32[256,2,128]{2,1,0:T(2,128)} %copy.413), calls=%async_computation.2 | async-start | bytes 524288 | tf_op jit(solution)/shard_map/all_to_all | solution.py:167
  175.3 4.2 %all-to-all-done.2 = f32[256,2,128]{2,1,0:T(2,128)S(1)} async-done(((f32[256,2,128]{2,1,0:T(2,128)}), f32[256,2,128]{2,1,0:T(2,128)S(1)}, u32[]{:S(2)}, u32[]{:S(2)}) %all-to-all-start.2) | async-done | bytes 262176 | tf_op jit(solution)/shard_map/all_to_all | solution.py:167
  (337 shorter events, 50.1 us)
Async XLA Ops:
  0.6 4.8 %copy-start.55 = (f32[64,8,128]{2,1,0:T(8,128)S(1)}, f32[64,8,128]{2,1,0:T(8,128)}, u32[]{:S(2)}) copy-start(f32[64,8,128]{2,1,0:T(8,128)} %param.12) | copy-start | bytes 786436
  0.6 4.8 %copy-start.53 = (f32[64,8,128]{2,1,0:T(8,128)S(1)}, f32[64,8,128]{2,1,0:T(8,128)}, u32[]{:S(2)}) copy-start(f32[64,8,128]{2,1,0:T(8,128)} %param.9) | copy-start | bytes 786436
  0.7 6.7 %copy-start.58 = (f32[64,8,128]{2,1,0:T(8,128)S(1)}, f32[64,8,128]{2,1,0:T(8,128)}, u32[]{:S(2)}) copy-start(f32[64,8,128]{2,1,0:T(8,128)} %param.10) | copy-start | bytes 786436
  1.9 7.5 %collective-permute-start = (s32[64,1,128]{2,0,1:T(8,128)S(1)}, s32[64,1,128]{2,0,1:T(8,128)S(1)}, u32[]{:S(2)}, u32[]{:S(2)}) collective-permute-start(s32[64,1,128]{2,0,1:T(8,128)S(1)} %get-tuple-element.123), channel_id=1, source_target_pairs={{0,8},{8,16},{16,24},{24,0},{1,9},{9,17},{17,25},{25,1},{2,10},{10... | collective-permute-start | bytes 98312 | tf_op jit(solution)/shard_map/ppermute | solution.py:28
  2.4 7.0 %collective-permute-start.1 = (s32[64,1,128]{2,0,1:T(8,128)S(1)}, s32[64,1,128]{2,0,1:T(8,128)S(1)}, u32[]{:S(2)}, u32[]{:S(2)}) collective-permute-start(s32[64,1,128]{2,0,1:T(8,128)S(1)} %get-tuple-element.124), channel_id=1, source_target_pairs={{8,0},{16,8},{24,16},{0,24},{9,1},{17,9},{25,17},{1,25},{10,2},{18... | collective-permute-start | bytes 98312 | tf_op jit(solution)/shard_map/ppermute | solution.py:31
  5.4 3.1 %copy-start.60 = (f32[2,12]{1,0:T(2,128)S(1)}, f32[2,12]{1,0:T(2,128)}, u32[]{:S(2)}) copy-start(f32[2,12]{1,0:T(2,128)} %param.17) | copy-start | bytes 292
  5.4 3.1 %copy-start.61 = (f32[2,12]{1,0:T(2,128)S(1)}, f32[2,12]{1,0:T(2,128)}, u32[]{:S(2)}) copy-start(f32[2,12]{1,0:T(2,128)} %param.15) | copy-start | bytes 292
  5.6 24.6 %collective-permute-start.4 = (f32[3,64,1,128]{3,1,2,0:T(8,128)S(1)}, f32[3,64,1,128]{3,1,2,0:T(8,128)S(1)}, u32[]{:S(2)}, u32[]{:S(2)}) collective-permute-start(f32[3,64,1,128]{3,1,2,0:T(8,128)S(1)} %get-tuple-element.92), channel_id=1, source_target_pairs={{0,8},{8,16},{16,24},{24,0},{1,9},{9,17},{17,25},{25,1},{2,10},{10... | collective-permute-start | bytes 294920 | tf_op jit(solution)/shard_map/ppermute | solution.py:28
  6.2 24.0 %collective-permute-start.5 = (f32[3,64,1,128]{3,1,2,0:T(8,128)S(1)}, f32[3,64,1,128]{3,1,2,0:T(8,128)S(1)}, u32[]{:S(2)}, u32[]{:S(2)}) collective-permute-start(f32[3,64,1,128]{3,1,2,0:T(8,128)S(1)} %get-tuple-element.93), channel_id=1, source_target_pairs={{8,0},{16,8},{24,16},{0,24},{9,1},{17,9},{25,17},{1,25},{10,2},{18... | collective-permute-start | bytes 294920 | tf_op jit(solution)/shard_map/ppermute | solution.py:31
  7.4 4.6 %copy-start.59 = (f32[12]{0:T(128)S(1)}, f32[12]{0:T(128)}, u32[]{:S(2)}) copy-start(f32[12]{0:T(128)} %param.16) | copy-start | bytes 148
  9.6 10.8 %collective-permute-start.2 = (s32[64,10,1]{2,0,1:T(8,128)S(1)}, s32[64,10,1]{2,0,1:T(8,128)S(1)}, u32[]{:S(2)}, u32[]{:S(2)}) collective-permute-start(s32[64,10,1]{2,0,1:T(8,128)S(1)} %get-tuple-element.109), channel_id=1, source_target_pairs={{0,4},{4,0},{1,5},{5,1},{2,6},{6,2},{3,7},{7,3},{8,12},{12,8},{9,1... | collective-permute-start | bytes 7688 | tf_op jit(solution)/shard_map/ppermute | solution.py:28
  11.9 15.0 %collective-permute-start.3 = (s32[64,10,1]{2,0,1:T(8,128)S(1)}, s32[64,10,1]{2,0,1:T(8,128)S(1)}, u32[]{:S(2)}, u32[]{:S(2)}) collective-permute-start(s32[64,10,1]{2,0,1:T(8,128)S(1)} %get-tuple-element.110), channel_id=1, source_target_pairs={{4,0},{0,4},{5,1},{1,5},{6,2},{2,6},{7,3},{3,7},{12,8},{8,12},{13,... | collective-permute-start | bytes 7688 | tf_op jit(solution)/shard_map/ppermute | solution.py:31
  31.5 7.6 %collective-permute-start.7 = (f32[3,64,10,1]{1,3,2,0:T(1,128)S(1)}, f32[3,64,10,1]{1,3,2,0:T(1,128)S(1)}, u32[]{:S(2)}, u32[]{:S(2)}) collective-permute-start(f32[3,64,10,1]{1,3,2,0:T(1,128)S(1)} %copy.285), channel_id=1, source_target_pairs={{4,0},{0,4},{5,1},{1,5},{6,2},{2,6},{7,3},{3,7},{12,8},{8,12},{13,... | collective-permute-start | bytes 23048 | tf_op jit(solution)/shard_map/ppermute | solution.py:31
  33.1 3.9 %collective-permute-start.6 = (f32[3,64,10,1]{1,3,2,0:T(1,128)S(1)}, f32[3,64,10,1]{1,3,2,0:T(1,128)}, u32[]{:S(2)}, u32[]{:S(2)}) collective-permute-start(f32[3,64,10,1]{1,3,2,0:T(1,128)S(1)} %copy.284), channel_id=1, source_target_pairs={{0,4},{4,0},{1,5},{5,1},{2,6},{6,2},{3,7},{7,3},{8,12},{12,8},{9,1... | collective-permute-start | bytes 23048 | tf_op jit(solution)/shard_map/ppermute | solution.py:28
  42.0 2.1 %copy-start.1 = (f32[3,64,10,1]{3,1,2,0:T(8,128)S(1)}, f32[3,64,10,1]{3,1,2,0:T(8,128)}, u32[]{:S(2)}) copy-start(f32[3,64,10,1]{3,1,2,0:T(8,128)} %copy.287) | copy-start | bytes 23044
  42.1 2.1 %copy-start.36 = (f32[3,64,1,128]{3,1,2,0:T(8,128)S(1)}, f32[3,64,1,128]{3,1,2,0:T(8,128)}, u32[]{:S(2)}) copy-start(f32[3,64,1,128]{3,1,2,0:T(8,128)} %copy-done.35) | copy-start | bytes 294916
  42.3 2.4 %copy-start.28 = (f32[64,9,128]{2,0,1:T(8,128)}, f32[64,9,128]{2,0,1:T(8,128)S(1)}, u32[]{:S(2)}) copy-start(f32[64,9,128]{2,0,1:T(8,128)S(1)} %get-tuple-element.94) | copy-start | bytes 884740
  42.3 2.4 %copy-start.29 = (f32[64,9,128]{2,0,1:T(8,128)}, f32[64,9,128]{2,0,1:T(8,128)S(1)}, u32[]{:S(2)}) copy-start(f32[64,9,128]{2,0,1:T(8,128)S(1)} %get-tuple-element.95) | copy-start | bytes 884740
  42.5 2.1 %copy-start.8 = (f32[64,8,129]{2,0,1:T(8,128)}, f32[64,8,129]{2,0,1:T(8,128)S(1)}, u32[]{:S(2)}) copy-start(f32[64,8,129]{2,0,1:T(8,128)S(1)} %get-tuple-element.96) | copy-start | bytes 792580
  42.5 2.1 %copy-start.12 = (f32[64,8,129]{2,0,1:T(8,128)}, f32[64,8,129]{2,0,1:T(8,128)S(1)}, u32[]{:S(2)}) copy-start(f32[64,8,129]{2,0,1:T(8,128)S(1)} %get-tuple-element.97) | copy-start | bytes 792580
  48.9 5.2 %copy-start.45 = (f32[64,8,128]{2,0,1:T(8,128)}, f32[64,8,128]{2,0,1:T(8,128)S(1)}, u32[]{:S(2)}) copy-start(f32[64,8,128]{2,0,1:T(8,128)S(1)} %get-tuple-element.51) | copy-start | bytes 786436
  48.9 4.4 %collective-permute-start.8 = (f32[3,64,1,128]{3,1,2,0:T(8,128)S(1)}, f32[3,64,1,128]{3,1,2,0:T(8,128)S(1)}, u32[]{:S(2)}, u32[]{:S(2)}) collective-permute-start(f32[3,64,1,128]{3,1,2,0:T(8,128)S(1)} %get-tuple-element.90), channel_id=1, source_target_pairs={{0,8},{8,16},{16,24},{24,0},{1,9},{9,17},{17,25},{25,1},{2,10},{10... | collective-permute-start | bytes 294920 | tf_op jit(solution)/shard_map/ppermute | solution.py:28
  49.0 4.4 %collective-permute-start.9 = (f32[3,64,1,128]{3,1,2,0:T(8,128)S(1)}, f32[3,64,1,128]{3,1,2,0:T(8,128)S(1)}, u32[]{:S(2)}, u32[]{:S(2)}) collective-permute-start(f32[3,64,1,128]{3,1,2,0:T(8,128)S(1)} %get-tuple-element.91), channel_id=1, source_target_pairs={{8,0},{16,8},{24,16},{0,24},{9,1},{17,9},{25,17},{1,25},{10,2},{18... | collective-permute-start | bytes 294920 | tf_op jit(solution)/shard_map/ppermute | solution.py:31
  58.8 7.4 %collective-permute-start.11 = (f32[3,64,10,1]{1,3,2,0:T(1,128)S(1)}, f32[3,64,10,1]{1,3,2,0:T(1,128)S(1)}, u32[]{:S(2)}, u32[]{:S(2)}) collective-permute-start(f32[3,64,10,1]{1,3,2,0:T(1,128)S(1)} %copy.296), channel_id=1, source_target_pairs={{4,0},{0,4},{5,1},{1,5},{6,2},{2,6},{7,3},{3,7},{12,8},{8,12},{13,... | collective-permute-start | bytes 23048 | tf_op jit(solution)/shard_map/ppermute | solution.py:31
  60.2 3.8 %collective-permute-start.10 = (f32[3,64,10,1]{1,3,2,0:T(1,128)S(1)}, f32[3,64,10,1]{1,3,2,0:T(1,128)}, u32[]{:S(2)}, u32[]{:S(2)}) collective-permute-start(f32[3,64,10,1]{1,3,2,0:T(1,128)S(1)} %copy.295), channel_id=1, source_target_pairs={{0,4},{4,0},{1,5},{5,1},{2,6},{6,2},{3,7},{7,3},{8,12},{12,8},{9,1... | collective-permute-start | bytes 23048 | tf_op jit(solution)/shard_map/ppermute | solution.py:28
  72.0 2.0 %copy-start.33 = (f32[3,64,8,128]{3,1,2,0:T(8,128)}, f32[3,64,8,128]{3,1,2,0:T(8,128)S(1)}, u32[]{:S(2)}) copy-start(f32[3,64,8,128]{3,1,2,0:T(8,128)S(1)} %slice_subtract_fusion.4) | copy-start | bytes 2359300
  77.0 4.7 %copy-start.20 = (f32[1,64,8,128]{3,1,2,0:T(8,128)}, f32[1,64,8,128]{3,1,2,0:T(8,128)S(1)}, u32[]{:S(2)}) copy-start(f32[1,64,8,128]{3,1,2,0:T(8,128)S(1)} %get-tuple-element.44) | copy-start | bytes 786436
  77.0 4.7 %copy-start.22 = (f32[1,64,8,128]{3,1,2,0:T(8,128)}, f32[1,64,8,128]{3,1,2,0:T(8,128)S(1)}, u32[]{:S(2)}) copy-start(f32[1,64,8,128]{3,1,2,0:T(8,128)S(1)} %get-tuple-element.64) | copy-start | bytes 786436
  77.0 4.7 %copy-start.43 = (f32[64,8,128]{2,0,1:T(8,128)}, f32[64,8,128]{2,0,1:T(8,128)S(1)}, u32[]{:S(2)}) copy-start(f32[64,8,128]{2,0,1:T(8,128)S(1)} %get-tuple-element.45) | copy-start | bytes 786436
  77.0 4.6 %collective-permute-start.12 = (f32[3,64,1,128]{3,1,2,0:T(8,128)S(1)}, f32[3,64,1,128]{3,1,2,0:T(8,128)S(1)}, u32[]{:S(2)}, u32[]{:S(2)}) collective-permute-start(f32[3,64,1,128]{3,1,2,0:T(8,128)S(1)} %get-tuple-element.88), channel_id=1, source_target_pairs={{0,8},{8,16},{16,24},{24,0},{1,9},{9,17},{17,25},{25,1},{2,10},{10... | collective-permute-start | bytes 294920 | tf_op jit(solution)/shard_map/ppermute | solution.py:28
  77.1 4.5 %collective-permute-start.13 = (f32[3,64,1,128]{3,1,2,0:T(8,128)S(1)}, f32[3,64,1,128]{3,1,2,0:T(8,128)S(1)}, u32[]{:S(2)}, u32[]{:S(2)}) collective-permute-start(f32[3,64,1,128]{3,1,2,0:T(8,128)S(1)} %get-tuple-element.89), channel_id=1, source_target_pairs={{8,0},{16,8},{24,16},{0,24},{9,1},{17,9},{25,17},{1,25},{10,2},{18... | collective-permute-start | bytes 294920 | tf_op jit(solution)/shard_map/ppermute | solution.py:31
  83.8 5.2 %copy-start.21 = (f32[1,64,8,128]{3,1,2,0:T(8,128)S(1)}, f32[1,64,8,128]{3,1,2,0:T(8,128)}, u32[]{:S(2)}) copy-start(f32[1,64,8,128]{3,1,2,0:T(8,128)} %copy-done.20) | copy-start | bytes 786436
  87.0 7.1 %collective-permute-start.15 = (f32[3,64,10,1]{1,3,2,0:T(1,128)S(1)}, f32[3,64,10,1]{1,3,2,0:T(1,128)S(1)}, u32[]{:S(2)}, u32[]{:S(2)}) collective-permute-start(f32[3,64,10,1]{1,3,2,0:T(1,128)S(1)} %copy.302), channel_id=1, source_target_pairs={{4,0},{0,4},{5,1},{1,5},{6,2},{2,6},{7,3},{3,7},{12,8},{8,12},{13,... | collective-permute-start | bytes 23048 | tf_op jit(solution)/shard_map/ppermute | solution.py:31
  88.0 4.0 %collective-permute-start.14 = (f32[3,64,10,1]{1,3,2,0:T(1,128)S(1)}, f32[3,64,10,1]{1,3,2,0:T(1,128)}, u32[]{:S(2)}, u32[]{:S(2)}) collective-permute-start(f32[3,64,10,1]{1,3,2,0:T(1,128)S(1)} %copy.301), channel_id=1, source_target_pairs={{0,4},{4,0},{1,5},{5,1},{2,6},{6,2},{3,7},{7,3},{8,12},{12,8},{9,1... | collective-permute-start | bytes 23048 | tf_op jit(solution)/shard_map/ppermute | solution.py:28
  95.4 1.7 copy-start.23
  95.4 1.7 copy-start.40
  99.9 2.0 %copy-start.34 = (f32[3,64,8,128]{3,1,2,0:T(8,128)}, f32[3,64,8,128]{3,1,2,0:T(8,128)S(1)}, u32[]{:S(2)}) copy-start(f32[3,64,8,128]{3,1,2,0:T(8,128)S(1)} %slice_subtract_fusion.2) | copy-start | bytes 2359300
  105.0 4.9 %copy-start.16 = (f32[1,64,8,128]{3,1,2,0:T(8,128)}, f32[1,64,8,128]{3,1,2,0:T(8,128)S(1)}, u32[]{:S(2)}) copy-start(f32[1,64,8,128]{3,1,2,0:T(8,128)S(1)} %get-tuple-element.38) | copy-start | bytes 786436
  105.0 4.9 %copy-start.18 = (f32[1,64,8,128]{3,1,2,0:T(8,128)}, f32[1,64,8,128]{3,1,2,0:T(8,128)S(1)}, u32[]{:S(2)}) copy-start(f32[1,64,8,128]{3,1,2,0:T(8,128)S(1)} %get-tuple-element.63) | copy-start | bytes 786436
  105.0 4.9 %copy-start.47 = (f32[64,8,128]{2,0,1:T(8,128)}, f32[64,8,128]{2,0,1:T(8,128)S(1)}, u32[]{:S(2)}) copy-start(f32[64,8,128]{2,0,1:T(8,128)S(1)} %get-tuple-element.39) | copy-start | bytes 786436
  105.1 4.8 %collective-permute-start.16 = (f32[3,64,1,128]{3,1,2,0:T(8,128)S(1)}, f32[3,64,1,128]{3,1,2,0:T(8,128)S(1)}, u32[]{:S(2)}, u32[]{:S(2)}) collective-permute-start(f32[3,64,1,128]{3,1,2,0:T(8,128)S(1)} %get-tuple-element.86), channel_id=1, source_target_pairs={{0,8},{8,16},{16,24},{24,0},{1,9},{9,17},{17,25},{25,1},{2,10},{10... | collective-permute-start | bytes 294920 | tf_op jit(solution)/shard_map/ppermute | solution.py:28
  105.1 4.7 %collective-permute-start.17 = (f32[3,64,1,128]{3,1,2,0:T(8,128)S(1)}, f32[3,64,1,128]{3,1,2,0:T(8,128)S(1)}, u32[]{:S(2)}, u32[]{:S(2)}) collective-permute-start(f32[3,64,1,128]{3,1,2,0:T(8,128)S(1)} %get-tuple-element.87), channel_id=1, source_target_pairs={{8,0},{16,8},{24,16},{0,24},{9,1},{17,9},{25,17},{1,25},{10,2},{18... | collective-permute-start | bytes 294920 | tf_op jit(solution)/shard_map/ppermute | solution.py:31
  112.1 5.2 %copy-start.17 = (f32[1,64,8,128]{3,1,2,0:T(8,128)S(1)}, f32[1,64,8,128]{3,1,2,0:T(8,128)}, u32[]{:S(2)}) copy-start(f32[1,64,8,128]{3,1,2,0:T(8,128)} %copy-done.16) | copy-start | bytes 786436
  115.2 7.1 %collective-permute-start.19 = (f32[3,64,10,1]{1,3,2,0:T(1,128)S(1)}, f32[3,64,10,1]{1,3,2,0:T(1,128)S(1)}, u32[]{:S(2)}, u32[]{:S(2)}) collective-permute-start(f32[3,64,10,1]{1,3,2,0:T(1,128)S(1)} %copy.308), channel_id=1, source_target_pairs={{4,0},{0,4},{5,1},{1,5},{6,2},{2,6},{7,3},{3,7},{12,8},{8,12},{13,... | collective-permute-start | bytes 23048 | tf_op jit(solution)/shard_map/ppermute | solution.py:31
  116.3 4.0 %collective-permute-start.18 = (f32[3,64,10,1]{1,3,2,0:T(1,128)S(1)}, f32[3,64,10,1]{1,3,2,0:T(1,128)}, u32[]{:S(2)}, u32[]{:S(2)}) collective-permute-start(f32[3,64,10,1]{1,3,2,0:T(1,128)S(1)} %copy.307), channel_id=1, source_target_pairs={{0,4},{4,0},{1,5},{5,1},{2,6},{6,2},{3,7},{7,3},{8,12},{12,8},{9,1... | collective-permute-start | bytes 23048 | tf_op jit(solution)/shard_map/ppermute | solution.py:28
  123.6 1.7 copy-start.38
  155.4 11.3 %all-to-all-start = ((f32[64,8,128]{2,0,1:T(8,128)}), f32[64,8,128]{2,0,1:T(8,128)S(1)}, u32[]{:S(2)}, u32[]{:S(2)}) async-start(f32[64,8,128]{2,0,1:T(8,128)} %get-tuple-element.33), calls=%async_computation | async-start | bytes 524288 | tf_op jit(solution)/shard_map/all_to_all | solution.py:153
  169.3 10.2 %all-to-all-start.2 = ((f32[256,2,128]{2,1,0:T(2,128)}), f32[256,2,128]{2,1,0:T(2,128)S(1)}, u32[]{:S(2)}, u32[]{:S(2)}) async-start(f32[256,2,128]{2,1,0:T(2,128)} %copy.413), calls=%async_computation.2 | async-start | bytes 524288 | tf_op jit(solution)/shard_map/all_to_all | solution.py:167
  (36 other events, 43.7 us)
where the time goes:
time: 182 us; the launch traced here: 180 us
  local copies, waits for them, and re-layouts  55.8 us (31%)
  other arithmetic  52.7 us (29%)
  waiting for transfers between devices  28.9 us (16%)
  starting transfers between devices  27.2 us (15%)
  blocking collectives  13.3 us (7%)
  between operations  2.45 us (1%)
    unnamed x149, local copies, waits for them, and re-layouts  17.1 us
    ppermute x10, starting transfers between devices, with_halo(): lax.ppermute(lax.slice_in_dim(block, 0, width, axis=dim), axis, backward)  13.5 us
    all_to_all x1, blocking collectives, local(): lax.all_to_all(conduct, 'depth', split_axis=1, concat_axis=0, tiled=True)  13.3 us
    ppermute x10, waiting for transfers between devices, with_halo(): lax.ppermute(lax.slice_in_dim(block, block.shape[dim] - width, None, axis...  13.3 us
    slice x10, local copies, waits for them, and re-layouts, with_halo(): lax.slice_in_dim(block, block.shape[dim] - width, None, axis=dim)  10.4 us
    mul x1, other arithmetic, local(): conduct = vertical_base * jnp.exp(-SOFTEN * lateral_thermal_diffusion)  9.87 us
    concatenate x9, other arithmetic, with_halo(): block = jnp.concatenate([low, block, high], axis=dim)  9.16 us
    ppermute x4, local copies, waits for them, and re-layouts, with_halo(): lax.ppermute(lax.slice_in_dim(block, block.shape[dim] - width, None, axis...  8.19 us
  transfers between devices with their start and end apart: 22, of which 8 were waited for; matrix products, arithmetic and copies ran while one was open for 20% of the time, Pallas kernels for 0%

commit v1 on v0

v1 whole, which is shorter than its diff:
```python
import jax
import jax.numpy as jnp
from jax import lax
from jax.experimental import pallas as pl
from jax.experimental.pallas import tpu as pltpu
from jax.sharding import PartitionSpec as P

SECTIONS = 4


SOFTEN = 0.5
HEAT_CARRY = 0.5
SILL_RATE = 0.3
SILL_HEAT = 2.5
WATER_INPUT = 0.2
CARBON_INPUT = 0.1
MELT_SHARPNESS = 4.0
SOLIDUS = 1.0
DEPRESSION = 0.5
MELT_RATE = 0.5
LATENT = 0.3


def ring_perms(axis):
    count = lax.axis_size(axis)
    forward = [(i, (i + 1) % count) for i in range(count)]
    backward = [((i + 1) % count, i) for i in range(count)]
    return forward, backward


def edges(block, axis, dim):
    forward, backward = ring_perms(axis)
    last = lax.index_in_dim(block, block.shape[dim] - 1, axis=dim, keepdims=False)
    first = lax.index_in_dim(block, 0, axis=dim, keepdims=False)
    low = lax.ppermute(last, axis, forward)
    high = lax.ppermute(first, axis, backward)
    return low, high


def shifted(block, low, high, dim):
    n = block.shape[dim]
    lo = jnp.expand_dims(low, dim)
    hi = jnp.expand_dims(high, dim)
    minus = jnp.concatenate([lo, lax.slice_in_dim(block, 0, n - 1, axis=dim)], axis=dim)
    plus = jnp.concatenate([lax.slice_in_dim(block, 1, n, axis=dim), hi], axis=dim)
    return minus, plus


def lookup(layers, row):
    result = jnp.zeros(layers.shape, jnp.float32)
    for layer_no in range(row.shape[0]):
        result = jnp.where(layers == layer_no, row[layer_no], result)
    return result


def lateral_step(state, coef, halos, sill):
    heat, water, carbon, melt = state
    cx, cx_m, cx_p, cy, cy_m, cy_p, vfx_m, vfx_p, vfy_m, vfy_p = coef
    xs_lo, xs_hi, ys_lo, ys_hi = halos
    mobile = jnp.stack([heat, water, carbon])
    q_xm, q_xp = shifted(mobile, xs_lo, xs_hi, 2)
    q_ym, q_yp = shifted(mobile, ys_lo, ys_hi, 3)
    soft = jnp.exp(-SOFTEN * heat)
    kx = cx * soft
    ky = cy * soft
    kx_m = cx_m * jnp.exp(-SOFTEN * q_xm[0])
    kx_p = cx_p * jnp.exp(-SOFTEN * q_xp[0])
    ky_m = cy_m * jnp.exp(-SOFTEN * q_ym[0])
    ky_p = cy_p * jnp.exp(-SOFTEN * q_yp[0])
    flux_x_lo = 0.5 * (kx_m + kx) * (heat - q_xm[0])
    flux_x_hi = 0.5 * (kx + kx_p) * (q_xp[0] - heat)
    flux_y_lo = 0.5 * (ky_m + ky) * (heat - q_ym[0])
    flux_y_hi = 0.5 * (ky + ky_p) * (q_yp[0] - heat)
    diffused = flux_x_hi - flux_x_lo + flux_y_hi - flux_y_lo
    carried_x_lo = jnp.maximum(vfx_m, 0.0) * q_xm + jnp.minimum(vfx_m, 0.0) * mobile
    carried_x_hi = jnp.maximum(vfx_p, 0.0) * mobile + jnp.minimum(vfx_p, 0.0) * q_xp
    carried_y_lo = jnp.maximum(vfy_m, 0.0) * q_ym + jnp.minimum(vfy_m, 0.0) * mobile
    carried_y_hi = jnp.maximum(vfy_p, 0.0) * mobile + jnp.minimum(vfy_p, 0.0) * q_yp
    inflow = carried_x_lo - carried_x_hi + carried_y_lo - carried_y_hi
    heat_one = heat + diffused + HEAT_CARRY * inflow[0]
    water_two = water + inflow[1] + sill * WATER_INPUT
    carbon_two = carbon + inflow[2] + sill * CARBON_INPUT
    heat_two = heat_one + sill * SILL_RATE * (SILL_HEAT - heat_one)
    target = jax.nn.sigmoid(MELT_SHARPNESS * (heat_two - SOLIDUS + DEPRESSION * water_two))
    melt_two = melt + MELT_RATE * (target - melt)
    heat_three = heat_two - LATENT * (melt_two - melt)
    return heat_three, water_two, carbon_two, melt_two


def sweep_kernel(r_ref, c_ref, y_ref, a_ref, b_ref, red_ref, g_s, vy_s, va_s):
    n = r_ref.shape[0]
    zero = jnp.zeros(r_ref.shape[1:], jnp.float32)
    one = jnp.ones(r_ref.shape[1:], jnp.float32)

    def forward(i, carry):
        g_prev, vy_prev, va_prev = carry
        up = 0.5 * (c_ref[i - 1] + c_ref[i])
        down = 0.5 * (c_ref[i] + c_ref[i + 1])
        inv = 1.0 / (1.0 + up + down - up * g_prev)
        g = down * inv
        vy = (r_ref[i] + up * vy_prev) * inv
        va = (up * va_prev) * inv
        g_s[i] = g
        vy_s[i] = vy
        va_s[i] = va
        return g, vy, va

    lax.fori_loop(1, n - 1, forward, (zero, zero, one))

    def backward(k, carry):
        i = n - 2 - k
        y_next, a_next, b_next = carry
        g = g_s[i]
        y = vy_s[i] + g * y_next
        a = va_s[i] + g * a_next
        b = g * b_next
        y_ref[i] = y
        a_ref[i] = a
        b_ref[i] = b
        return y, a, b

    lax.fori_loop(0, n - 2, backward, (zero, zero, one))
    y_ref[0] = zero
    a_ref[0] = one
    b_ref[0] = zero
    y_ref[n - 1] = zero
    a_ref[n - 1] = zero
    b_ref[n - 1] = one
    up_first = 0.5 * (c_ref[0] + c_ref[1])
    up_last = 0.5 * (c_ref[n - 2] + c_ref[n - 1])
    red_ref[0] = 1.0 + up_first * (1.0 - a_ref[1])
    red_ref[1] = up_first * b_ref[1]
    red_ref[2] = r_ref[0] + up_first * y_ref[1]
    red_ref[3] = 1.0 + up_last * (1.0 - b_ref[n - 2])
    red_ref[4] = up_last * a_ref[n - 2]
    red_ref[5] = r_ref[n - 1] + up_last * y_ref[n - 2]
    red_ref[6] = c_ref[0]
    red_ref[7] = c_ref[n - 1]


def local_sweep(heat, cond):
    shape = heat.shape
    plane = shape[1:]
    out_shape = (
        jax.ShapeDtypeStruct(shape, jnp.float32),
        jax.ShapeDtypeStruct(shape, jnp.float32),
        jax.ShapeDtypeStruct(shape, jnp.float32),
        jax.ShapeDtypeStruct((8,) + plane, jnp.float32),
    )
    return pl.pallas_call(
        sweep_kernel,
        out_shape=out_shape,
        scratch_shapes=[pltpu.VMEM(shape, jnp.float32)] * 3,
    )(heat, cond)


def reduced_solve(red_all):
    count = red_all.shape[0]
    lower, diag, upper, side = [], [], [], []
    for j in range(count):
        p0, q0, s0, p1, q1, s1, c_first, c_last = [red_all[j, k] for k in range(8)]
        if j == 0:
            face = c_first
            lower.append(jnp.zeros_like(face))
        else:
            face = 0.5 * (red_all[j - 1, 7] + c_first)
            lower.append(face)
        diag.append(p0 + face)
        upper.append(q0)
        side.append(s0)
        if j + 1 < count:
            below = 0.5 * (c_last + red_all[j + 1, 6])
        else:
            below = jnp.zeros_like(c_last)
        lower.append(q1)
        diag.append(p1 + below)
        upper.append(below)
        side.append(s1)
    size = len(diag)
    ratios, values = [], []
    g_prev = jnp.zeros_like(diag[0])
    v_prev = jnp.zeros_like(diag[0])
    for k in range(size):
        inv = 1.0 / (diag[k] - lower[k] * g_prev)
        g_prev = upper[k] * inv
        v_prev = (side[k] + lower[k] * v_prev) * inv
        ratios.append(g_prev)
        values.append(v_prev)
    solved = [None] * size
    following = jnp.zeros_like(diag[0])
    for k in reversed(range(size)):
        following = values[k] + ratios[k] * following
        solved[k] = following
    return jnp.stack(solved)


def local(
    thermal_field,
    liquid_fraction,
    steam_content_grid,
    carbonic_gas_grid,
    stratum_number_grid,
    injection_flags,
    lateral_transmissivity,
    vertical_transmissivity,
    stratum_advection_offsets,
):
    sill = injection_flags.astype(jnp.float32)
    layers = stratum_number_grid
    lx_lo, lx_hi = edges(layers, "east", 1)
    ly_lo, ly_hi = edges(layers, "north", 2)

    def coef_pair(table_row, dim, low, high):
        own = lookup(layers, table_row)
        minus, plus = shifted(own, lookup(low, table_row), lookup(high, table_row), dim)
        return own, minus, plus

    cx, cx_m, cx_p = coef_pair(lateral_transmissivity[0], 1, lx_lo, lx_hi)
    cy, cy_m, cy_p = coef_pair(lateral_transmissivity[1], 2, ly_lo, ly_hi)
    vx, vx_m, vx_p = coef_pair(stratum_advection_offsets[0], 1, lx_lo, lx_hi)
    vy, vy_m, vy_p = coef_pair(stratum_advection_offsets[1], 2, ly_lo, ly_hi)
    coef = (
        cx, cx_m, cx_p, cy, cy_m, cy_p,
        0.5 * (vx_m + vx), 0.5 * (vx + vx_p), 0.5 * (vy_m + vy), 0.5 * (vy + vy_p),
    )
    cz = lookup(layers, vertical_transmissivity)

    state = (thermal_field, steam_content_grid, carbonic_gas_grid, liquid_fraction)
    for section_no in range(SECTIONS):
        mobile = jnp.stack(state[:3])
        xs_lo, xs_hi = edges(mobile, "east", 2)
        ys_lo, ys_hi = edges(mobile, "north", 3)
        state = lateral_step(state, coef, (xs_lo, xs_hi, ys_lo, ys_hi), sill)
    heat = state[0]
    cond = cz * jnp.exp(-SOFTEN * heat)

    y, a, b, red = local_sweep(heat, cond)
    red_all = lax.all_gather(red, "depth")
    solved = reduced_solve(red_all)
    rank = lax.axis_index("depth")
    first = lax.dynamic_index_in_dim(solved, 2 * rank, keepdims=False)
    last = lax.dynamic_index_in_dim(solved, 2 * rank + 1, keepdims=False)
    heat_next = y + a * first[None] + b * last[None]
    return (heat_next, state[3], state[1], state[2])


def solution(mesh):
    placed = (
        P("depth", "east", "north"),
        P("depth", "east", "north"),
        P("depth", "east", "north"),
        P("depth", "east", "north"),
        P("depth", "east", "north"),
        P("depth", "east", "north"),
        P(),
        P(),
        P(),
    )
    return jax.shard_map(
        local,
        mesh=mesh,
        in_specs=placed,
        out_specs=(
            P("depth", "east", "north"),
            P("depth", "east", "north"),
            P("depth", "east", "north"),
            P("depth", "east", "north"),
        ),
        check_vma=False,
    )
```

time: 182 us -> 207 us (1.14)
  other arithmetic: 52.7 us -> 115 us
  waiting for transfers between devices: 28.9 us -> 2.07 us
  starting transfers between devices: 27.2 us -> 16.2 us
  local copies, waits for them, and re-layouts: 55.8 us -> 52 us
  Pallas kernels: 0 us -> 3.2 us
    select_n x1 -> x7, other arithmetic: 3.42 us -> 54.6 us  [lookup(): result = jnp.where(layers == layer_no, row[layer_no], result)]
    broadcast_in_dim x0 -> x3, other arithmetic: none -> 22.2 us  [the longest x2 14.7 us: shifted(): lo = jnp.expand_dims(low, dim)]
    ppermute x20, waiting for transfers between devices: 19.8 us -> 2.07 us  [the longest x10 2.04 us: edges(): low = lax.ppermute(last, axis, forward)]
    slice x75 -> x35, local copies, waits for them, and re-layouts: 19.3 us -> 33.8 us  [the longest x11 12.3 us: shifted(): lax.slice_in_dim(block, 0, n - 1, axis=dim)]
    all_gather x0 -> x1, blocking collectives: none -> 13.9 us  [local(): red_all = lax.all_gather(red, 'depth')]
    ppermute x8 -> x0, local copies, waits for them, and re-layouts: 13.5 us -> none  [the longest x4 8.19 us: with_halo(): lax.ppermute(lax.slice_in_dim(block, block.shape[dim] - width, None, axis...]
    all_to_all x1 -> x0, blocking collectives: 13.3 us -> none  [local(): lax.all_to_all(conduct, 'depth', split_axis=1, concat_axis=0, tiled=True)]
    mul x32 -> x2, other arithmetic: 22.7 us -> 10.5 us  [the longest x1 10.5 us: local(): cond = cz * jnp.exp(-SOFTEN * heat)]
  transfers between devices with their start and end apart: 22 -> 20, of which waited for: 8 -> 4; matrix products, arithmetic and copies ran while one was open for 20% -> 52% of each run, Pallas kernels for 0% -> 0%
where the time goes in v1:
time: 207 us; the launch traced here: 205 us
  other arithmetic  115 us (56%)
  local copies, waits for them, and re-layouts  52 us (25%)
  starting transfers between devices  16.2 us (8%)
  blocking collectives  13.9 us (7%)
  Pallas kernels  3.2 us (2%)
  between operations  2.26 us (1%)
  waiting for transfers between devices  2.07 us (1%)
    select_n x7, other arithmetic, lookup(): result = jnp.where(layers == layer_no, row[layer_no], result)  54.6 us
    broadcast_in_dim x2, other arithmetic, shifted(): lo = jnp.expand_dims(low, dim)  14.7 us
    all_gather x1, blocking collectives, local(): red_all = lax.all_gather(red, 'depth')  13.9 us
    sub x4, other arithmetic, lateral_step(): inflow = carried_x_lo - carried_x_hi + carried_y_lo - carried_y_hi  13.1 us
    slice x11, local copies, waits for them, and re-layouts, shifted(): lax.slice_in_dim(block, 0, n - 1, axis=dim)  12.3 us
    ppermute x10, starting transfers between devices, edges(): high = lax.ppermute(first, axis, backward)  12.2 us
    mul x1, other arithmetic, local(): cond = cz * jnp.exp(-SOFTEN * heat)  10.5 us
    slice x10, local copies, waits for them, and re-layouts, edges(): lax.index_in_dim(block, block.shape[dim] - 1, axis=dim, keepdims=False)  9.53 us
  transfers between devices with their start and end apart: 20, of which 4 were waited for; matrix products, arithmetic and copies ran while one was open for 52% of the time, Pallas kernels for 0%

profile of v1, /device:TPU:0, one launch (start us, length us, event | category | flops | bytes accessed | tf_op | source)
XLA Modules:
  0.0 204.9 jit_solution(15430716356781517698)
XLA Ops:
  0.6 1.7 fusion.184
  2.3 2.4 %collective-permute-start = (s32[64,128]{1,0:T(8,128)}, s32[64,128]{1,0:T(8,128)}, u32[]{:S(2)}, u32[]{:S(2)}) collective-permute-start(s32[64,128]{1,0:T(8,128)} %bitcast.12), channel_id=1, source_target_pairs={{8,0},{16,8},{24,16},{0,24},{9,1},{17,9},{25,17},{1,25},{10,2},{18... | collective-permute-start | bytes 98312 | tf_op jit(solution)/shard_map/ppermute | solution.py:36
  4.7 1.2 fusion.186
  6.1 1.6 collective-permute-start.4
  9.0 1.6 collective-permute-start.5
  13.3 1.2 fusion.179
  14.4 1.3 fusion.180
  16.7 7.8 %select_select_fusion.3 = (f32[64,8,128]{2,1,0:T(8,128)S(1)}, pred[64,8,128]{2,1,0:T(8,128)(4,1)S(1)}, pred[64,8,128]{2,1,0:T(8,128)(4,1)S(1)}, pred[64,8,128]{2...) fusion(f32[]{:T(128)} %bitcast.11, f32[]{:T(128)} %bitcast.10, ...), kind=kLoop, calls=%fused_computation.188 | loop fusion | flops 1572864 | bytes 1310768 | tf_op jit(solution)/shard_map/jit(_where)/select_n | solution.py:52
  24.6 7.9 %select_select_fusion.1 = f32[64,8,128]{2,1,0:T(8,128)S(1)} fusion(pred[64,8,128]{2,1,0:T(8,128)(4,1)S(1)} %get-tuple-element.89, pred[64,8,128]{2,1,0:T(8,128)(4,1)S(1)} %get-tuple-element.88, pred[64,8,128]{2,1,0:T(8,128)(4,1)S(1)} %get-tuple-element.87, pred[64,8,128]{2,1,0:T(8,128)(4,1)S(1)} %get-tuple-element.86, ...), kind=kLoop, calls=%fused_computation.186 | loop fusion | flops 786432 | bytes 1048624 | tf_op jit(solution)/shard_map/jit(_where)/select_n | solution.py:52
  33.4 7.8 %select_select_fusion = f32[64,8,128]{2,1,0:T(8,128)S(1)} fusion(pred[64,8,128]{2,1,0:T(8,128)(4,1)S(1)} %get-tuple-element.89, pred[64,8,128]{2,1,0:T(8,128)(4,1)S(1)} %get-tuple-element.88, pred[64,8,128]{2,1,0:T(8,128)(4,1)S(1)} %get-tuple-element.87, pred[64,8,128]{2,1,0:T(8,128)(4,1)S(1)} %get-tuple-element.86, ...), kind=kLoop, calls=%fused_computation.185 | loop fusion | flops 786432 | bytes 1048624 | tf_op jit(solution)/shard_map/jit(_where)/select_n | solution.py:52
  42.1 7.5 %select_select_fusion.2 = f32[64,8,128]{2,1,0:T(8,128)S(1)} fusion(pred[64,8,128]{2,1,0:T(8,128)(4,1)S(1)} %get-tuple-element.89, pred[64,8,128]{2,1,0:T(8,128)(4,1)S(1)} %get-tuple-element.88, pred[64,8,128]{2,1,0:T(8,128)(4,1)S(1)} %get-tuple-element.87, pred[64,8,128]{2,1,0:T(8,128)(4,1)S(1)} %get-tuple-element.86, ...), kind=kLoop, calls=%fused_computation.187 | loop fusion | flops 786432 | bytes 1048624 | tf_op jit(solution)/shard_map/jit(_where)/select_n | solution.py:52
  53.9 7.3 %select_bitcast_fusion.2 = (f32[64,8,1]{0,1,2:T(8,128)S(1)}, pred[64,8]{0,1:T(8,128)(4,1)S(1)}, pred[64,8]{0,1:T(8,128)(4,1)S(1)}, pred[64,8]{0,1:T(8,128)(4,1)S...) fusion(f32[]{:T(128)} %bitcast.38, f32[]{:T(128)} %bitcast.37, ...), kind=kLoop, calls=%fused_computation.330 | loop fusion | flops 24576 | bytes 20528 | tf_op jit(solution)/shard_map/broadcast_in_dim | solution.py:42
  61.2 7.5 %select_bitcast_fusion = f32[64,8,1]{0,1,2:T(8,128)S(1)} fusion(pred[64,8]{0,1:T(8,128)(4,1)S(1)} %get-tuple-element.259, pred[64,8]{0,1:T(8,128)(4,1)S(1)} %get-tuple-element.258, pred[64,8]{0,1:T(8,128)(4,1)S(1)} %get-tuple-element.257, pred[64,8]{0,1:T(8,128)(4,1)S(1)} %get-tuple-element.256, pred[64,8]{0,1:T(8,128)(4,1)S(1)} %get-tuple-element.255, ...), kind=kLoop, calls=%fused_computation.328 | loop fusion | flops 6144 | bytes 8240 | tf_op jit(solution)/shard_map/broadcast_in_dim | solution.py:43
  68.9 7.5 %select_bitcast_fusion.1 = f32[64,8,1]{0,1,2:T(8,128)S(1)} fusion(pred[64,8]{0,1:T(8,128)(4,1)S(1)} %get-tuple-element.115, pred[64,8]{0,1:T(8,128)(4,1)S(1)} %get-tuple-element.114, pred[64,8]{0,1:T(8,128)(4,1)S(1)} %get-tuple-element.113, pred[64,8]{0,1:T(8,128)(4,1)S(1)} %get-tuple-element.112, pred[64,8]{0,1:T(8,128)(4,1)S(1)} %get-tuple-element.111, ...), kind=kLoop, calls=%fused_computation.329 | loop fusion | flops 6144 | bytes 8240 | tf_op jit(solution)/shard_map/broadcast_in_dim | solution.py:42
  80.1 8.3 %select_select_fusion.6 = (f32[64,128]{1,0:T(8,128)S(1)}, pred[64,128]{1,0:T(8,128)(4,1)S(1)}, pred[64,128]{1,0:T(8,128)(4,1)S(1)}, pred[64,128]{1,0:T(8,128)(4,...) fusion(f32[]{:T(128)} %bitcast.11, f32[]{:T(128)} %bitcast.10, ...), kind=kLoop, calls=%fused_computation.213 | loop fusion | flops 393216 | bytes 327728 | tf_op jit(solution)/shard_map/jit(_where)/select_n | solution.py:52
  88.4 7.6 %select_select_fusion.5 = f32[64,128]{1,0:T(8,128)S(1)} fusion(pred[64,128]{1,0:T(8,128)(4,1)S(1)} %get-tuple-element.76, pred[64,128]{1,0:T(8,128)(4,1)S(1)} %get-tuple-element.75, pred[64,128]{1,0:T(8,128)(4,1)S(1)} %get-tuple-element.74, pred[64,128]{1,0:T(8,128)(4,1)S(1)} %get-tuple-element.73, pred[64,128]{1,0:T(8,128)(4,1)S(1)} %get-tuple-element.72, ...), kind=kLoop, calls=%fused_computation.212 | loop fusion | flops 98304 | bytes 131120 | tf_op jit(solution)/shard_map/jit(_where)/select_n | solution.py:52
  96.0 7.6 %select_select_fusion.4 = f32[64,128]{1,0:T(8,128)S(1)} fusion(pred[64,128]{1,0:T(8,128)(4,1)S(1)} %get-tuple-element.246, pred[64,128]{1,0:T(8,128)(4,1)S(1)} %get-tuple-element.245, pred[64,128]{1,0:T(8,128)(4,1)S(1)} %get-tuple-element.244, pred[64,128]{1,0:T(8,128)(4,1)S(1)} %get-tuple-element.243, pred[64,128]{1,0:T(8,128)(4,1)S(1)} %get-tuple-element.242, ...), kind=kLoop, calls=%fused_computation.211 | loop fusion | flops 98304 | bytes 131120 | tf_op jit(solution)/shard_map/jit(_where)/select_n | solution.py:52
  103.7 1.3 broadcast_maximum_fusion.3
  105.3 2.6 %fusion.25 = f32[3,64,8,128]{3,2,1,0:T(8,128)S(1)} fusion(f32[3,64,1,128]{3,2,1,0:T(1,128)} %bitcast.25, f32[3,64,1,128]{3,2,1,0:T(1,128)} %bitcast.20, f32[3,64,7,128]{3,2,1,0:T(8,128)S(1)} %copy-done.3, f32[3,64,7,128]{3,2,1,0:T(8,128)S(1)} %copy-done.2, f32[3,64,8,1]{3,2,1,0:T(8,128)S(1)} %copy.190, f32[3,64,8,127]{3,2,1,0:T(8,128)S(1)} %copy-done.1, ...), kind=kLoop, calls=%fused_computation.41 | loop fusion | flops 4128768 | bytes 6815744 | tf_op jit(solution)/shard_map/sub | solution.py:79
  109.5 2.6 %fusion.145 = (f32[1,64,8,128]{3,2,1,0:T(8,128)S(1)}, f32[64,8,128]{2,1,0:T(8,128)}, f32[64,8,128]{2,1,0:T(8,128)}, f32[64,8,128]{2,1,0:T(8,128)}, f32[64,8,128]{2,1,0:T(8,128)}, /*index=5*/f32[64,8,128]{2,1,0:T(8,128)S(1)}) fusion(f32[64,8,128]{2,1,0:T(8,128)S(1)} %copy-done.81, s32[64,8,128]{2,1,0:T(8,128)S(1)} %copy-done, ...), kind=kLoop, calls=%fused_computation.357 | loop fusion | flops 4063232 | bytes 7864320 | tf_op jit(solution)/shard_map/stack | solution.py:60
  113.0 1.1 fusion.174
  114.1 1.2 fusion.175
  116.0 1.4 copy.201
  117.5 1.2 collective-permute-start.10
  120.4 1.2 collective-permute-start.8
  121.6 1.3 fusion.176
  126.3 3.5 %fusion.18 = f32[3,64,8,128]{3,2,1,0:T(8,128)S(1)} fusion(f32[3,64,1,128]{3,2,1,0:T(1,128)} %bitcast.89, f32[3,64,1,128]{3,2,1,0:T(1,128)} %bitcast.86, f32[3,64,7,128]{3,2,1,0:T(8,128)} %get-tuple-element.137, f32[3,64,7,128]{3,2,1,0:T(8,128)} %get-tuple-element.136, f32[3,64,8,1]{3,2,1,0:T(8,128)S(1)} %copy.202, f32[3,64,8,127]{3,2,1,0:T(8,128)} %get-tuple-element.135, ...), kind=kLoop, calls=%fused_computation.34 | loop fusion | flops 4128768 | bytes 6815744 | tf_op jit(solution)/shard_map/sub | solution.py:79
  129.8 1.1 fusion.81
  131.1 2.5 %fusion.146 = (f32[1,64,8,128]{3,2,1,0:T(8,128)S(1)}, f32[64,8,128]{2,1,0:T(8,128)}, f32[64,8,128]{2,1,0:T(8,128)}, f32[64,8,128]{2,1,0:T(8,128)S(1)}) fusion(f32[64,8,128]{2,1,0:T(8,128)S(1)} %copy-done.50, s32[64,8,128]{2,1,0:T(8,128)S(1)} %copy-done, f32[3,64,8,128]{3,2,1,0:T(8,128)S(1)} %fusion.18, f32[64,8,128]{2,1,0:T(8,128)S(1)} %copy-done.33, ...), kind=kLoop, calls=%fused_computation.358 | loop fusion | flops 4128768 | bytes 7602176 | tf_op jit(solution)/shard_map/stack | solution.py:60
  134.5 1.1 fusion.170
  135.6 1.2 fusion.171
  137.6 1.4 copy.207
  139.0 1.2 collective-permute-start.14
  142.6 1.3 fusion.172
  147.4 3.5 %fusion.11 = f32[3,64,8,128]{3,2,1,0:T(8,128)S(1)} fusion(f32[3,64,1,128]{3,2,1,0:T(1,128)} %bitcast.107, f32[3,64,1,128]{3,2,1,0:T(1,128)} %bitcast.104, f32[3,64,7,128]{3,2,1,0:T(8,128)} %get-tuple-element.129, f32[3,64,7,128]{3,2,1,0:T(8,128)} %get-tuple-element.128, f32[3,64,8,1]{3,2,1,0:T(8,128)S(1)} %copy.208, ...), kind=kLoop, calls=%fused_computation.27 | loop fusion | flops 4128768 | bytes 6815744 | tf_op jit(solution)/shard_map/sub | solution.py:79
  151.1 1.3 copy-done.8
  152.5 2.3 %fusion.147 = (f32[1,64,8,128]{3,2,1,0:T(8,128)S(1)}, f32[64,8,128]{2,1,0:T(8,128)}, f32[64,8,128]{2,1,0:T(8,128)S(1)}) fusion(f32[64,8,128]{2,1,0:T(8,128)S(1)} %copy-done.48, s32[64,8,128]{2,1,0:T(8,128)S(1)} %copy-done, f32[3,64,8,128]{3,2,1,0:T(8,128)S(1)} %fusion.11, f32[64,8,128]{2,1,0:T(8,128)S(1)} %copy-done.34, ...), kind=kLoop, calls=%fused_computation.359 | loop fusion | flops 4128768 | bytes 7340032 | tf_op jit(solution)/shard_map/stack | solution.py:60
  155.7 1.1 fusion.166
  156.8 1.2 fusion.167
  158.8 1.4 copy.213
  160.2 1.2 collective-permute-start.18
  163.7 1.3 fusion.168
  168.5 3.5 %fusion.4 = f32[3,64,8,128]{3,2,1,0:T(8,128)S(1)} fusion(f32[3,64,1,128]{3,2,1,0:T(1,128)} %bitcast.125, f32[3,64,1,128]{3,2,1,0:T(1,128)} %bitcast.122, f32[3,64,7,128]{3,2,1,0:T(8,128)} %get-tuple-element.121, f32[3,64,7,128]{3,2,1,0:T(8,128)} %get-tuple-element.120, f32[3,64,8,1]{3,2,1,0:T(8,128)S(1)} %copy.214, f32[3,64,8,127]{3,2,1,0:T(8,128)} %get-tuple-element.119, ...), kind=kLoop, calls=%fused_computation.20 | loop fusion | flops 4128768 | bytes 6815744 | tf_op jit(solution)/shard_map/sub | solution.py:79
  172.1 1.8 fusion.69
  174.7 10.5 %exponential_multiply_fusion = (f32[64,8,128]{2,1,0:T(8,128)}, f32[64,8,128]{2,1,0:T(8,128)}, f32[64,8,128]{2,1,0:T(8,128)}, f32[64,8,128]{2,1,0:T(8,128)}) fusion(pred[64,8,128]{2,1,0:T(8,128)(4,1)S(1)} %copy-done.80, pred[64,8,128]{2,1,0:T(8,128)(4,1)S(1)} %copy-done.78, pred[64,8,128]{2,1,0:T(8,128)(4,1)S(1)} %copy-done.76, ...), kind=kLoop, calls=%fused_computation.169 | loop fusion | flops 5701632 | bytes 8126512 | tf_op jit(solution)/shard_map/mul | solution.py:235
  185.2 3.2 %shard_map.120 = (f32[64,8,128]{2,1,0:T(8,128)}, f32[64,8,128]{2,1,0:T(8,128)}, f32[64,8,128]{2,1,0:T(8,128)}, f32[8,8,128]{2,1,0:T(8,128)}) custom-call(f32[64,8,128]{2,1,0:T(8,128)} %get-tuple-element.35.r_ref, f32[64,8,128]{2,1,0:T(8,128)} %get-tuple-element.34.c_ref), custom_call_target="tpu_custom_call" | custom-call | tf_op jit(solution)/shard_map/pallas_call | solution.py:150
  188.4 13.9 %all-gather = f32[32,8,128]{2,1,0:T(8,128)S(1)} all-gather(f32[8,8,128]{2,1,0:T(8,128)} %get-tuple-element.10), channel_id=2, replica_groups=mesh['east'=4,'north'=2,'depth'=4] {'depth'}, dimensions={0}, use_global_device_ids=true | all-gather | bytes 163840 | tf_op jit(solution)/shard_map/all_gather | solution.py:238
  203.2 1.7 multiply_add_fusion
  (299 shorter events, 40.1 us)
Async XLA Ops:
  2.3 77.8 %collective-permute-start = (s32[64,128]{1,0:T(8,128)}, s32[64,128]{1,0:T(8,128)}, u32[]{:S(2)}, u32[]{:S(2)}) collective-permute-start(s32[64,128]{1,0:T(8,128)} %bitcast.12), channel_id=1, source_target_pairs={{8,0},{16,8},{24,16},{0,24},{9,1},{17,9},{25,17},{1,25},{10,2},{18... | collective-permute-start | bytes 98312 | tf_op jit(solution)/shard_map/ppermute | solution.py:36
  4.7 75.4 %collective-permute-start.2 = (s32[64,128]{1,0:T(8,128)}, s32[64,128]{1,0:T(8,128)}, u32[]{:S(2)}, u32[]{:S(2)}) collective-permute-start(s32[64,128]{1,0:T(8,128)} %bitcast.22), channel_id=1, source_target_pairs={{0,8},{8,16},{16,24},{24,0},{1,9},{9,17},{17,25},{25,1},{2,10},{10... | collective-permute-start | bytes 98312 | tf_op jit(solution)/shard_map/ppermute | solution.py:35
  6.1 46.3 %collective-permute-start.4 = (s32[64,8]{0,1:T(8,128)S(1)}, s32[64,8]{0,1:T(8,128)S(1)}, u32[]{:S(2)}, u32[]{:S(2)}) collective-permute-start(s32[64,8]{0,1:T(8,128)S(1)} %bitcast.570), channel_id=1, source_target_pairs={{4,0},{0,4},{5,1},{1,5},{6,2},{2,6},{7,3},{3,7},{12,8},{8,12},{13,... | collective-permute-start | bytes 6152 | tf_op jit(solution)/shard_map/ppermute | solution.py:36
  7.8 45.2 %collective-permute-start.6 = (s32[64,8]{0,1:T(8,128)S(1)}, s32[64,8]{0,1:T(8,128)S(1)}, u32[]{:S(2)}, u32[]{:S(2)}) collective-permute-start(s32[64,8]{0,1:T(8,128)S(1)} %bitcast.569), channel_id=1, source_target_pairs={{0,4},{4,0},{1,5},{5,1},{2,6},{6,2},{3,7},{7,3},{8,12},{12,8},{9,1... | collective-permute-start | bytes 6152 | tf_op jit(solution)/shard_map/ppermute | solution.py:35
  9.0 70.3 %collective-permute-start.5 = (f32[3,64,8]{1,2,0:T(8,128)S(1)}, f32[3,64,8]{1,2,0:T(8,128)S(1)}, u32[]{:S(2)}, u32[]{:S(2)}) collective-permute-start(f32[3,64,8]{1,2,0:T(8,128)S(1)} %bitcast.557), channel_id=1, source_target_pairs={{4,0},{0,4},{5,1},{1,5},{6,2},{2,6},{7,3},{3,7},{12,8},{8,12},{13,... | collective-permute-start | bytes 18440 | tf_op jit(solution)/shard_map/ppermute | solution.py:36
  24.5 17.5 %copy-start.61 = (pred[64,8,128]{2,1,0:T(8,128)(4,1)}, pred[64,8,128]{2,1,0:T(8,128)(4,1)S(1)}, u32[]{:S(2)}) copy-start(pred[64,8,128]{2,1,0:T(8,128)(4,1)S(1)} %get-tuple-element.80) | copy-start | bytes 196612
  24.5 17.5 %copy-start.63 = (pred[64,8,128]{2,1,0:T(8,128)(4,1)}, pred[64,8,128]{2,1,0:T(8,128)(4,1)S(1)}, u32[]{:S(2)}) copy-start(pred[64,8,128]{2,1,0:T(8,128)(4,1)S(1)} %get-tuple-element.81) | copy-start | bytes 196612
  24.5 17.5 %copy-start.65 = (pred[64,8,128]{2,1,0:T(8,128)(4,1)}, pred[64,8,128]{2,1,0:T(8,128)(4,1)S(1)}, u32[]{:S(2)}) copy-start(pred[64,8,128]{2,1,0:T(8,128)(4,1)S(1)} %get-tuple-element.82) | copy-start | bytes 196612
  24.5 17.5 %copy-start.67 = (pred[64,8,128]{2,1,0:T(8,128)(4,1)}, pred[64,8,128]{2,1,0:T(8,128)(4,1)S(1)}, u32[]{:S(2)}) copy-start(pred[64,8,128]{2,1,0:T(8,128)(4,1)S(1)} %get-tuple-element.83) | copy-start | bytes 196612
  24.5 17.5 %copy-start.69 = (pred[64,8,128]{2,1,0:T(8,128)(4,1)}, pred[64,8,128]{2,1,0:T(8,128)(4,1)S(1)}, u32[]{:S(2)}) copy-start(pred[64,8,128]{2,1,0:T(8,128)(4,1)S(1)} %get-tuple-element.84) | copy-start | bytes 196612
  24.5 17.5 %copy-start.71 = (pred[64,8,128]{2,1,0:T(8,128)(4,1)}, pred[64,8,128]{2,1,0:T(8,128)(4,1)S(1)}, u32[]{:S(2)}) copy-start(pred[64,8,128]{2,1,0:T(8,128)(4,1)S(1)} %get-tuple-element.85) | copy-start | bytes 196612
  24.6 17.5 %copy-start.73 = (pred[64,8,128]{2,1,0:T(8,128)(4,1)}, pred[64,8,128]{2,1,0:T(8,128)(4,1)S(1)}, u32[]{:S(2)}) copy-start(pred[64,8,128]{2,1,0:T(8,128)(4,1)S(1)} %get-tuple-element.86) | copy-start | bytes 196612
  24.6 17.5 %copy-start.75 = (pred[64,8,128]{2,1,0:T(8,128)(4,1)}, pred[64,8,128]{2,1,0:T(8,128)(4,1)S(1)}, u32[]{:S(2)}) copy-start(pred[64,8,128]{2,1,0:T(8,128)(4,1)S(1)} %get-tuple-element.87) | copy-start | bytes 196612
  24.6 17.5 %copy-start.77 = (pred[64,8,128]{2,1,0:T(8,128)(4,1)}, pred[64,8,128]{2,1,0:T(8,128)(4,1)S(1)}, u32[]{:S(2)}) copy-start(pred[64,8,128]{2,1,0:T(8,128)(4,1)S(1)} %get-tuple-element.88) | copy-start | bytes 196612
  24.6 17.5 %copy-start.79 = (pred[64,8,128]{2,1,0:T(8,128)(4,1)}, pred[64,8,128]{2,1,0:T(8,128)(4,1)S(1)}, u32[]{:S(2)}) copy-start(pred[64,8,128]{2,1,0:T(8,128)(4,1)S(1)} %get-tuple-element.89) | copy-start | bytes 196612
  52.3 27.4 %collective-permute-start.7 = (f32[3,64,8]{1,2,0:T(8,128)S(1)}, f32[3,64,8]{1,2,0:T(8,128)S(1)}, u32[]{:S(2)}, u32[]{:S(2)}) collective-permute-start(f32[3,64,8]{1,2,0:T(8,128)S(1)} %bitcast.558), channel_id=1, source_target_pairs={{0,4},{4,0},{1,5},{5,1},{2,6},{6,2},{3,7},{7,3},{8,12},{12,8},{9,1... | collective-permute-start | bytes 18440 | tf_op jit(solution)/shard_map/ppermute | solution.py:35
  53.0 52.0 %collective-permute-start.1 = (f32[3,64,128]{2,1,0:T(8,128)}, f32[3,64,128]{2,1,0:T(8,128)}, u32[]{:S(2)}, u32[]{:S(2)}) collective-permute-start(f32[3,64,128]{2,1,0:T(8,128)} %bitcast.18), channel_id=1, source_target_pairs={{8,0},{16,8},{24,16},{0,24},{9,1},{17,9},{25,17},{1,25},{10,2},{18... | collective-permute-start | bytes 294920 | tf_op jit(solution)/shard_map/ppermute | solution.py:36
  68.7 7.9 %copy-start.90 = (f32[64,8,127]{2,1,0:T(8,128)S(1)}, f32[64,8,127]{2,1,0:T(8,128)}, u32[]{:S(2)}) copy-start(f32[64,8,127]{2,1,0:T(8,128)} %get-tuple-element.170) | copy-start | bytes 780292
  68.7 7.9 %copy-start.91 = (f32[64,8,127]{2,1,0:T(8,128)S(1)}, f32[64,8,127]{2,1,0:T(8,128)}, u32[]{:S(2)}) copy-start(f32[64,8,127]{2,1,0:T(8,128)} %get-tuple-element.171) | copy-start | bytes 780292
  79.3 25.8 %collective-permute-start.3 = (f32[3,64,128]{2,1,0:T(8,128)}, f32[3,64,128]{2,1,0:T(8,128)}, u32[]{:S(2)}, u32[]{:S(2)}) collective-permute-start(f32[3,64,128]{2,1,0:T(8,128)} %bitcast.24), channel_id=1, source_target_pairs={{0,8},{8,16},{16,24},{24,0},{1,9},{9,17},{17,25},{25,1},{2,10},{10... | collective-permute-start | bytes 294920 | tf_op jit(solution)/shard_map/ppermute | solution.py:35
  79.7 24.0 %copy-start.46 = (f32[64,8,128]{2,1,0:T(8,128)S(1)}, f32[64,8,128]{2,1,0:T(8,128)}, u32[]{:S(2)}) copy-start(f32[64,8,128]{2,1,0:T(8,128)} %copy-done.45) | copy-start | bytes 786436
  80.1 25.0 %copy-start.3 = (f32[3,64,7,128]{3,2,1,0:T(8,128)S(1)}, f32[3,64,7,128]{3,2,1,0:T(8,128)}, u32[]{:S(2)}) copy-start(f32[3,64,7,128]{3,2,1,0:T(8,128)} %get-tuple-element.149) | copy-start | bytes 2064388
  88.4 19.7 %copy-start.92 = (f32[64,128]{1,0:T(8,128)}, f32[64,128]{1,0:T(8,128)S(1)}, u32[]{:S(2)}) copy-start(f32[64,128]{1,0:T(8,128)S(1)} %get-tuple-element.64) | copy-start | bytes 98308
  88.4 19.7 %copy-start.96 = (f32[64,128]{1,0:T(8,128)}, f32[64,128]{1,0:T(8,128)S(1)}, u32[]{:S(2)}) copy-start(f32[64,128]{1,0:T(8,128)S(1)} %get-tuple-element.234) | copy-start | bytes 98308
  117.5 5.4 %collective-permute-start.10 = (f32[3,64,8]{1,2,0:T(8,128)S(1)}, f32[3,64,8]{1,2,0:T(8,128)}, u32[]{:S(2)}, u32[]{:S(2)}) collective-permute-start(f32[3,64,8]{1,2,0:T(8,128)S(1)} %bitcast.560), channel_id=1, source_target_pairs={{4,0},{0,4},{5,1},{1,5},{6,2},{2,6},{7,3},{3,7},{12,8},{8,12},{13,... | collective-permute-start | bytes 18440 | tf_op jit(solution)/shard_map/ppermute | solution.py:36
  119.5 4.4 %collective-permute-start.11 = (f32[3,64,8]{1,2,0:T(8,128)}, f32[3,64,8]{1,2,0:T(8,128)S(1)}, u32[]{:S(2)}, u32[]{:S(2)}) collective-permute-start(f32[3,64,8]{1,2,0:T(8,128)} %bitcast.563), channel_id=1, source_target_pairs={{0,4},{4,0},{1,5},{5,1},{2,6},{6,2},{3,7},{7,3},{8,12},{12,8},{9,1... | collective-permute-start | bytes 18440 | tf_op jit(solution)/shard_map/ppermute | solution.py:35
  120.4 5.2 %collective-permute-start.8 = (f32[3,64,128]{2,1,0:T(8,128)}, f32[3,64,128]{2,1,0:T(8,128)}, u32[]{:S(2)}, u32[]{:S(2)}) collective-permute-start(f32[3,64,128]{2,1,0:T(8,128)} %bitcast.553), channel_id=1, source_target_pairs={{8,0},{16,8},{24,16},{0,24},{9,1},{17,9},{25,17},{1,25},{10,2},{18... | collective-permute-start | bytes 294920 | tf_op jit(solution)/shard_map/ppermute | solution.py:36
  121.6 4.6 %collective-permute-start.9 = (f32[3,64,128]{2,1,0:T(8,128)}, f32[3,64,128]{2,1,0:T(8,128)}, u32[]{:S(2)}, u32[]{:S(2)}) collective-permute-start(f32[3,64,128]{2,1,0:T(8,128)} %bitcast.550), channel_id=1, source_target_pairs={{0,8},{8,16},{16,24},{24,0},{1,9},{9,17},{17,25},{25,1},{2,10},{10... | collective-permute-start | bytes 294920 | tf_op jit(solution)/shard_map/ppermute | solution.py:35
  139.0 4.9 %collective-permute-start.14 = (f32[3,64,8]{1,2,0:T(8,128)S(1)}, f32[3,64,8]{1,2,0:T(8,128)}, u32[]{:S(2)}, u32[]{:S(2)}) collective-permute-start(f32[3,64,8]{1,2,0:T(8,128)S(1)} %bitcast.561), channel_id=1, source_target_pairs={{4,0},{0,4},{5,1},{1,5},{6,2},{2,6},{7,3},{3,7},{12,8},{8,12},{13,... | collective-permute-start | bytes 18440 | tf_op jit(solution)/shard_map/ppermute | solution.py:36
  141.0 3.9 %collective-permute-start.15 = (f32[3,64,8]{1,2,0:T(8,128)}, f32[3,64,8]{1,2,0:T(8,128)S(1)}, u32[]{:S(2)}, u32[]{:S(2)}) collective-permute-start(f32[3,64,8]{1,2,0:T(8,128)} %bitcast.565), channel_id=1, source_target_pairs={{0,4},{4,0},{1,5},{5,1},{2,6},{6,2},{3,7},{7,3},{8,12},{12,8},{9,1... | collective-permute-start | bytes 18440 | tf_op jit(solution)/shard_map/ppermute | solution.py:35
  141.9 4.6 %collective-permute-start.12 = (f32[3,64,128]{2,1,0:T(8,128)}, f32[3,64,128]{2,1,0:T(8,128)}, u32[]{:S(2)}, u32[]{:S(2)}) collective-permute-start(f32[3,64,128]{2,1,0:T(8,128)} %bitcast.554), channel_id=1, source_target_pairs={{8,0},{16,8},{24,16},{0,24},{9,1},{17,9},{25,17},{1,25},{10,2},{18... | collective-permute-start | bytes 294920 | tf_op jit(solution)/shard_map/ppermute | solution.py:36
  142.6 4.7 %collective-permute-start.13 = (f32[3,64,128]{2,1,0:T(8,128)}, f32[3,64,128]{2,1,0:T(8,128)}, u32[]{:S(2)}, u32[]{:S(2)}) collective-permute-start(f32[3,64,128]{2,1,0:T(8,128)} %bitcast.551), channel_id=1, source_target_pairs={{0,8},{8,16},{16,24},{24,0},{1,9},{9,17},{17,25},{25,1},{2,10},{10... | collective-permute-start | bytes 294920 | tf_op jit(solution)/shard_map/ppermute | solution.py:35
  160.2 4.7 %collective-permute-start.18 = (f32[3,64,8]{1,2,0:T(8,128)S(1)}, f32[3,64,8]{1,2,0:T(8,128)}, u32[]{:S(2)}, u32[]{:S(2)}) collective-permute-start(f32[3,64,8]{1,2,0:T(8,128)S(1)} %bitcast.562), channel_id=1, source_target_pairs={{4,0},{0,4},{5,1},{1,5},{6,2},{2,6},{7,3},{3,7},{12,8},{8,12},{13,... | collective-permute-start | bytes 18440 | tf_op jit(solution)/shard_map/ppermute | solution.py:36
  162.2 3.9 %collective-permute-start.19 = (f32[3,64,8]{1,2,0:T(8,128)}, f32[3,64,8]{1,2,0:T(8,128)S(1)}, u32[]{:S(2)}, u32[]{:S(2)}) collective-permute-start(f32[3,64,8]{1,2,0:T(8,128)} %bitcast.567), channel_id=1, source_target_pairs={{0,4},{4,0},{1,5},{5,1},{2,6},{6,2},{3,7},{7,3},{8,12},{12,8},{9,1... | collective-permute-start | bytes 18440 | tf_op jit(solution)/shard_map/ppermute | solution.py:35
  163.1 4.6 %collective-permute-start.16 = (f32[3,64,128]{2,1,0:T(8,128)}, f32[3,64,128]{2,1,0:T(8,128)}, u32[]{:S(2)}, u32[]{:S(2)}) collective-permute-start(f32[3,64,128]{2,1,0:T(8,128)} %bitcast.555), channel_id=1, source_target_pairs={{8,0},{16,8},{24,16},{0,24},{9,1},{17,9},{25,17},{1,25},{10,2},{18... | collective-permute-start | bytes 294920 | tf_op jit(solution)/shard_map/ppermute | solution.py:36
  163.6 4.7 %collective-permute-start.17 = (f32[3,64,128]{2,1,0:T(8,128)}, f32[3,64,128]{2,1,0:T(8,128)}, u32[]{:S(2)}, u32[]{:S(2)}) collective-permute-start(f32[3,64,128]{2,1,0:T(8,128)} %bitcast.552), channel_id=1, source_target_pairs={{0,8},{8,16},{16,24},{24,0},{1,9},{9,17},{17,25},{25,1},{2,10},{10... | collective-permute-start | bytes 294920 | tf_op jit(solution)/shard_map/ppermute | solution.py:35
  168.4 5.5 %copy-start.35 = (f32[64,8,128]{2,1,0:T(8,128)S(1)}, f32[64,8,128]{2,1,0:T(8,128)}, u32[]{:S(2)}) copy-start(f32[64,8,128]{2,1,0:T(8,128)} %get-tuple-element.49) | copy-start | bytes 786436
  168.4 5.5 %copy-start.37 = (f32[64,8,128]{2,1,0:T(8,128)S(1)}, f32[64,8,128]{2,1,0:T(8,128)}, u32[]{:S(2)}) copy-start(f32[64,8,128]{2,1,0:T(8,128)} %copy-done.36) | copy-start | bytes 786436
  168.4 5.5 %copy-start.49 = (f32[64,8,128]{2,1,0:T(8,128)S(1)}, f32[64,8,128]{2,1,0:T(8,128)}, u32[]{:S(2)}) copy-start(f32[64,8,128]{2,1,0:T(8,128)} %get-tuple-element.42) | copy-start | bytes 786436
  168.4 5.5 %copy-start.62 = (pred[64,8,128]{2,1,0:T(8,128)(4,1)S(1)}, pred[64,8,128]{2,1,0:T(8,128)(4,1)}, u32[]{:S(2)}) copy-start(pred[64,8,128]{2,1,0:T(8,128)(4,1)} %copy-done.61) | copy-start | bytes 196612
  168.4 5.5 %copy-start.64 = (pred[64,8,128]{2,1,0:T(8,128)(4,1)S(1)}, pred[64,8,128]{2,1,0:T(8,128)(4,1)}, u32[]{:S(2)}) copy-start(pred[64,8,128]{2,1,0:T(8,128)(4,1)} %copy-done.63) | copy-start | bytes 196612
  168.4 5.5 %copy-start.66 = (pred[64,8,128]{2,1,0:T(8,128)(4,1)S(1)}, pred[64,8,128]{2,1,0:T(8,128)(4,1)}, u32[]{:S(2)}) copy-start(pred[64,8,128]{2,1,0:T(8,128)(4,1)} %copy-done.65) | copy-start | bytes 196612
  168.4 5.5 %copy-start.68 = (pred[64,8,128]{2,1,0:T(8,128)(4,1)S(1)}, pred[64,8,128]{2,1,0:T(8,128)(4,1)}, u32[]{:S(2)}) copy-start(pred[64,8,128]{2,1,0:T(8,128)(4,1)} %copy-done.67) | copy-start | bytes 196612
  168.5 5.5 %copy-start.70 = (pred[64,8,128]{2,1,0:T(8,128)(4,1)S(1)}, pred[64,8,128]{2,1,0:T(8,128)(4,1)}, u32[]{:S(2)}) copy-start(pred[64,8,128]{2,1,0:T(8,128)(4,1)} %copy-done.69) | copy-start | bytes 196612
  168.5 5.5 %copy-start.72 = (pred[64,8,128]{2,1,0:T(8,128)(4,1)S(1)}, pred[64,8,128]{2,1,0:T(8,128)(4,1)}, u32[]{:S(2)}) copy-start(pred[64,8,128]{2,1,0:T(8,128)(4,1)} %copy-done.71) | copy-start | bytes 196612
  168.5 5.5 %copy-start.74 = (pred[64,8,128]{2,1,0:T(8,128)(4,1)S(1)}, pred[64,8,128]{2,1,0:T(8,128)(4,1)}, u32[]{:S(2)}) copy-start(pred[64,8,128]{2,1,0:T(8,128)(4,1)} %copy-done.73) | copy-start | bytes 196612
  168.5 5.5 %copy-start.76 = (pred[64,8,128]{2,1,0:T(8,128)(4,1)S(1)}, pred[64,8,128]{2,1,0:T(8,128)(4,1)}, u32[]{:S(2)}) copy-start(pred[64,8,128]{2,1,0:T(8,128)(4,1)} %copy-done.75) | copy-start | bytes 196612
  188.4 14.2 %copy-start.101 = (f32[64,8,128]{2,1,0:T(8,128)S(1)}, f32[64,8,128]{2,1,0:T(8,128)}, u32[]{:S(2)}) copy-start(f32[64,8,128]{2,1,0:T(8,128)} %get-tuple-element.9) | copy-start | bytes 786436
  (80 other events, 234.0 us)

commit v2 on v1

v2 whole, which is shorter than its diff:
```python
import jax
import jax.numpy as jnp
from jax import lax
from jax.experimental import pallas as pl
from jax.experimental.pallas import tpu as pltpu
from jax.sharding import PartitionSpec as P

SECTIONS = 4


SOFTEN = 0.5
HEAT_CARRY = 0.5
SILL_RATE = 0.3
SILL_HEAT = 2.5
WATER_INPUT = 0.2
CARBON_INPUT = 0.1
MELT_SHARPNESS = 4.0
SOLIDUS = 1.0
DEPRESSION = 0.5
MELT_RATE = 0.5
LATENT = 0.3

ROWS = 8
LANES = 128
f32 = jnp.float32


def ring_perms(axis):
    count = lax.axis_size(axis)
    forward = [(i, (i + 1) % count) for i in range(count)]
    backward = [((i + 1) % count, i) for i in range(count)]
    return forward, backward


def iotas():
    sub = lax.broadcasted_iota(jnp.int32, (ROWS, LANES), 0)
    lane = lax.broadcasted_iota(jnp.int32, (ROWS, LANES), 1)
    return sub, lane


class EdgeAcc:
    def __init__(self, count, y_first, y_last):
        zero = jnp.zeros((ROWS, LANES), f32)
        self.xf = [zero] * count
        self.xl = [zero] * count
        self.yf = list(y_first)
        self.yl = list(y_last)

    def add(self, planes, b, d, sub, lane):
        at_b = sub == b
        at_d = lane == d
        for f, v in enumerate(planes):
            self.xf[f] = jnp.where(at_b, pltpu.roll(v, b, 0), self.xf[f])
            self.xl[f] = jnp.where(at_b, pltpu.roll(v, (b + 1) % ROWS, 0), self.xl[f])
            self.yf[f] = jnp.where(at_d, pltpu.roll(v, d % LANES, 1), self.yf[f])
            self.yl[f] = jnp.where(at_d, pltpu.roll(v, (d + 1) % LANES, 1), self.yl[f])


def x_minus(v, lo_tile, b, sub):
    return jnp.where(sub == 0, pltpu.roll(lo_tile, (ROWS - b) % ROWS, 0), pltpu.roll(v, 1, 0))


def x_plus(v, hi_tile, b, sub):
    return jnp.where(
        sub == ROWS - 1, pltpu.roll(hi_tile, (ROWS - 1 - b) % ROWS, 0), pltpu.roll(v, ROWS - 1, 0)
    )


def y_minus(v, lo_cols, d, lane):
    return jnp.where(lane == 0, pltpu.roll(lo_cols, (LANES - d) % LANES, 1), pltpu.roll(v, 1, 1))


def y_plus(v, hi_cols, d, lane):
    return jnp.where(
        lane == LANES - 1,
        pltpu.roll(hi_cols, (LANES - 1 - d) % LANES, 1),
        pltpu.roll(v, LANES - 1, 1),
    )


def prep_kernel(tab_ref, layer_ref, h_ref, w_ref, c_ref,
                co_ref, sxf_ref, sxl_ref, syf_ref, syl_ref, cxf_ref, cxl_ref, cyf_ref, cyl_ref):
    groups = layer_ref.shape[0] // ROWS
    layers_count = tab_ref.shape[1]
    sub, lane = iotas()
    zero = jnp.zeros((ROWS, LANES), f32)

    def group(a, carry):
        sy_f, sy_l, cy_f, cy_l = carry
        s_acc = EdgeAcc(3, sy_f, sy_l)
        cx_acc = EdgeAcc(2, [zero, zero], [zero, zero])
        cy_acc = EdgeAcc(2, cy_f, cy_l)
        for b in range(ROWS):
            d = a * ROWS + b
            layer = layer_ref[d]
            vals = [zero] * 5
            for l in range(layers_count):
                hit = layer == l
                vals = [jnp.where(hit, tab_ref[k, l], vals[k]) for k in range(5)]
            for k in range(5):
                co_ref[k, d] = vals[k]
            s_acc.add([h_ref[d], w_ref[d], c_ref[d]], b, d, sub, lane)
            cx_acc.add([vals[0], vals[2]], b, d, sub, lane)
            cy_acc.add([vals[1], vals[3]], b, d, sub, lane)
        for f in range(3):
            sxf_ref[f, a] = s_acc.xf[f]
            sxl_ref[f, a] = s_acc.xl[f]
        for f in range(2):
            cxf_ref[f, a] = cx_acc.xf[f]
            cxl_ref[f, a] = cx_acc.xl[f]
        return (tuple(s_acc.yf), tuple(s_acc.yl), tuple(cy_acc.yf), tuple(cy_acc.yl))

    init = ((zero,) * 3, (zero,) * 3, (zero,) * 2, (zero,) * 2)
    sy_f, sy_l, cy_f, cy_l = lax.fori_loop(0, groups, group, init)
    for f in range(3):
        syf_ref[f] = sy_f[f]
        syl_ref[f] = sy_l[f]
    for f in range(2):
        cyf_ref[f] = cy_f[f]
        cyl_ref[f] = cy_l[f]


def section_kernel(h_ref, w_ref, c_ref, m_ref, sill_ref, co_ref,
                   sxlo_ref, sxhi_ref, sylo_ref, syhi_ref, cxlo_ref, cxhi_ref, cylo_ref, cyhi_ref,
                   ho_ref, wo_ref, co_out_ref, mo_ref, sxf_ref, sxl_ref, syf_ref, syl_ref):
    groups = h_ref.shape[0] // ROWS
    sub, lane = iotas()
    zero = jnp.zeros((ROWS, LANES), f32)
    sylo = [sylo_ref[f] for f in range(3)]
    syhi = [syhi_ref[f] for f in range(3)]
    cylo = [cylo_ref[f] for f in range(2)]
    cyhi = [cyhi_ref[f] for f in range(2)]

    def group(a, carry):
        y_f, y_l = carry
        acc = EdgeAcc(3, y_f, y_l)
        sxlo = [sxlo_ref[f, a] for f in range(3)]
        sxhi = [sxhi_ref[f, a] for f in range(3)]
        cxlo = [cxlo_ref[f, a] for f in range(2)]
        cxhi = [cxhi_ref[f, a] for f in range(2)]
        for b in range(ROWS):
            d = a * ROWS + b
            heat = h_ref[d]
            water = w_ref[d]
            carbon = c_ref[d]
            melt = m_ref[d]
            sill = sill_ref[d].astype(f32)
            cx = co_ref[0, d]
            cy = co_ref[1, d]
            vx = co_ref[2, d]
            vy = co_ref[3, d]
            mobile = [heat, water, carbon]
            q_xm = [x_minus(mobile[f], sxlo[f], b, sub) for f in range(3)]
            q_xp = [x_plus(mobile[f], sxhi[f], b, sub) for f in range(3)]
            q_ym = [y_minus(mobile[f], sylo[f], d, lane) for f in range(3)]
            q_yp = [y_plus(mobile[f], syhi[f], d, lane) for f in range(3)]
            cx_m = x_minus(cx, cxlo[0], b, sub)
            cx_p = x_plus(cx, cxhi[0], b, sub)
            vx_m = x_minus(vx, cxlo[1], b, sub)
            vx_p = x_plus(vx, cxhi[1], b, sub)
            cy_m = y_minus(cy, cylo[0], d, lane)
            cy_p = y_plus(cy, cyhi[0], d, lane)
            vy_m = y_minus(vy, cylo[1], d, lane)
            vy_p = y_plus(vy, cyhi[1], d, lane)
            soft = jnp.exp(-SOFTEN * heat)
            kx = cx * soft
            ky = cy * soft
            kx_m = cx_m * jnp.exp(-SOFTEN * q_xm[0])
            kx_p = cx_p * jnp.exp(-SOFTEN * q_xp[0])
            ky_m = cy_m * jnp.exp(-SOFTEN * q_ym[0])
            ky_p = cy_p * jnp.exp(-SOFTEN * q_yp[0])
            flux_x_lo = 0.5 * (kx_m + kx) * (heat - q_xm[0])
            flux_x_hi = 0.5 * (kx + kx_p) * (q_xp[0] - heat)
            flux_y_lo = 0.5 * (ky_m + ky) * (heat - q_ym[0])
            flux_y_hi = 0.5 * (ky + ky_p) * (q_yp[0] - heat)
            diffused = flux_x_hi - flux_x_lo + flux_y_hi - flux_y_lo
            fvx_m = 0.5 * (vx_m + vx)
            fvx_p = 0.5 * (vx + vx_p)
            fvy_m = 0.5 * (vy_m + vy)
            fvy_p = 0.5 * (vy + vy_p)
            inflow = []
            for f in range(3):
                lo_x = jnp.maximum(fvx_m, 0.0) * q_xm[f] + jnp.minimum(fvx_m, 0.0) * mobile[f]
                hi_x = jnp.maximum(fvx_p, 0.0) * mobile[f] + jnp.minimum(fvx_p, 0.0) * q_xp[f]
                lo_y = jnp.maximum(fvy_m, 0.0) * q_ym[f] + jnp.minimum(fvy_m, 0.0) * mobile[f]
                hi_y = jnp.maximum(fvy_p, 0.0) * mobile[f] + jnp.minimum(fvy_p, 0.0) * q_yp[f]
                inflow.append(lo_x - hi_x + lo_y - hi_y)
            heat_one = heat + diffused + HEAT_CARRY * inflow[0]
            water_two = water + inflow[1] + sill * WATER_INPUT
            carbon_two = carbon + inflow[2] + sill * CARBON_INPUT
            heat_two = heat_one + sill * SILL_RATE * (SILL_HEAT - heat_one)
            z = MELT_SHARPNESS * (heat_two - SOLIDUS + DEPRESSION * water_two)
            target = 1.0 / (1.0 + jnp.exp(-z))
            melt_two = melt + MELT_RATE * (target - melt)
            heat_three = heat_two - LATENT * (melt_two - melt)
            ho_ref[d] = heat_three
            wo_ref[d] = water_two
            co_out_ref[d] = carbon_two
            mo_ref[d] = melt_two
            acc.add([heat_three, water_two, carbon_two], b, d, sub, lane)
        for f in range(3):
            sxf_ref[f, a] = acc.xf[f]
            sxl_ref[f, a] = acc.xl[f]
        return (tuple(acc.yf), tuple(acc.yl))

    y_f, y_l = lax.fori_loop(0, groups, group, ((zero,) * 3, (zero,) * 3))
    for f in range(3):
        syf_ref[f] = y_f[f]
        syl_ref[f] = y_l[f]


def sweep_kernel(r_ref, cz_ref, y_ref, a_ref, b_ref, red_ref, c_s, g_s, vy_s, va_s):
    n = r_ref.shape[0]
    zero = jnp.zeros(r_ref.shape[1:], f32)
    one = jnp.ones(r_ref.shape[1:], f32)

    def conduct(i, carry):
        c_s[i] = cz_ref[i] * jnp.exp(-SOFTEN * r_ref[i])
        return carry

    lax.fori_loop(0, n, conduct, 0)

    def forward(i, carry):
        g_prev, vy_prev, va_prev = carry
        up = 0.5 * (c_s[i - 1] + c_s[i])
        down = 0.5 * (c_s[i] + c_s[i + 1])
        inv = 1.0 / (1.0 + up + down - up * g_prev)
        g = down * inv
        vy = (r_ref[i] + up * vy_prev) * inv
        va = (up * va_prev) * inv
        g_s[i] = g
        vy_s[i] = vy
        va_s[i] = va
        return g, vy, va

    lax.fori_loop(1, n - 1, forward, (zero, zero, one))

    def backward(k, carry):
        i = n - 2 - k
        y_next, a_next, b_next = carry
        g = g_s[i]
        y = vy_s[i] + g * y_next
        a = va_s[i] + g * a_next
        b = g * b_next
        y_ref[i] = y
        a_ref[i] = a
        b_ref[i] = b
        return y, a, b

    lax.fori_loop(0, n - 2, backward, (zero, zero, one))
    y_ref[0] = zero
    a_ref[0] = one
    b_ref[0] = zero
    y_ref[n - 1] = zero
    a_ref[n - 1] = zero
    b_ref[n - 1] = one
    up_first = 0.5 * (c_s[0] + c_s[1])
    up_last = 0.5 * (c_s[n - 2] + c_s[n - 1])
    red_ref[0] = 1.0 + up_first * (1.0 - a_ref[1])
    red_ref[1] = up_first * b_ref[1]
    red_ref[2] = r_ref[0] + up_first * y_ref[1]
    red_ref[3] = 1.0 + up_last * (1.0 - b_ref[n - 2])
    red_ref[4] = up_last * a_ref[n - 2]
    red_ref[5] = r_ref[n - 1] + up_last * y_ref[n - 2]
    red_ref[6] = c_s[0]
    red_ref[7] = c_s[n - 1]


def reduced_solve(red_all):
    count = red_all.shape[0]
    lower, diag, upper, side = [], [], [], []
    for j in range(count):
        p0, q0, s0, p1, q1, s1, c_first, c_last = [red_all[j, k] for k in range(8)]
        if j == 0:
            face = c_first
            lower.append(jnp.zeros_like(face))
        else:
            face = 0.5 * (red_all[j - 1, 7] + c_first)
            lower.append(face)
        diag.append(p0 + face)
        upper.append(q0)
        side.append(s0)
        if j + 1 < count:
            below = 0.5 * (c_last + red_all[j + 1, 6])
        else:
            below = jnp.zeros_like(c_last)
        lower.append(q1)
        diag.append(p1 + below)
        upper.append(below)
        side.append(s1)
    size = len(diag)
    ratios, values = [], []
    g_prev = jnp.zeros_like(diag[0])
    v_prev = jnp.zeros_like(diag[0])
    for k in range(size):
        inv = 1.0 / (diag[k] - lower[k] * g_prev)
        g_prev = upper[k] * inv
        v_prev = (side[k] + lower[k] * v_prev) * inv
        ratios.append(g_prev)
        values.append(v_prev)
    solved = [None] * size
    following = jnp.zeros_like(diag[0])
    for k in reversed(range(size)):
        following = values[k] + ratios[k] * following
        solved[k] = following
    return jnp.stack(solved)


def sds(shape):
    return jax.ShapeDtypeStruct(shape, f32)


def exchange(xf, xl, yf, yl):
    east_fwd, east_bwd = ring_perms("east")
    north_fwd, north_bwd = ring_perms("north")
    xlo = lax.ppermute(xl, "east", east_fwd)
    xhi = lax.ppermute(xf, "east", east_bwd)
    ylo = lax.ppermute(yl, "north", north_fwd)
    yhi = lax.ppermute(yf, "north", north_bwd)
    return xlo, xhi, ylo, yhi


def local(
    thermal_field,
    liquid_fraction,
    steam_content_grid,
    carbonic_gas_grid,
    stratum_number_grid,
    injection_flags,
    lateral_transmissivity,
    vertical_transmissivity,
    stratum_advection_offsets,
):
    shape = thermal_field.shape
    n = shape[0]
    groups = n // ROWS
    assert shape[1:] == (ROWS, LANES) and n % ROWS == 0 and n <= LANES
    table = jnp.concatenate(
        [lateral_transmissivity, stratum_advection_offsets, vertical_transmissivity[None]], 0
    )
    vmem = pltpu.MemorySpace.VMEM
    smem_spec = pl.BlockSpec(memory_space=pltpu.SMEM)
    vspec = pl.BlockSpec(memory_space=vmem)
    xs3 = sds((3, groups, ROWS, LANES))
    ys3 = sds((3, ROWS, LANES))
    xs2 = sds((2, groups, ROWS, LANES))
    ys2 = sds((2, ROWS, LANES))
    co, sxf, sxl, syf, syl, cxf, cxl, cyf, cyl = pl.pallas_call(
        prep_kernel,
        out_shape=(sds((5,) + shape), xs3, xs3, ys3, ys3, xs2, xs2, ys2, ys2),
        in_specs=[smem_spec, vspec, vspec, vspec, vspec],
    )(table, stratum_number_grid, thermal_field, steam_content_grid, carbonic_gas_grid)
    cxlo, cxhi, cylo, cyhi = exchange(cxf, cxl, cyf, cyl)

    heat, water, carbon, melt = thermal_field, steam_content_grid, carbonic_gas_grid, liquid_fraction
    for section_no in range(SECTIONS):
        sxlo, sxhi, sylo, syhi = exchange(sxf, sxl, syf, syl)
        heat, water, carbon, melt, sxf, sxl, syf, syl = pl.pallas_call(
            section_kernel,
            out_shape=(sds(shape), sds(shape), sds(shape), sds(shape), xs3, xs3, ys3, ys3),
        )(heat, water, carbon, melt, injection_flags, co,
          sxlo, sxhi, sylo, syhi, cxlo, cxhi, cylo, cyhi)

    y, a, b, red = pl.pallas_call(
        sweep_kernel,
        out_shape=(sds(shape), sds(shape), sds(shape), sds((8,) + shape[1:])),
        scratch_shapes=[pltpu.VMEM(shape, f32)] * 4,
    )(heat, co[4])
    count = lax.axis_size("depth")
    rank = lax.axis_index("depth")
    received = [red]
    for k in range(1, count):
        received.append(lax.ppermute(red, "depth", [(i, (i + k) % count) for i in range(count)]))
    stacked = jnp.stack(received)
    red_all = jnp.take(stacked, (rank - jnp.arange(count)) % count, axis=0)
    solved = reduced_solve(red_all)
    first = lax.dynamic_index_in_dim(solved, 2 * rank, keepdims=False)
    last = lax.dynamic_index_in_dim(solved, 2 * rank + 1, keepdims=False)
    heat_next = y + a * first[None] + b * last[None]
    return (heat_next, melt, water, carbon)


def solution(mesh):
    placed = (
        P("depth", "east", "north"),
        P("depth", "east", "north"),
        P("depth", "east", "north"),
        P("depth", "east", "north"),
        P("depth", "east", "north"),
        P("depth", "east", "north"),
        P(),
        P(),
        P(),
    )
    return jax.shard_map(
        local,
        mesh=mesh,
        in_specs=placed,
        out_specs=(
            P("depth", "east", "north"),
            P("depth", "east", "north"),
            P("depth", "east", "north"),
            P("depth", "east", "north"),
        ),
        check_vma=False,
    )
```

time: 207 us -> 91.7 us (0.44)
  other arithmetic: 115 us -> 3.06 us
  local copies, waits for them, and re-layouts: 52 us -> 4.9 us
  Pallas kernels: 3.2 us -> 34.6 us
  waiting for transfers between devices: 2.07 us -> 18.3 us
  blocking collectives: 13.9 us -> 0 us
  starting transfers between devices: 16.2 us -> 29.5 us
    select_n x7 -> x2, other arithmetic: 54.6 us -> 0.09 us  [local(): red_all = jnp.take(stacked, (rank - jnp.arange(count)) % count, axis=0)]
    slice x35 -> x0, local copies, waits for them, and re-layouts: 33.8 us -> none  [the longest x11 12.3 us: shifted(): lax.slice_in_dim(block, 0, n - 1, axis=dim)]
    pallas_call x1 -> x6, Pallas kernels: 3.2 us -> 34.6 us  [the longest x4 26.7 us: local(): pl.pallas_call(section_kernel, out_shape=(sds(shape), sds(shape), sds(sha...]
    broadcast_in_dim x3 -> x0, other arithmetic: 22.2 us -> none  [the longest x2 14.7 us: shifted(): lo = jnp.expand_dims(low, dim)]
    ppermute x20 -> x23, waiting for transfers between devices: 2.07 us -> 18.3 us  [the longest x5 7.76 us: exchange(): yhi = lax.ppermute(yf, 'north', north_bwd)]
    all_gather x1 -> x0, blocking collectives: 13.9 us -> none  [local(): red_all = lax.all_gather(red, 'depth')]
    ppermute x20 -> x23, starting transfers between devices: 16.2 us -> 29.5 us  [the longest x5 8.28 us: exchange(): ylo = lax.ppermute(yl, 'north', north_fwd)]
    sub x4 -> x0, other arithmetic: 13.1 us -> none  [lateral_step(): inflow = carried_x_lo - carried_x_hi + carried_y_lo - carried_y_hi]
  transfers between devices with their start and end apart: 20 -> 23, of which waited for: 4 -> 13; matrix products, arithmetic and copies ran while one was open for 52% -> 2% of each run, Pallas kernels for 0% -> 0%
where the time goes in v2:
time: 91.7 us; the launch traced here: 91.3 us
  Pallas kernels  34.6 us (38%)
  starting transfers between devices  29.5 us (32%)
  waiting for transfers between devices  18.3 us (20%)
  local copies, waits for them, and re-layouts  4.9 us (5%)
  other arithmetic  3.06 us (3%)
  between operations  0.93 us (1%)
    pallas_call x4, Pallas kernels, local(): pl.pallas_call(section_kernel, out_shape=(sds(shape), sds(shape), sds(sha...  26.7 us
    ppermute x5, starting transfers between devices, exchange(): ylo = lax.ppermute(yl, 'north', north_fwd)  8.28 us
    ppermute x5, starting transfers between devices, exchange(): xhi = lax.ppermute(xf, 'east', east_bwd)  8.26 us
    ppermute x5, waiting for transfers between devices, exchange(): yhi = lax.ppermute(yf, 'north', north_bwd)  7.76 us
    ppermute x5, waiting for transfers between devices, exchange(): ylo = lax.ppermute(yl, 'north', north_fwd)  7.74 us
    ppermute x5, starting transfers between devices, exchange(): yhi = lax.ppermute(yf, 'north', north_bwd)  6.07 us
    ppermute x3, starting transfers between devices, local(): lax.ppermute(red, 'depth', [(i, (i + k) % count) for i in range(count)])  5.57 us
    pallas_call x1, Pallas kernels, local(): pl.pallas_call(prep_kernel, out_shape=(sds((5,) + shape), xs3, xs3, ys3,...  4.03 us
  transfers between devices with their start and end apart: 23, of which 13 were waited for; matrix products, arithmetic and copies ran while one was open for 2% of the time, Pallas kernels for 0%

profile of v2, /device:TPU:0, one launch (start us, length us, event | category | flops | bytes accessed | tf_op | source)
XLA Modules:
  0.0 91.3 jit_solution(5278759512248424919)
XLA Ops:
  0.6 1.3 %pad_maximum_fusion.1.tab_ref = f32[5,12]{1,0:T(8,128)} fusion(f32[1,12]{1,0:T(1,128)} %bitcast.221, f32[2,12]{1,0:T(2,128)} %param.17, f32[2,12]{1,0:T(2,128)} %param.15), kind=kLoop, calls=%fused_computation.87 | loop fusion | flops 120 | bytes 480 | tf_op jit(solution)/shard_map/concatenate | solution.py:338
  1.9 4.0 %shard_map.120 = (f32[5,64,8,128]{3,2,1,0:T(8,128)}, f32[3,8,8,128]{3,2,1,0:T(8,128)}, f32[3,8,8,128]{3,2,1,0:T(8,128)}, f32[3,8,128]{2,1,0:T(8,128)}, f32[3,8,1...) custom-call(f32[5,12]{1,0:T(8,128)} %pad_maximum_fusion.1.tab_ref, ...), custom_call_target="tpu_custom_call" | custom-call | tf_op jit(solution)/shard_map/pallas_call | solution.py:348
  6.0 0.5 collective-permute-start
  6.5 2.0 %collective-permute-start.1 = (f32[3,8,8,128]{3,2,1,0:T(8,128)}, f32[3,8,8,128]{3,2,1,0:T(8,128)S(1)}, u32[]{:S(2)}, u32[]{:S(2)}) collective-permute-start(f32[3,8,8,128]{3,2,1,0:T(8,128)} %get-tuple-element.47), channel_id=1, source_target_pairs={{8,0},{16,8},{24,16},{0,24},{9,1},{17,9},{25,17},{1,25},{10,2},{18... | collective-permute-start | bytes 294920 | tf_op jit(solution)/shard_map/ppermute | solution.py:317
  8.5 0.6 collective-permute-start.4
  9.1 1.1 %collective-permute-start.5 = (f32[2,8,8,128]{3,2,1,0:T(8,128)}, f32[2,8,8,128]{3,2,1,0:T(8,128)S(1)}, u32[]{:S(2)}, u32[]{:S(2)}) collective-permute-start(f32[2,8,8,128]{3,2,1,0:T(8,128)} %get-tuple-element.51), channel_id=1, source_target_pairs={{8,0},{16,8},{24,16},{0,24},{9,1},{17,9},{25,17},{1,25},{10,2},{18... | collective-permute-start | bytes 196616 | tf_op jit(solution)/shard_map/ppermute | solution.py:317
  10.2 2.3 %collective-permute-start.6 = (f32[2,8,128]{2,1,0:T(8,128)}, f32[2,8,128]{2,1,0:T(8,128)S(1)}, u32[]{:S(2)}, u32[]{:S(2)}) collective-permute-start(f32[2,8,128]{2,1,0:T(8,128)} %get-tuple-element.52), channel_id=1, source_target_pairs={{0,4},{4,0},{1,5},{5,1},{2,6},{6,2},{3,7},{7,3},{8,12},{12,8},{9,1... | collective-permute-start | bytes 24584 | tf_op jit(solution)/shard_map/ppermute | solution.py:318
  12.5 1.8 %collective-permute-done.6.cylo_ref = f32[2,8,128]{2,1,0:T(8,128)S(1)} collective-permute-done((f32[2,8,128]{2,1,0:T(8,128)}, f32[2,8,128]{2,1,0:T(8,128)S(1)}, u32[]{:S(2)}, u32[]{:S(2)}) %collective-permute-start.6) | collective-permute-done | bytes 8224 | tf_op jit(solution)/shard_map/ppermute | solution.py:318
  14.3 2.0 %collective-permute-start.7 = (f32[2,8,128]{2,1,0:T(8,128)}, f32[2,8,128]{2,1,0:T(8,128)S(1)}, u32[]{:S(2)}, u32[]{:S(2)}) collective-permute-start(f32[2,8,128]{2,1,0:T(8,128)} %get-tuple-element.53), channel_id=1, source_target_pairs={{4,0},{0,4},{5,1},{1,5},{6,2},{2,6},{7,3},{3,7},{12,8},{8,12},{13,... | collective-permute-start | bytes 24584 | tf_op jit(solution)/shard_map/ppermute | solution.py:319
  16.3 1.8 %collective-permute-done.7.cyhi_ref = f32[2,8,128]{2,1,0:T(8,128)S(1)} collective-permute-done((f32[2,8,128]{2,1,0:T(8,128)}, f32[2,8,128]{2,1,0:T(8,128)S(1)}, u32[]{:S(2)}, u32[]{:S(2)}) %collective-permute-start.7) | collective-permute-done | bytes 8224 | tf_op jit(solution)/shard_map/ppermute | solution.py:319
  18.2 2.0 %collective-permute-start.2 = (f32[3,8,128]{2,1,0:T(8,128)}, f32[3,8,128]{2,1,0:T(8,128)S(1)}, u32[]{:S(2)}, u32[]{:S(2)}) collective-permute-start(f32[3,8,128]{2,1,0:T(8,128)} %get-tuple-element.48), channel_id=1, source_target_pairs={{0,4},{4,0},{1,5},{5,1},{2,6},{6,2},{3,7},{7,3},{8,12},{12,8},{9,1... | collective-permute-start | bytes 36872 | tf_op jit(solution)/shard_map/ppermute | solution.py:318
  20.2 1.9 %collective-permute-done.2.sylo_ref = f32[3,8,128]{2,1,0:T(8,128)S(1)} collective-permute-done((f32[3,8,128]{2,1,0:T(8,128)}, f32[3,8,128]{2,1,0:T(8,128)S(1)}, u32[]{:S(2)}, u32[]{:S(2)}) %collective-permute-start.2) | collective-permute-done | bytes 12320 | tf_op jit(solution)/shard_map/ppermute | solution.py:318
  22.2 2.0 %collective-permute-start.3 = (f32[3,8,128]{2,1,0:T(8,128)}, f32[3,8,128]{2,1,0:T(8,128)S(1)}, u32[]{:S(2)}, u32[]{:S(2)}) collective-permute-start(f32[3,8,128]{2,1,0:T(8,128)} %get-tuple-element.49), channel_id=1, source_target_pairs={{4,0},{0,4},{5,1},{1,5},{6,2},{2,6},{7,3},{3,7},{12,8},{8,12},{13,... | collective-permute-start | bytes 36872 | tf_op jit(solution)/shard_map/ppermute | solution.py:319
  24.1 1.9 %collective-permute-done.3.syhi_ref = f32[3,8,128]{2,1,0:T(8,128)S(1)} collective-permute-done((f32[3,8,128]{2,1,0:T(8,128)}, f32[3,8,128]{2,1,0:T(8,128)S(1)}, u32[]{:S(2)}, u32[]{:S(2)}) %collective-permute-start.3) | collective-permute-done | bytes 12320 | tf_op jit(solution)/shard_map/ppermute | solution.py:319
  26.2 0.5 copy-done.22
  26.8 6.7 %shard_map.121 = (f32[64,8,128]{2,1,0:T(8,128)}, f32[64,8,128]{2,1,0:T(8,128)}, f32[64,8,128]{2,1,0:T(8,128)}, f32[64,8,128]{2,1,0:T(8,128)}, f32[3,8,8,128]{3,2...) custom-call(f32[64,8,128]{2,1,0:T(8,128)} %h_ref.3, f32[64,8,128]{2,1,0:T(8,128)} %w_ref.3, ...), custom_call_target="tpu_custom_call" | custom-call | tf_op jit(solution)/shard_map/pallas_call | solution.py:358
  33.5 1.7 %collective-permute-start.9 = (f32[3,8,8,128]{3,2,1,0:T(8,128)}, f32[3,8,8,128]{3,2,1,0:T(8,128)S(1)}, u32[]{:S(2)}, u32[]{:S(2)}) collective-permute-start(f32[3,8,8,128]{3,2,1,0:T(8,128)} %get-tuple-element.59), channel_id=1, source_target_pairs={{8,0},{16,8},{24,16},{0,24},{9,1},{17,9},{25,17},{1,25},{10,2},{18... | collective-permute-start | bytes 294920 | tf_op jit(solution)/shard_map/ppermute | solution.py:317
  35.3 2.0 %collective-permute-start.10 = (f32[3,8,128]{2,1,0:T(8,128)}, f32[3,8,128]{2,1,0:T(8,128)S(1)}, u32[]{:S(2)}, u32[]{:S(2)}) collective-permute-start(f32[3,8,128]{2,1,0:T(8,128)} %get-tuple-element.60), channel_id=1, source_target_pairs={{0,4},{4,0},{1,5},{5,1},{2,6},{6,2},{3,7},{7,3},{8,12},{12,8},{9,1... | collective-permute-start | bytes 36872 | tf_op jit(solution)/shard_map/ppermute | solution.py:318
  37.3 1.7 %slice_bitcast_fusion.cz_ref = f32[64,8,128]{2,1,0:T(8,128)} fusion(f32[5,64,8,128]{3,2,1,0:T(8,128)} %get-tuple-element.45.co_ref), kind=kLoop, calls=%fused_computation.2 | loop fusion | bytes 524288 | tf_op jit(solution)/shard_map/squeeze | solution.py:368
  39.0 0.2 collective-permute-done.10.sylo_ref
  39.2 2.0 %collective-permute-done.11.syhi_ref = f32[3,8,128]{2,1,0:T(8,128)S(1)} collective-permute-done((f32[3,8,128]{2,1,0:T(8,128)}, f32[3,8,128]{2,1,0:T(8,128)S(1)}, u32[]{:S(2)}, u32[]{:S(2)}) %collective-permute-start.11) | collective-permute-done | bytes 12320 | tf_op jit(solution)/shard_map/ppermute | solution.py:319
  41.2 0.6 copy-done.18
  41.8 6.7 %shard_map.122 = (f32[64,8,128]{2,1,0:T(8,128)}, f32[64,8,128]{2,1,0:T(8,128)}, f32[64,8,128]{2,1,0:T(8,128)}, f32[64,8,128]{2,1,0:T(8,128)}, f32[3,8,8,128]{3,2...) custom-call(f32[64,8,128]{2,1,0:T(8,128)} %get-tuple-element.54.h_ref, ...), custom_call_target="tpu_custom_call" | custom-call | tf_op jit(solution)/shard_map/pallas_call | solution.py:358
  48.6 1.7 %collective-permute-start.13 = (f32[3,8,8,128]{3,2,1,0:T(8,128)}, f32[3,8,8,128]{3,2,1,0:T(8,128)S(1)}, u32[]{:S(2)}, u32[]{:S(2)}) collective-permute-start(f32[3,8,8,128]{3,2,1,0:T(8,128)} %get-tuple-element.67), channel_id=1, source_target_pairs={{8,0},{16,8},{24,16},{0,24},{9,1},{17,9},{25,17},{1,25},{10,2},{18... | collective-permute-start | bytes 294920 | tf_op jit(solution)/shard_map/ppermute | solution.py:317
  50.3 0.1 collective-permute-start.14
  50.5 1.9 %collective-permute-start.15 = (f32[3,8,128]{2,1,0:T(8,128)}, f32[3,8,128]{2,1,0:T(8,128)S(1)}, u32[]{:S(2)}, u32[]{:S(2)}) collective-permute-start(f32[3,8,128]{2,1,0:T(8,128)} %get-tuple-element.69), channel_id=1, source_target_pairs={{4,0},{0,4},{5,1},{1,5},{6,2},{2,6},{7,3},{3,7},{12,8},{8,12},{13,... | collective-permute-start | bytes 36872 | tf_op jit(solution)/shard_map/ppermute | solution.py:319
  52.4 1.9 %collective-permute-done.14.sylo_ref = f32[3,8,128]{2,1,0:T(8,128)S(1)} collective-permute-done((f32[3,8,128]{2,1,0:T(8,128)}, f32[3,8,128]{2,1,0:T(8,128)S(1)}, u32[]{:S(2)}, u32[]{:S(2)}) %collective-permute-start.14) | collective-permute-done | bytes 12320 | tf_op jit(solution)/shard_map/ppermute | solution.py:318
  54.2 0.1 collective-permute-done.15.syhi_ref
  54.4 0.4 copy-done.20
  54.8 0.1 copy-done.21
  55.1 6.7 %shard_map.123 = (f32[64,8,128]{2,1,0:T(8,128)}, f32[64,8,128]{2,1,0:T(8,128)}, f32[64,8,128]{2,1,0:T(8,128)}, f32[64,8,128]{2,1,0:T(8,128)}, f32[3,8,8,128]{3,2...) custom-call(f32[64,8,128]{2,1,0:T(8,128)} %get-tuple-element.62.h_ref, ...), custom_call_target="tpu_custom_call" | custom-call | tf_op jit(solution)/shard_map/pallas_call | solution.py:358
  61.9 1.7 %collective-permute-start.17 = (f32[3,8,8,128]{3,2,1,0:T(8,128)}, f32[3,8,8,128]{3,2,1,0:T(8,128)S(1)}, u32[]{:S(2)}, u32[]{:S(2)}) collective-permute-start(f32[3,8,8,128]{3,2,1,0:T(8,128)} %get-tuple-element.75), channel_id=1, source_target_pairs={{8,0},{16,8},{24,16},{0,24},{9,1},{17,9},{25,17},{1,25},{10,2},{18... | collective-permute-start | bytes 294920 | tf_op jit(solution)/shard_map/ppermute | solution.py:317
  63.5 1.9 %collective-permute-start.18 = (f32[3,8,128]{2,1,0:T(8,128)}, f32[3,8,128]{2,1,0:T(8,128)S(1)}, u32[]{:S(2)}, u32[]{:S(2)}) collective-permute-start(f32[3,8,128]{2,1,0:T(8,128)} %get-tuple-element.76), channel_id=1, source_target_pairs={{0,4},{4,0},{1,5},{5,1},{2,6},{6,2},{3,7},{7,3},{8,12},{12,8},{9,1... | collective-permute-start | bytes 36872 | tf_op jit(solution)/shard_map/ppermute | solution.py:318
  65.4 0.1 collective-permute-start.19
  65.6 1.9 %collective-permute-done.18.sylo_ref = f32[3,8,128]{2,1,0:T(8,128)S(1)} collective-permute-done((f32[3,8,128]{2,1,0:T(8,128)}, f32[3,8,128]{2,1,0:T(8,128)S(1)}, u32[]{:S(2)}, u32[]{:S(2)}) %collective-permute-start.18) | collective-permute-done | bytes 12320 | tf_op jit(solution)/shard_map/ppermute | solution.py:318
  67.4 1.9 %collective-permute-done.19.syhi_ref = f32[3,8,128]{2,1,0:T(8,128)S(1)} collective-permute-done((f32[3,8,128]{2,1,0:T(8,128)}, f32[3,8,128]{2,1,0:T(8,128)S(1)}, u32[]{:S(2)}, u32[]{:S(2)}) %collective-permute-start.19) | collective-permute-done | bytes 12320 | tf_op jit(solution)/shard_map/ppermute | solution.py:319
  69.4 0.6 copy-done.19
  70.0 6.7 %shard_map.124 = (f32[64,8,128]{2,1,0:T(8,128)}, f32[64,8,128]{2,1,0:T(8,128)}, f32[64,8,128]{2,1,0:T(8,128)}, f32[64,8,128]{2,1,0:T(8,128)}, f32[3,8,8,128]{3,2...) custom-call(f32[64,8,128]{2,1,0:T(8,128)} %get-tuple-element.70.h_ref, ...), custom_call_target="tpu_custom_call" | custom-call | tf_op jit(solution)/shard_map/pallas_call | solution.py:358
  76.7 3.8 %shard_map.125 = (f32[64,8,128]{2,1,0:T(8,128)}, f32[64,8,128]{2,1,0:T(8,128)}, f32[64,8,128]{2,1,0:T(8,128)}, f32[8,8,128]{2,1,0:T(8,128)}) custom-call(f32[64,8,128]{2,1,0:T(8,128)} %get-tuple-element.78.r_ref, f32[64,8,128]{2,1,0:T(8,128)} %slice_bitcast_fusion.cz_ref), custom_call_target="tpu_custom_call" | custom-call | tf_op jit(solution)/shard_map/pallas_call | solution.py:364
  80.5 1.6 %collective-permute-start.20 = (f32[8,8,128]{2,1,0:T(8,128)}, f32[8,8,128]{2,1,0:T(8,128)S(1)}, u32[]{:S(2)}, u32[]{:S(2)}) collective-permute-start(f32[8,8,128]{2,1,0:T(8,128)} %get-tuple-element.81), channel_id=1, source_target_pairs={{0,1},{1,2},{2,3},{3,0},{4,5},{5,6},{6,7},{7,4},{8,9},{9,10},{10,1... | collective-permute-start | bytes 98312 | tf_op jit(solution)/shard_map/ppermute | solution.py:373
  82.2 2.6 %collective-permute-start.21 = (f32[8,8,128]{2,1,0:T(8,128)}, f32[8,8,128]{2,1,0:T(8,128)S(1)}, u32[]{:S(2)}, u32[]{:S(2)}) collective-permute-start(f32[8,8,128]{2,1,0:T(8,128)} %get-tuple-element.81), channel_id=1, source_target_pairs={{0,2},{1,3},{2,0},{3,1},{4,6},{5,7},{6,4},{7,5},{8,10},{9,11},{10,... | collective-permute-start | bytes 98312 | tf_op jit(solution)/shard_map/ppermute | solution.py:373
  84.7 1.3 %collective-permute-start.22 = (f32[8,8,128]{2,1,0:T(8,128)}, f32[8,8,128]{2,1,0:T(8,128)S(1)}, u32[]{:S(2)}, u32[]{:S(2)}) collective-permute-start(f32[8,8,128]{2,1,0:T(8,128)} %get-tuple-element.81), channel_id=1, source_target_pairs={{0,3},{1,0},{2,1},{3,2},{4,7},{5,4},{6,5},{7,6},{8,11},{9,8},{10,9... | collective-permute-start | bytes 98312 | tf_op jit(solution)/shard_map/ppermute | solution.py:373
  86.1 0.4 collective-permute-done.20
  86.5 0.7 collective-permute-done.21
  87.2 1.7 %collective-permute-done.22 = f32[8,8,128]{2,1,0:T(8,128)S(1)} collective-permute-done((f32[8,8,128]{2,1,0:T(8,128)}, f32[8,8,128]{2,1,0:T(8,128)S(1)}, u32[]{:S(2)}, u32[]{:S(2)}) %collective-permute-start.22) | collective-permute-done | bytes 32800 | tf_op jit(solution)/shard_map/ppermute | solution.py:373
  88.9 0.8 pad_maximum_fusion
  89.6 0.6 gather_fusion
  90.5 0.7 multiply_add_fusion
  (70 shorter events, 1.1 us)
Async XLA Ops:
  6.0 20.1 %collective-permute-start = (f32[3,8,8,128]{3,2,1,0:T(8,128)}, f32[3,8,8,128]{3,2,1,0:T(8,128)S(1)}, u32[]{:S(2)}, u32[]{:S(2)}) collective-permute-start(f32[3,8,8,128]{3,2,1,0:T(8,128)} %get-tuple-element.46), channel_id=1, source_target_pairs={{0,8},{8,16},{16,24},{24,0},{1,9},{9,17},{17,25},{25,1},{2,10},{10... | collective-permute-start | bytes 294920 | tf_op jit(solution)/shard_map/ppermute | solution.py:316
  6.5 19.6 %collective-permute-start.1 = (f32[3,8,8,128]{3,2,1,0:T(8,128)}, f32[3,8,8,128]{3,2,1,0:T(8,128)S(1)}, u32[]{:S(2)}, u32[]{:S(2)}) collective-permute-start(f32[3,8,8,128]{3,2,1,0:T(8,128)} %get-tuple-element.47), channel_id=1, source_target_pairs={{8,0},{16,8},{24,16},{0,24},{9,1},{17,9},{25,17},{1,25},{10,2},{18... | collective-permute-start | bytes 294920 | tf_op jit(solution)/shard_map/ppermute | solution.py:317
  8.5 17.6 %collective-permute-start.4 = (f32[2,8,8,128]{3,2,1,0:T(8,128)}, f32[2,8,8,128]{3,2,1,0:T(8,128)S(1)}, u32[]{:S(2)}, u32[]{:S(2)}) collective-permute-start(f32[2,8,8,128]{3,2,1,0:T(8,128)} %get-tuple-element.50), channel_id=1, source_target_pairs={{0,8},{8,16},{16,24},{24,0},{1,9},{9,17},{17,25},{25,1},{2,10},{10... | collective-permute-start | bytes 196616 | tf_op jit(solution)/shard_map/ppermute | solution.py:316
  9.1 17.0 %collective-permute-start.5 = (f32[2,8,8,128]{3,2,1,0:T(8,128)}, f32[2,8,8,128]{3,2,1,0:T(8,128)S(1)}, u32[]{:S(2)}, u32[]{:S(2)}) collective-permute-start(f32[2,8,8,128]{3,2,1,0:T(8,128)} %get-tuple-element.51), channel_id=1, source_target_pairs={{8,0},{16,8},{24,16},{0,24},{9,1},{17,9},{25,17},{1,25},{10,2},{18... | collective-permute-start | bytes 196616 | tf_op jit(solution)/shard_map/ppermute | solution.py:317
  10.2 4.1 %collective-permute-start.6 = (f32[2,8,128]{2,1,0:T(8,128)}, f32[2,8,128]{2,1,0:T(8,128)S(1)}, u32[]{:S(2)}, u32[]{:S(2)}) collective-permute-start(f32[2,8,128]{2,1,0:T(8,128)} %get-tuple-element.52), channel_id=1, source_target_pairs={{0,4},{4,0},{1,5},{5,1},{2,6},{6,2},{3,7},{7,3},{8,12},{12,8},{9,1... | collective-permute-start | bytes 24584 | tf_op jit(solution)/shard_map/ppermute | solution.py:318
  14.3 11.8 %copy-start.5 = (f32[2,8,128]{2,1,0:T(8,128)}, f32[2,8,128]{2,1,0:T(8,128)S(1)}, u32[]{:S(2)}) copy-start(f32[2,8,128]{2,1,0:T(8,128)S(1)} %collective-permute-done.6.cylo_ref) | copy-start | bytes 24580
  14.3 3.9 %collective-permute-start.7 = (f32[2,8,128]{2,1,0:T(8,128)}, f32[2,8,128]{2,1,0:T(8,128)S(1)}, u32[]{:S(2)}, u32[]{:S(2)}) collective-permute-start(f32[2,8,128]{2,1,0:T(8,128)} %get-tuple-element.53), channel_id=1, source_target_pairs={{4,0},{0,4},{5,1},{1,5},{6,2},{2,6},{7,3},{3,7},{12,8},{8,12},{13,... | collective-permute-start | bytes 24584 | tf_op jit(solution)/shard_map/ppermute | solution.py:319
  18.2 8.0 %copy-start.6 = (f32[2,8,128]{2,1,0:T(8,128)}, f32[2,8,128]{2,1,0:T(8,128)S(1)}, u32[]{:S(2)}) copy-start(f32[2,8,128]{2,1,0:T(8,128)S(1)} %collective-permute-done.7.cyhi_ref) | copy-start | bytes 24580
  18.2 4.0 %collective-permute-start.2 = (f32[3,8,128]{2,1,0:T(8,128)}, f32[3,8,128]{2,1,0:T(8,128)S(1)}, u32[]{:S(2)}, u32[]{:S(2)}) collective-permute-start(f32[3,8,128]{2,1,0:T(8,128)} %get-tuple-element.48), channel_id=1, source_target_pairs={{0,4},{4,0},{1,5},{5,1},{2,6},{6,2},{3,7},{7,3},{8,12},{12,8},{9,1... | collective-permute-start | bytes 36872 | tf_op jit(solution)/shard_map/ppermute | solution.py:318
  22.2 4.0 %copy-start.17 = (f32[3,8,128]{2,1,0:T(8,128)}, f32[3,8,128]{2,1,0:T(8,128)S(1)}, u32[]{:S(2)}) copy-start(f32[3,8,128]{2,1,0:T(8,128)S(1)} %collective-permute-done.2.sylo_ref) | copy-start | bytes 36868
  22.2 3.9 %collective-permute-start.3 = (f32[3,8,128]{2,1,0:T(8,128)}, f32[3,8,128]{2,1,0:T(8,128)S(1)}, u32[]{:S(2)}, u32[]{:S(2)}) collective-permute-start(f32[3,8,128]{2,1,0:T(8,128)} %get-tuple-element.49), channel_id=1, source_target_pairs={{4,0},{0,4},{5,1},{1,5},{6,2},{2,6},{7,3},{3,7},{12,8},{8,12},{13,... | collective-permute-start | bytes 36872 | tf_op jit(solution)/shard_map/ppermute | solution.py:319
  26.1 0.6 copy-start.22
  26.1 0.6 copy-start
  26.1 0.6 copy-start.1
  26.1 0.7 copy-start.7
  26.1 0.7 copy-start.8
  33.5 7.7 %collective-permute-start.8 = (f32[3,8,8,128]{3,2,1,0:T(8,128)}, f32[3,8,8,128]{3,2,1,0:T(8,128)S(1)}, u32[]{:S(2)}, u32[]{:S(2)}) collective-permute-start(f32[3,8,8,128]{3,2,1,0:T(8,128)} %get-tuple-element.58), channel_id=1, source_target_pairs={{0,8},{8,16},{16,24},{24,0},{1,9},{9,17},{17,25},{25,1},{2,10},{10... | collective-permute-start | bytes 294920 | tf_op jit(solution)/shard_map/ppermute | solution.py:316
  33.5 7.6 %collective-permute-start.9 = (f32[3,8,8,128]{3,2,1,0:T(8,128)}, f32[3,8,8,128]{3,2,1,0:T(8,128)S(1)}, u32[]{:S(2)}, u32[]{:S(2)}) collective-permute-start(f32[3,8,8,128]{3,2,1,0:T(8,128)} %get-tuple-element.59), channel_id=1, source_target_pairs={{8,0},{16,8},{24,16},{0,24},{9,1},{17,9},{25,17},{1,25},{10,2},{18... | collective-permute-start | bytes 294920 | tf_op jit(solution)/shard_map/ppermute | solution.py:317
  35.3 3.9 %collective-permute-start.10 = (f32[3,8,128]{2,1,0:T(8,128)}, f32[3,8,128]{2,1,0:T(8,128)S(1)}, u32[]{:S(2)}, u32[]{:S(2)}) collective-permute-start(f32[3,8,128]{2,1,0:T(8,128)} %get-tuple-element.60), channel_id=1, source_target_pairs={{0,4},{4,0},{1,5},{5,1},{2,6},{6,2},{3,7},{7,3},{8,12},{12,8},{9,1... | collective-permute-start | bytes 36872 | tf_op jit(solution)/shard_map/ppermute | solution.py:318
  37.2 3.9 %collective-permute-start.11 = (f32[3,8,128]{2,1,0:T(8,128)}, f32[3,8,128]{2,1,0:T(8,128)S(1)}, u32[]{:S(2)}, u32[]{:S(2)}) collective-permute-start(f32[3,8,128]{2,1,0:T(8,128)} %get-tuple-element.61), channel_id=1, source_target_pairs={{4,0},{0,4},{5,1},{1,5},{6,2},{2,6},{7,3},{3,7},{12,8},{8,12},{13,... | collective-permute-start | bytes 36872 | tf_op jit(solution)/shard_map/ppermute | solution.py:319
  39.2 2.0 %copy-start.15 = (f32[3,8,128]{2,1,0:T(8,128)}, f32[3,8,128]{2,1,0:T(8,128)S(1)}, u32[]{:S(2)}) copy-start(f32[3,8,128]{2,1,0:T(8,128)S(1)} %collective-permute-done.10.sylo_ref) | copy-start | bytes 36868
  41.2 0.6 copy-start.18
  41.2 0.6 copy-start.9
  41.2 0.7 copy-start.11
  48.5 5.8 %collective-permute-start.12 = (f32[3,8,8,128]{3,2,1,0:T(8,128)}, f32[3,8,8,128]{3,2,1,0:T(8,128)S(1)}, u32[]{:S(2)}, u32[]{:S(2)}) collective-permute-start(f32[3,8,8,128]{3,2,1,0:T(8,128)} %get-tuple-element.66), channel_id=1, source_target_pairs={{0,8},{8,16},{16,24},{24,0},{1,9},{9,17},{17,25},{25,1},{2,10},{10... | collective-permute-start | bytes 294920 | tf_op jit(solution)/shard_map/ppermute | solution.py:316
  48.6 5.8 %collective-permute-start.13 = (f32[3,8,8,128]{3,2,1,0:T(8,128)}, f32[3,8,8,128]{3,2,1,0:T(8,128)S(1)}, u32[]{:S(2)}, u32[]{:S(2)}) collective-permute-start(f32[3,8,8,128]{3,2,1,0:T(8,128)} %get-tuple-element.67), channel_id=1, source_target_pairs={{8,0},{16,8},{24,16},{0,24},{9,1},{17,9},{25,17},{1,25},{10,2},{18... | collective-permute-start | bytes 294920 | tf_op jit(solution)/shard_map/ppermute | solution.py:317
  50.3 3.9 %collective-permute-start.14 = (f32[3,8,128]{2,1,0:T(8,128)}, f32[3,8,128]{2,1,0:T(8,128)S(1)}, u32[]{:S(2)}, u32[]{:S(2)}) collective-permute-start(f32[3,8,128]{2,1,0:T(8,128)} %get-tuple-element.68), channel_id=1, source_target_pairs={{0,4},{4,0},{1,5},{5,1},{2,6},{6,2},{3,7},{7,3},{8,12},{12,8},{9,1... | collective-permute-start | bytes 36872 | tf_op jit(solution)/shard_map/ppermute | solution.py:318
  50.5 3.9 %collective-permute-start.15 = (f32[3,8,128]{2,1,0:T(8,128)}, f32[3,8,128]{2,1,0:T(8,128)S(1)}, u32[]{:S(2)}, u32[]{:S(2)}) collective-permute-start(f32[3,8,128]{2,1,0:T(8,128)} %get-tuple-element.69), channel_id=1, source_target_pairs={{4,0},{0,4},{5,1},{1,5},{6,2},{2,6},{7,3},{3,7},{12,8},{8,12},{13,... | collective-permute-start | bytes 36872 | tf_op jit(solution)/shard_map/ppermute | solution.py:319
  54.2 0.6 copy-start.20
  54.4 0.6 copy-start.21
  54.4 0.6 copy-start.13
  54.4 0.7 copy-start.14
  61.7 7.6 %collective-permute-start.16 = (f32[3,8,8,128]{3,2,1,0:T(8,128)}, f32[3,8,8,128]{3,2,1,0:T(8,128)S(1)}, u32[]{:S(2)}, u32[]{:S(2)}) collective-permute-start(f32[3,8,8,128]{3,2,1,0:T(8,128)} %get-tuple-element.74), channel_id=1, source_target_pairs={{0,8},{8,16},{16,24},{24,0},{1,9},{9,17},{17,25},{25,1},{2,10},{10... | collective-permute-start | bytes 294920 | tf_op jit(solution)/shard_map/ppermute | solution.py:316
  61.9 7.5 %collective-permute-start.17 = (f32[3,8,8,128]{3,2,1,0:T(8,128)}, f32[3,8,8,128]{3,2,1,0:T(8,128)S(1)}, u32[]{:S(2)}, u32[]{:S(2)}) collective-permute-start(f32[3,8,8,128]{3,2,1,0:T(8,128)} %get-tuple-element.75), channel_id=1, source_target_pairs={{8,0},{16,8},{24,16},{0,24},{9,1},{17,9},{25,17},{1,25},{10,2},{18... | collective-permute-start | bytes 294920 | tf_op jit(solution)/shard_map/ppermute | solution.py:317
  63.5 3.9 %collective-permute-start.18 = (f32[3,8,128]{2,1,0:T(8,128)}, f32[3,8,128]{2,1,0:T(8,128)S(1)}, u32[]{:S(2)}, u32[]{:S(2)}) collective-permute-start(f32[3,8,128]{2,1,0:T(8,128)} %get-tuple-element.76), channel_id=1, source_target_pairs={{0,4},{4,0},{1,5},{5,1},{2,6},{6,2},{3,7},{7,3},{8,12},{12,8},{9,1... | collective-permute-start | bytes 36872 | tf_op jit(solution)/shard_map/ppermute | solution.py:318
  65.4 3.9 %collective-permute-start.19 = (f32[3,8,128]{2,1,0:T(8,128)}, f32[3,8,128]{2,1,0:T(8,128)S(1)}, u32[]{:S(2)}, u32[]{:S(2)}) collective-permute-start(f32[3,8,128]{2,1,0:T(8,128)} %get-tuple-element.77), channel_id=1, source_target_pairs={{4,0},{0,4},{5,1},{1,5},{6,2},{2,6},{7,3},{3,7},{12,8},{8,12},{13,... | collective-permute-start | bytes 36872 | tf_op jit(solution)/shard_map/ppermute | solution.py:319
  67.4 1.9 %copy-start.16 = (f32[3,8,128]{2,1,0:T(8,128)}, f32[3,8,128]{2,1,0:T(8,128)S(1)}, u32[]{:S(2)}) copy-start(f32[3,8,128]{2,1,0:T(8,128)S(1)} %collective-permute-done.18.sylo_ref) | copy-start | bytes 36868
  69.3 0.6 copy-start.19
  69.3 0.6 copy-start.10
  69.3 0.7 copy-start.12
  80.5 10.0 %copy-start.2 = (f32[64,8,128]{2,1,0:T(8,128)S(1)}, f32[64,8,128]{2,1,0:T(8,128)}, u32[]{:S(2)}) copy-start(f32[64,8,128]{2,1,0:T(8,128)} %get-tuple-element.79) | copy-start | bytes 786436
  80.5 10.0 %copy-start.3 = (f32[64,8,128]{2,1,0:T(8,128)S(1)}, f32[64,8,128]{2,1,0:T(8,128)}, u32[]{:S(2)}) copy-start(f32[64,8,128]{2,1,0:T(8,128)} %get-tuple-element.80) | copy-start | bytes 786436
  80.5 10.0 %copy-start.4 = (f32[64,8,128]{2,1,0:T(8,128)S(1)}, f32[64,8,128]{2,1,0:T(8,128)}, u32[]{:S(2)}) copy-start(f32[64,8,128]{2,1,0:T(8,128)} %get-tuple-element.82) | copy-start | bytes 786436
  80.5 6.0 %collective-permute-start.20 = (f32[8,8,128]{2,1,0:T(8,128)}, f32[8,8,128]{2,1,0:T(8,128)S(1)}, u32[]{:S(2)}, u32[]{:S(2)}) collective-permute-start(f32[8,8,128]{2,1,0:T(8,128)} %get-tuple-element.81), channel_id=1, source_target_pairs={{0,1},{1,2},{2,3},{3,0},{4,5},{5,6},{6,7},{7,4},{8,9},{9,10},{10,1... | collective-permute-start | bytes 98312 | tf_op jit(solution)/shard_map/ppermute | solution.py:373
  82.2 5.0 %collective-permute-start.21 = (f32[8,8,128]{2,1,0:T(8,128)}, f32[8,8,128]{2,1,0:T(8,128)S(1)}, u32[]{:S(2)}, u32[]{:S(2)}) collective-permute-start(f32[8,8,128]{2,1,0:T(8,128)} %get-tuple-element.81), channel_id=1, source_target_pairs={{0,2},{1,3},{2,0},{3,1},{4,6},{5,7},{6,4},{7,5},{8,10},{9,11},{10,... | collective-permute-start | bytes 98312 | tf_op jit(solution)/shard_map/ppermute | solution.py:373
  84.7 4.1 %collective-permute-start.22 = (f32[8,8,128]{2,1,0:T(8,128)}, f32[8,8,128]{2,1,0:T(8,128)S(1)}, u32[]{:S(2)}, u32[]{:S(2)}) collective-permute-start(f32[8,8,128]{2,1,0:T(8,128)} %get-tuple-element.81), channel_id=1, source_target_pairs={{0,3},{1,0},{2,1},{3,2},{4,7},{5,4},{6,5},{7,6},{8,11},{9,8},{10,9... | collective-permute-start | bytes 98312 | tf_op jit(solution)/shard_map/ppermute | solution.py:373

commit v3 on v2

v3 whole, which is shorter than its diff:
```python
import jax
import jax.numpy as jnp
from jax import lax
from jax.experimental import pallas as pl
from jax.experimental.pallas import tpu as pltpu
from jax.sharding import PartitionSpec as P

SECTIONS = 4


SOFTEN = 0.5
HEAT_CARRY = 0.5
SILL_RATE = 0.3
SILL_HEAT = 2.5
WATER_INPUT = 0.2
CARBON_INPUT = 0.1
MELT_SHARPNESS = 4.0
SOLIDUS = 1.0
DEPRESSION = 0.5
MELT_RATE = 0.5
LATENT = 0.3

ROWS = 8
CHUNKS = 2
LANES = 128
f32 = jnp.float32


def ring_perms(axis):
    count = lax.axis_size(axis)
    forward = [(i, (i + 1) % count) for i in range(count)]
    backward = [((i + 1) % count, i) for i in range(count)]
    return forward, backward


def iotas():
    sub = lax.broadcasted_iota(jnp.int32, (ROWS, LANES), 0)
    lane = lax.broadcasted_iota(jnp.int32, (ROWS, LANES), 1)
    return sub, lane


class EdgeAcc:
    def __init__(self, count, y_first, y_last):
        zero = jnp.zeros((ROWS, LANES), f32)
        self.xf = [zero] * count
        self.xl = [zero] * count
        self.yf = list(y_first)
        self.yl = list(y_last)

    def add_x(self, planes, b):
        at_b = lax.broadcasted_iota(jnp.int32, (ROWS, LANES), 0) == b
        for f, v in enumerate(planes):
            self.xf[f] = jnp.where(at_b, pltpu.roll(v, b, 0), self.xf[f])
            self.xl[f] = jnp.where(at_b, pltpu.roll(v, (b + 1) % ROWS, 0), self.xl[f])

    def add_y(self, planes, d, lane):
        at_d = lane == d
        for f, v in enumerate(planes):
            self.yf[f] = jnp.where(at_d, pltpu.roll(v, d % LANES, 1), self.yf[f])
            self.yl[f] = jnp.where(at_d, pltpu.roll(v, (d + 1) % LANES, 1), self.yl[f])


def x_minus(v, lo_tile, b, sub):
    return jnp.where(sub == 0, pltpu.roll(lo_tile, (ROWS - b) % ROWS, 0), pltpu.roll(v, 1, 0))


def x_plus(v, hi_tile, b, sub):
    return jnp.where(
        sub == ROWS - 1, pltpu.roll(hi_tile, (ROWS - 1 - b) % ROWS, 0), pltpu.roll(v, ROWS - 1, 0)
    )


def y_minus(v, lo_cols, d, lane):
    return jnp.where(lane == 0, pltpu.roll(lo_cols, (LANES - d) % LANES, 1), pltpu.roll(v, 1, 1))


def y_plus(v, hi_cols, d, lane):
    return jnp.where(
        lane == LANES - 1,
        pltpu.roll(hi_cols, (LANES - 1 - d) % LANES, 1),
        pltpu.roll(v, LANES - 1, 1),
    )


def prep_kernel(tab_ref, layer_ref, h_ref, w_ref, c_ref, m_ref,
                ho_ref, wo_ref, cbo_ref, mo_ref, co_ref, xf_ref, xl_ref, y_ref):
    groups = layer_ref.shape[0] // ROWS
    layers_count = tab_ref.shape[1]
    sub, lane = iotas()
    zero = jnp.zeros((ROWS, LANES), f32)

    def group(a, carry):
        y_f, y_l = carry
        acc = EdgeAcc(5, y_f, y_l)
        for b in range(ROWS):
            d = a * ROWS + b
            layer = layer_ref[d]
            vals = [zero] * 5
            for l in range(layers_count):
                hit = layer == l
                vals = [jnp.where(hit, tab_ref[k, l], vals[k]) for k in range(5)]
            for k in range(5):
                co_ref[k, d] = vals[k]
            heat, water, carbon = h_ref[d], w_ref[d], c_ref[d]
            ho_ref[d] = heat
            wo_ref[d] = water
            cbo_ref[d] = carbon
            mo_ref[d] = m_ref[d]
            acc.add_x([heat, water, carbon, vals[0], vals[2]], b)
            acc.add_y([heat, water, carbon, vals[1], vals[3]], d, lane)
        for f in range(5):
            xf_ref[f, a] = acc.xf[f]
            xl_ref[f, a] = acc.xl[f]
        return (tuple(acc.yf), tuple(acc.yl))

    y_f, y_l = lax.fori_loop(0, groups, group, ((zero,) * 5, (zero,) * 5))
    for f in range(5):
        y_ref[0, f] = y_f[f]
        y_ref[1, f] = y_l[f]


def make_section_kernel(chunk, first):
    def kernel(h_ref, w_ref, c_ref, m_ref, sill_ref, co_ref, xflo_ref, xfhi_ref, yflo_ref, yfhi_ref,
               *rest):
        if first:
            ho_ref, wo_ref, cbo_ref, mo_ref, xf_ref, xl_ref, y_ref = rest
            xslo_ref, xshi_ref, yslo_ref, yshi_ref = xflo_ref, xfhi_ref, yflo_ref, yfhi_ref
        else:
            xslo_ref, xshi_ref, yslo_ref, yshi_ref = rest[:4]
            ho_ref, wo_ref, cbo_ref, mo_ref, xf_ref, xl_ref, y_ref = rest[4:]
        depth = h_ref.shape[0]
        groups = depth // ROWS
        sub, lane = iotas()
        zero = jnp.zeros((ROWS, LANES), f32)
        sylo = [yslo_ref[1, f] for f in range(3)]
        syhi = [yshi_ref[0, f] for f in range(3)]
        cylo = [yflo_ref[1, f] for f in (3, 4)]
        cyhi = [yfhi_ref[0, f] for f in (3, 4)]

        def group(a, carry):
            y_f, y_l = carry
            acc = EdgeAcc(3, y_f, y_l)
            sxlo = [xslo_ref[f, a] for f in range(3)]
            sxhi = [xshi_ref[f, a] for f in range(3)]
            cxlo = [xflo_ref[f, a] for f in (3, 4)]
            cxhi = [xfhi_ref[f, a] for f in (3, 4)]
            for b in range(ROWS):
                i = a * ROWS + b
                d = chunk * depth + i
                heat = h_ref[i]
                water = w_ref[i]
                carbon = c_ref[i]
                melt = m_ref[i]
                sill = sill_ref[i].astype(f32)
                cx = co_ref[0, i]
                cy = co_ref[1, i]
                vx = co_ref[2, i]
                vy = co_ref[3, i]
                mobile = [heat, water, carbon]
                q_xm = [x_minus(mobile[f], sxlo[f], b, sub) for f in range(3)]
                q_xp = [x_plus(mobile[f], sxhi[f], b, sub) for f in range(3)]
                q_ym = [y_minus(mobile[f], sylo[f], d, lane) for f in range(3)]
                q_yp = [y_plus(mobile[f], syhi[f], d, lane) for f in range(3)]
                cx_m = x_minus(cx, cxlo[0], b, sub)
                cx_p = x_plus(cx, cxhi[0], b, sub)
                vx_m = x_minus(vx, cxlo[1], b, sub)
                vx_p = x_plus(vx, cxhi[1], b, sub)
                cy_m = y_minus(cy, cylo[0], d, lane)
                cy_p = y_plus(cy, cyhi[0], d, lane)
                vy_m = y_minus(vy, cylo[1], d, lane)
                vy_p = y_plus(vy, cyhi[1], d, lane)
                soft = jnp.exp(-SOFTEN * heat)
                kx = cx * soft
                ky = cy * soft
                kx_m = cx_m * jnp.exp(-SOFTEN * q_xm[0])
                kx_p = cx_p * jnp.exp(-SOFTEN * q_xp[0])
                ky_m = cy_m * jnp.exp(-SOFTEN * q_ym[0])
                ky_p = cy_p * jnp.exp(-SOFTEN * q_yp[0])
                flux_x_lo = 0.5 * (kx_m + kx) * (heat - q_xm[0])
                flux_x_hi = 0.5 * (kx + kx_p) * (q_xp[0] - heat)
                flux_y_lo = 0.5 * (ky_m + ky) * (heat - q_ym[0])
                flux_y_hi = 0.5 * (ky + ky_p) * (q_yp[0] - heat)
                diffused = flux_x_hi - flux_x_lo + flux_y_hi - flux_y_lo
                fvx_m = 0.5 * (vx_m + vx)
                fvx_p = 0.5 * (vx + vx_p)
                fvy_m = 0.5 * (vy_m + vy)
                fvy_p = 0.5 * (vy + vy_p)
                inflow = []
                for f in range(3):
                    lo_x = jnp.maximum(fvx_m, 0.0) * q_xm[f] + jnp.minimum(fvx_m, 0.0) * mobile[f]
                    hi_x = jnp.maximum(fvx_p, 0.0) * mobile[f] + jnp.minimum(fvx_p, 0.0) * q_xp[f]
                    lo_y = jnp.maximum(fvy_m, 0.0) * q_ym[f] + jnp.minimum(fvy_m, 0.0) * mobile[f]
                    hi_y = jnp.maximum(fvy_p, 0.0) * mobile[f] + jnp.minimum(fvy_p, 0.0) * q_yp[f]
                    inflow.append(lo_x - hi_x + lo_y - hi_y)
                heat_one = heat + diffused + HEAT_CARRY * inflow[0]
                water_two = water + inflow[1] + sill * WATER_INPUT
                carbon_two = carbon + inflow[2] + sill * CARBON_INPUT
                heat_two = heat_one + sill * SILL_RATE * (SILL_HEAT - heat_one)
                z = MELT_SHARPNESS * (heat_two - SOLIDUS + DEPRESSION * water_two)
                target = 1.0 / (1.0 + jnp.exp(-z))
                melt_two = melt + MELT_RATE * (target - melt)
                heat_three = heat_two - LATENT * (melt_two - melt)
                ho_ref[i] = heat_three
                wo_ref[i] = water_two
                cbo_ref[i] = carbon_two
                mo_ref[i] = melt_two
                acc.add_x([heat_three, water_two, carbon_two], b)
                acc.add_y([heat_three, water_two, carbon_two], d, lane)
            for f in range(3):
                xf_ref[f, a] = acc.xf[f]
                xl_ref[f, a] = acc.xl[f]
            return (tuple(acc.yf), tuple(acc.yl))

        y_f, y_l = lax.fori_loop(0, groups, group, ((zero,) * 3, (zero,) * 3))
        for f in range(3):
            y_ref[0, f] = y_f[f]
            y_ref[1, f] = y_l[f]

    return kernel


def sweep_kernel(r_ref, cz_ref, y_ref, a_ref, b_ref, red_ref, c_s, g_s, vy_s, va_s):
    n = r_ref.shape[0]
    zero = jnp.zeros(r_ref.shape[1:], f32)
    one = jnp.ones(r_ref.shape[1:], f32)

    def conduct(i, carry):
        c_s[i] = cz_ref[0, i] * jnp.exp(-SOFTEN * r_ref[i])
        return carry

    lax.fori_loop(0, n, conduct, 0)

    def forward(i, carry):
        g_prev, vy_prev, va_prev = carry
        up = 0.5 * (c_s[i - 1] + c_s[i])
        down = 0.5 * (c_s[i] + c_s[i + 1])
        inv = 1.0 / (1.0 + up + down - up * g_prev)
        g = down * inv
        vy = (r_ref[i] + up * vy_prev) * inv
        va = (up * va_prev) * inv
        g_s[i] = g
        vy_s[i] = vy
        va_s[i] = va
        return g, vy, va

    lax.fori_loop(1, n - 1, forward, (zero, zero, one))

    def backward(k, carry):
        i = n - 2 - k
        y_next, a_next, b_next = carry
        g = g_s[i]
        y = vy_s[i] + g * y_next
        a = va_s[i] + g * a_next
        b = g * b_next
        y_ref[i] = y
        a_ref[i] = a
        b_ref[i] = b
        return y, a, b

    lax.fori_loop(0, n - 2, backward, (zero, zero, one))
    y_ref[0] = zero
    a_ref[0] = one
    b_ref[0] = zero
    y_ref[n - 1] = zero
    a_ref[n - 1] = zero
    b_ref[n - 1] = one
    up_first = 0.5 * (c_s[0] + c_s[1])
    up_last = 0.5 * (c_s[n - 2] + c_s[n - 1])
    red_ref[0] = 1.0 + up_first * (1.0 - a_ref[1])
    red_ref[1] = up_first * b_ref[1]
    red_ref[2] = r_ref[0] + up_first * y_ref[1]
    red_ref[3] = 1.0 + up_last * (1.0 - b_ref[n - 2])
    red_ref[4] = up_last * a_ref[n - 2]
    red_ref[5] = r_ref[n - 1] + up_last * y_ref[n - 2]
    red_ref[6] = c_s[0]
    red_ref[7] = c_s[n - 1]


def reduced_solve(red_all):
    count = red_all.shape[0]
    lower, diag, upper, side = [], [], [], []
    for j in range(count):
        p0, q0, s0, p1, q1, s1, c_first, c_last = [red_all[j, k] for k in range(8)]
        if j == 0:
            face = c_first
            lower.append(jnp.zeros_like(face))
        else:
            face = 0.5 * (red_all[j - 1, 7] + c_first)
            lower.append(face)
        diag.append(p0 + face)
        upper.append(q0)
        side.append(s0)
        if j + 1 < count:
            below = 0.5 * (c_last + red_all[j + 1, 6])
        else:
            below = jnp.zeros_like(c_last)
        lower.append(q1)
        diag.append(p1 + below)
        upper.append(below)
        side.append(s1)
    size = len(diag)
    ratios, values = [], []
    g_prev = jnp.zeros_like(diag[0])
    v_prev = jnp.zeros_like(diag[0])
    for k in range(size):
        inv = 1.0 / (diag[k] - lower[k] * g_prev)
        g_prev = upper[k] * inv
        v_prev = (side[k] + lower[k] * v_prev) * inv
        ratios.append(g_prev)
        values.append(v_prev)
    solved = [None] * size
    following = jnp.zeros_like(diag[0])
    for k in reversed(range(size)):
        following = values[k] + ratios[k] * following
        solved[k] = following
    return jnp.stack(solved)


def sds(shape):
    return jax.ShapeDtypeStruct(shape, f32)


def exchange(xf, xl, ys):
    east_fwd, east_bwd = ring_perms("east")
    north_fwd, north_bwd = ring_perms("north")
    xlo = lax.ppermute(xl, "east", east_fwd)
    xhi = lax.ppermute(xf, "east", east_bwd)
    ylo = lax.ppermute(ys, "north", north_fwd)
    if lax.axis_size("north") == 2:
        yhi = ylo
    else:
        yhi = lax.ppermute(ys, "north", north_bwd)
    return xlo, xhi, ylo, yhi


def full_spec(shape):
    zeros = (0,) * len(shape)
    return pl.BlockSpec(shape, lambda i: zeros)


def local(
    thermal_field,
    liquid_fraction,
    steam_content_grid,
    carbonic_gas_grid,
    stratum_number_grid,
    injection_flags,
    lateral_transmissivity,
    vertical_transmissivity,
    stratum_advection_offsets,
):
    shape = thermal_field.shape
    n = shape[0]
    groups = n // ROWS
    assert shape[1:] == (ROWS, LANES) and n % ROWS == 0 and n <= LANES
    chunks = CHUNKS if groups % CHUNKS == 0 else 1
    depth = n // chunks
    cgroups = depth // ROWS
    table = jnp.concatenate(
        [lateral_transmissivity, stratum_advection_offsets, vertical_transmissivity[None]], 0
    )
    smem_spec = pl.BlockSpec(memory_space=pltpu.SMEM)
    vspec = pl.BlockSpec(memory_space=pltpu.MemorySpace.VMEM)
    heat, water, carbon, melt, co, xf0, xl0, y0 = pl.pallas_call(
        prep_kernel,
        out_shape=(sds(shape), sds(shape), sds(shape), sds(shape), sds((5,) + shape),
                   sds((5, groups, ROWS, LANES)), sds((5, groups, ROWS, LANES)),
                   sds((2, 5, ROWS, LANES))),
        in_specs=[smem_spec, vspec, vspec, vspec, vspec, vspec],
    )(table, stratum_number_grid, thermal_field, steam_content_grid, carbonic_gas_grid,
      liquid_fraction)
    xflo, xfhi, yflo, yfhi = exchange(xf0, xl0, y0)

    def block_spec(k):
        return pl.BlockSpec((depth, ROWS, LANES), lambda i: (k, 0, 0))

    halos = [None] * chunks
    for section_no in range(SECTIONS):
        first = section_no == 0
        for k in range(chunks):
            x5 = pl.BlockSpec((5, cgroups, ROWS, LANES), lambda i, k=k: (0, k, 0, 0))
            y5 = full_spec((2, 5, ROWS, LANES))
            in_specs = [block_spec(k)] * 5 + [
                pl.BlockSpec((4, depth, ROWS, LANES), lambda i, k=k: (0, k, 0, 0)),
                x5, x5, y5, y5,
            ]
            args = [heat, water, carbon, melt, injection_flags, co, xflo, xfhi, yflo, yfhi]
            if not first:
                in_specs += [full_spec((3, cgroups, ROWS, LANES))] * 2
                in_specs += [full_spec((2, 3, ROWS, LANES))] * 2
                args += list(halos[k])
            heat, water, carbon, melt, xf, xl, ys = pl.pallas_call(
                make_section_kernel(k, first),
                grid=(1,),
                out_shape=(sds(shape), sds(shape), sds(shape), sds(shape),
                           sds((3, cgroups, ROWS, LANES)), sds((3, cgroups, ROWS, LANES)),
                           sds((2, 3, ROWS, LANES))),
                in_specs=in_specs,
                out_specs=[block_spec(k)] * 4 + [
                    full_spec((3, cgroups, ROWS, LANES)), full_spec((3, cgroups, ROWS, LANES)),
                    full_spec((2, 3, ROWS, LANES)),
                ],
                input_output_aliases={0: 0, 1: 1, 2: 2, 3: 3},
            )(*args)
            if section_no + 1 < SECTIONS:
                halos[k] = exchange(xf, xl, ys)

    y, a, b, red = pl.pallas_call(
        sweep_kernel,
        grid=(1,),
        out_shape=(sds(shape), sds(shape), sds(shape), sds((8,) + shape[1:])),
        in_specs=[full_spec(shape), pl.BlockSpec((1,) + shape, lambda i: (4, 0, 0, 0))],
        out_specs=[full_spec(shape)] * 3 + [full_spec((8,) + shape[1:])],
        scratch_shapes=[pltpu.VMEM(shape, f32)] * 4,
    )(heat, co)
    count = lax.axis_size("depth")
    rank = lax.axis_index("depth")
    received = [red]
    for k in range(1, count):
        received.append(lax.ppermute(red, "depth", [(i, (i + k) % count) for i in range(count)]))
    stacked = jnp.stack(received)
    red_all = jnp.take(stacked, (rank - jnp.arange(count)) % count, axis=0)
    solved = reduced_solve(red_all)
    first = lax.dynamic_index_in_dim(solved, 2 * rank, keepdims=False)
    last = lax.dynamic_index_in_dim(solved, 2 * rank + 1, keepdims=False)
    heat_next = y + a * first[None] + b * last[None]
    return (heat_next, melt, water, carbon)


def solution(mesh):
    placed = (
        P("depth", "east", "north"),
        P("depth", "east", "north"),
        P("depth", "east", "north"),
        P("depth", "east", "north"),
        P("depth", "east", "north"),
        P("depth", "east", "north"),
        P(),
        P(),
        P(),
    )
    return jax.shard_map(
        local,
        mesh=mesh,
        in_specs=placed,
        out_specs=(
            P("depth", "east", "north"),
            P("depth", "east", "north"),
            P("depth", "east", "north"),
            P("depth", "east", "north"),
        ),
        check_vma=False,
    )
```

time: 91.7 us -> 81.8 us (0.89)
  waiting for transfers between devices: 18.3 us -> 5.36 us
  Pallas kernels: 34.6 us -> 41 us
  starting transfers between devices: 29.5 us -> 26 us
    ppermute x10 -> x7, waiting for transfers between devices: 15.5 us -> 2.2 us  [exchange(): ylo = lax.ppermute(ys, 'north', north_fwd)]
    pallas_call x6 -> x10, Pallas kernels: 34.6 us -> 41 us  [the longest x8 32.7 us: local(): pl.pallas_call(make_section_kernel(k, first), grid=(1,), out_shape=(sds(s...]
    ppermute x10 -> x7, starting transfers between devices: 14.4 us -> 8.43 us  [exchange(): ylo = lax.ppermute(ys, 'north', north_fwd)]
    unnamed x49 -> x51, local copies, waits for them, and re-layouts: 2.66 us -> 4.36 us
    squeeze x1 -> x0, local copies, waits for them, and re-layouts: 1.66 us -> none  [local(): co[4]]
    ppermute x5 -> x7, starting transfers between devices: 8.26 us -> 9.57 us  [exchange(): xhi = lax.ppermute(xf, 'east', east_bwd)]
    ppermute x5 -> x7, starting transfers between devices: 1.35 us -> 2.62 us  [exchange(): xlo = lax.ppermute(xl, 'east', east_fwd)]
  transfers between devices with their start and end apart: 23 -> 24, of which waited for: 13 -> 5; matrix products, arithmetic and copies ran while one was open for 2% -> 0% of each run, Pallas kernels for 0% -> 30%
where the time goes in v3:
time: 81.8 us; the launch traced here: 81.4 us
  Pallas kernels  41 us (50%)
  starting transfers between devices  26 us (32%)
  waiting for transfers between devices  5.36 us (7%)
  local copies, waits for them, and re-layouts  4.93 us (6%)
  other arithmetic  3.07 us (4%)
  between operations  0.98 us (1%)
    pallas_call x8, Pallas kernels, local(): pl.pallas_call(make_section_kernel(k, first), grid=(1,), out_shape=(sds(s...  32.7 us
    ppermute x7, starting transfers between devices, exchange(): xhi = lax.ppermute(xf, 'east', east_bwd)  9.57 us
    ppermute x7, starting transfers between devices, exchange(): ylo = lax.ppermute(ys, 'north', north_fwd)  8.43 us
    ppermute x3, starting transfers between devices, local(): lax.ppermute(red, 'depth', [(i, (i + k) % count) for i in range(count)])  5.41 us
    pallas_call x1, Pallas kernels, local(): pl.pallas_call(prep_kernel, out_shape=(sds(shape), sds(shape), sds(shape)...  4.42 us
    unnamed x51, local copies, waits for them, and re-layouts  4.36 us
    pallas_call x1, Pallas kernels, local(): pl.pallas_call(sweep_kernel, grid=(1,), out_shape=(sds(shape), sds(shape)...  3.86 us
    ppermute x3, waiting for transfers between devices, local(): lax.ppermute(red, 'depth', [(i, (i + k) % count) for i in range(count)])  2.76 us
  transfers between devices with their start and end apart: 24, of which 5 were waited for; matrix products, arithmetic and copies ran while one was open for 0% of the time, Pallas kernels for 30%

profile of v3, /device:TPU:0, one launch (start us, length us, event | category | flops | bytes accessed | tf_op | source)
XLA Modules:
  0.0 81.4 jit_solution(5002652975972337292)
XLA Ops:
  0.6 1.3 %pad_maximum_fusion.1.tab_ref = f32[5,12]{1,0:T(8,128)} fusion(f32[1,12]{1,0:T(1,128)} %bitcast.219, f32[2,12]{1,0:T(2,128)} %param.17, f32[2,12]{1,0:T(2,128)} %param.15), kind=kLoop, calls=%fused_computation.86 | loop fusion | flops 120 | bytes 480 | tf_op jit(solution)/shard_map/concatenate | solution.py:359
  1.9 4.4 %shard_map.120 = (f32[64,8,128]{2,1,0:T(8,128)}, f32[64,8,128]{2,1,0:T(8,128)}, f32[64,8,128]{2,1,0:T(8,128)}, f32[64,8,128]{2,1,0:T(8,128)}, f32[5,64,8,128]{3,...) custom-call(f32[5,12]{1,0:T(8,128)} %pad_maximum_fusion.1.tab_ref, ...), custom_call_target="tpu_custom_call" | custom-call | tf_op jit(solution)/shard_map/pallas_call | solution.py:364
  6.4 0.5 collective-permute-start
  6.8 2.0 %collective-permute-start.1 = (f32[5,8,8,128]{3,2,1,0:T(8,128)}, f32[5,8,8,128]{3,2,1,0:T(8,128)S(1)}, u32[]{:S(2)}, u32[]{:S(2)}) collective-permute-start(f32[5,8,8,128]{3,2,1,0:T(8,128)} %get-tuple-element.72), channel_id=1, source_target_pairs={{8,0},{16,8},{24,16},{0,24},{9,1},{17,9},{25,17},{1,25},{10,2},{18... | collective-permute-start | bytes 491528 | tf_op jit(solution)/shard_map/ppermute | solution.py:327
  8.8 2.3 %collective-permute-start.2 = (f32[2,5,8,128]{3,2,1,0:T(8,128)}, f32[2,5,8,128]{3,2,1,0:T(8,128)S(1)}, u32[]{:S(2)}, u32[]{:S(2)}) collective-permute-start(f32[2,5,8,128]{3,2,1,0:T(8,128)} %get-tuple-element.73), channel_id=1, source_target_pairs={{0,4},{4,0},{1,5},{5,1},{2,6},{6,2},{3,7},{7,3},{8,12},{12,8},{9,1... | collective-permute-start | bytes 122888 | tf_op jit(solution)/shard_map/ppermute | solution.py:328
  11.1 2.2 %collective-permute-done.2.yflo_ref.yfhi_ref = f32[2,5,8,128]{3,2,1,0:T(8,128)S(1)} collective-permute-done((f32[2,5,8,128]{3,2,1,0:T(8,128)}, f32[2,5,8,128]{3,2,1,0:T(8,128)S(1)}, u32[]{:S(2)}, u32[]{:S(2)}) %collective-permute-start.2) | collective-permute-done | bytes 40992 | tf_op jit(solution)/shard_map/ppermute | solution.py:328
  13.3 0.4 collective-permute-done.1.xfhi_ref
  13.6 0.2 copy-done.2
  13.9 0.4 copy-done.1
  14.3 4.1 %shard_map.121 = (f32[64,8,128]{2,1,0:T(8,128)}, f32[64,8,128]{2,1,0:T(8,128)}, f32[64,8,128]{2,1,0:T(8,128)}, f32[64,8,128]{2,1,0:T(8,128)}, f32[3,4,8,128]{3,2...) custom-call(f32[64,8,128]{2,1,0:T(8,128)} %get-tuple-element.66.h_re, ...), custom_call_target="tpu_custom_call", output_to_operand_aliasing={{0}: (0, {}), {1}: (1, {}), {2}: (2, {}), {3}: (3, {})} | custom-call | tf_op jit(solution)/shard_map/pallas_call | solution.py:392
  18.4 0.7 collective-permute-start.3
  19.1 1.3 %collective-permute-start.4 = (f32[3,4,8,128]{3,2,1,0:T(8,128)}, f32[3,4,8,128]{3,2,1,0:T(8,128)S(1)}, u32[]{:S(2)}, u32[]{:S(2)}) collective-permute-start(f32[3,4,8,128]{3,2,1,0:T(8,128)} %get-tuple-element.83), channel_id=1, source_target_pairs={{8,0},{16,8},{24,16},{0,24},{9,1},{17,9},{25,17},{1,25},{10,2},{18... | collective-permute-start | bytes 147464 | tf_op jit(solution)/shard_map/ppermute | solution.py:327
  20.5 1.4 %collective-permute-start.5 = (f32[2,3,8,128]{3,2,1,0:T(8,128)}, f32[2,3,8,128]{3,2,1,0:T(8,128)S(1)}, u32[]{:S(2)}, u32[]{:S(2)}) collective-permute-start(f32[2,3,8,128]{3,2,1,0:T(8,128)} %get-tuple-element.84), channel_id=1, source_target_pairs={{0,4},{4,0},{1,5},{5,1},{2,6},{6,2},{3,7},{7,3},{8,12},{12,8},{9,1... | collective-permute-start | bytes 73736 | tf_op jit(solution)/shard_map/ppermute | solution.py:328
  21.9 4.1 %shard_map.122 = (f32[64,8,128]{2,1,0:T(8,128)}, f32[64,8,128]{2,1,0:T(8,128)}, f32[64,8,128]{2,1,0:T(8,128)}, f32[64,8,128]{2,1,0:T(8,128)}, f32[3,4,8,128]{3,2...) custom-call(f32[64,8,128]{2,1,0:T(8,128)} %get-tuple-element.74.h_re, ...), custom_call_target="tpu_custom_call", output_to_operand_aliasing={{0}: (0, {}), {1}: (1, {}), {2}: (2, {}), {3}: (3, {})} | custom-call | tf_op jit(solution)/shard_map/pallas_call | solution.py:392
  26.0 1.7 %collective-permute-start.7 = (f32[3,4,8,128]{3,2,1,0:T(8,128)}, f32[3,4,8,128]{3,2,1,0:T(8,128)S(1)}, u32[]{:S(2)}, u32[]{:S(2)}) collective-permute-start(f32[3,4,8,128]{3,2,1,0:T(8,128)} %get-tuple-element.90), channel_id=1, source_target_pairs={{8,0},{16,8},{24,16},{0,24},{9,1},{17,9},{25,17},{1,25},{10,2},{18... | collective-permute-start | bytes 147464 | tf_op jit(solution)/shard_map/ppermute | solution.py:327
  27.7 0.7 collective-permute-start.8
  28.4 0.6 copy-done.22
  29.0 4.1 %shard_map.123 = (f32[64,8,128]{2,1,0:T(8,128)}, f32[64,8,128]{2,1,0:T(8,128)}, f32[64,8,128]{2,1,0:T(8,128)}, f32[64,8,128]{2,1,0:T(8,128)}, f32[3,4,8,128]{3,2...) custom-call(f32[64,8,128]{2,1,0:T(8,128)} %get-tuple-element.78.h_re, ...), custom_call_target="tpu_custom_call", output_to_operand_aliasing={{0}: (0, {}), {1}: (1, {}), {2}: (2, {}), {3}: (3, {})} | custom-call | tf_op jit(solution)/shard_map/pallas_call | solution.py:392
  33.1 0.2 collective-permute-start.10
  33.3 0.4 collective-permute-start.9
  33.7 1.4 %collective-permute-start.11 = (f32[2,3,8,128]{3,2,1,0:T(8,128)}, f32[2,3,8,128]{3,2,1,0:T(8,128)S(1)}, u32[]{:S(2)}, u32[]{:S(2)}) collective-permute-start(f32[2,3,8,128]{3,2,1,0:T(8,128)} %get-tuple-element.98), channel_id=1, source_target_pairs={{0,4},{4,0},{1,5},{5,1},{2,6},{6,2},{3,7},{7,3},{8,12},{12,8},{9,1... | collective-permute-start | bytes 73736 | tf_op jit(solution)/shard_map/ppermute | solution.py:328
  35.1 0.6 copy-done.12
  35.6 4.1 %shard_map.124 = (f32[64,8,128]{2,1,0:T(8,128)}, f32[64,8,128]{2,1,0:T(8,128)}, f32[64,8,128]{2,1,0:T(8,128)}, f32[64,8,128]{2,1,0:T(8,128)}, f32[3,4,8,128]{3,2...) custom-call(f32[64,8,128]{2,1,0:T(8,128)} %get-tuple-element.85.h_re, ...), custom_call_target="tpu_custom_call", output_to_operand_aliasing={{0}: (0, {}), {1}: (1, {}), {2}: (2, {}), {3}: (3, {})} | custom-call | tf_op jit(solution)/shard_map/pallas_call | solution.py:392
  39.7 0.9 %collective-permute-start.12 = (f32[3,4,8,128]{3,2,1,0:T(8,128)}, f32[3,4,8,128]{3,2,1,0:T(8,128)S(1)}, u32[]{:S(2)}, u32[]{:S(2)}) collective-permute-start(f32[3,4,8,128]{3,2,1,0:T(8,128)} %get-tuple-element.103), channel_id=1, source_target_pairs={{0,8},{8,16},{16,24},{24,0},{1,9},{9,17},{17,25},{25,1},{2,10},{10... | collective-permute-start | bytes 147464 | tf_op jit(solution)/shard_map/ppermute | solution.py:326
  40.7 0.9 %collective-permute-start.13 = (f32[3,4,8,128]{3,2,1,0:T(8,128)}, f32[3,4,8,128]{3,2,1,0:T(8,128)S(1)}, u32[]{:S(2)}, u32[]{:S(2)}) collective-permute-start(f32[3,4,8,128]{3,2,1,0:T(8,128)} %get-tuple-element.104), channel_id=1, source_target_pairs={{8,0},{16,8},{24,16},{0,24},{9,1},{17,9},{25,17},{1,25},{10,2},{18... | collective-permute-start | bytes 147464 | tf_op jit(solution)/shard_map/ppermute | solution.py:327
  41.5 0.7 collective-permute-start.14
  42.2 0.6 copy-done.13
  42.9 4.1 %shard_map.125 = (f32[64,8,128]{2,1,0:T(8,128)}, f32[64,8,128]{2,1,0:T(8,128)}, f32[64,8,128]{2,1,0:T(8,128)}, f32[64,8,128]{2,1,0:T(8,128)}, f32[3,4,8,128]{3,2...) custom-call(f32[64,8,128]{2,1,0:T(8,128)} %get-tuple-element.92.h_re, ...), custom_call_target="tpu_custom_call", output_to_operand_aliasing={{0}: (0, {}), {1}: (1, {}), {2}: (2, {}), {3}: (3, {})} | custom-call | tf_op jit(solution)/shard_map/pallas_call | solution.py:392
  47.0 1.4 %collective-permute-start.17 = (f32[2,3,8,128]{3,2,1,0:T(8,128)}, f32[2,3,8,128]{3,2,1,0:T(8,128)S(1)}, u32[]{:S(2)}, u32[]{:S(2)}) collective-permute-start(f32[2,3,8,128]{3,2,1,0:T(8,128)} %get-tuple-element.112), channel_id=1, source_target_pairs={{0,4},{4,0},{1,5},{5,1},{2,6},{6,2},{3,7},{7,3},{8,12},{12,8},{9,1... | collective-permute-start | bytes 73736 | tf_op jit(solution)/shard_map/ppermute | solution.py:328
  48.5 1.7 %collective-permute-start.16 = (f32[3,4,8,128]{3,2,1,0:T(8,128)}, f32[3,4,8,128]{3,2,1,0:T(8,128)S(1)}, u32[]{:S(2)}, u32[]{:S(2)}) collective-permute-start(f32[3,4,8,128]{3,2,1,0:T(8,128)} %get-tuple-element.111), channel_id=1, source_target_pairs={{8,0},{16,8},{24,16},{0,24},{9,1},{17,9},{25,17},{1,25},{10,2},{18... | collective-permute-start | bytes 147464 | tf_op jit(solution)/shard_map/ppermute | solution.py:327
  50.2 0.6 copy-done.16
  50.8 4.1 %shard_map.126 = (f32[64,8,128]{2,1,0:T(8,128)}, f32[64,8,128]{2,1,0:T(8,128)}, f32[64,8,128]{2,1,0:T(8,128)}, f32[64,8,128]{2,1,0:T(8,128)}, f32[3,4,8,128]{3,2...) custom-call(f32[64,8,128]{2,1,0:T(8,128)} %get-tuple-element.99.h_re, ...), custom_call_target="tpu_custom_call", output_to_operand_aliasing={{0}: (0, {}), {1}: (1, {}), {2}: (2, {}), {3}: (3, {})} | custom-call | tf_op jit(solution)/shard_map/pallas_call | solution.py:392
  55.0 1.7 %collective-permute-start.19 = (f32[3,4,8,128]{3,2,1,0:T(8,128)}, f32[3,4,8,128]{3,2,1,0:T(8,128)S(1)}, u32[]{:S(2)}, u32[]{:S(2)}) collective-permute-start(f32[3,4,8,128]{3,2,1,0:T(8,128)} %get-tuple-element.118), channel_id=1, source_target_pairs={{8,0},{16,8},{24,16},{0,24},{9,1},{17,9},{25,17},{1,25},{10,2},{18... | collective-permute-start | bytes 147464 | tf_op jit(solution)/shard_map/ppermute | solution.py:327
  56.7 0.7 collective-permute-start.20
  57.4 0.6 copy-done.17
  58.0 4.1 %shard_map.127 = (f32[64,8,128]{2,1,0:T(8,128)}, f32[64,8,128]{2,1,0:T(8,128)}, f32[64,8,128]{2,1,0:T(8,128)}, f32[64,8,128]{2,1,0:T(8,128)}, f32[3,4,8,128]{3,2...) custom-call(f32[64,8,128]{2,1,0:T(8,128)} %get-tuple-element.106.h_r, ...), custom_call_target="tpu_custom_call", output_to_operand_aliasing={{0}: (0, {}), {1}: (1, {}), {2}: (2, {}), {3}: (3, {})} | custom-call | tf_op jit(solution)/shard_map/pallas_call | solution.py:392
  62.2 0.6 copy-done.10
  62.8 4.1 %shard_map.128 = (f32[64,8,128]{2,1,0:T(8,128)}, f32[64,8,128]{2,1,0:T(8,128)}, f32[64,8,128]{2,1,0:T(8,128)}, f32[64,8,128]{2,1,0:T(8,128)}, f32[3,4,8,128]{3,2...) custom-call(f32[64,8,128]{2,1,0:T(8,128)} %get-tuple-element.113.h_r, ...), custom_call_target="tpu_custom_call", output_to_operand_aliasing={{0}: (0, {}), {1}: (1, {}), {2}: (2, {}), {3}: (3, {})} | custom-call | tf_op jit(solution)/shard_map/pallas_call | solution.py:392
  66.9 3.9 %shard_map.129 = (f32[64,8,128]{2,1,0:T(8,128)}, f32[64,8,128]{2,1,0:T(8,128)}, f32[64,8,128]{2,1,0:T(8,128)}, f32[8,8,128]{2,1,0:T(8,128)}) custom-call(f32[64,8,128]{2,1,0:T(8,128)} %get-tuple-element.120.r_ref, f32[5,64,8,128]{3,2,1,0:T(8,128)} %get-tuple-element.70.co_ref.cz_ref), custom_call_target="tpu_custom_call" | custom-call | tf_op jit(solution)/shard_map/pallas_call | solution.py:408
  70.8 1.5 %collective-permute-start.21 = (f32[8,8,128]{2,1,0:T(8,128)}, f32[8,8,128]{2,1,0:T(8,128)S(1)}, u32[]{:S(2)}, u32[]{:S(2)}) collective-permute-start(f32[8,8,128]{2,1,0:T(8,128)} %get-tuple-element.123), channel_id=1, source_target_pairs={{0,1},{1,2},{2,3},{3,0},{4,5},{5,6},{6,7},{7,4},{8,9},{9,10},{10,1... | collective-permute-start | bytes 98312 | tf_op jit(solution)/shard_map/ppermute | solution.py:420
  72.2 2.6 %collective-permute-start.22 = (f32[8,8,128]{2,1,0:T(8,128)}, f32[8,8,128]{2,1,0:T(8,128)S(1)}, u32[]{:S(2)}, u32[]{:S(2)}) collective-permute-start(f32[8,8,128]{2,1,0:T(8,128)} %get-tuple-element.123), channel_id=1, source_target_pairs={{0,2},{1,3},{2,0},{3,1},{4,6},{5,7},{6,4},{7,5},{8,10},{9,11},{10,... | collective-permute-start | bytes 98312 | tf_op jit(solution)/shard_map/ppermute | solution.py:420
  74.8 1.3 %collective-permute-start.23 = (f32[8,8,128]{2,1,0:T(8,128)}, f32[8,8,128]{2,1,0:T(8,128)S(1)}, u32[]{:S(2)}, u32[]{:S(2)}) collective-permute-start(f32[8,8,128]{2,1,0:T(8,128)} %get-tuple-element.123), channel_id=1, source_target_pairs={{0,3},{1,0},{2,1},{3,2},{4,7},{5,4},{6,5},{7,6},{8,11},{9,8},{10,9... | collective-permute-start | bytes 98312 | tf_op jit(solution)/shard_map/ppermute | solution.py:420
  76.2 1.0 %collective-permute-done.21 = f32[8,8,128]{2,1,0:T(8,128)S(1)} collective-permute-done((f32[8,8,128]{2,1,0:T(8,128)}, f32[8,8,128]{2,1,0:T(8,128)S(1)}, u32[]{:S(2)}, u32[]{:S(2)}) %collective-permute-start.21) | collective-permute-done | bytes 32800 | tf_op jit(solution)/shard_map/ppermute | solution.py:420
  77.2 0.5 collective-permute-done.22
  77.7 1.3 %collective-permute-done.23 = f32[8,8,128]{2,1,0:T(8,128)S(1)} collective-permute-done((f32[8,8,128]{2,1,0:T(8,128)}, f32[8,8,128]{2,1,0:T(8,128)S(1)}, u32[]{:S(2)}, u32[]{:S(2)}) %collective-permute-start.23) | collective-permute-done | bytes 32800 | tf_op jit(solution)/shard_map/ppermute | solution.py:420
  79.0 0.8 pad_maximum_fusion
  79.7 0.6 gather_fusion
  80.6 0.7 multiply_add_fusion
  (77 shorter events, 0.7 us)
Async XLA Ops:
  6.4 6.9 %collective-permute-start = (f32[5,8,8,128]{3,2,1,0:T(8,128)}, f32[5,8,8,128]{3,2,1,0:T(8,128)S(1)}, u32[]{:S(2)}, u32[]{:S(2)}) collective-permute-start(f32[5,8,8,128]{3,2,1,0:T(8,128)} %get-tuple-element.71), channel_id=1, source_target_pairs={{0,8},{8,16},{16,24},{24,0},{1,9},{9,17},{17,25},{25,1},{2,10},{10... | collective-permute-start | bytes 491528 | tf_op jit(solution)/shard_map/ppermute | solution.py:326
  6.8 6.8 %collective-permute-start.1 = (f32[5,8,8,128]{3,2,1,0:T(8,128)}, f32[5,8,8,128]{3,2,1,0:T(8,128)S(1)}, u32[]{:S(2)}, u32[]{:S(2)}) collective-permute-start(f32[5,8,8,128]{3,2,1,0:T(8,128)} %get-tuple-element.72), channel_id=1, source_target_pairs={{8,0},{16,8},{24,16},{0,24},{9,1},{17,9},{25,17},{1,25},{10,2},{18... | collective-permute-start | bytes 491528 | tf_op jit(solution)/shard_map/ppermute | solution.py:327
  8.8 4.5 %collective-permute-start.2 = (f32[2,5,8,128]{3,2,1,0:T(8,128)}, f32[2,5,8,128]{3,2,1,0:T(8,128)S(1)}, u32[]{:S(2)}, u32[]{:S(2)}) collective-permute-start(f32[2,5,8,128]{3,2,1,0:T(8,128)} %get-tuple-element.73), channel_id=1, source_target_pairs={{0,4},{4,0},{1,5},{5,1},{2,6},{6,2},{3,7},{7,3},{8,12},{12,8},{9,1... | collective-permute-start | bytes 122888 | tf_op jit(solution)/shard_map/ppermute | solution.py:328
  13.3 0.6 copy-start.2
  13.3 0.7 copy-start
  13.6 0.7 copy-start.1
  18.4 10.0 %collective-permute-start.3 = (f32[3,4,8,128]{3,2,1,0:T(8,128)}, f32[3,4,8,128]{3,2,1,0:T(8,128)S(1)}, u32[]{:S(2)}, u32[]{:S(2)}) collective-permute-start(f32[3,4,8,128]{3,2,1,0:T(8,128)} %get-tuple-element.82), channel_id=1, source_target_pairs={{0,8},{8,16},{16,24},{24,0},{1,9},{9,17},{17,25},{25,1},{2,10},{10... | collective-permute-start | bytes 147464 | tf_op jit(solution)/shard_map/ppermute | solution.py:326
  19.1 9.3 %collective-permute-start.4 = (f32[3,4,8,128]{3,2,1,0:T(8,128)}, f32[3,4,8,128]{3,2,1,0:T(8,128)S(1)}, u32[]{:S(2)}, u32[]{:S(2)}) collective-permute-start(f32[3,4,8,128]{3,2,1,0:T(8,128)} %get-tuple-element.83), channel_id=1, source_target_pairs={{8,0},{16,8},{24,16},{0,24},{9,1},{17,9},{25,17},{1,25},{10,2},{18... | collective-permute-start | bytes 147464 | tf_op jit(solution)/shard_map/ppermute | solution.py:327
  20.5 7.2 %collective-permute-start.5 = (f32[2,3,8,128]{3,2,1,0:T(8,128)}, f32[2,3,8,128]{3,2,1,0:T(8,128)S(1)}, u32[]{:S(2)}, u32[]{:S(2)}) collective-permute-start(f32[2,3,8,128]{3,2,1,0:T(8,128)} %get-tuple-element.84), channel_id=1, source_target_pairs={{0,4},{4,0},{1,5},{5,1},{2,6},{6,2},{3,7},{7,3},{8,12},{12,8},{9,1... | collective-permute-start | bytes 73736 | tf_op jit(solution)/shard_map/ppermute | solution.py:328
  26.0 9.1 %collective-permute-start.6 = (f32[3,4,8,128]{3,2,1,0:T(8,128)}, f32[3,4,8,128]{3,2,1,0:T(8,128)S(1)}, u32[]{:S(2)}, u32[]{:S(2)}) collective-permute-start(f32[3,4,8,128]{3,2,1,0:T(8,128)} %get-tuple-element.89), channel_id=1, source_target_pairs={{0,8},{8,16},{16,24},{24,0},{1,9},{9,17},{17,25},{25,1},{2,10},{10... | collective-permute-start | bytes 147464 | tf_op jit(solution)/shard_map/ppermute | solution.py:326
  26.0 9.0 %collective-permute-start.7 = (f32[3,4,8,128]{3,2,1,0:T(8,128)}, f32[3,4,8,128]{3,2,1,0:T(8,128)S(1)}, u32[]{:S(2)}, u32[]{:S(2)}) collective-permute-start(f32[3,4,8,128]{3,2,1,0:T(8,128)} %get-tuple-element.90), channel_id=1, source_target_pairs={{8,0},{16,8},{24,16},{0,24},{9,1},{17,9},{25,17},{1,25},{10,2},{18... | collective-permute-start | bytes 147464 | tf_op jit(solution)/shard_map/ppermute | solution.py:327
  27.7 0.7 copy-start.11
  27.7 5.9 %collective-permute-start.8 = (f32[2,3,8,128]{3,2,1,0:T(8,128)}, f32[2,3,8,128]{3,2,1,0:T(8,128)S(1)}, u32[]{:S(2)}, u32[]{:S(2)}) collective-permute-start(f32[2,3,8,128]{3,2,1,0:T(8,128)} %get-tuple-element.91), channel_id=1, source_target_pairs={{0,4},{4,0},{1,5},{5,1},{2,6},{6,2},{3,7},{7,3},{8,12},{12,8},{9,1... | collective-permute-start | bytes 73736 | tf_op jit(solution)/shard_map/ppermute | solution.py:328
  28.4 0.6 copy-start.22
  28.4 0.6 copy-start.23
  33.1 9.1 %collective-permute-start.10 = (f32[3,4,8,128]{3,2,1,0:T(8,128)}, f32[3,4,8,128]{3,2,1,0:T(8,128)S(1)}, u32[]{:S(2)}, u32[]{:S(2)}) collective-permute-start(f32[3,4,8,128]{3,2,1,0:T(8,128)} %get-tuple-element.97), channel_id=1, source_target_pairs={{8,0},{16,8},{24,16},{0,24},{9,1},{17,9},{25,17},{1,25},{10,2},{18... | collective-permute-start | bytes 147464 | tf_op jit(solution)/shard_map/ppermute | solution.py:327
  33.3 8.9 %collective-permute-start.9 = (f32[3,4,8,128]{3,2,1,0:T(8,128)}, f32[3,4,8,128]{3,2,1,0:T(8,128)S(1)}, u32[]{:S(2)}, u32[]{:S(2)}) collective-permute-start(f32[3,4,8,128]{3,2,1,0:T(8,128)} %get-tuple-element.96), channel_id=1, source_target_pairs={{0,8},{8,16},{16,24},{24,0},{1,9},{9,17},{17,25},{25,1},{2,10},{10... | collective-permute-start | bytes 147464 | tf_op jit(solution)/shard_map/ppermute | solution.py:326
  33.7 1.4 %copy-start.7 = (f32[2,3,8,128]{3,2,1,0:T(8,128)}, f32[2,3,8,128]{3,2,1,0:T(8,128)S(1)}, u32[]{:S(2)}) copy-start(f32[2,3,8,128]{3,2,1,0:T(8,128)S(1)} %collective-permute-done.8.rest_2_.rest_3_) | copy-start | bytes 73732
  33.7 7.9 %collective-permute-start.11 = (f32[2,3,8,128]{3,2,1,0:T(8,128)}, f32[2,3,8,128]{3,2,1,0:T(8,128)S(1)}, u32[]{:S(2)}, u32[]{:S(2)}) collective-permute-start(f32[2,3,8,128]{3,2,1,0:T(8,128)} %get-tuple-element.98), channel_id=1, source_target_pairs={{0,4},{4,0},{1,5},{5,1},{2,6},{6,2},{3,7},{7,3},{8,12},{12,8},{9,1... | collective-permute-start | bytes 73736 | tf_op jit(solution)/shard_map/ppermute | solution.py:328
  35.0 0.6 copy-start.12
  35.0 0.6 copy-start.14
  39.7 10.4 %collective-permute-start.12 = (f32[3,4,8,128]{3,2,1,0:T(8,128)}, f32[3,4,8,128]{3,2,1,0:T(8,128)S(1)}, u32[]{:S(2)}, u32[]{:S(2)}) collective-permute-start(f32[3,4,8,128]{3,2,1,0:T(8,128)} %get-tuple-element.103), channel_id=1, source_target_pairs={{0,8},{8,16},{16,24},{24,0},{1,9},{9,17},{17,25},{25,1},{2,10},{10... | collective-permute-start | bytes 147464 | tf_op jit(solution)/shard_map/ppermute | solution.py:326
  40.7 9.5 %collective-permute-start.13 = (f32[3,4,8,128]{3,2,1,0:T(8,128)}, f32[3,4,8,128]{3,2,1,0:T(8,128)S(1)}, u32[]{:S(2)}, u32[]{:S(2)}) collective-permute-start(f32[3,4,8,128]{3,2,1,0:T(8,128)} %get-tuple-element.104), channel_id=1, source_target_pairs={{8,0},{16,8},{24,16},{0,24},{9,1},{17,9},{25,17},{1,25},{10,2},{18... | collective-permute-start | bytes 147464 | tf_op jit(solution)/shard_map/ppermute | solution.py:327
  41.5 0.7 copy-start.8
  41.5 6.9 %collective-permute-start.14 = (f32[2,3,8,128]{3,2,1,0:T(8,128)}, f32[2,3,8,128]{3,2,1,0:T(8,128)S(1)}, u32[]{:S(2)}, u32[]{:S(2)}) collective-permute-start(f32[2,3,8,128]{3,2,1,0:T(8,128)} %get-tuple-element.105), channel_id=1, source_target_pairs={{0,4},{4,0},{1,5},{5,1},{2,6},{6,2},{3,7},{7,3},{8,12},{12,8},{9,1... | collective-permute-start | bytes 73736 | tf_op jit(solution)/shard_map/ppermute | solution.py:328
  42.2 0.6 copy-start.13
  42.2 0.6 copy-start.15
  47.0 9.8 %collective-permute-start.17 = (f32[2,3,8,128]{3,2,1,0:T(8,128)}, f32[2,3,8,128]{3,2,1,0:T(8,128)S(1)}, u32[]{:S(2)}, u32[]{:S(2)}) collective-permute-start(f32[2,3,8,128]{3,2,1,0:T(8,128)} %get-tuple-element.112), channel_id=1, source_target_pairs={{0,4},{4,0},{1,5},{5,1},{2,6},{6,2},{3,7},{7,3},{8,12},{12,8},{9,1... | collective-permute-start | bytes 73736 | tf_op jit(solution)/shard_map/ppermute | solution.py:328
  48.4 9.0 %collective-permute-start.15 = (f32[3,4,8,128]{3,2,1,0:T(8,128)}, f32[3,4,8,128]{3,2,1,0:T(8,128)S(1)}, u32[]{:S(2)}, u32[]{:S(2)}) collective-permute-start(f32[3,4,8,128]{3,2,1,0:T(8,128)} %get-tuple-element.110), channel_id=1, source_target_pairs={{0,8},{8,16},{16,24},{24,0},{1,9},{9,17},{17,25},{25,1},{2,10},{10... | collective-permute-start | bytes 147464 | tf_op jit(solution)/shard_map/ppermute | solution.py:326
  48.4 1.8 %copy-start.9 = (f32[2,3,8,128]{3,2,1,0:T(8,128)}, f32[2,3,8,128]{3,2,1,0:T(8,128)S(1)}, u32[]{:S(2)}) copy-start(f32[2,3,8,128]{3,2,1,0:T(8,128)S(1)} %collective-permute-done.14.rest_2_.rest_3_) | copy-start | bytes 73732
  48.5 9.0 %collective-permute-start.16 = (f32[3,4,8,128]{3,2,1,0:T(8,128)}, f32[3,4,8,128]{3,2,1,0:T(8,128)S(1)}, u32[]{:S(2)}, u32[]{:S(2)}) collective-permute-start(f32[3,4,8,128]{3,2,1,0:T(8,128)} %get-tuple-element.111), channel_id=1, source_target_pairs={{8,0},{16,8},{24,16},{0,24},{9,1},{17,9},{25,17},{1,25},{10,2},{18... | collective-permute-start | bytes 147464 | tf_op jit(solution)/shard_map/ppermute | solution.py:327
  50.2 0.6 copy-start.16
  50.2 0.6 copy-start.18
  54.9 7.2 %collective-permute-start.18 = (f32[3,4,8,128]{3,2,1,0:T(8,128)}, f32[3,4,8,128]{3,2,1,0:T(8,128)S(1)}, u32[]{:S(2)}, u32[]{:S(2)}) collective-permute-start(f32[3,4,8,128]{3,2,1,0:T(8,128)} %get-tuple-element.117), channel_id=1, source_target_pairs={{0,8},{8,16},{16,24},{24,0},{1,9},{9,17},{17,25},{25,1},{2,10},{10... | collective-permute-start | bytes 147464 | tf_op jit(solution)/shard_map/ppermute | solution.py:326
  55.0 7.2 %collective-permute-start.19 = (f32[3,4,8,128]{3,2,1,0:T(8,128)}, f32[3,4,8,128]{3,2,1,0:T(8,128)S(1)}, u32[]{:S(2)}, u32[]{:S(2)}) collective-permute-start(f32[3,4,8,128]{3,2,1,0:T(8,128)} %get-tuple-element.118), channel_id=1, source_target_pairs={{8,0},{16,8},{24,16},{0,24},{9,1},{17,9},{25,17},{1,25},{10,2},{18... | collective-permute-start | bytes 147464 | tf_op jit(solution)/shard_map/ppermute | solution.py:327
  56.7 0.7 copy-start.6
  56.7 5.4 %collective-permute-start.20 = (f32[2,3,8,128]{3,2,1,0:T(8,128)}, f32[2,3,8,128]{3,2,1,0:T(8,128)S(1)}, u32[]{:S(2)}, u32[]{:S(2)}) collective-permute-start(f32[2,3,8,128]{3,2,1,0:T(8,128)} %get-tuple-element.119), channel_id=1, source_target_pairs={{0,4},{4,0},{1,5},{5,1},{2,6},{6,2},{3,7},{7,3},{8,12},{12,8},{9,1... | collective-permute-start | bytes 73736 | tf_op jit(solution)/shard_map/ppermute | solution.py:328
  57.4 0.6 copy-start.17
  57.4 0.6 copy-start.21
  62.2 0.6 copy-start.10
  62.2 0.6 copy-start.19
  62.2 0.6 copy-start.20
  70.8 9.8 %copy-start.3 = (f32[64,8,128]{2,1,0:T(8,128)S(1)}, f32[64,8,128]{2,1,0:T(8,128)}, u32[]{:S(2)}) copy-start(f32[64,8,128]{2,1,0:T(8,128)} %get-tuple-element.121) | copy-start | bytes 786436
  70.8 9.9 %copy-start.4 = (f32[64,8,128]{2,1,0:T(8,128)S(1)}, f32[64,8,128]{2,1,0:T(8,128)}, u32[]{:S(2)}) copy-start(f32[64,8,128]{2,1,0:T(8,128)} %get-tuple-element.122) | copy-start | bytes 786436
  70.8 9.9 %copy-start.5 = (f32[64,8,128]{2,1,0:T(8,128)S(1)}, f32[64,8,128]{2,1,0:T(8,128)}, u32[]{:S(2)}) copy-start(f32[64,8,128]{2,1,0:T(8,128)} %get-tuple-element.124) | copy-start | bytes 786436
  70.8 6.4 %collective-permute-start.21 = (f32[8,8,128]{2,1,0:T(8,128)}, f32[8,8,128]{2,1,0:T(8,128)S(1)}, u32[]{:S(2)}, u32[]{:S(2)}) collective-permute-start(f32[8,8,128]{2,1,0:T(8,128)} %get-tuple-element.123), channel_id=1, source_target_pairs={{0,1},{1,2},{2,3},{3,0},{4,5},{5,6},{6,7},{7,4},{8,9},{9,10},{10,1... | collective-permute-start | bytes 98312 | tf_op jit(solution)/shard_map/ppermute | solution.py:420
  72.2 5.5 %collective-permute-start.22 = (f32[8,8,128]{2,1,0:T(8,128)}, f32[8,8,128]{2,1,0:T(8,128)S(1)}, u32[]{:S(2)}, u32[]{:S(2)}) collective-permute-start(f32[8,8,128]{2,1,0:T(8,128)} %get-tuple-element.123), channel_id=1, source_target_pairs={{0,2},{1,3},{2,0},{3,1},{4,6},{5,7},{6,4},{7,5},{8,10},{9,11},{10,... | collective-permute-start | bytes 98312 | tf_op jit(solution)/shard_map/ppermute | solution.py:420
  74.8 4.1 %collective-permute-start.23 = (f32[8,8,128]{2,1,0:T(8,128)}, f32[8,8,128]{2,1,0:T(8,128)S(1)}, u32[]{:S(2)}, u32[]{:S(2)}) collective-permute-start(f32[8,8,128]{2,1,0:T(8,128)} %get-tuple-element.123), channel_id=1, source_target_pairs={{0,3},{1,0},{2,1},{3,2},{4,7},{5,4},{6,5},{7,6},{8,11},{9,8},{10,9... | collective-permute-start | bytes 98312 | tf_op jit(solution)/shard_map/ppermute | solution.py:420

commit v4 on v3

--- a/solution.py
+++ b/solution.py
@@ -119,7 +119,7 @@
         y_ref[1, f] = y_l[f]
 
 
-def make_section_kernel(chunk, first):
+def make_section_kernel(chunk, first, cgroups):
     def kernel(h_ref, w_ref, c_ref, m_ref, sill_ref, co_ref, xflo_ref, xfhi_ref, yflo_ref, yfhi_ref,
                *rest):
         if first:
@@ -128,25 +128,31 @@
         else:
             xslo_ref, xshi_ref, yslo_ref, yshi_ref = rest[:4]
             ho_ref, wo_ref, cbo_ref, mo_ref, xf_ref, xl_ref, y_ref = rest[4:]
-        depth = h_ref.shape[0]
-        groups = depth // ROWS
         sub, lane = iotas()
         zero = jnp.zeros((ROWS, LANES), f32)
+        step = pl.program_id(0)
+
+        @pl.when(step == 0)
+        def _():
+            for f in range(3):
+                y_ref[0, f] = zero
+                y_ref[1, f] = zero
+
         sylo = [yslo_ref[1, f] for f in range(3)]
         syhi = [yshi_ref[0, f] for f in range(3)]
         cylo = [yflo_ref[1, f] for f in (3, 4)]
         cyhi = [yfhi_ref[0, f] for f in (3, 4)]
 
-        def group(a, carry):
-            y_f, y_l = carry
-            acc = EdgeAcc(3, y_f, y_l)
+        if True:
+            a = 0
+            acc = EdgeAcc(3, [y_ref[0, f] for f in range(3)], [y_ref[1, f] for f in range(3)])
             sxlo = [xslo_ref[f, a] for f in range(3)]
             sxhi = [xshi_ref[f, a] for f in range(3)]
             cxlo = [xflo_ref[f, a] for f in (3, 4)]
             cxhi = [xfhi_ref[f, a] for f in (3, 4)]
             for b in range(ROWS):
-                i = a * ROWS + b
-                d = chunk * depth + i
+                i = b
+                d = (chunk * cgroups + step) * ROWS + b
                 heat = h_ref[i]
                 water = w_ref[i]
                 carbon = c_ref[i]
@@ -209,12 +215,8 @@
             for f in range(3):
                 xf_ref[f, a] = acc.xf[f]
                 xl_ref[f, a] = acc.xl[f]
-            return (tuple(acc.yf), tuple(acc.yl))
-
-        y_f, y_l = lax.fori_loop(0, groups, group, ((zero,) * 3, (zero,) * 3))
-        for f in range(3):
-            y_ref[0, f] = y_f[f]
-            y_ref[1, f] = y_l[f]
+                y_ref[0, f] = acc.yf[f]
+                y_ref[1, f] = acc.yl[f]
 
     return kernel
 
@@ -378,28 +380,29 @@
     for section_no in range(SECTIONS):
         first = section_no == 0
         for k in range(chunks):
-            x5 = pl.BlockSpec((5, cgroups, ROWS, LANES), lambda i, k=k: (0, k, 0, 0))
-            y5 = full_spec((2, 5, ROWS, LANES))
-            in_specs = [block_spec(k)] * 5 + [
-                pl.BlockSpec((4, depth, ROWS, LANES), lambda i, k=k: (0, k, 0, 0)),
-                x5, x5, y5, y5,
+            def at(shift_fields, k=k, base=True):
+                return lambda g: (0,) * shift_fields + ((k * cgroups + g) if base else g, 0, 0)
+
+            plane = pl.BlockSpec((ROWS, ROWS, LANES), at(0))
+            x5 = pl.BlockSpec((5, 1, ROWS, LANES), at(1))
+            y5 = pl.BlockSpec((2, 5, ROWS, LANES), lambda g: (0, 0, 0, 0))
+            x3 = pl.BlockSpec((3, 1, ROWS, LANES), at(1, base=False))
+            y3 = pl.BlockSpec((2, 3, ROWS, LANES), lambda g: (0, 0, 0, 0))
+            in_specs = [plane] * 5 + [
+                pl.BlockSpec((4, ROWS, ROWS, LANES), at(1)), x5, x5, y5, y5,
             ]
             args = [heat, water, carbon, melt, injection_flags, co, xflo, xfhi, yflo, yfhi]
             if not first:
-                in_specs += [full_spec((3, cgroups, ROWS, LANES))] * 2
-                in_specs += [full_spec((2, 3, ROWS, LANES))] * 2
+                in_specs += [x3, x3, y3, y3]
                 args += list(halos[k])
             heat, water, carbon, melt, xf, xl, ys = pl.pallas_call(
-                make_section_kernel(k, first),
-                grid=(1,),
+                make_section_kernel(k, first, cgroups),
+                grid=(cgroups,),
                 out_shape=(sds(shape), sds(shape), sds(shape), sds(shape),
                            sds((3, cgroups, ROWS, LANES)), sds((3, cgroups, ROWS, LANES)),
                            sds((2, 3, ROWS, LANES))),
                 in_specs=in_specs,
-                out_specs=[block_spec(k)] * 4 + [
-                    full_spec((3, cgroups, ROWS, LANES)), full_spec((3, cgroups, ROWS, LANES)),
-                    full_spec((2, 3, ROWS, LANES)),
-                ],
+                out_specs=[plane] * 4 + [x3, x3, y3],
                 input_output_aliases={0: 0, 1: 1, 2: 2, 3: 3},
             )(*args)
             if section_no + 1 < SECTIONS:

time: 81.8 us -> 84.5 us (1.033)
  Pallas kernels: 41 us -> 43.2 us
    pallas_call x8, Pallas kernels: 32.7 us -> 34.9 us  [local(): pl.pallas_call(make_section_kernel(k, first, cgroups), grid=(cgroups,), o...]
  transfers between devices with their start and end apart: 24 -> 24, of which waited for: 5 -> 5; matrix products, arithmetic and copies ran while one was open for 0% -> 0% of each run, Pallas kernels for 30% -> 31%
where the time goes in v4:
time: 84.5 us; the launch traced here: 83.7 us
  Pallas kernels  43.2 us (51%)
  starting transfers between devices  26.1 us (31%)
  waiting for transfers between devices  5.36 us (6%)
  local copies, waits for them, and re-layouts  4.93 us (6%)
  other arithmetic  3.07 us (4%)
  between operations  1.04 us (1%)
    pallas_call x8, Pallas kernels, local(): pl.pallas_call(make_section_kernel(k, first, cgroups), grid=(cgroups,), o...  34.9 us
    ppermute x7, starting transfers between devices, exchange(): xhi = lax.ppermute(xf, 'east', east_bwd)  9.57 us
    ppermute x7, starting transfers between devices, exchange(): ylo = lax.ppermute(ys, 'north', north_fwd)  8.45 us
    ppermute x3, starting transfers between devices, local(): lax.ppermute(red, 'depth', [(i, (i + k) % count) for i in range(count)])  5.41 us
    pallas_call x1, Pallas kernels, local(): pl.pallas_call(prep_kernel, out_shape=(sds(shape), sds(shape), sds(shape)...  4.42 us
    unnamed x51, local copies, waits for them, and re-layouts  4.36 us
    pallas_call x1, Pallas kernels, local(): pl.pallas_call(sweep_kernel, grid=(1,), out_shape=(sds(shape), sds(shape)...  3.86 us
    ppermute x3, waiting for transfers between devices, local(): lax.ppermute(red, 'depth', [(i, (i + k) % count) for i in range(count)])  2.76 us
  transfers between devices with their start and end apart: 24, of which 5 were waited for; matrix products, arithmetic and copies ran while one was open for 0% of the time, Pallas kernels for 31%

profile of v4, /device:TPU:0, one launch (start us, length us, event | category | flops | bytes accessed | tf_op | source)
XLA Modules:
  0.0 83.7 jit_solution(14912624486897882906)
XLA Ops:
  0.6 1.3 %pad_maximum_fusion.1.tab_ref = f32[5,12]{1,0:T(8,128)} fusion(f32[1,12]{1,0:T(1,128)} %bitcast.219, f32[2,12]{1,0:T(2,128)} %param.17, f32[2,12]{1,0:T(2,128)} %param.15), kind=kLoop, calls=%fused_computation.86 | loop fusion | flops 120 | bytes 480 | tf_op jit(solution)/shard_map/concatenate | solution.py:361
  1.9 4.4 %shard_map.120 = (f32[64,8,128]{2,1,0:T(8,128)}, f32[64,8,128]{2,1,0:T(8,128)}, f32[64,8,128]{2,1,0:T(8,128)}, f32[64,8,128]{2,1,0:T(8,128)}, f32[5,64,8,128]{3,...) custom-call(f32[5,12]{1,0:T(8,128)} %pad_maximum_fusion.1.tab_ref, ...), custom_call_target="tpu_custom_call" | custom-call | tf_op jit(solution)/shard_map/pallas_call | solution.py:366
  6.4 0.5 collective-permute-start
  6.8 2.0 %collective-permute-start.1 = (f32[5,8,8,128]{3,2,1,0:T(8,128)}, f32[5,8,8,128]{3,2,1,0:T(8,128)S(1)}, u32[]{:S(2)}, u32[]{:S(2)}) collective-permute-start(f32[5,8,8,128]{3,2,1,0:T(8,128)} %get-tuple-element.72), channel_id=1, source_target_pairs={{8,0},{16,8},{24,16},{0,24},{9,1},{17,9},{25,17},{1,25},{10,2},{18... | collective-permute-start | bytes 491528 | tf_op jit(solution)/shard_map/ppermute | solution.py:329
  8.8 2.3 %collective-permute-start.2 = (f32[2,5,8,128]{3,2,1,0:T(8,128)}, f32[2,5,8,128]{3,2,1,0:T(8,128)S(1)}, u32[]{:S(2)}, u32[]{:S(2)}) collective-permute-start(f32[2,5,8,128]{3,2,1,0:T(8,128)} %get-tuple-element.73), channel_id=1, source_target_pairs={{0,4},{4,0},{1,5},{5,1},{2,6},{6,2},{3,7},{7,3},{8,12},{12,8},{9,1... | collective-permute-start | bytes 122888 | tf_op jit(solution)/shard_map/ppermute | solution.py:330
  11.1 2.2 %collective-permute-done.2.yflo_ref.yfhi_ref = f32[2,5,8,128]{3,2,1,0:T(8,128)S(1)} collective-permute-done((f32[2,5,8,128]{3,2,1,0:T(8,128)}, f32[2,5,8,128]{3,2,1,0:T(8,128)S(1)}, u32[]{:S(2)}, u32[]{:S(2)}) %collective-permute-start.2) | collective-permute-done | bytes 40992 | tf_op jit(solution)/shard_map/ppermute | solution.py:330
  13.3 0.4 collective-permute-done.1.xfhi_ref
  13.6 0.2 copy-done.2
  13.9 0.4 copy-done.1
  14.3 4.3 %shard_map.121 = (f32[64,8,128]{2,1,0:T(8,128)}, f32[64,8,128]{2,1,0:T(8,128)}, f32[64,8,128]{2,1,0:T(8,128)}, f32[64,8,128]{2,1,0:T(8,128)}, f32[3,4,8,128]{3,2...) custom-call(f32[64,8,128]{2,1,0:T(8,128)} %get-tuple-element.66.h_re, ...), custom_call_target="tpu_custom_call", output_to_operand_aliasing={{0}: (0, {}), {1}: (1, {}), {2}: (2, {}), {3}: (3, {})} | custom-call | tf_op jit(solution)/shard_map/pallas_call | solution.py:398
  18.6 0.8 collective-permute-start.3
  19.4 1.3 %collective-permute-start.4 = (f32[3,4,8,128]{3,2,1,0:T(8,128)}, f32[3,4,8,128]{3,2,1,0:T(8,128)S(1)}, u32[]{:S(2)}, u32[]{:S(2)}) collective-permute-start(f32[3,4,8,128]{3,2,1,0:T(8,128)} %get-tuple-element.83), channel_id=1, source_target_pairs={{8,0},{16,8},{24,16},{0,24},{9,1},{17,9},{25,17},{1,25},{10,2},{18... | collective-permute-start | bytes 147464 | tf_op jit(solution)/shard_map/ppermute | solution.py:329
  20.7 1.4 %collective-permute-start.5 = (f32[2,3,8,128]{3,2,1,0:T(8,128)}, f32[2,3,8,128]{3,2,1,0:T(8,128)S(1)}, u32[]{:S(2)}, u32[]{:S(2)}) collective-permute-start(f32[2,3,8,128]{3,2,1,0:T(8,128)} %get-tuple-element.84), channel_id=1, source_target_pairs={{0,4},{4,0},{1,5},{5,1},{2,6},{6,2},{3,7},{7,3},{8,12},{12,8},{9,1... | collective-permute-start | bytes 73736 | tf_op jit(solution)/shard_map/ppermute | solution.py:330
  22.1 4.3 %shard_map.122 = (f32[64,8,128]{2,1,0:T(8,128)}, f32[64,8,128]{2,1,0:T(8,128)}, f32[64,8,128]{2,1,0:T(8,128)}, f32[64,8,128]{2,1,0:T(8,128)}, f32[3,4,8,128]{3,2...) custom-call(f32[64,8,128]{2,1,0:T(8,128)} %get-tuple-element.74.h_re, ...), custom_call_target="tpu_custom_call", output_to_operand_aliasing={{0}: (0, {}), {1}: (1, {}), {2}: (2, {}), {3}: (3, {})} | custom-call | tf_op jit(solution)/shard_map/pallas_call | solution.py:398
  26.5 1.7 %collective-permute-start.7 = (f32[3,4,8,128]{3,2,1,0:T(8,128)}, f32[3,4,8,128]{3,2,1,0:T(8,128)S(1)}, u32[]{:S(2)}, u32[]{:S(2)}) collective-permute-start(f32[3,4,8,128]{3,2,1,0:T(8,128)} %get-tuple-element.90), channel_id=1, source_target_pairs={{8,0},{16,8},{24,16},{0,24},{9,1},{17,9},{25,17},{1,25},{10,2},{18... | collective-permute-start | bytes 147464 | tf_op jit(solution)/shard_map/ppermute | solution.py:329
  28.3 0.7 collective-permute-start.8
  29.0 0.6 copy-done.22
  29.6 4.3 %shard_map.123 = (f32[64,8,128]{2,1,0:T(8,128)}, f32[64,8,128]{2,1,0:T(8,128)}, f32[64,8,128]{2,1,0:T(8,128)}, f32[64,8,128]{2,1,0:T(8,128)}, f32[3,4,8,128]{3,2...) custom-call(f32[64,8,128]{2,1,0:T(8,128)} %get-tuple-element.78.h_re, ...), custom_call_target="tpu_custom_call", output_to_operand_aliasing={{0}: (0, {}), {1}: (1, {}), {2}: (2, {}), {3}: (3, {})} | custom-call | tf_op jit(solution)/shard_map/pallas_call | solution.py:398
  33.9 0.2 collective-permute-start.10
  34.1 0.4 collective-permute-start.9
  34.5 1.4 %collective-permute-start.11 = (f32[2,3,8,128]{3,2,1,0:T(8,128)}, f32[2,3,8,128]{3,2,1,0:T(8,128)S(1)}, u32[]{:S(2)}, u32[]{:S(2)}) collective-permute-start(f32[2,3,8,128]{3,2,1,0:T(8,128)} %get-tuple-element.98), channel_id=1, source_target_pairs={{0,4},{4,0},{1,5},{5,1},{2,6},{6,2},{3,7},{7,3},{8,12},{12,8},{9,1... | collective-permute-start | bytes 73736 | tf_op jit(solution)/shard_map/ppermute | solution.py:330
  35.9 0.6 copy-done.12
  36.4 4.4 %shard_map.124 = (f32[64,8,128]{2,1,0:T(8,128)}, f32[64,8,128]{2,1,0:T(8,128)}, f32[64,8,128]{2,1,0:T(8,128)}, f32[64,8,128]{2,1,0:T(8,128)}, f32[3,4,8,128]{3,2...) custom-call(f32[64,8,128]{2,1,0:T(8,128)} %get-tuple-element.85.h_re, ...), custom_call_target="tpu_custom_call", output_to_operand_aliasing={{0}: (0, {}), {1}: (1, {}), {2}: (2, {}), {3}: (3, {})} | custom-call | tf_op jit(solution)/shard_map/pallas_call | solution.py:398
  40.9 0.9 %collective-permute-start.12 = (f32[3,4,8,128]{3,2,1,0:T(8,128)}, f32[3,4,8,128]{3,2,1,0:T(8,128)S(1)}, u32[]{:S(2)}, u32[]{:S(2)}) collective-permute-start(f32[3,4,8,128]{3,2,1,0:T(8,128)} %get-tuple-element.103), channel_id=1, source_target_pairs={{0,8},{8,16},{16,24},{24,0},{1,9},{9,17},{17,25},{25,1},{2,10},{10... | collective-permute-start | bytes 147464 | tf_op jit(solution)/shard_map/ppermute | solution.py:328
  41.8 0.9 %collective-permute-start.13 = (f32[3,4,8,128]{3,2,1,0:T(8,128)}, f32[3,4,8,128]{3,2,1,0:T(8,128)S(1)}, u32[]{:S(2)}, u32[]{:S(2)}) collective-permute-start(f32[3,4,8,128]{3,2,1,0:T(8,128)} %get-tuple-element.104), channel_id=1, source_target_pairs={{8,0},{16,8},{24,16},{0,24},{9,1},{17,9},{25,17},{1,25},{10,2},{18... | collective-permute-start | bytes 147464 | tf_op jit(solution)/shard_map/ppermute | solution.py:329
  42.7 0.7 collective-permute-start.14
  43.4 0.6 copy-done.13
  44.0 4.3 %shard_map.125 = (f32[64,8,128]{2,1,0:T(8,128)}, f32[64,8,128]{2,1,0:T(8,128)}, f32[64,8,128]{2,1,0:T(8,128)}, f32[64,8,128]{2,1,0:T(8,128)}, f32[3,4,8,128]{3,2...) custom-call(f32[64,8,128]{2,1,0:T(8,128)} %get-tuple-element.92.h_re, ...), custom_call_target="tpu_custom_call", output_to_operand_aliasing={{0}: (0, {}), {1}: (1, {}), {2}: (2, {}), {3}: (3, {})} | custom-call | tf_op jit(solution)/shard_map/pallas_call | solution.py:398
  48.3 1.4 %collective-permute-start.17 = (f32[2,3,8,128]{3,2,1,0:T(8,128)}, f32[2,3,8,128]{3,2,1,0:T(8,128)S(1)}, u32[]{:S(2)}, u32[]{:S(2)}) collective-permute-start(f32[2,3,8,128]{3,2,1,0:T(8,128)} %get-tuple-element.112), channel_id=1, source_target_pairs={{0,4},{4,0},{1,5},{5,1},{2,6},{6,2},{3,7},{7,3},{8,12},{12,8},{9,1... | collective-permute-start | bytes 73736 | tf_op jit(solution)/shard_map/ppermute | solution.py:330
  49.9 1.7 %collective-permute-start.16 = (f32[3,4,8,128]{3,2,1,0:T(8,128)}, f32[3,4,8,128]{3,2,1,0:T(8,128)S(1)}, u32[]{:S(2)}, u32[]{:S(2)}) collective-permute-start(f32[3,4,8,128]{3,2,1,0:T(8,128)} %get-tuple-element.111), channel_id=1, source_target_pairs={{8,0},{16,8},{24,16},{0,24},{9,1},{17,9},{25,17},{1,25},{10,2},{18... | collective-permute-start | bytes 147464 | tf_op jit(solution)/shard_map/ppermute | solution.py:329
  51.6 0.6 copy-done.16
  52.2 4.4 %shard_map.126 = (f32[64,8,128]{2,1,0:T(8,128)}, f32[64,8,128]{2,1,0:T(8,128)}, f32[64,8,128]{2,1,0:T(8,128)}, f32[64,8,128]{2,1,0:T(8,128)}, f32[3,4,8,128]{3,2...) custom-call(f32[64,8,128]{2,1,0:T(8,128)} %get-tuple-element.99.h_re, ...), custom_call_target="tpu_custom_call", output_to_operand_aliasing={{0}: (0, {}), {1}: (1, {}), {2}: (2, {}), {3}: (3, {})} | custom-call | tf_op jit(solution)/shard_map/pallas_call | solution.py:398
  56.7 1.7 %collective-permute-start.19 = (f32[3,4,8,128]{3,2,1,0:T(8,128)}, f32[3,4,8,128]{3,2,1,0:T(8,128)S(1)}, u32[]{:S(2)}, u32[]{:S(2)}) collective-permute-start(f32[3,4,8,128]{3,2,1,0:T(8,128)} %get-tuple-element.118), channel_id=1, source_target_pairs={{8,0},{16,8},{24,16},{0,24},{9,1},{17,9},{25,17},{1,25},{10,2},{18... | collective-permute-start | bytes 147464 | tf_op jit(solution)/shard_map/ppermute | solution.py:329
  58.4 0.7 collective-permute-start.20
  59.2 0.6 copy-done.17
  59.8 4.3 %shard_map.127 = (f32[64,8,128]{2,1,0:T(8,128)}, f32[64,8,128]{2,1,0:T(8,128)}, f32[64,8,128]{2,1,0:T(8,128)}, f32[64,8,128]{2,1,0:T(8,128)}, f32[3,4,8,128]{3,2...) custom-call(f32[64,8,128]{2,1,0:T(8,128)} %get-tuple-element.106.h_r, ...), custom_call_target="tpu_custom_call", output_to_operand_aliasing={{0}: (0, {}), {1}: (1, {}), {2}: (2, {}), {3}: (3, {})} | custom-call | tf_op jit(solution)/shard_map/pallas_call | solution.py:398
  64.2 0.6 copy-done.10
  64.8 4.4 %shard_map.128 = (f32[64,8,128]{2,1,0:T(8,128)}, f32[64,8,128]{2,1,0:T(8,128)}, f32[64,8,128]{2,1,0:T(8,128)}, f32[64,8,128]{2,1,0:T(8,128)}, f32[3,4,8,128]{3,2...) custom-call(f32[64,8,128]{2,1,0:T(8,128)} %get-tuple-element.113.h_r, ...), custom_call_target="tpu_custom_call", output_to_operand_aliasing={{0}: (0, {}), {1}: (1, {}), {2}: (2, {}), {3}: (3, {})} | custom-call | tf_op jit(solution)/shard_map/pallas_call | solution.py:398
  69.2 3.9 %shard_map.129 = (f32[64,8,128]{2,1,0:T(8,128)}, f32[64,8,128]{2,1,0:T(8,128)}, f32[64,8,128]{2,1,0:T(8,128)}, f32[8,8,128]{2,1,0:T(8,128)}) custom-call(f32[64,8,128]{2,1,0:T(8,128)} %get-tuple-element.120.r_ref, f32[5,64,8,128]{3,2,1,0:T(8,128)} %get-tuple-element.70.co_ref.cz_ref), custom_call_target="tpu_custom_call" | custom-call | tf_op jit(solution)/shard_map/pallas_call | solution.py:411
  73.1 1.5 %collective-permute-start.21 = (f32[8,8,128]{2,1,0:T(8,128)}, f32[8,8,128]{2,1,0:T(8,128)S(1)}, u32[]{:S(2)}, u32[]{:S(2)}) collective-permute-start(f32[8,8,128]{2,1,0:T(8,128)} %get-tuple-element.123), channel_id=1, source_target_pairs={{0,1},{1,2},{2,3},{3,0},{4,5},{5,6},{6,7},{7,4},{8,9},{9,10},{10,1... | collective-permute-start | bytes 98312 | tf_op jit(solution)/shard_map/ppermute | solution.py:423
  74.6 2.6 %collective-permute-start.22 = (f32[8,8,128]{2,1,0:T(8,128)}, f32[8,8,128]{2,1,0:T(8,128)S(1)}, u32[]{:S(2)}, u32[]{:S(2)}) collective-permute-start(f32[8,8,128]{2,1,0:T(8,128)} %get-tuple-element.123), channel_id=1, source_target_pairs={{0,2},{1,3},{2,0},{3,1},{4,6},{5,7},{6,4},{7,5},{8,10},{9,11},{10,... | collective-permute-start | bytes 98312 | tf_op jit(solution)/shard_map/ppermute | solution.py:423
  77.2 1.3 %collective-permute-start.23 = (f32[8,8,128]{2,1,0:T(8,128)}, f32[8,8,128]{2,1,0:T(8,128)S(1)}, u32[]{:S(2)}, u32[]{:S(2)}) collective-permute-start(f32[8,8,128]{2,1,0:T(8,128)} %get-tuple-element.123), channel_id=1, source_target_pairs={{0,3},{1,0},{2,1},{3,2},{4,7},{5,4},{6,5},{7,6},{8,11},{9,8},{10,9... | collective-permute-start | bytes 98312 | tf_op jit(solution)/shard_map/ppermute | solution.py:423
  78.5 1.0 %collective-permute-done.21 = f32[8,8,128]{2,1,0:T(8,128)S(1)} collective-permute-done((f32[8,8,128]{2,1,0:T(8,128)}, f32[8,8,128]{2,1,0:T(8,128)S(1)}, u32[]{:S(2)}, u32[]{:S(2)}) %collective-permute-start.21) | collective-permute-done | bytes 32800 | tf_op jit(solution)/shard_map/ppermute | solution.py:423
  79.5 0.5 collective-permute-done.22
  80.0 1.3 %collective-permute-done.23 = f32[8,8,128]{2,1,0:T(8,128)S(1)} collective-permute-done((f32[8,8,128]{2,1,0:T(8,128)}, f32[8,8,128]{2,1,0:T(8,128)S(1)}, u32[]{:S(2)}, u32[]{:S(2)}) %collective-permute-start.23) | collective-permute-done | bytes 32800 | tf_op jit(solution)/shard_map/ppermute | solution.py:423
  81.3 0.8 pad_maximum_fusion
  82.1 0.6 gather_fusion
  83.0 0.7 multiply_add_fusion
  (77 shorter events, 0.8 us)
Async XLA Ops:
  6.4 6.9 %collective-permute-start = (f32[5,8,8,128]{3,2,1,0:T(8,128)}, f32[5,8,8,128]{3,2,1,0:T(8,128)S(1)}, u32[]{:S(2)}, u32[]{:S(2)}) collective-permute-start(f32[5,8,8,128]{3,2,1,0:T(8,128)} %get-tuple-element.71), channel_id=1, source_target_pairs={{0,8},{8,16},{16,24},{24,0},{1,9},{9,17},{17,25},{25,1},{2,10},{10... | collective-permute-start | bytes 491528 | tf_op jit(solution)/shard_map/ppermute | solution.py:328
  6.8 6.8 %collective-permute-start.1 = (f32[5,8,8,128]{3,2,1,0:T(8,128)}, f32[5,8,8,128]{3,2,1,0:T(8,128)S(1)}, u32[]{:S(2)}, u32[]{:S(2)}) collective-permute-start(f32[5,8,8,128]{3,2,1,0:T(8,128)} %get-tuple-element.72), channel_id=1, source_target_pairs={{8,0},{16,8},{24,16},{0,24},{9,1},{17,9},{25,17},{1,25},{10,2},{18... | collective-permute-start | bytes 491528 | tf_op jit(solution)/shard_map/ppermute | solution.py:329
  8.8 4.5 %collective-permute-start.2 = (f32[2,5,8,128]{3,2,1,0:T(8,128)}, f32[2,5,8,128]{3,2,1,0:T(8,128)S(1)}, u32[]{:S(2)}, u32[]{:S(2)}) collective-permute-start(f32[2,5,8,128]{3,2,1,0:T(8,128)} %get-tuple-element.73), channel_id=1, source_target_pairs={{0,4},{4,0},{1,5},{5,1},{2,6},{6,2},{3,7},{7,3},{8,12},{12,8},{9,1... | collective-permute-start | bytes 122888 | tf_op jit(solution)/shard_map/ppermute | solution.py:330
  13.3 0.6 copy-start.2
  13.3 0.7 copy-start
  13.6 0.7 copy-start.1
  18.6 10.4 %collective-permute-start.3 = (f32[3,4,8,128]{3,2,1,0:T(8,128)}, f32[3,4,8,128]{3,2,1,0:T(8,128)S(1)}, u32[]{:S(2)}, u32[]{:S(2)}) collective-permute-start(f32[3,4,8,128]{3,2,1,0:T(8,128)} %get-tuple-element.82), channel_id=1, source_target_pairs={{0,8},{8,16},{16,24},{24,0},{1,9},{9,17},{17,25},{25,1},{2,10},{10... | collective-permute-start | bytes 147464 | tf_op jit(solution)/shard_map/ppermute | solution.py:328
  19.4 9.6 %collective-permute-start.4 = (f32[3,4,8,128]{3,2,1,0:T(8,128)}, f32[3,4,8,128]{3,2,1,0:T(8,128)S(1)}, u32[]{:S(2)}, u32[]{:S(2)}) collective-permute-start(f32[3,4,8,128]{3,2,1,0:T(8,128)} %get-tuple-element.83), channel_id=1, source_target_pairs={{8,0},{16,8},{24,16},{0,24},{9,1},{17,9},{25,17},{1,25},{10,2},{18... | collective-permute-start | bytes 147464 | tf_op jit(solution)/shard_map/ppermute | solution.py:329
  20.7 7.5 %collective-permute-start.5 = (f32[2,3,8,128]{3,2,1,0:T(8,128)}, f32[2,3,8,128]{3,2,1,0:T(8,128)S(1)}, u32[]{:S(2)}, u32[]{:S(2)}) collective-permute-start(f32[2,3,8,128]{3,2,1,0:T(8,128)} %get-tuple-element.84), channel_id=1, source_target_pairs={{0,4},{4,0},{1,5},{5,1},{2,6},{6,2},{3,7},{7,3},{8,12},{12,8},{9,1... | collective-permute-start | bytes 73736 | tf_op jit(solution)/shard_map/ppermute | solution.py:330
  26.5 9.4 %collective-permute-start.6 = (f32[3,4,8,128]{3,2,1,0:T(8,128)}, f32[3,4,8,128]{3,2,1,0:T(8,128)S(1)}, u32[]{:S(2)}, u32[]{:S(2)}) collective-permute-start(f32[3,4,8,128]{3,2,1,0:T(8,128)} %get-tuple-element.89), channel_id=1, source_target_pairs={{0,8},{8,16},{16,24},{24,0},{1,9},{9,17},{17,25},{25,1},{2,10},{10... | collective-permute-start | bytes 147464 | tf_op jit(solution)/shard_map/ppermute | solution.py:328
  26.5 9.3 %collective-permute-start.7 = (f32[3,4,8,128]{3,2,1,0:T(8,128)}, f32[3,4,8,128]{3,2,1,0:T(8,128)S(1)}, u32[]{:S(2)}, u32[]{:S(2)}) collective-permute-start(f32[3,4,8,128]{3,2,1,0:T(8,128)} %get-tuple-element.90), channel_id=1, source_target_pairs={{8,0},{16,8},{24,16},{0,24},{9,1},{17,9},{25,17},{1,25},{10,2},{18... | collective-permute-start | bytes 147464 | tf_op jit(solution)/shard_map/ppermute | solution.py:329
  28.3 0.7 copy-start.11
  28.3 6.2 %collective-permute-start.8 = (f32[2,3,8,128]{3,2,1,0:T(8,128)}, f32[2,3,8,128]{3,2,1,0:T(8,128)S(1)}, u32[]{:S(2)}, u32[]{:S(2)}) collective-permute-start(f32[2,3,8,128]{3,2,1,0:T(8,128)} %get-tuple-element.91), channel_id=1, source_target_pairs={{0,4},{4,0},{1,5},{5,1},{2,6},{6,2},{3,7},{7,3},{8,12},{12,8},{9,1... | collective-permute-start | bytes 73736 | tf_op jit(solution)/shard_map/ppermute | solution.py:330
  28.9 0.6 copy-start.22
  29.0 0.6 copy-start.23
  33.9 9.4 %collective-permute-start.10 = (f32[3,4,8,128]{3,2,1,0:T(8,128)}, f32[3,4,8,128]{3,2,1,0:T(8,128)S(1)}, u32[]{:S(2)}, u32[]{:S(2)}) collective-permute-start(f32[3,4,8,128]{3,2,1,0:T(8,128)} %get-tuple-element.97), channel_id=1, source_target_pairs={{8,0},{16,8},{24,16},{0,24},{9,1},{17,9},{25,17},{1,25},{10,2},{18... | collective-permute-start | bytes 147464 | tf_op jit(solution)/shard_map/ppermute | solution.py:329
  34.1 9.3 %collective-permute-start.9 = (f32[3,4,8,128]{3,2,1,0:T(8,128)}, f32[3,4,8,128]{3,2,1,0:T(8,128)S(1)}, u32[]{:S(2)}, u32[]{:S(2)}) collective-permute-start(f32[3,4,8,128]{3,2,1,0:T(8,128)} %get-tuple-element.96), channel_id=1, source_target_pairs={{0,8},{8,16},{16,24},{24,0},{1,9},{9,17},{17,25},{25,1},{2,10},{10... | collective-permute-start | bytes 147464 | tf_op jit(solution)/shard_map/ppermute | solution.py:328
  34.5 1.4 %copy-start.7 = (f32[2,3,8,128]{3,2,1,0:T(8,128)}, f32[2,3,8,128]{3,2,1,0:T(8,128)S(1)}, u32[]{:S(2)}) copy-start(f32[2,3,8,128]{3,2,1,0:T(8,128)S(1)} %collective-permute-done.8.rest_2_.rest_3_) | copy-start | bytes 73732
  34.5 8.2 %collective-permute-start.11 = (f32[2,3,8,128]{3,2,1,0:T(8,128)}, f32[2,3,8,128]{3,2,1,0:T(8,128)S(1)}, u32[]{:S(2)}, u32[]{:S(2)}) collective-permute-start(f32[2,3,8,128]{3,2,1,0:T(8,128)} %get-tuple-element.98), channel_id=1, source_target_pairs={{0,4},{4,0},{1,5},{5,1},{2,6},{6,2},{3,7},{7,3},{8,12},{12,8},{9,1... | collective-permute-start | bytes 73736 | tf_op jit(solution)/shard_map/ppermute | solution.py:330
  35.8 0.6 copy-start.12
  35.8 0.6 copy-start.14
  40.9 10.7 %collective-permute-start.12 = (f32[3,4,8,128]{3,2,1,0:T(8,128)}, f32[3,4,8,128]{3,2,1,0:T(8,128)S(1)}, u32[]{:S(2)}, u32[]{:S(2)}) collective-permute-start(f32[3,4,8,128]{3,2,1,0:T(8,128)} %get-tuple-element.103), channel_id=1, source_target_pairs={{0,8},{8,16},{16,24},{24,0},{1,9},{9,17},{17,25},{25,1},{2,10},{10... | collective-permute-start | bytes 147464 | tf_op jit(solution)/shard_map/ppermute | solution.py:328
  41.8 9.8 %collective-permute-start.13 = (f32[3,4,8,128]{3,2,1,0:T(8,128)}, f32[3,4,8,128]{3,2,1,0:T(8,128)S(1)}, u32[]{:S(2)}, u32[]{:S(2)}) collective-permute-start(f32[3,4,8,128]{3,2,1,0:T(8,128)} %get-tuple-element.104), channel_id=1, source_target_pairs={{8,0},{16,8},{24,16},{0,24},{9,1},{17,9},{25,17},{1,25},{10,2},{18... | collective-permute-start | bytes 147464 | tf_op jit(solution)/shard_map/ppermute | solution.py:329
  42.7 0.7 copy-start.8
  42.7 7.2 %collective-permute-start.14 = (f32[2,3,8,128]{3,2,1,0:T(8,128)}, f32[2,3,8,128]{3,2,1,0:T(8,128)S(1)}, u32[]{:S(2)}, u32[]{:S(2)}) collective-permute-start(f32[2,3,8,128]{3,2,1,0:T(8,128)} %get-tuple-element.105), channel_id=1, source_target_pairs={{0,4},{4,0},{1,5},{5,1},{2,6},{6,2},{3,7},{7,3},{8,12},{12,8},{9,1... | collective-permute-start | bytes 73736 | tf_op jit(solution)/shard_map/ppermute | solution.py:330
  43.3 0.6 copy-start.13
  43.4 0.6 copy-start.15
  48.3 10.1 %collective-permute-start.17 = (f32[2,3,8,128]{3,2,1,0:T(8,128)}, f32[2,3,8,128]{3,2,1,0:T(8,128)S(1)}, u32[]{:S(2)}, u32[]{:S(2)}) collective-permute-start(f32[2,3,8,128]{3,2,1,0:T(8,128)} %get-tuple-element.112), channel_id=1, source_target_pairs={{0,4},{4,0},{1,5},{5,1},{2,6},{6,2},{3,7},{7,3},{8,12},{12,8},{9,1... | collective-permute-start | bytes 73736 | tf_op jit(solution)/shard_map/ppermute | solution.py:330
  49.8 9.4 %collective-permute-start.15 = (f32[3,4,8,128]{3,2,1,0:T(8,128)}, f32[3,4,8,128]{3,2,1,0:T(8,128)S(1)}, u32[]{:S(2)}, u32[]{:S(2)}) collective-permute-start(f32[3,4,8,128]{3,2,1,0:T(8,128)} %get-tuple-element.110), channel_id=1, source_target_pairs={{0,8},{8,16},{16,24},{24,0},{1,9},{9,17},{17,25},{25,1},{2,10},{10... | collective-permute-start | bytes 147464 | tf_op jit(solution)/shard_map/ppermute | solution.py:328
  49.8 1.8 %copy-start.9 = (f32[2,3,8,128]{3,2,1,0:T(8,128)}, f32[2,3,8,128]{3,2,1,0:T(8,128)S(1)}, u32[]{:S(2)}) copy-start(f32[2,3,8,128]{3,2,1,0:T(8,128)S(1)} %collective-permute-done.14.rest_2_.rest_3_) | copy-start | bytes 73732
  49.9 9.3 %collective-permute-start.16 = (f32[3,4,8,128]{3,2,1,0:T(8,128)}, f32[3,4,8,128]{3,2,1,0:T(8,128)S(1)}, u32[]{:S(2)}, u32[]{:S(2)}) collective-permute-start(f32[3,4,8,128]{3,2,1,0:T(8,128)} %get-tuple-element.111), channel_id=1, source_target_pairs={{8,0},{16,8},{24,16},{0,24},{9,1},{17,9},{25,17},{1,25},{10,2},{18... | collective-permute-start | bytes 147464 | tf_op jit(solution)/shard_map/ppermute | solution.py:329
  51.6 0.6 copy-start.16
  51.6 0.6 copy-start.18
  56.6 7.5 %collective-permute-start.18 = (f32[3,4,8,128]{3,2,1,0:T(8,128)}, f32[3,4,8,128]{3,2,1,0:T(8,128)S(1)}, u32[]{:S(2)}, u32[]{:S(2)}) collective-permute-start(f32[3,4,8,128]{3,2,1,0:T(8,128)} %get-tuple-element.117), channel_id=1, source_target_pairs={{0,8},{8,16},{16,24},{24,0},{1,9},{9,17},{17,25},{25,1},{2,10},{10... | collective-permute-start | bytes 147464 | tf_op jit(solution)/shard_map/ppermute | solution.py:328
  56.7 7.4 %collective-permute-start.19 = (f32[3,4,8,128]{3,2,1,0:T(8,128)}, f32[3,4,8,128]{3,2,1,0:T(8,128)S(1)}, u32[]{:S(2)}, u32[]{:S(2)}) collective-permute-start(f32[3,4,8,128]{3,2,1,0:T(8,128)} %get-tuple-element.118), channel_id=1, source_target_pairs={{8,0},{16,8},{24,16},{0,24},{9,1},{17,9},{25,17},{1,25},{10,2},{18... | collective-permute-start | bytes 147464 | tf_op jit(solution)/shard_map/ppermute | solution.py:329
  58.4 0.7 copy-start.6
  58.4 5.7 %collective-permute-start.20 = (f32[2,3,8,128]{3,2,1,0:T(8,128)}, f32[2,3,8,128]{3,2,1,0:T(8,128)S(1)}, u32[]{:S(2)}, u32[]{:S(2)}) collective-permute-start(f32[2,3,8,128]{3,2,1,0:T(8,128)} %get-tuple-element.119), channel_id=1, source_target_pairs={{0,4},{4,0},{1,5},{5,1},{2,6},{6,2},{3,7},{7,3},{8,12},{12,8},{9,1... | collective-permute-start | bytes 73736 | tf_op jit(solution)/shard_map/ppermute | solution.py:330
  59.1 0.6 copy-start.17
  59.1 0.6 copy-start.21
  64.1 0.6 copy-start.10
  64.1 0.6 copy-start.19
  64.2 0.6 copy-start.20
  73.1 9.8 %copy-start.3 = (f32[64,8,128]{2,1,0:T(8,128)S(1)}, f32[64,8,128]{2,1,0:T(8,128)}, u32[]{:S(2)}) copy-start(f32[64,8,128]{2,1,0:T(8,128)} %get-tuple-element.121) | copy-start | bytes 786436
  73.1 9.9 %copy-start.4 = (f32[64,8,128]{2,1,0:T(8,128)S(1)}, f32[64,8,128]{2,1,0:T(8,128)}, u32[]{:S(2)}) copy-start(f32[64,8,128]{2,1,0:T(8,128)} %get-tuple-element.122) | copy-start | bytes 786436
  73.1 9.9 %copy-start.5 = (f32[64,8,128]{2,1,0:T(8,128)S(1)}, f32[64,8,128]{2,1,0:T(8,128)}, u32[]{:S(2)}) copy-start(f32[64,8,128]{2,1,0:T(8,128)} %get-tuple-element.124) | copy-start | bytes 786436
  73.1 6.4 %collective-permute-start.21 = (f32[8,8,128]{2,1,0:T(8,128)}, f32[8,8,128]{2,1,0:T(8,128)S(1)}, u32[]{:S(2)}, u32[]{:S(2)}) collective-permute-start(f32[8,8,128]{2,1,0:T(8,128)} %get-tuple-element.123), channel_id=1, source_target_pairs={{0,1},{1,2},{2,3},{3,0},{4,5},{5,6},{6,7},{7,4},{8,9},{9,10},{10,1... | collective-permute-start | bytes 98312 | tf_op jit(solution)/shard_map/ppermute | solution.py:423
  74.6 5.5 %collective-permute-start.22 = (f32[8,8,128]{2,1,0:T(8,128)}, f32[8,8,128]{2,1,0:T(8,128)S(1)}, u32[]{:S(2)}, u32[]{:S(2)}) collective-permute-start(f32[8,8,128]{2,1,0:T(8,128)} %get-tuple-element.123), channel_id=1, source_target_pairs={{0,2},{1,3},{2,0},{3,1},{4,6},{5,7},{6,4},{7,5},{8,10},{9,11},{10,... | collective-permute-start | bytes 98312 | tf_op jit(solution)/shard_map/ppermute | solution.py:423
  77.2 4.1 %collective-permute-start.23 = (f32[8,8,128]{2,1,0:T(8,128)}, f32[8,8,128]{2,1,0:T(8,128)S(1)}, u32[]{:S(2)}, u32[]{:S(2)}) collective-permute-start(f32[8,8,128]{2,1,0:T(8,128)} %get-tuple-element.123), channel_id=1, source_target_pairs={{0,3},{1,0},{2,1},{3,2},{4,7},{5,4},{6,5},{7,6},{8,11},{9,8},{10,9... | collective-permute-start | bytes 98312 | tf_op jit(solution)/shard_map/ppermute | solution.py:423

commit v5 on v3

--- a/solution.py
+++ b/solution.py
@@ -82,10 +82,10 @@
     )
 
 
-def prep_kernel(tab_ref, layer_ref, h_ref, w_ref, c_ref, m_ref,
+def prep_kernel(lat_ref, vert_ref, adv_ref, layer_ref, h_ref, w_ref, c_ref, m_ref,
                 ho_ref, wo_ref, cbo_ref, mo_ref, co_ref, xf_ref, xl_ref, y_ref):
     groups = layer_ref.shape[0] // ROWS
-    layers_count = tab_ref.shape[1]
+    layers_count = vert_ref.shape[0]
     sub, lane = iotas()
     zero = jnp.zeros((ROWS, LANES), f32)
 
@@ -98,7 +98,8 @@
             vals = [zero] * 5
             for l in range(layers_count):
                 hit = layer == l
-                vals = [jnp.where(hit, tab_ref[k, l], vals[k]) for k in range(5)]
+                entries = (lat_ref[0, l], lat_ref[1, l], adv_ref[0, l], adv_ref[1, l], vert_ref[l])
+                vals = [jnp.where(hit, entries[k], vals[k]) for k in range(5)]
             for k in range(5):
                 co_ref[k, d] = vals[k]
             heat, water, carbon = h_ref[d], w_ref[d], c_ref[d]
@@ -277,21 +278,21 @@
 
 
 def reduced_solve(red_all):
-    count = red_all.shape[0]
+    count = len(red_all)
     lower, diag, upper, side = [], [], [], []
     for j in range(count):
-        p0, q0, s0, p1, q1, s1, c_first, c_last = [red_all[j, k] for k in range(8)]
+        p0, q0, s0, p1, q1, s1, c_first, c_last = red_all[j]
         if j == 0:
             face = c_first
             lower.append(jnp.zeros_like(face))
         else:
-            face = 0.5 * (red_all[j - 1, 7] + c_first)
+            face = 0.5 * (red_all[j - 1][7] + c_first)
             lower.append(face)
         diag.append(p0 + face)
         upper.append(q0)
         side.append(s0)
         if j + 1 < count:
-            below = 0.5 * (c_last + red_all[j + 1, 6])
+            below = 0.5 * (c_last + red_all[j + 1][6])
         else:
             below = jnp.zeros_like(c_last)
         lower.append(q1)
@@ -313,7 +314,36 @@
     for k in reversed(range(size)):
         following = values[k] + ratios[k] * following
         solved[k] = following
-    return jnp.stack(solved)
+    return solved
+
+
+def finish_kernel(rank_ref, y_ref, a_ref, b_ref, *rest):
+    recv = rest[:-1]
+    t_ref = rest[-1]
+    count = len(recv)
+    rank = rank_ref[0]
+    red_all = []
+    for j in range(count):
+        source = (rank - j + count) % count
+        planes = []
+        for k in range(8):
+            v = recv[count - 1][k]
+            for m in reversed(range(count - 1)):
+                v = jnp.where(source == m, recv[m][k], v)
+            planes.append(v)
+        red_all.append(planes)
+    solved = reduced_solve(red_all)
+    first = solved[2 * (count - 1)]
+    last = solved[2 * (count - 1) + 1]
+    for j in reversed(range(count - 1)):
+        first = jnp.where(rank == j, solved[2 * j], first)
+        last = jnp.where(rank == j, solved[2 * j + 1], last)
+
+    def combine(i, carry):
+        t_ref[i] = y_ref[i] + a_ref[i] * first + b_ref[i] * last
+        return carry
+
+    lax.fori_loop(0, y_ref.shape[0], combine, 0)
 
 
 def sds(shape):
@@ -356,9 +386,6 @@
     chunks = CHUNKS if groups % CHUNKS == 0 else 1
     depth = n // chunks
     cgroups = depth // ROWS
-    table = jnp.concatenate(
-        [lateral_transmissivity, stratum_advection_offsets, vertical_transmissivity[None]], 0
-    )
     smem_spec = pl.BlockSpec(memory_space=pltpu.SMEM)
     vspec = pl.BlockSpec(memory_space=pltpu.MemorySpace.VMEM)
     heat, water, carbon, melt, co, xf0, xl0, y0 = pl.pallas_call(
@@ -366,8 +393,8 @@
         out_shape=(sds(shape), sds(shape), sds(shape), sds(shape), sds((5,) + shape),
                    sds((5, groups, ROWS, LANES)), sds((5, groups, ROWS, LANES)),
                    sds((2, 5, ROWS, LANES))),
-        in_specs=[smem_spec, vspec, vspec, vspec, vspec, vspec],
-    )(table, stratum_number_grid, thermal_field, steam_content_grid, carbonic_gas_grid,
+        in_specs=[smem_spec] * 3 + [vspec] * 5,
+    )(lateral_transmissivity, vertical_transmissivity, stratum_advection_offsets, stratum_number_grid, thermal_field, steam_content_grid, carbonic_gas_grid,
       liquid_fraction)
     xflo, xfhi, yflo, yfhi = exchange(xf0, xl0, y0)
 
@@ -418,12 +445,12 @@
     received = [red]
     for k in range(1, count):
         received.append(lax.ppermute(red, "depth", [(i, (i + k) % count) for i in range(count)]))
-    stacked = jnp.stack(received)
-    red_all = jnp.take(stacked, (rank - jnp.arange(count)) % count, axis=0)
-    solved = reduced_solve(red_all)
-    first = lax.dynamic_index_in_dim(solved, 2 * rank, keepdims=False)
-    last = lax.dynamic_index_in_dim(solved, 2 * rank + 1, keepdims=False)
-    heat_next = y + a * first[None] + b * last[None]
+    rank_arr = jnp.full((1,), rank, jnp.int32)
+    heat_next = pl.pallas_call(
+        finish_kernel,
+        out_shape=sds(shape),
+        in_specs=[smem_spec] + [vspec] * (3 + count),
+    )(rank_arr, y, a, b, *received)
     return (heat_next, melt, water, carbon)
 
 

time: 81.8 us -> 80.9 us (0.989)
  other arithmetic: 3.07 us -> 0 us
  Pallas kernels: 41 us -> 43.4 us
    pallas_call x0 -> x1, Pallas kernels: none -> 2.38 us  [local(): pl.pallas_call(finish_kernel, out_shape=sds(shape), in_specs=[smem_spec]...]
    concatenate x1 -> x0, other arithmetic: 1.32 us -> none  [local(): jnp.concatenate([lateral_transmissivity, stratum_advection_offsets, verti...]
    unnamed x51 -> x48, local copies, waits for them, and re-layouts: 4.36 us -> 4.98 us
where the time goes in v5:
time: 80.9 us; the launch traced here: 80.5 us
  Pallas kernels  43.4 us (54%)
  starting transfers between devices  25.9 us (32%)
  waiting for transfers between devices  5.37 us (7%)
  local copies, waits for them, and re-layouts  4.98 us (6%)
  between operations  0.83 us (1%)
    pallas_call x8, Pallas kernels, local(): pl.pallas_call(make_section_kernel(k, first), grid=(1,), out_shape=(sds(s...  32.7 us
    ppermute x7, starting transfers between devices, exchange(): xhi = lax.ppermute(xf, 'east', east_bwd)  9.42 us
    ppermute x7, starting transfers between devices, exchange(): ylo = lax.ppermute(ys, 'north', north_fwd)  8.39 us
    ppermute x3, starting transfers between devices, local(): lax.ppermute(red, 'depth', [(i, (i + k) % count) for i in range(count)])  5.37 us
    unnamed x48, local copies, waits for them, and re-layouts  4.98 us
    pallas_call x1, Pallas kernels, local(): pl.pallas_call(prep_kernel, out_shape=(sds(shape), sds(shape), sds(shape)...  4.45 us
    pallas_call x1, Pallas kernels, local(): pl.pallas_call(sweep_kernel, grid=(1,), out_shape=(sds(shape), sds(shape)...  3.87 us
    ppermute x3, waiting for transfers between devices, local(): lax.ppermute(red, 'depth', [(i, (i + k) % count) for i in range(count)])  2.77 us
  transfers between devices with their start and end apart: 24, of which 5 were waited for; matrix products, arithmetic and copies ran while one was open for 0% of the time, Pallas kernels for 30%

profile of v5, /device:TPU:0, one launch (start us, length us, event | category | flops | bytes accessed | tf_op | source)
XLA Modules:
  0.0 80.5 jit_solution(4936333061614358391)
XLA Ops:
  0.6 4.4 %shard_map.120 = (f32[64,8,128]{2,1,0:T(8,128)}, f32[64,8,128]{2,1,0:T(8,128)}, f32[64,8,128]{2,1,0:T(8,128)}, f32[64,8,128]{2,1,0:T(8,128)}, f32[5,64,8,128]{3,...) custom-call(f32[2,12]{1,0:T(2,128)} %lat_ref.1, f32[12]{0:T(128)} %vert_ref.1, ...), custom_call_target="tpu_custom_call" | custom-call | tf_op jit(solution)/shard_map/pallas_call | solution.py:391
  5.1 0.5 collective-permute-start
  5.5 2.0 %collective-permute-start.1 = (f32[5,8,8,128]{3,2,1,0:T(8,128)}, f32[5,8,8,128]{3,2,1,0:T(8,128)S(1)}, u32[]{:S(2)}, u32[]{:S(2)}) collective-permute-start(f32[5,8,8,128]{3,2,1,0:T(8,128)} %get-tuple-element.72), channel_id=1, source_target_pairs={{8,0},{16,8},{24,16},{0,24},{9,1},{17,9},{25,17},{1,25},{10,2},{18... | collective-permute-start | bytes 491528 | tf_op jit(solution)/shard_map/ppermute | solution.py:357
  7.5 2.3 %collective-permute-start.2 = (f32[2,5,8,128]{3,2,1,0:T(8,128)}, f32[2,5,8,128]{3,2,1,0:T(8,128)S(1)}, u32[]{:S(2)}, u32[]{:S(2)}) collective-permute-start(f32[2,5,8,128]{3,2,1,0:T(8,128)} %get-tuple-element.73), channel_id=1, source_target_pairs={{0,4},{4,0},{1,5},{5,1},{2,6},{6,2},{3,7},{7,3},{8,12},{12,8},{9,1... | collective-permute-start | bytes 122888 | tf_op jit(solution)/shard_map/ppermute | solution.py:358
  9.8 2.2 %collective-permute-done.2.yflo_ref.yfhi_ref = f32[2,5,8,128]{3,2,1,0:T(8,128)S(1)} collective-permute-done((f32[2,5,8,128]{3,2,1,0:T(8,128)}, f32[2,5,8,128]{3,2,1,0:T(8,128)S(1)}, u32[]{:S(2)}, u32[]{:S(2)}) %collective-permute-start.2) | collective-permute-done | bytes 40992 | tf_op jit(solution)/shard_map/ppermute | solution.py:358
  12.0 0.4 collective-permute-done.1.xfhi_ref
  12.4 0.2 copy-done.2
  12.6 0.1 copy-done
  12.7 0.3 copy-done.1
  13.0 4.1 %shard_map.121 = (f32[64,8,128]{2,1,0:T(8,128)}, f32[64,8,128]{2,1,0:T(8,128)}, f32[64,8,128]{2,1,0:T(8,128)}, f32[64,8,128]{2,1,0:T(8,128)}, f32[3,4,8,128]{3,2...) custom-call(f32[64,8,128]{2,1,0:T(8,128)} %get-tuple-element.66.h_re, ...), custom_call_target="tpu_custom_call", output_to_operand_aliasing={{0}: (0, {}), {1}: (1, {}), {2}: (2, {}), {3}: (3, {})} | custom-call | tf_op jit(solution)/shard_map/pallas_call | solution.py:419
  17.1 0.7 collective-permute-start.3
  17.8 1.3 %collective-permute-start.4 = (f32[3,4,8,128]{3,2,1,0:T(8,128)}, f32[3,4,8,128]{3,2,1,0:T(8,128)S(1)}, u32[]{:S(2)}, u32[]{:S(2)}) collective-permute-start(f32[3,4,8,128]{3,2,1,0:T(8,128)} %get-tuple-element.83), channel_id=1, source_target_pairs={{8,0},{16,8},{24,16},{0,24},{9,1},{17,9},{25,17},{1,25},{10,2},{18... | collective-permute-start | bytes 147464 | tf_op jit(solution)/shard_map/ppermute | solution.py:357
  19.2 1.4 %collective-permute-start.5 = (f32[2,3,8,128]{3,2,1,0:T(8,128)}, f32[2,3,8,128]{3,2,1,0:T(8,128)S(1)}, u32[]{:S(2)}, u32[]{:S(2)}) collective-permute-start(f32[2,3,8,128]{3,2,1,0:T(8,128)} %get-tuple-element.84), channel_id=1, source_target_pairs={{0,4},{4,0},{1,5},{5,1},{2,6},{6,2},{3,7},{7,3},{8,12},{12,8},{9,1... | collective-permute-start | bytes 73736 | tf_op jit(solution)/shard_map/ppermute | solution.py:358
  20.6 4.1 %shard_map.122 = (f32[64,8,128]{2,1,0:T(8,128)}, f32[64,8,128]{2,1,0:T(8,128)}, f32[64,8,128]{2,1,0:T(8,128)}, f32[64,8,128]{2,1,0:T(8,128)}, f32[3,4,8,128]{3,2...) custom-call(f32[64,8,128]{2,1,0:T(8,128)} %get-tuple-element.74.h_re, ...), custom_call_target="tpu_custom_call", output_to_operand_aliasing={{0}: (0, {}), {1}: (1, {}), {2}: (2, {}), {3}: (3, {})} | custom-call | tf_op jit(solution)/shard_map/pallas_call | solution.py:419
  24.7 1.7 %collective-permute-start.7 = (f32[3,4,8,128]{3,2,1,0:T(8,128)}, f32[3,4,8,128]{3,2,1,0:T(8,128)S(1)}, u32[]{:S(2)}, u32[]{:S(2)}) collective-permute-start(f32[3,4,8,128]{3,2,1,0:T(8,128)} %get-tuple-element.90), channel_id=1, source_target_pairs={{8,0},{16,8},{24,16},{0,24},{9,1},{17,9},{25,17},{1,25},{10,2},{18... | collective-permute-start | bytes 147464 | tf_op jit(solution)/shard_map/ppermute | solution.py:357
  26.4 0.7 collective-permute-start.8
  27.1 0.6 copy-done.19
  27.7 4.1 %shard_map.123 = (f32[64,8,128]{2,1,0:T(8,128)}, f32[64,8,128]{2,1,0:T(8,128)}, f32[64,8,128]{2,1,0:T(8,128)}, f32[64,8,128]{2,1,0:T(8,128)}, f32[3,4,8,128]{3,2...) custom-call(f32[64,8,128]{2,1,0:T(8,128)} %get-tuple-element.78.h_re, ...), custom_call_target="tpu_custom_call", output_to_operand_aliasing={{0}: (0, {}), {1}: (1, {}), {2}: (2, {}), {3}: (3, {})} | custom-call | tf_op jit(solution)/shard_map/pallas_call | solution.py:419
  31.8 0.2 collective-permute-start.10
  32.0 0.4 collective-permute-start.9
  32.4 1.4 %collective-permute-start.11 = (f32[2,3,8,128]{3,2,1,0:T(8,128)}, f32[2,3,8,128]{3,2,1,0:T(8,128)S(1)}, u32[]{:S(2)}, u32[]{:S(2)}) collective-permute-start(f32[2,3,8,128]{3,2,1,0:T(8,128)} %get-tuple-element.98), channel_id=1, source_target_pairs={{0,4},{4,0},{1,5},{5,1},{2,6},{6,2},{3,7},{7,3},{8,12},{12,8},{9,1... | collective-permute-start | bytes 73736 | tf_op jit(solution)/shard_map/ppermute | solution.py:358
  33.8 0.6 copy-done.9
  34.4 4.1 %shard_map.124 = (f32[64,8,128]{2,1,0:T(8,128)}, f32[64,8,128]{2,1,0:T(8,128)}, f32[64,8,128]{2,1,0:T(8,128)}, f32[64,8,128]{2,1,0:T(8,128)}, f32[3,4,8,128]{3,2...) custom-call(f32[64,8,128]{2,1,0:T(8,128)} %get-tuple-element.85.h_re, ...), custom_call_target="tpu_custom_call", output_to_operand_aliasing={{0}: (0, {}), {1}: (1, {}), {2}: (2, {}), {3}: (3, {})} | custom-call | tf_op jit(solution)/shard_map/pallas_call | solution.py:419
  38.5 0.9 %collective-permute-start.12 = (f32[3,4,8,128]{3,2,1,0:T(8,128)}, f32[3,4,8,128]{3,2,1,0:T(8,128)S(1)}, u32[]{:S(2)}, u32[]{:S(2)}) collective-permute-start(f32[3,4,8,128]{3,2,1,0:T(8,128)} %get-tuple-element.103), channel_id=1, source_target_pairs={{0,8},{8,16},{16,24},{24,0},{1,9},{9,17},{17,25},{25,1},{2,10},{10... | collective-permute-start | bytes 147464 | tf_op jit(solution)/shard_map/ppermute | solution.py:356
  39.4 0.9 %collective-permute-start.13 = (f32[3,4,8,128]{3,2,1,0:T(8,128)}, f32[3,4,8,128]{3,2,1,0:T(8,128)S(1)}, u32[]{:S(2)}, u32[]{:S(2)}) collective-permute-start(f32[3,4,8,128]{3,2,1,0:T(8,128)} %get-tuple-element.104), channel_id=1, source_target_pairs={{8,0},{16,8},{24,16},{0,24},{9,1},{17,9},{25,17},{1,25},{10,2},{18... | collective-permute-start | bytes 147464 | tf_op jit(solution)/shard_map/ppermute | solution.py:357
  40.3 0.7 collective-permute-start.14
  41.0 0.6 copy-done.10
  41.6 4.1 %shard_map.125 = (f32[64,8,128]{2,1,0:T(8,128)}, f32[64,8,128]{2,1,0:T(8,128)}, f32[64,8,128]{2,1,0:T(8,128)}, f32[64,8,128]{2,1,0:T(8,128)}, f32[3,4,8,128]{3,2...) custom-call(f32[64,8,128]{2,1,0:T(8,128)} %get-tuple-element.92.h_re, ...), custom_call_target="tpu_custom_call", output_to_operand_aliasing={{0}: (0, {}), {1}: (1, {}), {2}: (2, {}), {3}: (3, {})} | custom-call | tf_op jit(solution)/shard_map/pallas_call | solution.py:419
  45.7 0.2 collective-permute-start.15
  45.9 1.6 %collective-permute-start.16 = (f32[3,4,8,128]{3,2,1,0:T(8,128)}, f32[3,4,8,128]{3,2,1,0:T(8,128)S(1)}, u32[]{:S(2)}, u32[]{:S(2)}) collective-permute-start(f32[3,4,8,128]{3,2,1,0:T(8,128)} %get-tuple-element.111), channel_id=1, source_target_pairs={{8,0},{16,8},{24,16},{0,24},{9,1},{17,9},{25,17},{1,25},{10,2},{18... | collective-permute-start | bytes 147464 | tf_op jit(solution)/shard_map/ppermute | solution.py:357
  47.5 1.4 %collective-permute-start.17 = (f32[2,3,8,128]{3,2,1,0:T(8,128)}, f32[2,3,8,128]{3,2,1,0:T(8,128)S(1)}, u32[]{:S(2)}, u32[]{:S(2)}) collective-permute-start(f32[2,3,8,128]{3,2,1,0:T(8,128)} %get-tuple-element.112), channel_id=1, source_target_pairs={{0,4},{4,0},{1,5},{5,1},{2,6},{6,2},{3,7},{7,3},{8,12},{12,8},{9,1... | collective-permute-start | bytes 73736 | tf_op jit(solution)/shard_map/ppermute | solution.py:358
  48.9 0.6 copy-done.11
  49.5 4.1 %shard_map.126 = (f32[64,8,128]{2,1,0:T(8,128)}, f32[64,8,128]{2,1,0:T(8,128)}, f32[64,8,128]{2,1,0:T(8,128)}, f32[64,8,128]{2,1,0:T(8,128)}, f32[3,4,8,128]{3,2...) custom-call(f32[64,8,128]{2,1,0:T(8,128)} %get-tuple-element.99.h_re, ...), custom_call_target="tpu_custom_call", output_to_operand_aliasing={{0}: (0, {}), {1}: (1, {}), {2}: (2, {}), {3}: (3, {})} | custom-call | tf_op jit(solution)/shard_map/pallas_call | solution.py:419
  53.6 1.7 %collective-permute-start.19 = (f32[3,4,8,128]{3,2,1,0:T(8,128)}, f32[3,4,8,128]{3,2,1,0:T(8,128)S(1)}, u32[]{:S(2)}, u32[]{:S(2)}) collective-permute-start(f32[3,4,8,128]{3,2,1,0:T(8,128)} %get-tuple-element.118), channel_id=1, source_target_pairs={{8,0},{16,8},{24,16},{0,24},{9,1},{17,9},{25,17},{1,25},{10,2},{18... | collective-permute-start | bytes 147464 | tf_op jit(solution)/shard_map/ppermute | solution.py:357
  55.4 0.7 collective-permute-start.20
  56.1 0.6 copy-done.12
  56.7 4.1 %shard_map.127 = (f32[64,8,128]{2,1,0:T(8,128)}, f32[64,8,128]{2,1,0:T(8,128)}, f32[64,8,128]{2,1,0:T(8,128)}, f32[64,8,128]{2,1,0:T(8,128)}, f32[3,4,8,128]{3,2...) custom-call(f32[64,8,128]{2,1,0:T(8,128)} %get-tuple-element.106.h_r, ...), custom_call_target="tpu_custom_call", output_to_operand_aliasing={{0}: (0, {}), {1}: (1, {}), {2}: (2, {}), {3}: (3, {})} | custom-call | tf_op jit(solution)/shard_map/pallas_call | solution.py:419
  60.8 0.6 copy-done.7
  61.4 4.1 %shard_map.128 = (f32[64,8,128]{2,1,0:T(8,128)}, f32[64,8,128]{2,1,0:T(8,128)}, f32[64,8,128]{2,1,0:T(8,128)}, f32[64,8,128]{2,1,0:T(8,128)}, f32[3,4,8,128]{3,2...) custom-call(f32[64,8,128]{2,1,0:T(8,128)} %get-tuple-element.113.h_r, ...), custom_call_target="tpu_custom_call", output_to_operand_aliasing={{0}: (0, {}), {1}: (1, {}), {2}: (2, {}), {3}: (3, {})} | custom-call | tf_op jit(solution)/shard_map/pallas_call | solution.py:419
  65.5 3.9 %shard_map.129 = (f32[64,8,128]{2,1,0:T(8,128)}, f32[64,8,128]{2,1,0:T(8,128)}, f32[64,8,128]{2,1,0:T(8,128)}, f32[8,8,128]{2,1,0:T(8,128)}) custom-call(f32[64,8,128]{2,1,0:T(8,128)} %get-tuple-element.120.r_ref, f32[5,64,8,128]{3,2,1,0:T(8,128)} %get-tuple-element.70.co_ref.cz_ref), custom_call_target="tpu_custom_call" | custom-call | tf_op jit(solution)/shard_map/pallas_call | solution.py:435
  69.4 1.4 %collective-permute-start.21 = (f32[8,8,128]{2,1,0:T(8,128)}, f32[8,8,128]{2,1,0:T(8,128)S(1)}, u32[]{:S(2)}, u32[]{:S(2)}) collective-permute-start(f32[8,8,128]{2,1,0:T(8,128)} %get-tuple-element.124.rest_0_), channel_id=1, source_target_pairs={{0,1},{1,2},{2,3},{3,0},{4,5},{5,6},{6,7},{7,4},{8,9},{9,10},{10,1... | collective-permute-start | bytes 98312 | tf_op jit(solution)/shard_map/ppermute | solution.py:447
  70.8 2.6 %collective-permute-start.22 = (f32[8,8,128]{2,1,0:T(8,128)}, f32[8,8,128]{2,1,0:T(8,128)S(1)}, u32[]{:S(2)}, u32[]{:S(2)}) collective-permute-start(f32[8,8,128]{2,1,0:T(8,128)} %get-tuple-element.124.rest_0_), channel_id=1, source_target_pairs={{0,2},{1,3},{2,0},{3,1},{4,6},{5,7},{6,4},{7,5},{8,10},{9,11},{10,... | collective-permute-start | bytes 98312 | tf_op jit(solution)/shard_map/ppermute | solution.py:447
  73.4 1.3 %collective-permute-start.23 = (f32[8,8,128]{2,1,0:T(8,128)}, f32[8,8,128]{2,1,0:T(8,128)S(1)}, u32[]{:S(2)}, u32[]{:S(2)}) collective-permute-start(f32[8,8,128]{2,1,0:T(8,128)} %get-tuple-element.124.rest_0_), channel_id=1, source_target_pairs={{0,3},{1,0},{2,1},{3,2},{4,7},{5,4},{6,5},{7,6},{8,11},{9,8},{10,9... | collective-permute-start | bytes 98312 | tf_op jit(solution)/shard_map/ppermute | solution.py:447
  74.8 1.0 %collective-permute-done.21.rest_1_ = f32[8,8,128]{2,1,0:T(8,128)S(1)} collective-permute-done((f32[8,8,128]{2,1,0:T(8,128)}, f32[8,8,128]{2,1,0:T(8,128)S(1)}, u32[]{:S(2)}, u32[]{:S(2)}) %collective-permute-start.21) | collective-permute-done | bytes 32800 | tf_op jit(solution)/shard_map/ppermute | solution.py:447
  75.8 0.5 collective-permute-done.22.rest_2_
  76.3 1.3 %collective-permute-done.23.rest_3_ = f32[8,8,128]{2,1,0:T(8,128)S(1)} collective-permute-done((f32[8,8,128]{2,1,0:T(8,128)}, f32[8,8,128]{2,1,0:T(8,128)S(1)}, u32[]{:S(2)}, u32[]{:S(2)}) %collective-permute-start.23) | collective-permute-done | bytes 32800 | tf_op jit(solution)/shard_map/ppermute | solution.py:447
  77.6 0.6 copy-done.23
  78.2 2.4 %shard_map.130 = f32[64,8,128]{2,1,0:T(8,128)} custom-call(s32[1]{0:T(128)} %bitcast.rank_ref, f32[64,8,128]{2,1,0:T(8,128)} %get-tuple-element.121.y_ref, f32[64,8,128]{2,1,0:T(8,128)} %get-tuple-element.122.a_ref, f32[64,8,128]{2,1,0:T(8,128)} %get-tuple-element.123.b_ref, f32[8,8,128]{2,1,0:T(8,128)} %get-tuple-element.124.rest_0_, ...), custom_call_target="tpu_custom_call" | custom-call | tf_op jit(solution)/shard_map/pallas_call | solution.py:449
  (59 shorter events, 0.3 us)
Async XLA Ops:
  5.1 6.9 %collective-permute-start = (f32[5,8,8,128]{3,2,1,0:T(8,128)}, f32[5,8,8,128]{3,2,1,0:T(8,128)S(1)}, u32[]{:S(2)}, u32[]{:S(2)}) collective-permute-start(f32[5,8,8,128]{3,2,1,0:T(8,128)} %get-tuple-element.71), channel_id=1, source_target_pairs={{0,8},{8,16},{16,24},{24,0},{1,9},{9,17},{17,25},{25,1},{2,10},{10... | collective-permute-start | bytes 491528 | tf_op jit(solution)/shard_map/ppermute | solution.py:356
  5.5 6.8 %collective-permute-start.1 = (f32[5,8,8,128]{3,2,1,0:T(8,128)}, f32[5,8,8,128]{3,2,1,0:T(8,128)S(1)}, u32[]{:S(2)}, u32[]{:S(2)}) collective-permute-start(f32[5,8,8,128]{3,2,1,0:T(8,128)} %get-tuple-element.72), channel_id=1, source_target_pairs={{8,0},{16,8},{24,16},{0,24},{9,1},{17,9},{25,17},{1,25},{10,2},{18... | collective-permute-start | bytes 491528 | tf_op jit(solution)/shard_map/ppermute | solution.py:357
  7.5 4.5 %collective-permute-start.2 = (f32[2,5,8,128]{3,2,1,0:T(8,128)}, f32[2,5,8,128]{3,2,1,0:T(8,128)S(1)}, u32[]{:S(2)}, u32[]{:S(2)}) collective-permute-start(f32[2,5,8,128]{3,2,1,0:T(8,128)} %get-tuple-element.73), channel_id=1, source_target_pairs={{0,4},{4,0},{1,5},{5,1},{2,6},{6,2},{3,7},{7,3},{8,12},{12,8},{9,1... | collective-permute-start | bytes 122888 | tf_op jit(solution)/shard_map/ppermute | solution.py:358
  12.0 0.6 copy-start.2
  12.0 0.7 copy-start
  12.4 0.7 copy-start.1
  17.1 10.0 %collective-permute-start.3 = (f32[3,4,8,128]{3,2,1,0:T(8,128)}, f32[3,4,8,128]{3,2,1,0:T(8,128)S(1)}, u32[]{:S(2)}, u32[]{:S(2)}) collective-permute-start(f32[3,4,8,128]{3,2,1,0:T(8,128)} %get-tuple-element.82), channel_id=1, source_target_pairs={{0,8},{8,16},{16,24},{24,0},{1,9},{9,17},{17,25},{25,1},{2,10},{10... | collective-permute-start | bytes 147464 | tf_op jit(solution)/shard_map/ppermute | solution.py:356
  17.8 9.3 %collective-permute-start.4 = (f32[3,4,8,128]{3,2,1,0:T(8,128)}, f32[3,4,8,128]{3,2,1,0:T(8,128)S(1)}, u32[]{:S(2)}, u32[]{:S(2)}) collective-permute-start(f32[3,4,8,128]{3,2,1,0:T(8,128)} %get-tuple-element.83), channel_id=1, source_target_pairs={{8,0},{16,8},{24,16},{0,24},{9,1},{17,9},{25,17},{1,25},{10,2},{18... | collective-permute-start | bytes 147464 | tf_op jit(solution)/shard_map/ppermute | solution.py:357
  19.2 7.2 %collective-permute-start.5 = (f32[2,3,8,128]{3,2,1,0:T(8,128)}, f32[2,3,8,128]{3,2,1,0:T(8,128)S(1)}, u32[]{:S(2)}, u32[]{:S(2)}) collective-permute-start(f32[2,3,8,128]{3,2,1,0:T(8,128)} %get-tuple-element.84), channel_id=1, source_target_pairs={{0,4},{4,0},{1,5},{5,1},{2,6},{6,2},{3,7},{7,3},{8,12},{12,8},{9,1... | collective-permute-start | bytes 73736 | tf_op jit(solution)/shard_map/ppermute | solution.py:358
  24.7 9.1 %collective-permute-start.6 = (f32[3,4,8,128]{3,2,1,0:T(8,128)}, f32[3,4,8,128]{3,2,1,0:T(8,128)S(1)}, u32[]{:S(2)}, u32[]{:S(2)}) collective-permute-start(f32[3,4,8,128]{3,2,1,0:T(8,128)} %get-tuple-element.89), channel_id=1, source_target_pairs={{0,8},{8,16},{16,24},{24,0},{1,9},{9,17},{17,25},{25,1},{2,10},{10... | collective-permute-start | bytes 147464 | tf_op jit(solution)/shard_map/ppermute | solution.py:356
  24.7 9.1 %collective-permute-start.7 = (f32[3,4,8,128]{3,2,1,0:T(8,128)}, f32[3,4,8,128]{3,2,1,0:T(8,128)S(1)}, u32[]{:S(2)}, u32[]{:S(2)}) collective-permute-start(f32[3,4,8,128]{3,2,1,0:T(8,128)} %get-tuple-element.90), channel_id=1, source_target_pairs={{8,0},{16,8},{24,16},{0,24},{9,1},{17,9},{25,17},{1,25},{10,2},{18... | collective-permute-start | bytes 147464 | tf_op jit(solution)/shard_map/ppermute | solution.py:357
  26.4 0.7 copy-start.8
  26.4 6.0 %collective-permute-start.8 = (f32[2,3,8,128]{3,2,1,0:T(8,128)}, f32[2,3,8,128]{3,2,1,0:T(8,128)S(1)}, u32[]{:S(2)}, u32[]{:S(2)}) collective-permute-start(f32[2,3,8,128]{3,2,1,0:T(8,128)} %get-tuple-element.91), channel_id=1, source_target_pairs={{0,4},{4,0},{1,5},{5,1},{2,6},{6,2},{3,7},{7,3},{8,12},{12,8},{9,1... | collective-permute-start | bytes 73736 | tf_op jit(solution)/shard_map/ppermute | solution.py:358
  27.1 0.6 copy-start.19
  27.1 0.6 copy-start.20
  31.8 9.1 %collective-permute-start.10 = (f32[3,4,8,128]{3,2,1,0:T(8,128)}, f32[3,4,8,128]{3,2,1,0:T(8,128)S(1)}, u32[]{:S(2)}, u32[]{:S(2)}) collective-permute-start(f32[3,4,8,128]{3,2,1,0:T(8,128)} %get-tuple-element.97), channel_id=1, source_target_pairs={{8,0},{16,8},{24,16},{0,24},{9,1},{17,9},{25,17},{1,25},{10,2},{18... | collective-permute-start | bytes 147464 | tf_op jit(solution)/shard_map/ppermute | solution.py:357
  32.0 8.9 %collective-permute-start.9 = (f32[3,4,8,128]{3,2,1,0:T(8,128)}, f32[3,4,8,128]{3,2,1,0:T(8,128)S(1)}, u32[]{:S(2)}, u32[]{:S(2)}) collective-permute-start(f32[3,4,8,128]{3,2,1,0:T(8,128)} %get-tuple-element.96), channel_id=1, source_target_pairs={{0,8},{8,16},{16,24},{24,0},{1,9},{9,17},{17,25},{25,1},{2,10},{10... | collective-permute-start | bytes 147464 | tf_op jit(solution)/shard_map/ppermute | solution.py:356
  32.4 1.4 %copy-start.3 = (f32[2,3,8,128]{3,2,1,0:T(8,128)}, f32[2,3,8,128]{3,2,1,0:T(8,128)S(1)}, u32[]{:S(2)}) copy-start(f32[2,3,8,128]{3,2,1,0:T(8,128)S(1)} %collective-permute-done.8.rest_2_.rest_3_) | copy-start | bytes 73732
  32.4 7.9 %collective-permute-start.11 = (f32[2,3,8,128]{3,2,1,0:T(8,128)}, f32[2,3,8,128]{3,2,1,0:T(8,128)S(1)}, u32[]{:S(2)}, u32[]{:S(2)}) collective-permute-start(f32[2,3,8,128]{3,2,1,0:T(8,128)} %get-tuple-element.98), channel_id=1, source_target_pairs={{0,4},{4,0},{1,5},{5,1},{2,6},{6,2},{3,7},{7,3},{8,12},{12,8},{9,1... | collective-permute-start | bytes 73736 | tf_op jit(solution)/shard_map/ppermute | solution.py:358
  33.8 0.6 copy-start.9
  33.8 0.6 copy-start.13
  38.5 10.4 %collective-permute-start.12 = (f32[3,4,8,128]{3,2,1,0:T(8,128)}, f32[3,4,8,128]{3,2,1,0:T(8,128)S(1)}, u32[]{:S(2)}, u32[]{:S(2)}) collective-permute-start(f32[3,4,8,128]{3,2,1,0:T(8,128)} %get-tuple-element.103), channel_id=1, source_target_pairs={{0,8},{8,16},{16,24},{24,0},{1,9},{9,17},{17,25},{25,1},{2,10},{10... | collective-permute-start | bytes 147464 | tf_op jit(solution)/shard_map/ppermute | solution.py:356
  39.4 9.4 %collective-permute-start.13 = (f32[3,4,8,128]{3,2,1,0:T(8,128)}, f32[3,4,8,128]{3,2,1,0:T(8,128)S(1)}, u32[]{:S(2)}, u32[]{:S(2)}) collective-permute-start(f32[3,4,8,128]{3,2,1,0:T(8,128)} %get-tuple-element.104), channel_id=1, source_target_pairs={{8,0},{16,8},{24,16},{0,24},{9,1},{17,9},{25,17},{1,25},{10,2},{18... | collective-permute-start | bytes 147464 | tf_op jit(solution)/shard_map/ppermute | solution.py:357
  40.3 0.7 copy-start.4
  40.3 7.2 %collective-permute-start.14 = (f32[2,3,8,128]{3,2,1,0:T(8,128)}, f32[2,3,8,128]{3,2,1,0:T(8,128)S(1)}, u32[]{:S(2)}, u32[]{:S(2)}) collective-permute-start(f32[2,3,8,128]{3,2,1,0:T(8,128)} %get-tuple-element.105), channel_id=1, source_target_pairs={{0,4},{4,0},{1,5},{5,1},{2,6},{6,2},{3,7},{7,3},{8,12},{12,8},{9,1... | collective-permute-start | bytes 73736 | tf_op jit(solution)/shard_map/ppermute | solution.py:358
  41.0 0.6 copy-start.10
  41.0 0.6 copy-start.14
  45.7 10.4 %collective-permute-start.15 = (f32[3,4,8,128]{3,2,1,0:T(8,128)}, f32[3,4,8,128]{3,2,1,0:T(8,128)S(1)}, u32[]{:S(2)}, u32[]{:S(2)}) collective-permute-start(f32[3,4,8,128]{3,2,1,0:T(8,128)} %get-tuple-element.110), channel_id=1, source_target_pairs={{0,8},{8,16},{16,24},{24,0},{1,9},{9,17},{17,25},{25,1},{2,10},{10... | collective-permute-start | bytes 147464 | tf_op jit(solution)/shard_map/ppermute | solution.py:356
  45.9 10.2 %collective-permute-start.16 = (f32[3,4,8,128]{3,2,1,0:T(8,128)}, f32[3,4,8,128]{3,2,1,0:T(8,128)S(1)}, u32[]{:S(2)}, u32[]{:S(2)}) collective-permute-start(f32[3,4,8,128]{3,2,1,0:T(8,128)} %get-tuple-element.111), channel_id=1, source_target_pairs={{8,0},{16,8},{24,16},{0,24},{9,1},{17,9},{25,17},{1,25},{10,2},{18... | collective-permute-start | bytes 147464 | tf_op jit(solution)/shard_map/ppermute | solution.py:357
  47.5 1.4 %copy-start.5 = (f32[2,3,8,128]{3,2,1,0:T(8,128)}, f32[2,3,8,128]{3,2,1,0:T(8,128)S(1)}, u32[]{:S(2)}) copy-start(f32[2,3,8,128]{3,2,1,0:T(8,128)S(1)} %collective-permute-done.14.rest_2_.rest_3_) | copy-start | bytes 73732
  47.5 7.9 %collective-permute-start.17 = (f32[2,3,8,128]{3,2,1,0:T(8,128)}, f32[2,3,8,128]{3,2,1,0:T(8,128)S(1)}, u32[]{:S(2)}, u32[]{:S(2)}) collective-permute-start(f32[2,3,8,128]{3,2,1,0:T(8,128)} %get-tuple-element.112), channel_id=1, source_target_pairs={{0,4},{4,0},{1,5},{5,1},{2,6},{6,2},{3,7},{7,3},{8,12},{12,8},{9,1... | collective-permute-start | bytes 73736 | tf_op jit(solution)/shard_map/ppermute | solution.py:358
  48.8 0.6 copy-start.11
  48.9 0.6 copy-start.15
  53.6 7.2 %collective-permute-start.18 = (f32[3,4,8,128]{3,2,1,0:T(8,128)}, f32[3,4,8,128]{3,2,1,0:T(8,128)S(1)}, u32[]{:S(2)}, u32[]{:S(2)}) collective-permute-start(f32[3,4,8,128]{3,2,1,0:T(8,128)} %get-tuple-element.117), channel_id=1, source_target_pairs={{0,8},{8,16},{16,24},{24,0},{1,9},{9,17},{17,25},{25,1},{2,10},{10... | collective-permute-start | bytes 147464 | tf_op jit(solution)/shard_map/ppermute | solution.py:356
  53.6 7.2 %collective-permute-start.19 = (f32[3,4,8,128]{3,2,1,0:T(8,128)}, f32[3,4,8,128]{3,2,1,0:T(8,128)S(1)}, u32[]{:S(2)}, u32[]{:S(2)}) collective-permute-start(f32[3,4,8,128]{3,2,1,0:T(8,128)} %get-tuple-element.118), channel_id=1, source_target_pairs={{8,0},{16,8},{24,16},{0,24},{9,1},{17,9},{25,17},{1,25},{10,2},{18... | collective-permute-start | bytes 147464 | tf_op jit(solution)/shard_map/ppermute | solution.py:357
  55.4 0.7 copy-start.6
  55.4 5.4 %collective-permute-start.20 = (f32[2,3,8,128]{3,2,1,0:T(8,128)}, f32[2,3,8,128]{3,2,1,0:T(8,128)S(1)}, u32[]{:S(2)}, u32[]{:S(2)}) collective-permute-start(f32[2,3,8,128]{3,2,1,0:T(8,128)} %get-tuple-element.119), channel_id=1, source_target_pairs={{0,4},{4,0},{1,5},{5,1},{2,6},{6,2},{3,7},{7,3},{8,12},{12,8},{9,1... | collective-permute-start | bytes 73736 | tf_op jit(solution)/shard_map/ppermute | solution.py:358
  56.0 0.6 copy-start.12
  56.1 0.6 copy-start.16
  60.8 0.6 copy-start.7
  60.8 0.6 copy-start.17
  60.8 0.6 copy-start.18
  69.4 6.4 %collective-permute-start.21 = (f32[8,8,128]{2,1,0:T(8,128)}, f32[8,8,128]{2,1,0:T(8,128)S(1)}, u32[]{:S(2)}, u32[]{:S(2)}) collective-permute-start(f32[8,8,128]{2,1,0:T(8,128)} %get-tuple-element.124.rest_0_), channel_id=1, source_target_pairs={{0,1},{1,2},{2,3},{3,0},{4,5},{5,6},{6,7},{7,4},{8,9},{9,10},{10,1... | collective-permute-start | bytes 98312 | tf_op jit(solution)/shard_map/ppermute | solution.py:447
  70.8 5.5 %collective-permute-start.22 = (f32[8,8,128]{2,1,0:T(8,128)}, f32[8,8,128]{2,1,0:T(8,128)S(1)}, u32[]{:S(2)}, u32[]{:S(2)}) collective-permute-start(f32[8,8,128]{2,1,0:T(8,128)} %get-tuple-element.124.rest_0_), channel_id=1, source_target_pairs={{0,2},{1,3},{2,0},{3,1},{4,6},{5,7},{6,4},{7,5},{8,10},{9,11},{10,... | collective-permute-start | bytes 98312 | tf_op jit(solution)/shard_map/ppermute | solution.py:447
  73.4 4.1 %collective-permute-start.23 = (f32[8,8,128]{2,1,0:T(8,128)}, f32[8,8,128]{2,1,0:T(8,128)S(1)}, u32[]{:S(2)}, u32[]{:S(2)}) collective-permute-start(f32[8,8,128]{2,1,0:T(8,128)} %get-tuple-element.124.rest_0_), channel_id=1, source_target_pairs={{0,3},{1,0},{2,1},{3,2},{4,7},{5,4},{6,5},{7,6},{8,11},{9,8},{10,9... | collective-permute-start | bytes 98312 | tf_op jit(solution)/shard_map/ppermute | solution.py:447
  75.8 1.8 %copy-start.21 = (f32[8,8,128]{2,1,0:T(8,128)}, f32[8,8,128]{2,1,0:T(8,128)S(1)}, u32[]{:S(2)}) copy-start(f32[8,8,128]{2,1,0:T(8,128)S(1)} %collective-permute-done.21.rest_1_) | copy-start | bytes 98308
  76.3 1.3 %copy-start.22 = (f32[8,8,128]{2,1,0:T(8,128)}, f32[8,8,128]{2,1,0:T(8,128)S(1)}, u32[]{:S(2)}) copy-start(f32[8,8,128]{2,1,0:T(8,128)S(1)} %collective-permute-done.22.rest_2_) | copy-start | bytes 98308
  77.5 0.6 copy-start.23

commit v6 on v5

--- a/solution.py
+++ b/solution.py
@@ -60,14 +60,12 @@
             self.yl[f] = jnp.where(at_d, pltpu.roll(v, (d + 1) % LANES, 1), self.yl[f])
 
 
-def x_minus(v, lo_tile, b, sub):
-    return jnp.where(sub == 0, pltpu.roll(lo_tile, (ROWS - b) % ROWS, 0), pltpu.roll(v, 1, 0))
-
-
-def x_plus(v, hi_tile, b, sub):
-    return jnp.where(
-        sub == ROWS - 1, pltpu.roll(hi_tile, (ROWS - 1 - b) % ROWS, 0), pltpu.roll(v, ROWS - 1, 0)
-    )
+def x_minus(v, lo_row, b, sub):
+    return jnp.where(sub == 0, lo_row, pltpu.roll(v, 1, 0))
+
+
+def x_plus(v, hi_row, b, sub):
+    return jnp.where(sub == ROWS - 1, hi_row, pltpu.roll(v, ROWS - 1, 0))
 
 
 def y_minus(v, lo_cols, d, lane):
@@ -107,11 +105,16 @@
             wo_ref[d] = water
             cbo_ref[d] = carbon
             mo_ref[d] = m_ref[d]
-            acc.add_x([heat, water, carbon, vals[0], vals[2]], b)
             acc.add_y([heat, water, carbon, vals[1], vals[3]], d, lane)
-        for f in range(5):
-            xf_ref[f, a] = acc.xf[f]
-            xl_ref[f, a] = acc.xl[f]
+        planes = pl.ds(a * ROWS, ROWS)
+        sources = ((ho_ref, None), (wo_ref, None), (cbo_ref, None), (co_ref, 0), (co_ref, 2))
+        for f, (out, field) in enumerate(sources):
+            if field is None:
+                xf_ref[f, a] = out[planes, 0, :]
+                xl_ref[f, a] = out[planes, ROWS - 1, :]
+            else:
+                xf_ref[f, a] = out[field, planes, 0, :]
+                xl_ref[f, a] = out[field, planes, ROWS - 1, :]
         return (tuple(acc.yf), tuple(acc.yl))
 
     y_f, y_l = lax.fori_loop(0, groups, group, ((zero,) * 5, (zero,) * 5))
@@ -141,12 +144,13 @@
         def group(a, carry):
             y_f, y_l = carry
             acc = EdgeAcc(3, y_f, y_l)
-            sxlo = [xslo_ref[f, a] for f in range(3)]
-            sxhi = [xshi_ref[f, a] for f in range(3)]
-            cxlo = [xflo_ref[f, a] for f in (3, 4)]
-            cxhi = [xfhi_ref[f, a] for f in (3, 4)]
             for b in range(ROWS):
                 i = a * ROWS + b
+                row = pl.ds(b, ROWS, stride=0)
+                sxlo = [xslo_ref[f, a, row, :] for f in range(3)]
+                sxhi = [xshi_ref[f, a, row, :] for f in range(3)]
+                cxlo = [xflo_ref[f, a, row, :] for f in (3, 4)]
+                cxhi = [xfhi_ref[f, a, row, :] for f in (3, 4)]
                 d = chunk * depth + i
                 heat = h_ref[i]
                 water = w_ref[i]
@@ -205,11 +209,11 @@
                 wo_ref[i] = water_two
                 cbo_ref[i] = carbon_two
                 mo_ref[i] = melt_two
-                acc.add_x([heat_three, water_two, carbon_two], b)
                 acc.add_y([heat_three, water_two, carbon_two], d, lane)
-            for f in range(3):
-                xf_ref[f, a] = acc.xf[f]
-                xl_ref[f, a] = acc.xl[f]
+            planes = pl.ds(a * ROWS, ROWS)
+            for f, out in enumerate((ho_ref, wo_ref, cbo_ref)):
+                xf_ref[f, a] = out[planes, 0, :]
+                xl_ref[f, a] = out[planes, ROWS - 1, :]
             return (tuple(acc.yf), tuple(acc.yl))
 
         y_f, y_l = lax.fori_loop(0, groups, group, ((zero,) * 3, (zero,) * 3))

time: 80.9 us -> 81.5 us (level)
  transfers between devices with their start and end apart: 24 -> 24, of which waited for: 5 -> 5; matrix products, arithmetic and copies ran while one was open for 0% -> 0% of each run, Pallas kernels for 30% -> 31%
where the time goes in v6:
time: 81.5 us; the launch traced here: 81.1 us
  Pallas kernels  44 us (54%)
  starting transfers between devices  26 us (32%)
  waiting for transfers between devices  5.37 us (7%)
  local copies, waits for them, and re-layouts  4.98 us (6%)
  between operations  0.83 us (1%)
    pallas_call x8, Pallas kernels, local(): pl.pallas_call(make_section_kernel(k, first), grid=(1,), out_shape=(sds(s...  33.1 us
    ppermute x7, starting transfers between devices, exchange(): xhi = lax.ppermute(xf, 'east', east_bwd)  9.43 us
    ppermute x7, starting transfers between devices, exchange(): ylo = lax.ppermute(ys, 'north', north_fwd)  8.38 us
    ppermute x3, starting transfers between devices, local(): lax.ppermute(red, 'depth', [(i, (i + k) % count) for i in range(count)])  5.37 us
    unnamed x48, local copies, waits for them, and re-layouts  4.98 us
    pallas_call x1, Pallas kernels, local(): pl.pallas_call(prep_kernel, out_shape=(sds(shape), sds(shape), sds(shape)...  4.57 us
    pallas_call x1, Pallas kernels, local(): pl.pallas_call(sweep_kernel, grid=(1,), out_shape=(sds(shape), sds(shape)...  3.87 us
    ppermute x7, starting transfers between devices, exchange(): xlo = lax.ppermute(xl, 'east', east_fwd)  2.81 us
  transfers between devices with their start and end apart: 24, of which 5 were waited for; matrix products, arithmetic and copies ran while one was open for 0% of the time, Pallas kernels for 31%

profile of v6, /device:TPU:0, one launch (start us, length us, event | category | flops | bytes accessed | tf_op | source)
XLA Modules:
  0.0 81.1 jit_solution(11437053774251756801)
XLA Ops:
  0.6 4.6 %shard_map.120 = (f32[64,8,128]{2,1,0:T(8,128)}, f32[64,8,128]{2,1,0:T(8,128)}, f32[64,8,128]{2,1,0:T(8,128)}, f32[64,8,128]{2,1,0:T(8,128)}, f32[5,64,8,128]{3,...) custom-call(f32[2,12]{1,0:T(2,128)} %lat_ref.1, f32[12]{0:T(128)} %vert_ref.1, ...), custom_call_target="tpu_custom_call" | custom-call | tf_op jit(solution)/shard_map/pallas_call | solution.py:395
  5.2 0.5 collective-permute-start
  5.7 2.0 %collective-permute-start.1 = (f32[5,8,8,128]{3,2,1,0:T(8,128)}, f32[5,8,8,128]{3,2,1,0:T(8,128)S(1)}, u32[]{:S(2)}, u32[]{:S(2)}) collective-permute-start(f32[5,8,8,128]{3,2,1,0:T(8,128)} %get-tuple-element.72), channel_id=1, source_target_pairs={{8,0},{16,8},{24,16},{0,24},{9,1},{17,9},{25,17},{1,25},{10,2},{18... | collective-permute-start | bytes 491528 | tf_op jit(solution)/shard_map/ppermute | solution.py:361
  7.7 2.3 %collective-permute-start.2 = (f32[2,5,8,128]{3,2,1,0:T(8,128)}, f32[2,5,8,128]{3,2,1,0:T(8,128)S(1)}, u32[]{:S(2)}, u32[]{:S(2)}) collective-permute-start(f32[2,5,8,128]{3,2,1,0:T(8,128)} %get-tuple-element.73), channel_id=1, source_target_pairs={{0,4},{4,0},{1,5},{5,1},{2,6},{6,2},{3,7},{7,3},{8,12},{12,8},{9,1... | collective-permute-start | bytes 122888 | tf_op jit(solution)/shard_map/ppermute | solution.py:362
  10.0 2.2 %collective-permute-done.2.yflo_ref.yfhi_ref = f32[2,5,8,128]{3,2,1,0:T(8,128)S(1)} collective-permute-done((f32[2,5,8,128]{3,2,1,0:T(8,128)}, f32[2,5,8,128]{3,2,1,0:T(8,128)S(1)}, u32[]{:S(2)}, u32[]{:S(2)}) %collective-permute-start.2) | collective-permute-done | bytes 40992 | tf_op jit(solution)/shard_map/ppermute | solution.py:362
  12.2 0.4 collective-permute-done.1.xfhi_ref
  12.5 0.2 copy-done.2
  12.8 0.1 copy-done
  12.8 0.3 copy-done.1
  13.2 4.1 %shard_map.121 = (f32[64,8,128]{2,1,0:T(8,128)}, f32[64,8,128]{2,1,0:T(8,128)}, f32[64,8,128]{2,1,0:T(8,128)}, f32[64,8,128]{2,1,0:T(8,128)}, f32[3,4,8,128]{3,2...) custom-call(f32[64,8,128]{2,1,0:T(8,128)} %get-tuple-element.66.h_re, ...), custom_call_target="tpu_custom_call", output_to_operand_aliasing={{0}: (0, {}), {1}: (1, {}), {2}: (2, {}), {3}: (3, {})} | custom-call | tf_op jit(solution)/shard_map/pallas_call | solution.py:423
  17.3 0.8 collective-permute-start.3
  18.1 1.3 %collective-permute-start.4 = (f32[3,4,8,128]{3,2,1,0:T(8,128)}, f32[3,4,8,128]{3,2,1,0:T(8,128)S(1)}, u32[]{:S(2)}, u32[]{:S(2)}) collective-permute-start(f32[3,4,8,128]{3,2,1,0:T(8,128)} %get-tuple-element.83), channel_id=1, source_target_pairs={{8,0},{16,8},{24,16},{0,24},{9,1},{17,9},{25,17},{1,25},{10,2},{18... | collective-permute-start | bytes 147464 | tf_op jit(solution)/shard_map/ppermute | solution.py:361
  19.4 1.4 %collective-permute-start.5 = (f32[2,3,8,128]{3,2,1,0:T(8,128)}, f32[2,3,8,128]{3,2,1,0:T(8,128)S(1)}, u32[]{:S(2)}, u32[]{:S(2)}) collective-permute-start(f32[2,3,8,128]{3,2,1,0:T(8,128)} %get-tuple-element.84), channel_id=1, source_target_pairs={{0,4},{4,0},{1,5},{5,1},{2,6},{6,2},{3,7},{7,3},{8,12},{12,8},{9,1... | collective-permute-start | bytes 73736 | tf_op jit(solution)/shard_map/ppermute | solution.py:362
  20.8 4.1 %shard_map.122 = (f32[64,8,128]{2,1,0:T(8,128)}, f32[64,8,128]{2,1,0:T(8,128)}, f32[64,8,128]{2,1,0:T(8,128)}, f32[64,8,128]{2,1,0:T(8,128)}, f32[3,4,8,128]{3,2...) custom-call(f32[64,8,128]{2,1,0:T(8,128)} %get-tuple-element.74.h_re, ...), custom_call_target="tpu_custom_call", output_to_operand_aliasing={{0}: (0, {}), {1}: (1, {}), {2}: (2, {}), {3}: (3, {})} | custom-call | tf_op jit(solution)/shard_map/pallas_call | solution.py:423
  25.0 1.7 %collective-permute-start.7 = (f32[3,4,8,128]{3,2,1,0:T(8,128)}, f32[3,4,8,128]{3,2,1,0:T(8,128)S(1)}, u32[]{:S(2)}, u32[]{:S(2)}) collective-permute-start(f32[3,4,8,128]{3,2,1,0:T(8,128)} %get-tuple-element.90), channel_id=1, source_target_pairs={{8,0},{16,8},{24,16},{0,24},{9,1},{17,9},{25,17},{1,25},{10,2},{18... | collective-permute-start | bytes 147464 | tf_op jit(solution)/shard_map/ppermute | solution.py:361
  26.7 0.7 collective-permute-start.8
  27.4 0.6 copy-done.19
  28.0 4.1 %shard_map.123 = (f32[64,8,128]{2,1,0:T(8,128)}, f32[64,8,128]{2,1,0:T(8,128)}, f32[64,8,128]{2,1,0:T(8,128)}, f32[64,8,128]{2,1,0:T(8,128)}, f32[3,4,8,128]{3,2...) custom-call(f32[64,8,128]{2,1,0:T(8,128)} %get-tuple-element.78.h_re, ...), custom_call_target="tpu_custom_call", output_to_operand_aliasing={{0}: (0, {}), {1}: (1, {}), {2}: (2, {}), {3}: (3, {})} | custom-call | tf_op jit(solution)/shard_map/pallas_call | solution.py:423
  32.2 0.2 collective-permute-start.10
  32.3 0.4 collective-permute-start.9
  32.7 1.4 %collective-permute-start.11 = (f32[2,3,8,128]{3,2,1,0:T(8,128)}, f32[2,3,8,128]{3,2,1,0:T(8,128)S(1)}, u32[]{:S(2)}, u32[]{:S(2)}) collective-permute-start(f32[2,3,8,128]{3,2,1,0:T(8,128)} %get-tuple-element.98), channel_id=1, source_target_pairs={{0,4},{4,0},{1,5},{5,1},{2,6},{6,2},{3,7},{7,3},{8,12},{12,8},{9,1... | collective-permute-start | bytes 73736 | tf_op jit(solution)/shard_map/ppermute | solution.py:362
  34.1 0.6 copy-done.9
  34.7 4.1 %shard_map.124 = (f32[64,8,128]{2,1,0:T(8,128)}, f32[64,8,128]{2,1,0:T(8,128)}, f32[64,8,128]{2,1,0:T(8,128)}, f32[64,8,128]{2,1,0:T(8,128)}, f32[3,4,8,128]{3,2...) custom-call(f32[64,8,128]{2,1,0:T(8,128)} %get-tuple-element.85.h_re, ...), custom_call_target="tpu_custom_call", output_to_operand_aliasing={{0}: (0, {}), {1}: (1, {}), {2}: (2, {}), {3}: (3, {})} | custom-call | tf_op jit(solution)/shard_map/pallas_call | solution.py:423
  38.9 0.9 %collective-permute-start.12 = (f32[3,4,8,128]{3,2,1,0:T(8,128)}, f32[3,4,8,128]{3,2,1,0:T(8,128)S(1)}, u32[]{:S(2)}, u32[]{:S(2)}) collective-permute-start(f32[3,4,8,128]{3,2,1,0:T(8,128)} %get-tuple-element.103), channel_id=1, source_target_pairs={{0,8},{8,16},{16,24},{24,0},{1,9},{9,17},{17,25},{25,1},{2,10},{10... | collective-permute-start | bytes 147464 | tf_op jit(solution)/shard_map/ppermute | solution.py:360
  39.8 0.9 %collective-permute-start.13 = (f32[3,4,8,128]{3,2,1,0:T(8,128)}, f32[3,4,8,128]{3,2,1,0:T(8,128)S(1)}, u32[]{:S(2)}, u32[]{:S(2)}) collective-permute-start(f32[3,4,8,128]{3,2,1,0:T(8,128)} %get-tuple-element.104), channel_id=1, source_target_pairs={{8,0},{16,8},{24,16},{0,24},{9,1},{17,9},{25,17},{1,25},{10,2},{18... | collective-permute-start | bytes 147464 | tf_op jit(solution)/shard_map/ppermute | solution.py:361
  40.7 0.7 collective-permute-start.14
  41.4 0.6 copy-done.10
  42.0 4.1 %shard_map.125 = (f32[64,8,128]{2,1,0:T(8,128)}, f32[64,8,128]{2,1,0:T(8,128)}, f32[64,8,128]{2,1,0:T(8,128)}, f32[64,8,128]{2,1,0:T(8,128)}, f32[3,4,8,128]{3,2...) custom-call(f32[64,8,128]{2,1,0:T(8,128)} %get-tuple-element.92.h_re, ...), custom_call_target="tpu_custom_call", output_to_operand_aliasing={{0}: (0, {}), {1}: (1, {}), {2}: (2, {}), {3}: (3, {})} | custom-call | tf_op jit(solution)/shard_map/pallas_call | solution.py:423
  46.1 0.2 collective-permute-start.15
  46.3 1.6 %collective-permute-start.16 = (f32[3,4,8,128]{3,2,1,0:T(8,128)}, f32[3,4,8,128]{3,2,1,0:T(8,128)S(1)}, u32[]{:S(2)}, u32[]{:S(2)}) collective-permute-start(f32[3,4,8,128]{3,2,1,0:T(8,128)} %get-tuple-element.111), channel_id=1, source_target_pairs={{8,0},{16,8},{24,16},{0,24},{9,1},{17,9},{25,17},{1,25},{10,2},{18... | collective-permute-start | bytes 147464 | tf_op jit(solution)/shard_map/ppermute | solution.py:361
  47.9 1.4 %collective-permute-start.17 = (f32[2,3,8,128]{3,2,1,0:T(8,128)}, f32[2,3,8,128]{3,2,1,0:T(8,128)S(1)}, u32[]{:S(2)}, u32[]{:S(2)}) collective-permute-start(f32[2,3,8,128]{3,2,1,0:T(8,128)} %get-tuple-element.112), channel_id=1, source_target_pairs={{0,4},{4,0},{1,5},{5,1},{2,6},{6,2},{3,7},{7,3},{8,12},{12,8},{9,1... | collective-permute-start | bytes 73736 | tf_op jit(solution)/shard_map/ppermute | solution.py:362
  49.3 0.6 copy-done.11
  49.9 4.1 %shard_map.126 = (f32[64,8,128]{2,1,0:T(8,128)}, f32[64,8,128]{2,1,0:T(8,128)}, f32[64,8,128]{2,1,0:T(8,128)}, f32[64,8,128]{2,1,0:T(8,128)}, f32[3,4,8,128]{3,2...) custom-call(f32[64,8,128]{2,1,0:T(8,128)} %get-tuple-element.99.h_re, ...), custom_call_target="tpu_custom_call", output_to_operand_aliasing={{0}: (0, {}), {1}: (1, {}), {2}: (2, {}), {3}: (3, {})} | custom-call | tf_op jit(solution)/shard_map/pallas_call | solution.py:423
  54.1 1.7 %collective-permute-start.19 = (f32[3,4,8,128]{3,2,1,0:T(8,128)}, f32[3,4,8,128]{3,2,1,0:T(8,128)S(1)}, u32[]{:S(2)}, u32[]{:S(2)}) collective-permute-start(f32[3,4,8,128]{3,2,1,0:T(8,128)} %get-tuple-element.118), channel_id=1, source_target_pairs={{8,0},{16,8},{24,16},{0,24},{9,1},{17,9},{25,17},{1,25},{10,2},{18... | collective-permute-start | bytes 147464 | tf_op jit(solution)/shard_map/ppermute | solution.py:361
  55.9 0.7 collective-permute-start.20
  56.6 0.6 copy-done.12
  57.2 4.1 %shard_map.127 = (f32[64,8,128]{2,1,0:T(8,128)}, f32[64,8,128]{2,1,0:T(8,128)}, f32[64,8,128]{2,1,0:T(8,128)}, f32[64,8,128]{2,1,0:T(8,128)}, f32[3,4,8,128]{3,2...) custom-call(f32[64,8,128]{2,1,0:T(8,128)} %get-tuple-element.106.h_r, ...), custom_call_target="tpu_custom_call", output_to_operand_aliasing={{0}: (0, {}), {1}: (1, {}), {2}: (2, {}), {3}: (3, {})} | custom-call | tf_op jit(solution)/shard_map/pallas_call | solution.py:423
  61.4 0.6 copy-done.7
  62.0 4.1 %shard_map.128 = (f32[64,8,128]{2,1,0:T(8,128)}, f32[64,8,128]{2,1,0:T(8,128)}, f32[64,8,128]{2,1,0:T(8,128)}, f32[64,8,128]{2,1,0:T(8,128)}, f32[3,4,8,128]{3,2...) custom-call(f32[64,8,128]{2,1,0:T(8,128)} %get-tuple-element.113.h_r, ...), custom_call_target="tpu_custom_call", output_to_operand_aliasing={{0}: (0, {}), {1}: (1, {}), {2}: (2, {}), {3}: (3, {})} | custom-call | tf_op jit(solution)/shard_map/pallas_call | solution.py:423
  66.1 3.9 %shard_map.129 = (f32[64,8,128]{2,1,0:T(8,128)}, f32[64,8,128]{2,1,0:T(8,128)}, f32[64,8,128]{2,1,0:T(8,128)}, f32[8,8,128]{2,1,0:T(8,128)}) custom-call(f32[64,8,128]{2,1,0:T(8,128)} %get-tuple-element.120.r_ref, f32[5,64,8,128]{3,2,1,0:T(8,128)} %get-tuple-element.70.co_ref.cz_ref), custom_call_target="tpu_custom_call" | custom-call | tf_op jit(solution)/shard_map/pallas_call | solution.py:439
  70.0 1.4 %collective-permute-start.21 = (f32[8,8,128]{2,1,0:T(8,128)}, f32[8,8,128]{2,1,0:T(8,128)S(1)}, u32[]{:S(2)}, u32[]{:S(2)}) collective-permute-start(f32[8,8,128]{2,1,0:T(8,128)} %get-tuple-element.124.rest_0_), channel_id=1, source_target_pairs={{0,1},{1,2},{2,3},{3,0},{4,5},{5,6},{6,7},{7,4},{8,9},{9,10},{10,1... | collective-permute-start | bytes 98312 | tf_op jit(solution)/shard_map/ppermute | solution.py:451
  71.4 2.6 %collective-permute-start.22 = (f32[8,8,128]{2,1,0:T(8,128)}, f32[8,8,128]{2,1,0:T(8,128)S(1)}, u32[]{:S(2)}, u32[]{:S(2)}) collective-permute-start(f32[8,8,128]{2,1,0:T(8,128)} %get-tuple-element.124.rest_0_), channel_id=1, source_target_pairs={{0,2},{1,3},{2,0},{3,1},{4,6},{5,7},{6,4},{7,5},{8,10},{9,11},{10,... | collective-permute-start | bytes 98312 | tf_op jit(solution)/shard_map/ppermute | solution.py:451
  74.0 1.3 %collective-permute-start.23 = (f32[8,8,128]{2,1,0:T(8,128)}, f32[8,8,128]{2,1,0:T(8,128)S(1)}, u32[]{:S(2)}, u32[]{:S(2)}) collective-permute-start(f32[8,8,128]{2,1,0:T(8,128)} %get-tuple-element.124.rest_0_), channel_id=1, source_target_pairs={{0,3},{1,0},{2,1},{3,2},{4,7},{5,4},{6,5},{7,6},{8,11},{9,8},{10,9... | collective-permute-start | bytes 98312 | tf_op jit(solution)/shard_map/ppermute | solution.py:451
  75.4 1.0 %collective-permute-done.21.rest_1_ = f32[8,8,128]{2,1,0:T(8,128)S(1)} collective-permute-done((f32[8,8,128]{2,1,0:T(8,128)}, f32[8,8,128]{2,1,0:T(8,128)S(1)}, u32[]{:S(2)}, u32[]{:S(2)}) %collective-permute-start.21) | collective-permute-done | bytes 32800 | tf_op jit(solution)/shard_map/ppermute | solution.py:451
  76.3 0.5 collective-permute-done.22.rest_2_
  76.9 1.3 %collective-permute-done.23.rest_3_ = f32[8,8,128]{2,1,0:T(8,128)S(1)} collective-permute-done((f32[8,8,128]{2,1,0:T(8,128)}, f32[8,8,128]{2,1,0:T(8,128)S(1)}, u32[]{:S(2)}, u32[]{:S(2)}) %collective-permute-start.23) | collective-permute-done | bytes 32800 | tf_op jit(solution)/shard_map/ppermute | solution.py:451
  78.1 0.6 copy-done.23
  78.7 2.4 %shard_map.130 = f32[64,8,128]{2,1,0:T(8,128)} custom-call(s32[1]{0:T(128)} %bitcast.rank_ref, f32[64,8,128]{2,1,0:T(8,128)} %get-tuple-element.121.y_ref, f32[64,8,128]{2,1,0:T(8,128)} %get-tuple-element.122.a_ref, f32[64,8,128]{2,1,0:T(8,128)} %get-tuple-element.123.b_ref, f32[8,8,128]{2,1,0:T(8,128)} %get-tuple-element.124.rest_0_, ...), custom_call_target="tpu_custom_call" | custom-call | tf_op jit(solution)/shard_map/pallas_call | solution.py:453
  (59 shorter events, 0.3 us)
Async XLA Ops:
  5.2 7.0 %collective-permute-start = (f32[5,8,8,128]{3,2,1,0:T(8,128)}, f32[5,8,8,128]{3,2,1,0:T(8,128)S(1)}, u32[]{:S(2)}, u32[]{:S(2)}) collective-permute-start(f32[5,8,8,128]{3,2,1,0:T(8,128)} %get-tuple-element.71), channel_id=1, source_target_pairs={{0,8},{8,16},{16,24},{24,0},{1,9},{9,17},{17,25},{25,1},{2,10},{10... | collective-permute-start | bytes 491528 | tf_op jit(solution)/shard_map/ppermute | solution.py:360
  5.7 6.8 %collective-permute-start.1 = (f32[5,8,8,128]{3,2,1,0:T(8,128)}, f32[5,8,8,128]{3,2,1,0:T(8,128)S(1)}, u32[]{:S(2)}, u32[]{:S(2)}) collective-permute-start(f32[5,8,8,128]{3,2,1,0:T(8,128)} %get-tuple-element.72), channel_id=1, source_target_pairs={{8,0},{16,8},{24,16},{0,24},{9,1},{17,9},{25,17},{1,25},{10,2},{18... | collective-permute-start | bytes 491528 | tf_op jit(solution)/shard_map/ppermute | solution.py:361
  7.7 4.5 %collective-permute-start.2 = (f32[2,5,8,128]{3,2,1,0:T(8,128)}, f32[2,5,8,128]{3,2,1,0:T(8,128)S(1)}, u32[]{:S(2)}, u32[]{:S(2)}) collective-permute-start(f32[2,5,8,128]{3,2,1,0:T(8,128)} %get-tuple-element.73), channel_id=1, source_target_pairs={{0,4},{4,0},{1,5},{5,1},{2,6},{6,2},{3,7},{7,3},{8,12},{12,8},{9,1... | collective-permute-start | bytes 122888 | tf_op jit(solution)/shard_map/ppermute | solution.py:362
  12.2 0.6 copy-start.2
  12.2 0.7 copy-start
  12.5 0.7 copy-start.1
  17.3 10.0 %collective-permute-start.3 = (f32[3,4,8,128]{3,2,1,0:T(8,128)}, f32[3,4,8,128]{3,2,1,0:T(8,128)S(1)}, u32[]{:S(2)}, u32[]{:S(2)}) collective-permute-start(f32[3,4,8,128]{3,2,1,0:T(8,128)} %get-tuple-element.82), channel_id=1, source_target_pairs={{0,8},{8,16},{16,24},{24,0},{1,9},{9,17},{17,25},{25,1},{2,10},{10... | collective-permute-start | bytes 147464 | tf_op jit(solution)/shard_map/ppermute | solution.py:360
  18.1 9.3 %collective-permute-start.4 = (f32[3,4,8,128]{3,2,1,0:T(8,128)}, f32[3,4,8,128]{3,2,1,0:T(8,128)S(1)}, u32[]{:S(2)}, u32[]{:S(2)}) collective-permute-start(f32[3,4,8,128]{3,2,1,0:T(8,128)} %get-tuple-element.83), channel_id=1, source_target_pairs={{8,0},{16,8},{24,16},{0,24},{9,1},{17,9},{25,17},{1,25},{10,2},{18... | collective-permute-start | bytes 147464 | tf_op jit(solution)/shard_map/ppermute | solution.py:361
  19.4 7.3 %collective-permute-start.5 = (f32[2,3,8,128]{3,2,1,0:T(8,128)}, f32[2,3,8,128]{3,2,1,0:T(8,128)S(1)}, u32[]{:S(2)}, u32[]{:S(2)}) collective-permute-start(f32[2,3,8,128]{3,2,1,0:T(8,128)} %get-tuple-element.84), channel_id=1, source_target_pairs={{0,4},{4,0},{1,5},{5,1},{2,6},{6,2},{3,7},{7,3},{8,12},{12,8},{9,1... | collective-permute-start | bytes 73736 | tf_op jit(solution)/shard_map/ppermute | solution.py:362
  25.0 9.1 %collective-permute-start.6 = (f32[3,4,8,128]{3,2,1,0:T(8,128)}, f32[3,4,8,128]{3,2,1,0:T(8,128)S(1)}, u32[]{:S(2)}, u32[]{:S(2)}) collective-permute-start(f32[3,4,8,128]{3,2,1,0:T(8,128)} %get-tuple-element.89), channel_id=1, source_target_pairs={{0,8},{8,16},{16,24},{24,0},{1,9},{9,17},{17,25},{25,1},{2,10},{10... | collective-permute-start | bytes 147464 | tf_op jit(solution)/shard_map/ppermute | solution.py:360
  25.0 9.1 %collective-permute-start.7 = (f32[3,4,8,128]{3,2,1,0:T(8,128)}, f32[3,4,8,128]{3,2,1,0:T(8,128)S(1)}, u32[]{:S(2)}, u32[]{:S(2)}) collective-permute-start(f32[3,4,8,128]{3,2,1,0:T(8,128)} %get-tuple-element.90), channel_id=1, source_target_pairs={{8,0},{16,8},{24,16},{0,24},{9,1},{17,9},{25,17},{1,25},{10,2},{18... | collective-permute-start | bytes 147464 | tf_op jit(solution)/shard_map/ppermute | solution.py:361
  26.7 0.7 copy-start.8
  26.7 6.0 %collective-permute-start.8 = (f32[2,3,8,128]{3,2,1,0:T(8,128)}, f32[2,3,8,128]{3,2,1,0:T(8,128)S(1)}, u32[]{:S(2)}, u32[]{:S(2)}) collective-permute-start(f32[2,3,8,128]{3,2,1,0:T(8,128)} %get-tuple-element.91), channel_id=1, source_target_pairs={{0,4},{4,0},{1,5},{5,1},{2,6},{6,2},{3,7},{7,3},{8,12},{12,8},{9,1... | collective-permute-start | bytes 73736 | tf_op jit(solution)/shard_map/ppermute | solution.py:362
  27.4 0.6 copy-start.19
  27.4 0.6 copy-start.20
  32.2 9.2 %collective-permute-start.10 = (f32[3,4,8,128]{3,2,1,0:T(8,128)}, f32[3,4,8,128]{3,2,1,0:T(8,128)S(1)}, u32[]{:S(2)}, u32[]{:S(2)}) collective-permute-start(f32[3,4,8,128]{3,2,1,0:T(8,128)} %get-tuple-element.97), channel_id=1, source_target_pairs={{8,0},{16,8},{24,16},{0,24},{9,1},{17,9},{25,17},{1,25},{10,2},{18... | collective-permute-start | bytes 147464 | tf_op jit(solution)/shard_map/ppermute | solution.py:361
  32.3 9.0 %collective-permute-start.9 = (f32[3,4,8,128]{3,2,1,0:T(8,128)}, f32[3,4,8,128]{3,2,1,0:T(8,128)S(1)}, u32[]{:S(2)}, u32[]{:S(2)}) collective-permute-start(f32[3,4,8,128]{3,2,1,0:T(8,128)} %get-tuple-element.96), channel_id=1, source_target_pairs={{0,8},{8,16},{16,24},{24,0},{1,9},{9,17},{17,25},{25,1},{2,10},{10... | collective-permute-start | bytes 147464 | tf_op jit(solution)/shard_map/ppermute | solution.py:360
  32.7 1.4 %copy-start.3 = (f32[2,3,8,128]{3,2,1,0:T(8,128)}, f32[2,3,8,128]{3,2,1,0:T(8,128)S(1)}, u32[]{:S(2)}) copy-start(f32[2,3,8,128]{3,2,1,0:T(8,128)S(1)} %collective-permute-done.8.rest_2_.rest_3_) | copy-start | bytes 73732
  32.7 8.0 %collective-permute-start.11 = (f32[2,3,8,128]{3,2,1,0:T(8,128)}, f32[2,3,8,128]{3,2,1,0:T(8,128)S(1)}, u32[]{:S(2)}, u32[]{:S(2)}) collective-permute-start(f32[2,3,8,128]{3,2,1,0:T(8,128)} %get-tuple-element.98), channel_id=1, source_target_pairs={{0,4},{4,0},{1,5},{5,1},{2,6},{6,2},{3,7},{7,3},{8,12},{12,8},{9,1... | collective-permute-start | bytes 73736 | tf_op jit(solution)/shard_map/ppermute | solution.py:362
  34.1 0.6 copy-start.9
  34.1 0.6 copy-start.13
  38.9 10.4 %collective-permute-start.12 = (f32[3,4,8,128]{3,2,1,0:T(8,128)}, f32[3,4,8,128]{3,2,1,0:T(8,128)S(1)}, u32[]{:S(2)}, u32[]{:S(2)}) collective-permute-start(f32[3,4,8,128]{3,2,1,0:T(8,128)} %get-tuple-element.103), channel_id=1, source_target_pairs={{0,8},{8,16},{16,24},{24,0},{1,9},{9,17},{17,25},{25,1},{2,10},{10... | collective-permute-start | bytes 147464 | tf_op jit(solution)/shard_map/ppermute | solution.py:360
  39.8 9.5 %collective-permute-start.13 = (f32[3,4,8,128]{3,2,1,0:T(8,128)}, f32[3,4,8,128]{3,2,1,0:T(8,128)S(1)}, u32[]{:S(2)}, u32[]{:S(2)}) collective-permute-start(f32[3,4,8,128]{3,2,1,0:T(8,128)} %get-tuple-element.104), channel_id=1, source_target_pairs={{8,0},{16,8},{24,16},{0,24},{9,1},{17,9},{25,17},{1,25},{10,2},{18... | collective-permute-start | bytes 147464 | tf_op jit(solution)/shard_map/ppermute | solution.py:361
  40.7 0.7 copy-start.4
  40.7 7.2 %collective-permute-start.14 = (f32[2,3,8,128]{3,2,1,0:T(8,128)}, f32[2,3,8,128]{3,2,1,0:T(8,128)S(1)}, u32[]{:S(2)}, u32[]{:S(2)}) collective-permute-start(f32[2,3,8,128]{3,2,1,0:T(8,128)} %get-tuple-element.105), channel_id=1, source_target_pairs={{0,4},{4,0},{1,5},{5,1},{2,6},{6,2},{3,7},{7,3},{8,12},{12,8},{9,1... | collective-permute-start | bytes 73736 | tf_op jit(solution)/shard_map/ppermute | solution.py:362
  41.3 0.6 copy-start.10
  41.3 0.6 copy-start.14
  46.1 10.4 %collective-permute-start.15 = (f32[3,4,8,128]{3,2,1,0:T(8,128)}, f32[3,4,8,128]{3,2,1,0:T(8,128)S(1)}, u32[]{:S(2)}, u32[]{:S(2)}) collective-permute-start(f32[3,4,8,128]{3,2,1,0:T(8,128)} %get-tuple-element.110), channel_id=1, source_target_pairs={{0,8},{8,16},{16,24},{24,0},{1,9},{9,17},{17,25},{25,1},{2,10},{10... | collective-permute-start | bytes 147464 | tf_op jit(solution)/shard_map/ppermute | solution.py:360
  46.3 10.2 %collective-permute-start.16 = (f32[3,4,8,128]{3,2,1,0:T(8,128)}, f32[3,4,8,128]{3,2,1,0:T(8,128)S(1)}, u32[]{:S(2)}, u32[]{:S(2)}) collective-permute-start(f32[3,4,8,128]{3,2,1,0:T(8,128)} %get-tuple-element.111), channel_id=1, source_target_pairs={{8,0},{16,8},{24,16},{0,24},{9,1},{17,9},{25,17},{1,25},{10,2},{18... | collective-permute-start | bytes 147464 | tf_op jit(solution)/shard_map/ppermute | solution.py:361
  47.9 1.4 %copy-start.5 = (f32[2,3,8,128]{3,2,1,0:T(8,128)}, f32[2,3,8,128]{3,2,1,0:T(8,128)S(1)}, u32[]{:S(2)}) copy-start(f32[2,3,8,128]{3,2,1,0:T(8,128)S(1)} %collective-permute-done.14.rest_2_.rest_3_) | copy-start | bytes 73732
  47.9 8.0 %collective-permute-start.17 = (f32[2,3,8,128]{3,2,1,0:T(8,128)}, f32[2,3,8,128]{3,2,1,0:T(8,128)S(1)}, u32[]{:S(2)}, u32[]{:S(2)}) collective-permute-start(f32[2,3,8,128]{3,2,1,0:T(8,128)} %get-tuple-element.112), channel_id=1, source_target_pairs={{0,4},{4,0},{1,5},{5,1},{2,6},{6,2},{3,7},{7,3},{8,12},{12,8},{9,1... | collective-permute-start | bytes 73736 | tf_op jit(solution)/shard_map/ppermute | solution.py:362
  49.3 0.6 copy-start.11
  49.3 0.6 copy-start.15
  54.1 7.2 %collective-permute-start.18 = (f32[3,4,8,128]{3,2,1,0:T(8,128)}, f32[3,4,8,128]{3,2,1,0:T(8,128)S(1)}, u32[]{:S(2)}, u32[]{:S(2)}) collective-permute-start(f32[3,4,8,128]{3,2,1,0:T(8,128)} %get-tuple-element.117), channel_id=1, source_target_pairs={{0,8},{8,16},{16,24},{24,0},{1,9},{9,17},{17,25},{25,1},{2,10},{10... | collective-permute-start | bytes 147464 | tf_op jit(solution)/shard_map/ppermute | solution.py:360
  54.1 7.2 %collective-permute-start.19 = (f32[3,4,8,128]{3,2,1,0:T(8,128)}, f32[3,4,8,128]{3,2,1,0:T(8,128)S(1)}, u32[]{:S(2)}, u32[]{:S(2)}) collective-permute-start(f32[3,4,8,128]{3,2,1,0:T(8,128)} %get-tuple-element.118), channel_id=1, source_target_pairs={{8,0},{16,8},{24,16},{0,24},{9,1},{17,9},{25,17},{1,25},{10,2},{18... | collective-permute-start | bytes 147464 | tf_op jit(solution)/shard_map/ppermute | solution.py:361
  55.9 0.7 copy-start.6
  55.9 5.4 %collective-permute-start.20 = (f32[2,3,8,128]{3,2,1,0:T(8,128)}, f32[2,3,8,128]{3,2,1,0:T(8,128)S(1)}, u32[]{:S(2)}, u32[]{:S(2)}) collective-permute-start(f32[2,3,8,128]{3,2,1,0:T(8,128)} %get-tuple-element.119), channel_id=1, source_target_pairs={{0,4},{4,0},{1,5},{5,1},{2,6},{6,2},{3,7},{7,3},{8,12},{12,8},{9,1... | collective-permute-start | bytes 73736 | tf_op jit(solution)/shard_map/ppermute | solution.py:362
  56.5 0.6 copy-start.12
  56.5 0.6 copy-start.16
  61.3 0.6 copy-start.7
  61.3 0.6 copy-start.17
  61.3 0.6 copy-start.18
  70.0 6.4 %collective-permute-start.21 = (f32[8,8,128]{2,1,0:T(8,128)}, f32[8,8,128]{2,1,0:T(8,128)S(1)}, u32[]{:S(2)}, u32[]{:S(2)}) collective-permute-start(f32[8,8,128]{2,1,0:T(8,128)} %get-tuple-element.124.rest_0_), channel_id=1, source_target_pairs={{0,1},{1,2},{2,3},{3,0},{4,5},{5,6},{6,7},{7,4},{8,9},{9,10},{10,1... | collective-permute-start | bytes 98312 | tf_op jit(solution)/shard_map/ppermute | solution.py:451
  71.4 5.5 %collective-permute-start.22 = (f32[8,8,128]{2,1,0:T(8,128)}, f32[8,8,128]{2,1,0:T(8,128)S(1)}, u32[]{:S(2)}, u32[]{:S(2)}) collective-permute-start(f32[8,8,128]{2,1,0:T(8,128)} %get-tuple-element.124.rest_0_), channel_id=1, source_target_pairs={{0,2},{1,3},{2,0},{3,1},{4,6},{5,7},{6,4},{7,5},{8,10},{9,11},{10,... | collective-permute-start | bytes 98312 | tf_op jit(solution)/shard_map/ppermute | solution.py:451
  74.0 4.1 %collective-permute-start.23 = (f32[8,8,128]{2,1,0:T(8,128)}, f32[8,8,128]{2,1,0:T(8,128)S(1)}, u32[]{:S(2)}, u32[]{:S(2)}) collective-permute-start(f32[8,8,128]{2,1,0:T(8,128)} %get-tuple-element.124.rest_0_), channel_id=1, source_target_pairs={{0,3},{1,0},{2,1},{3,2},{4,7},{5,4},{6,5},{7,6},{8,11},{9,8},{10,9... | collective-permute-start | bytes 98312 | tf_op jit(solution)/shard_map/ppermute | solution.py:451
  76.3 1.8 %copy-start.21 = (f32[8,8,128]{2,1,0:T(8,128)}, f32[8,8,128]{2,1,0:T(8,128)S(1)}, u32[]{:S(2)}) copy-start(f32[8,8,128]{2,1,0:T(8,128)S(1)} %collective-permute-done.21.rest_1_) | copy-start | bytes 98308
  76.9 1.3 %copy-start.22 = (f32[8,8,128]{2,1,0:T(8,128)}, f32[8,8,128]{2,1,0:T(8,128)S(1)}, u32[]{:S(2)}) copy-start(f32[8,8,128]{2,1,0:T(8,128)S(1)} %collective-permute-done.22.rest_2_) | copy-start | bytes 98308
  78.1 0.6 copy-start.23

commit v7 on v6

--- a/solution.py
+++ b/solution.py
@@ -80,66 +80,63 @@
     )
 
 
+def lookup_planes(tables, layer, count):
+    zero = jnp.zeros(layer.shape, f32)
+    vals = [zero] * len(tables)
+    for l in range(count):
+        hit = layer == l
+        vals = [jnp.where(hit, tab(l), vals[k]) for k, tab in enumerate(tables)]
+    return vals
+
+
 def prep_kernel(lat_ref, vert_ref, adv_ref, layer_ref, h_ref, w_ref, c_ref, m_ref,
-                ho_ref, wo_ref, cbo_ref, mo_ref, co_ref, xf_ref, xl_ref, y_ref):
-    groups = layer_ref.shape[0] // ROWS
-    layers_count = vert_ref.shape[0]
-    sub, lane = iotas()
-    zero = jnp.zeros((ROWS, LANES), f32)
-
-    def group(a, carry):
-        y_f, y_l = carry
-        acc = EdgeAcc(5, y_f, y_l)
-        for b in range(ROWS):
-            d = a * ROWS + b
-            layer = layer_ref[d]
-            vals = [zero] * 5
-            for l in range(layers_count):
-                hit = layer == l
-                entries = (lat_ref[0, l], lat_ref[1, l], adv_ref[0, l], adv_ref[1, l], vert_ref[l])
-                vals = [jnp.where(hit, entries[k], vals[k]) for k in range(5)]
-            for k in range(5):
-                co_ref[k, d] = vals[k]
-            heat, water, carbon = h_ref[d], w_ref[d], c_ref[d]
-            ho_ref[d] = heat
-            wo_ref[d] = water
-            cbo_ref[d] = carbon
-            mo_ref[d] = m_ref[d]
-            acc.add_y([heat, water, carbon, vals[1], vals[3]], d, lane)
-        planes = pl.ds(a * ROWS, ROWS)
-        sources = ((ho_ref, None), (wo_ref, None), (cbo_ref, None), (co_ref, 0), (co_ref, 2))
-        for f, (out, field) in enumerate(sources):
-            if field is None:
-                xf_ref[f, a] = out[planes, 0, :]
-                xl_ref[f, a] = out[planes, ROWS - 1, :]
-            else:
-                xf_ref[f, a] = out[field, planes, 0, :]
-                xl_ref[f, a] = out[field, planes, ROWS - 1, :]
-        return (tuple(acc.yf), tuple(acc.yl))
-
-    y_f, y_l = lax.fori_loop(0, groups, group, ((zero,) * 5, (zero,) * 5))
-    for f in range(5):
-        y_ref[0, f] = y_f[f]
-        y_ref[1, f] = y_l[f]
+                ho_ref, wo_ref, cbo_ref, mo_ref, co_ref):
+    count = vert_ref.shape[0]
+    tables = (
+        lambda l: lat_ref[0, l], lambda l: lat_ref[1, l],
+        lambda l: adv_ref[0, l], lambda l: adv_ref[1, l], lambda l: vert_ref[l],
+    )
+
+    def plane(d, carry):
+        vals = lookup_planes(tables, layer_ref[d], count)
+        for k in range(5):
+            co_ref[k, d] = vals[k]
+        ho_ref[d] = h_ref[d]
+        wo_ref[d] = w_ref[d]
+        cbo_ref[d] = c_ref[d]
+        mo_ref[d] = m_ref[d]
+        return carry
+
+    lax.fori_loop(0, layer_ref.shape[0], plane, 0)
 
 
 def make_section_kernel(chunk, first):
-    def kernel(h_ref, w_ref, c_ref, m_ref, sill_ref, co_ref, xflo_ref, xfhi_ref, yflo_ref, yfhi_ref,
-               *rest):
+    def kernel(lat_ref, adv_ref, h_ref, w_ref, c_ref, m_ref, sill_ref, co_ref,
+               xflo_ref, xfhi_ref, yflo_ref, yfhi_ref, *rest):
         if first:
-            ho_ref, wo_ref, cbo_ref, mo_ref, xf_ref, xl_ref, y_ref = rest
+            ho_ref, wo_ref, cbo_ref, mo_ref, xf_ref, xl_ref, y_ref, cx_s = rest
             xslo_ref, xshi_ref, yslo_ref, yshi_ref = xflo_ref, xfhi_ref, yflo_ref, yfhi_ref
         else:
             xslo_ref, xshi_ref, yslo_ref, yshi_ref = rest[:4]
-            ho_ref, wo_ref, cbo_ref, mo_ref, xf_ref, xl_ref, y_ref = rest[4:]
+            ho_ref, wo_ref, cbo_ref, mo_ref, xf_ref, xl_ref, y_ref, cx_s = rest[4:]
         depth = h_ref.shape[0]
         groups = depth // ROWS
+        count = lat_ref.shape[1]
         sub, lane = iotas()
         zero = jnp.zeros((ROWS, LANES), f32)
+        x_tables = (lambda l: lat_ref[0, l], lambda l: adv_ref[0, l])
+        y_tables = (lambda l: lat_ref[1, l], lambda l: adv_ref[1, l])
+        for a in range(groups):
+            lo = lookup_planes(x_tables, xflo_ref[3, a], count)
+            hi = lookup_planes(x_tables, xfhi_ref[3, a], count)
+            cx_s[0, a] = lo[0]
+            cx_s[1, a] = lo[1]
+            cx_s[2, a] = hi[0]
+            cx_s[3, a] = hi[1]
         sylo = [yslo_ref[1, f] for f in range(3)]
         syhi = [yshi_ref[0, f] for f in range(3)]
-        cylo = [yflo_ref[1, f] for f in (3, 4)]
-        cyhi = [yfhi_ref[0, f] for f in (3, 4)]
+        cylo = lookup_planes(y_tables, yflo_ref[1, 3], count)
+        cyhi = lookup_planes(y_tables, yfhi_ref[0, 3], count)
 
         def group(a, carry):
             y_f, y_l = carry
@@ -149,8 +146,8 @@
                 row = pl.ds(b, ROWS, stride=0)
                 sxlo = [xslo_ref[f, a, row, :] for f in range(3)]
                 sxhi = [xshi_ref[f, a, row, :] for f in range(3)]
-                cxlo = [xflo_ref[f, a, row, :] for f in (3, 4)]
-                cxhi = [xfhi_ref[f, a, row, :] for f in (3, 4)]
+                cxlo = [cx_s[f, a, row, :] for f in (0, 1)]
+                cxhi = [cx_s[f, a, row, :] for f in (2, 3)]
                 d = chunk * depth + i
                 heat = h_ref[i]
                 water = w_ref[i]
@@ -392,15 +389,20 @@
     cgroups = depth // ROWS
     smem_spec = pl.BlockSpec(memory_space=pltpu.SMEM)
     vspec = pl.BlockSpec(memory_space=pltpu.MemorySpace.VMEM)
-    heat, water, carbon, melt, co, xf0, xl0, y0 = pl.pallas_call(
+    layer_f = stratum_number_grid.astype(f32)
+    initial = (thermal_field, steam_content_grid, carbonic_gas_grid, layer_f)
+    xf0 = jnp.stack([v[:, 0, :] for v in initial]).reshape(4, groups, ROWS, LANES)
+    xl0 = jnp.stack([v[:, ROWS - 1, :] for v in initial]).reshape(4, groups, ROWS, LANES)
+    cols = jnp.stack([jnp.stack([v[:, :, 0] for v in initial]),
+                      jnp.stack([v[:, :, LANES - 1] for v in initial])])
+    y0 = jnp.pad(jnp.swapaxes(cols, 2, 3), ((0, 0), (0, 0), (0, 0), (0, LANES - n)))
+    xflo, xfhi, yflo, yfhi = exchange(xf0, xl0, y0)
+    heat, water, carbon, melt, co = pl.pallas_call(
         prep_kernel,
-        out_shape=(sds(shape), sds(shape), sds(shape), sds(shape), sds((5,) + shape),
-                   sds((5, groups, ROWS, LANES)), sds((5, groups, ROWS, LANES)),
-                   sds((2, 5, ROWS, LANES))),
+        out_shape=(sds(shape), sds(shape), sds(shape), sds(shape), sds((5,) + shape)),
         in_specs=[smem_spec] * 3 + [vspec] * 5,
     )(lateral_transmissivity, vertical_transmissivity, stratum_advection_offsets, stratum_number_grid, thermal_field, steam_content_grid, carbonic_gas_grid,
       liquid_fraction)
-    xflo, xfhi, yflo, yfhi = exchange(xf0, xl0, y0)
 
     def block_spec(k):
         return pl.BlockSpec((depth, ROWS, LANES), lambda i: (k, 0, 0))
@@ -409,13 +411,14 @@
     for section_no in range(SECTIONS):
         first = section_no == 0
         for k in range(chunks):
-            x5 = pl.BlockSpec((5, cgroups, ROWS, LANES), lambda i, k=k: (0, k, 0, 0))
-            y5 = full_spec((2, 5, ROWS, LANES))
-            in_specs = [block_spec(k)] * 5 + [
+            x4 = pl.BlockSpec((4, cgroups, ROWS, LANES), lambda i, k=k: (0, k, 0, 0))
+            y4 = full_spec((2, 4, ROWS, LANES))
+            in_specs = [smem_spec, smem_spec] + [block_spec(k)] * 5 + [
                 pl.BlockSpec((4, depth, ROWS, LANES), lambda i, k=k: (0, k, 0, 0)),
-                x5, x5, y5, y5,
+                x4, x4, y4, y4,
             ]
-            args = [heat, water, carbon, melt, injection_flags, co, xflo, xfhi, yflo, yfhi]
+            args = [lateral_transmissivity, stratum_advection_offsets,
+                    heat, water, carbon, melt, injection_flags, co, xflo, xfhi, yflo, yfhi]
             if not first:
                 in_specs += [full_spec((3, cgroups, ROWS, LANES))] * 2
                 in_specs += [full_spec((2, 3, ROWS, LANES))] * 2
@@ -431,7 +434,8 @@
                     full_spec((3, cgroups, ROWS, LANES)), full_spec((3, cgroups, ROWS, LANES)),
                     full_spec((2, 3, ROWS, LANES)),
                 ],
-                input_output_aliases={0: 0, 1: 1, 2: 2, 3: 3},
+                input_output_aliases={2: 0, 3: 1, 4: 2, 5: 3},
+                scratch_shapes=[pltpu.VMEM((4, cgroups, ROWS, LANES), f32)],
             )(*args)
             if section_no + 1 < SECTIONS:
                 halos[k] = exchange(xf, xl, ys)

time: 81.5 us -> 82.3 us (level)
  local copies, waits for them, and re-layouts: 4.98 us -> 7.94 us
  waiting for transfers between devices: 5.37 us -> 2.83 us
    unnamed x48 -> x61, local copies, waits for them, and re-layouts: 4.98 us -> 7.21 us
    ppermute x7, waiting for transfers between devices: 2.2 us -> 0.02 us  [exchange(): ylo = lax.ppermute(ys, 'north', north_fwd)]
  transfers between devices with their start and end apart: 24 -> 24, of which waited for: 5 -> 3; matrix products, arithmetic and copies ran while one was open for 0% -> 2% of each run, Pallas kernels for 31% -> 36%
where the time goes in v7:
time: 82.3 us; the launch traced here: 81.9 us
  Pallas kernels  44 us (53%)
  starting transfers between devices  26 us (32%)
  local copies, waits for them, and re-layouts  7.94 us (10%)
  waiting for transfers between devices  2.83 us (3%)
  between operations  1.03 us (1%)
    pallas_call x8, Pallas kernels, local(): pl.pallas_call(make_section_kernel(k, first), grid=(1,), out_shape=(sds(s...  33.5 us
    ppermute x7, starting transfers between devices, exchange(): xhi = lax.ppermute(xf, 'east', east_bwd)  9.16 us
    ppermute x7, starting transfers between devices, exchange(): ylo = lax.ppermute(ys, 'north', north_fwd)  8.47 us
    unnamed x61, local copies, waits for them, and re-layouts  7.21 us
    ppermute x3, starting transfers between devices, local(): lax.ppermute(red, 'depth', [(i, (i + k) % count) for i in range(count)])  5.53 us
    pallas_call x1, Pallas kernels, local(): pl.pallas_call(prep_kernel, out_shape=(sds(shape), sds(shape), sds(shape)...  4.25 us
    pallas_call x1, Pallas kernels, local(): pl.pallas_call(sweep_kernel, grid=(1,), out_shape=(sds(shape), sds(shape)...  3.87 us
    ppermute x7, starting transfers between devices, exchange(): xlo = lax.ppermute(xl, 'east', east_fwd)  2.83 us
  transfers between devices with their start and end apart: 24, of which 3 were waited for; matrix products, arithmetic and copies ran while one was open for 2% of the time, Pallas kernels for 36%

profile of v7, /device:TPU:0, one launch (start us, length us, event | category | flops | bytes accessed | tf_op | source)
XLA Modules:
  0.0 81.9 jit_solution(2217104198817662614)
XLA Ops:
  0.7 1.3 %copy.54 = s32[64,8,128]{0,1,2:T(8,128)S(1)} copy(s32[64,8,128]{2,1,0:T(8,128)} %layer_ref.1) | data formatting | bytes 524288 | tf_op args[4]
  2.3 0.5 collective-permute-start
  2.9 2.0 %collective-permute-start.1 = (f32[4,8,8,128]{3,2,1,0:T(8,128)S(1)}, f32[4,8,8,128]{3,2,1,0:T(8,128)S(1)}, u32[]{:S(2)}, u32[]{:S(2)}) collective-permute-start(f32[4,8,8,128]{3,2,1,0:T(8,128)S(1)} %pad_maximum_fusion.1), channel_id=1, source_target_pairs={{8,0},{16,8},{24,16},{0,24},{9,1},{17,9},{25,17},{1,25},{10,2},{18... | collective-permute-start | bytes 393224 | tf_op jit(solution)/shard_map/ppermute | solution.py:358
  5.1 0.1 fusion.3
  5.2 0.1 fusion.1
  5.3 0.1 copy.64
  5.5 0.2 copy.65
  5.6 0.2 copy.66
  5.8 0.2 copy.67
  6.0 0.2 copy.68
  6.1 0.2 copy.63
  6.3 2.4 %collective-permute-start.2 = (f32[2,4,8,128]{3,2,1,0:T(8,128)S(1)}, f32[2,4,8,128]{3,2,1,0:T(8,128)S(1)}, u32[]{:S(2)}, u32[]{:S(2)}) collective-permute-start(f32[2,4,8,128]{3,2,1,0:T(8,128)S(1)} %pad.4), channel_id=1, source_target_pairs={{0,4},{4,0},{1,5},{5,1},{2,6},{6,2},{3,7},{7,3},{8,12},{12,8},{9,1... | collective-permute-start | bytes 98312 | tf_op jit(solution)/shard_map/ppermute | solution.py:359
  8.7 4.2 %shard_map.120 = (f32[64,8,128]{2,1,0:T(8,128)}, f32[64,8,128]{2,1,0:T(8,128)}, f32[64,8,128]{2,1,0:T(8,128)}, f32[64,8,128]{2,1,0:T(8,128)}, f32[5,64,8,128]{3,2,1,0:T(8,128)}) custom-call(f32[2,12]{1,0:T(2,128)} %lat_ref.17, f32[12]{0:T(128)} %vert_ref.1, f32[2,12]{1,0:T(2,128)} %adv_ref.17, s32[64,8,128]{2,1,0:T(8,128)} %layer_ref.1, ...), custom_call_target="tpu_custom_call" | custom-call | tf_op jit(solution)/shard_map/pallas_call | solution.py:400
  13.0 0.6 copy-done
  13.7 4.2 %shard_map.121 = (f32[64,8,128]{2,1,0:T(8,128)}, f32[64,8,128]{2,1,0:T(8,128)}, f32[64,8,128]{2,1,0:T(8,128)}, f32[64,8,128]{2,1,0:T(8,128)}, f32[3,4,8,128]{3,2...) custom-call(f32[2,12]{1,0:T(2,128)} %lat_ref.17, ...), custom_call_target="tpu_custom_call", output_to_operand_aliasing={{0}: (2, {}), {1}: (3, {}), {2}: (4, {}), {3}: (5, {})} | custom-call | tf_op jit(solution)/shard_map/pallas_call | solution.py:426
  17.9 1.7 %collective-permute-start.4 = (f32[3,4,8,128]{3,2,1,0:T(8,128)}, f32[3,4,8,128]{3,2,1,0:T(8,128)S(1)}, u32[]{:S(2)}, u32[]{:S(2)}) collective-permute-start(f32[3,4,8,128]{3,2,1,0:T(8,128)} %get-tuple-element.77), channel_id=1, source_target_pairs={{8,0},{16,8},{24,16},{0,24},{9,1},{17,9},{25,17},{1,25},{10,2},{18... | collective-permute-start | bytes 147464 | tf_op jit(solution)/shard_map/ppermute | solution.py:358
  19.7 4.2 %shard_map.122 = (f32[64,8,128]{2,1,0:T(8,128)}, f32[64,8,128]{2,1,0:T(8,128)}, f32[64,8,128]{2,1,0:T(8,128)}, f32[64,8,128]{2,1,0:T(8,128)}, f32[3,4,8,128]{3,2...) custom-call(f32[2,12]{1,0:T(2,128)} %lat_ref.17, ...), custom_call_target="tpu_custom_call", output_to_operand_aliasing={{0}: (2, {}), {1}: (3, {}), {2}: (4, {}), {3}: (5, {})} | custom-call | tf_op jit(solution)/shard_map/pallas_call | solution.py:426
  24.0 1.7 %collective-permute-start.7 = (f32[3,4,8,128]{3,2,1,0:T(8,128)}, f32[3,4,8,128]{3,2,1,0:T(8,128)S(1)}, u32[]{:S(2)}, u32[]{:S(2)}) collective-permute-start(f32[3,4,8,128]{3,2,1,0:T(8,128)} %get-tuple-element.84), channel_id=1, source_target_pairs={{8,0},{16,8},{24,16},{0,24},{9,1},{17,9},{25,17},{1,25},{10,2},{18... | collective-permute-start | bytes 147464 | tf_op jit(solution)/shard_map/ppermute | solution.py:358
  25.7 2.0 %collective-permute-start.8 = (f32[2,3,8,128]{3,2,1,0:T(8,128)}, f32[2,3,8,128]{3,2,1,0:T(8,128)S(1)}, u32[]{:S(2)}, u32[]{:S(2)}) collective-permute-start(f32[2,3,8,128]{3,2,1,0:T(8,128)} %get-tuple-element.85), channel_id=1, source_target_pairs={{0,4},{4,0},{1,5},{5,1},{2,6},{6,2},{3,7},{7,3},{8,12},{12,8},{9,1... | collective-permute-start | bytes 73736 | tf_op jit(solution)/shard_map/ppermute | solution.py:359
  27.7 0.6 copy-done.22
  28.3 4.2 %shard_map.123 = (f32[64,8,128]{2,1,0:T(8,128)}, f32[64,8,128]{2,1,0:T(8,128)}, f32[64,8,128]{2,1,0:T(8,128)}, f32[64,8,128]{2,1,0:T(8,128)}, f32[3,4,8,128]{3,2...) custom-call(f32[2,12]{1,0:T(2,128)} %lat_ref.17, ...), custom_call_target="tpu_custom_call", output_to_operand_aliasing={{0}: (2, {}), {1}: (3, {}), {2}: (4, {}), {3}: (5, {})} | custom-call | tf_op jit(solution)/shard_map/pallas_call | solution.py:426
  32.6 0.5 collective-permute-start.9
  33.1 0.6 copy-done.6
  33.7 4.2 %shard_map.124 = (f32[64,8,128]{2,1,0:T(8,128)}, f32[64,8,128]{2,1,0:T(8,128)}, f32[64,8,128]{2,1,0:T(8,128)}, f32[64,8,128]{2,1,0:T(8,128)}, f32[3,4,8,128]{3,2...) custom-call(f32[2,12]{1,0:T(2,128)} %lat_ref.17, ...), custom_call_target="tpu_custom_call", output_to_operand_aliasing={{0}: (2, {}), {1}: (3, {}), {2}: (4, {}), {3}: (5, {})} | custom-call | tf_op jit(solution)/shard_map/pallas_call | solution.py:426
  37.9 1.4 %collective-permute-start.12 = (f32[3,4,8,128]{3,2,1,0:T(8,128)}, f32[3,4,8,128]{3,2,1,0:T(8,128)S(1)}, u32[]{:S(2)}, u32[]{:S(2)}) collective-permute-start(f32[3,4,8,128]{3,2,1,0:T(8,128)} %get-tuple-element.97), channel_id=1, source_target_pairs={{0,8},{8,16},{16,24},{24,0},{1,9},{9,17},{17,25},{25,1},{2,10},{10... | collective-permute-start | bytes 147464 | tf_op jit(solution)/shard_map/ppermute | solution.py:357
  39.3 0.4 collective-permute-start.13
  39.7 2.0 %collective-permute-start.14 = (f32[2,3,8,128]{3,2,1,0:T(8,128)}, f32[2,3,8,128]{3,2,1,0:T(8,128)S(1)}, u32[]{:S(2)}, u32[]{:S(2)}) collective-permute-start(f32[2,3,8,128]{3,2,1,0:T(8,128)} %get-tuple-element.99), channel_id=1, source_target_pairs={{0,4},{4,0},{1,5},{5,1},{2,6},{6,2},{3,7},{7,3},{8,12},{12,8},{9,1... | collective-permute-start | bytes 73736 | tf_op jit(solution)/shard_map/ppermute | solution.py:359
  41.7 0.6 copy-done.13
  42.4 4.2 %shard_map.125 = (f32[64,8,128]{2,1,0:T(8,128)}, f32[64,8,128]{2,1,0:T(8,128)}, f32[64,8,128]{2,1,0:T(8,128)}, f32[64,8,128]{2,1,0:T(8,128)}, f32[3,4,8,128]{3,2...) custom-call(f32[2,12]{1,0:T(2,128)} %lat_ref.17, ...), custom_call_target="tpu_custom_call", output_to_operand_aliasing={{0}: (2, {}), {1}: (3, {}), {2}: (4, {}), {3}: (5, {})} | custom-call | tf_op jit(solution)/shard_map/pallas_call | solution.py:426
  46.6 1.7 %collective-permute-start.16 = (f32[3,4,8,128]{3,2,1,0:T(8,128)}, f32[3,4,8,128]{3,2,1,0:T(8,128)S(1)}, u32[]{:S(2)}, u32[]{:S(2)}) collective-permute-start(f32[3,4,8,128]{3,2,1,0:T(8,128)} %get-tuple-element.105), channel_id=1, source_target_pairs={{8,0},{16,8},{24,16},{0,24},{9,1},{17,9},{25,17},{1,25},{10,2},{18... | collective-permute-start | bytes 147464 | tf_op jit(solution)/shard_map/ppermute | solution.py:358
  48.4 0.5 copy-done.8
  49.0 4.2 %shard_map.126 = (f32[64,8,128]{2,1,0:T(8,128)}, f32[64,8,128]{2,1,0:T(8,128)}, f32[64,8,128]{2,1,0:T(8,128)}, f32[64,8,128]{2,1,0:T(8,128)}, f32[3,4,8,128]{3,2...) custom-call(f32[2,12]{1,0:T(2,128)} %lat_ref.17, ...), custom_call_target="tpu_custom_call", output_to_operand_aliasing={{0}: (2, {}), {1}: (3, {}), {2}: (4, {}), {3}: (5, {})} | custom-call | tf_op jit(solution)/shard_map/pallas_call | solution.py:426
  53.2 0.2 collective-permute-start.18
  53.4 1.6 %collective-permute-start.19 = (f32[3,4,8,128]{3,2,1,0:T(8,128)}, f32[3,4,8,128]{3,2,1,0:T(8,128)S(1)}, u32[]{:S(2)}, u32[]{:S(2)}) collective-permute-start(f32[3,4,8,128]{3,2,1,0:T(8,128)} %get-tuple-element.112), channel_id=1, source_target_pairs={{8,0},{16,8},{24,16},{0,24},{9,1},{17,9},{25,17},{1,25},{10,2},{18... | collective-permute-start | bytes 147464 | tf_op jit(solution)/shard_map/ppermute | solution.py:358
  55.0 2.0 %collective-permute-start.20 = (f32[2,3,8,128]{3,2,1,0:T(8,128)}, f32[2,3,8,128]{3,2,1,0:T(8,128)S(1)}, u32[]{:S(2)}, u32[]{:S(2)}) collective-permute-start(f32[2,3,8,128]{3,2,1,0:T(8,128)} %get-tuple-element.113), channel_id=1, source_target_pairs={{0,4},{4,0},{1,5},{5,1},{2,6},{6,2},{3,7},{7,3},{8,12},{12,8},{9,1... | collective-permute-start | bytes 73736 | tf_op jit(solution)/shard_map/ppermute | solution.py:359
  57.0 0.6 copy-done.15
  57.7 4.2 %shard_map.127 = (f32[64,8,128]{2,1,0:T(8,128)}, f32[64,8,128]{2,1,0:T(8,128)}, f32[64,8,128]{2,1,0:T(8,128)}, f32[64,8,128]{2,1,0:T(8,128)}, f32[3,4,8,128]{3,2...) custom-call(f32[2,12]{1,0:T(2,128)} %lat_ref.17, ...), custom_call_target="tpu_custom_call", output_to_operand_aliasing={{0}: (2, {}), {1}: (3, {}), {2}: (4, {}), {3}: (5, {})} | custom-call | tf_op jit(solution)/shard_map/pallas_call | solution.py:426
  61.9 0.6 copy-done.10
  62.5 4.2 %shard_map.128 = (f32[64,8,128]{2,1,0:T(8,128)}, f32[64,8,128]{2,1,0:T(8,128)}, f32[64,8,128]{2,1,0:T(8,128)}, f32[64,8,128]{2,1,0:T(8,128)}, f32[3,4,8,128]{3,2...) custom-call(f32[2,12]{1,0:T(2,128)} %lat_ref.17, ...), custom_call_target="tpu_custom_call", output_to_operand_aliasing={{0}: (2, {}), {1}: (3, {}), {2}: (4, {}), {3}: (5, {})} | custom-call | tf_op jit(solution)/shard_map/pallas_call | solution.py:426
  66.7 3.9 %shard_map.129 = (f32[64,8,128]{2,1,0:T(8,128)}, f32[64,8,128]{2,1,0:T(8,128)}, f32[64,8,128]{2,1,0:T(8,128)}, f32[8,8,128]{2,1,0:T(8,128)}) custom-call(f32[64,8,128]{2,1,0:T(8,128)} %get-tuple-element.114.r_ref, f32[5,64,8,128]{3,2,1,0:T(8,128)} %get-tuple-element.67.co_ref.cz_ref), custom_call_target="tpu_custom_call" | custom-call | tf_op jit(solution)/shard_map/pallas_call | solution.py:443
  70.6 1.6 %collective-permute-start.21 = (f32[8,8,128]{2,1,0:T(8,128)}, f32[8,8,128]{2,1,0:T(8,128)S(1)}, u32[]{:S(2)}, u32[]{:S(2)}) collective-permute-start(f32[8,8,128]{2,1,0:T(8,128)} %get-tuple-element.118.rest_0_), channel_id=1, source_target_pairs={{0,1},{1,2},{2,3},{3,0},{4,5},{5,6},{6,7},{7,4},{8,9},{9,10},{10,1... | collective-permute-start | bytes 98312 | tf_op jit(solution)/shard_map/ppermute | solution.py:455
  72.2 2.6 %collective-permute-start.22 = (f32[8,8,128]{2,1,0:T(8,128)}, f32[8,8,128]{2,1,0:T(8,128)S(1)}, u32[]{:S(2)}, u32[]{:S(2)}) collective-permute-start(f32[8,8,128]{2,1,0:T(8,128)} %get-tuple-element.118.rest_0_), channel_id=1, source_target_pairs={{0,2},{1,3},{2,0},{3,1},{4,6},{5,7},{6,4},{7,5},{8,10},{9,11},{10,... | collective-permute-start | bytes 98312 | tf_op jit(solution)/shard_map/ppermute | solution.py:455
  74.8 1.3 %collective-permute-start.23 = (f32[8,8,128]{2,1,0:T(8,128)}, f32[8,8,128]{2,1,0:T(8,128)S(1)}, u32[]{:S(2)}, u32[]{:S(2)}) collective-permute-start(f32[8,8,128]{2,1,0:T(8,128)} %get-tuple-element.118.rest_0_), channel_id=1, source_target_pairs={{0,3},{1,0},{2,1},{3,2},{4,7},{5,4},{6,5},{7,6},{8,11},{9,8},{10,9... | collective-permute-start | bytes 98312 | tf_op jit(solution)/shard_map/ppermute | solution.py:455
  76.1 0.7 collective-permute-done.21.rest_1_
  76.8 0.8 collective-permute-done.22.rest_2_
  77.6 1.3 %collective-permute-done.23.rest_3_ = f32[8,8,128]{2,1,0:T(8,128)S(1)} collective-permute-done((f32[8,8,128]{2,1,0:T(8,128)}, f32[8,8,128]{2,1,0:T(8,128)S(1)}, u32[]{:S(2)}, u32[]{:S(2)}) %collective-permute-start.23) | collective-permute-done | bytes 32800 | tf_op jit(solution)/shard_map/ppermute | solution.py:455
  78.9 0.6 copy-done.26
  79.5 2.4 %shard_map.130 = f32[64,8,128]{2,1,0:T(8,128)} custom-call(s32[1]{0:T(128)} %bitcast.rank_ref, f32[64,8,128]{2,1,0:T(8,128)} %get-tuple-element.115.y_ref, f32[64,8,128]{2,1,0:T(8,128)} %get-tuple-element.116.a_ref, f32[64,8,128]{2,1,0:T(8,128)} %get-tuple-element.117.b_ref, f32[8,8,128]{2,1,0:T(8,128)} %get-tuple-element.118.rest_0_, ...), custom_call_target="tpu_custom_call" | custom-call | tf_op jit(solution)/shard_map/pallas_call | solution.py:457
  (88 shorter events, 1.4 us)
Async XLA Ops:
  0.6 1.5 %copy-start.3 = (f32[64,8,128]{2,1,0:T(8,128)S(1)}, f32[64,8,128]{2,1,0:T(8,128)}, u32[]{:S(2)}) copy-start(f32[64,8,128]{2,1,0:T(8,128)} %h_ref.1) | copy-start | bytes 786436
  0.6 1.6 %copy-start.4 = (f32[64,8,128]{2,1,0:T(8,128)S(1)}, f32[64,8,128]{2,1,0:T(8,128)}, u32[]{:S(2)}) copy-start(f32[64,8,128]{2,1,0:T(8,128)} %w_ref.1) | copy-start | bytes 786436
  0.7 1.6 %copy-start.5 = (f32[64,8,128]{2,1,0:T(8,128)S(1)}, f32[64,8,128]{2,1,0:T(8,128)}, u32[]{:S(2)}) copy-start(f32[64,8,128]{2,1,0:T(8,128)} %c_ref.1) | copy-start | bytes 786436
  2.3 10.6 %collective-permute-start = (f32[4,8,8,128]{3,2,1,0:T(8,128)S(1)}, f32[4,8,8,128]{3,2,1,0:T(8,128)S(1)}, u32[]{:S(2)}, u32[]{:S(2)}) collective-permute-start(f32[4,8,8,128]{3,2,1,0:T(8,128)S(1)} %pad_maximum_fusion), channel_id=1, source_target_pairs={{0,8},{8,16},{16,24},{24,0},{1,9},{9,17},{17,25},{25,1},{2,10},{10... | collective-permute-start | bytes 393224 | tf_op jit(solution)/shard_map/ppermute | solution.py:357
  2.9 10.1 %collective-permute-start.1 = (f32[4,8,8,128]{3,2,1,0:T(8,128)S(1)}, f32[4,8,8,128]{3,2,1,0:T(8,128)S(1)}, u32[]{:S(2)}, u32[]{:S(2)}) collective-permute-start(f32[4,8,8,128]{3,2,1,0:T(8,128)S(1)} %pad_maximum_fusion.1), channel_id=1, source_target_pairs={{8,0},{16,8},{24,16},{0,24},{9,1},{17,9},{25,17},{1,25},{10,2},{18... | collective-permute-start | bytes 393224 | tf_op jit(solution)/shard_map/ppermute | solution.py:358
  6.3 6.6 %collective-permute-start.2 = (f32[2,4,8,128]{3,2,1,0:T(8,128)S(1)}, f32[2,4,8,128]{3,2,1,0:T(8,128)S(1)}, u32[]{:S(2)}, u32[]{:S(2)}) collective-permute-start(f32[2,4,8,128]{3,2,1,0:T(8,128)S(1)} %pad.4), channel_id=1, source_target_pairs={{0,4},{4,0},{1,5},{5,1},{2,6},{6,2},{3,7},{7,3},{8,12},{12,8},{9,1... | collective-permute-start | bytes 98312 | tf_op jit(solution)/shard_map/ppermute | solution.py:359
  13.0 0.6 copy-start.1
  13.0 0.7 copy-start.2
  17.9 9.8 %collective-permute-start.3 = (f32[3,4,8,128]{3,2,1,0:T(8,128)}, f32[3,4,8,128]{3,2,1,0:T(8,128)S(1)}, u32[]{:S(2)}, u32[]{:S(2)}) collective-permute-start(f32[3,4,8,128]{3,2,1,0:T(8,128)} %get-tuple-element.76), channel_id=1, source_target_pairs={{0,8},{8,16},{16,24},{24,0},{1,9},{9,17},{17,25},{25,1},{2,10},{10... | collective-permute-start | bytes 147464 | tf_op jit(solution)/shard_map/ppermute | solution.py:357
  17.9 9.8 %collective-permute-start.4 = (f32[3,4,8,128]{3,2,1,0:T(8,128)}, f32[3,4,8,128]{3,2,1,0:T(8,128)S(1)}, u32[]{:S(2)}, u32[]{:S(2)}) collective-permute-start(f32[3,4,8,128]{3,2,1,0:T(8,128)} %get-tuple-element.77), channel_id=1, source_target_pairs={{8,0},{16,8},{24,16},{0,24},{9,1},{17,9},{25,17},{1,25},{10,2},{18... | collective-permute-start | bytes 147464 | tf_op jit(solution)/shard_map/ppermute | solution.py:358
  19.6 6.0 %collective-permute-start.5 = (f32[2,3,8,128]{3,2,1,0:T(8,128)}, f32[2,3,8,128]{3,2,1,0:T(8,128)S(1)}, u32[]{:S(2)}, u32[]{:S(2)}) collective-permute-start(f32[2,3,8,128]{3,2,1,0:T(8,128)} %get-tuple-element.78), channel_id=1, source_target_pairs={{0,4},{4,0},{1,5},{5,1},{2,6},{6,2},{3,7},{7,3},{8,12},{12,8},{9,1... | collective-permute-start | bytes 73736 | tf_op jit(solution)/shard_map/ppermute | solution.py:359
  23.9 9.2 %collective-permute-start.6 = (f32[3,4,8,128]{3,2,1,0:T(8,128)}, f32[3,4,8,128]{3,2,1,0:T(8,128)S(1)}, u32[]{:S(2)}, u32[]{:S(2)}) collective-permute-start(f32[3,4,8,128]{3,2,1,0:T(8,128)} %get-tuple-element.83), channel_id=1, source_target_pairs={{0,8},{8,16},{16,24},{24,0},{1,9},{9,17},{17,25},{25,1},{2,10},{10... | collective-permute-start | bytes 147464 | tf_op jit(solution)/shard_map/ppermute | solution.py:357
  24.0 9.1 %collective-permute-start.7 = (f32[3,4,8,128]{3,2,1,0:T(8,128)}, f32[3,4,8,128]{3,2,1,0:T(8,128)S(1)}, u32[]{:S(2)}, u32[]{:S(2)}) collective-permute-start(f32[3,4,8,128]{3,2,1,0:T(8,128)} %get-tuple-element.84), channel_id=1, source_target_pairs={{8,0},{16,8},{24,16},{0,24},{9,1},{17,9},{25,17},{1,25},{10,2},{18... | collective-permute-start | bytes 147464 | tf_op jit(solution)/shard_map/ppermute | solution.py:358
  25.7 2.0 %copy-start.11 = (f32[2,3,8,128]{3,2,1,0:T(8,128)}, f32[2,3,8,128]{3,2,1,0:T(8,128)S(1)}, u32[]{:S(2)}) copy-start(f32[2,3,8,128]{3,2,1,0:T(8,128)S(1)} %collective-permute-done.5.rest_2_.rest_3_) | copy-start | bytes 73732
  25.7 7.4 %collective-permute-start.8 = (f32[2,3,8,128]{3,2,1,0:T(8,128)}, f32[2,3,8,128]{3,2,1,0:T(8,128)S(1)}, u32[]{:S(2)}, u32[]{:S(2)}) collective-permute-start(f32[2,3,8,128]{3,2,1,0:T(8,128)} %get-tuple-element.85), channel_id=1, source_target_pairs={{0,4},{4,0},{1,5},{5,1},{2,6},{6,2},{3,7},{7,3},{8,12},{12,8},{9,1... | collective-permute-start | bytes 73736 | tf_op jit(solution)/shard_map/ppermute | solution.py:359
  27.7 0.6 copy-start.22
  27.7 0.6 copy-start.23
  32.5 9.2 %collective-permute-start.10 = (f32[3,4,8,128]{3,2,1,0:T(8,128)}, f32[3,4,8,128]{3,2,1,0:T(8,128)S(1)}, u32[]{:S(2)}, u32[]{:S(2)}) collective-permute-start(f32[3,4,8,128]{3,2,1,0:T(8,128)} %get-tuple-element.91), channel_id=1, source_target_pairs={{8,0},{16,8},{24,16},{0,24},{9,1},{17,9},{25,17},{1,25},{10,2},{18... | collective-permute-start | bytes 147464 | tf_op jit(solution)/shard_map/ppermute | solution.py:358
  32.6 9.2 %collective-permute-start.9 = (f32[3,4,8,128]{3,2,1,0:T(8,128)}, f32[3,4,8,128]{3,2,1,0:T(8,128)S(1)}, u32[]{:S(2)}, u32[]{:S(2)}) collective-permute-start(f32[3,4,8,128]{3,2,1,0:T(8,128)} %get-tuple-element.90), channel_id=1, source_target_pairs={{0,8},{8,16},{16,24},{24,0},{1,9},{9,17},{17,25},{25,1},{2,10},{10... | collective-permute-start | bytes 147464 | tf_op jit(solution)/shard_map/ppermute | solution.py:357
  33.1 6.7 %collective-permute-start.11 = (f32[2,3,8,128]{3,2,1,0:T(8,128)}, f32[2,3,8,128]{3,2,1,0:T(8,128)S(1)}, u32[]{:S(2)}, u32[]{:S(2)}) collective-permute-start(f32[2,3,8,128]{3,2,1,0:T(8,128)} %get-tuple-element.92), channel_id=1, source_target_pairs={{0,4},{4,0},{1,5},{5,1},{2,6},{6,2},{3,7},{7,3},{8,12},{12,8},{9,1... | collective-permute-start | bytes 73736 | tf_op jit(solution)/shard_map/ppermute | solution.py:359
  33.1 0.6 copy-start.12
  33.1 0.6 copy-start.16
  37.9 10.5 %collective-permute-start.12 = (f32[3,4,8,128]{3,2,1,0:T(8,128)}, f32[3,4,8,128]{3,2,1,0:T(8,128)S(1)}, u32[]{:S(2)}, u32[]{:S(2)}) collective-permute-start(f32[3,4,8,128]{3,2,1,0:T(8,128)} %get-tuple-element.97), channel_id=1, source_target_pairs={{0,8},{8,16},{16,24},{24,0},{1,9},{9,17},{17,25},{25,1},{2,10},{10... | collective-permute-start | bytes 147464 | tf_op jit(solution)/shard_map/ppermute | solution.py:357
  39.3 9.1 %collective-permute-start.13 = (f32[3,4,8,128]{3,2,1,0:T(8,128)}, f32[3,4,8,128]{3,2,1,0:T(8,128)S(1)}, u32[]{:S(2)}, u32[]{:S(2)}) collective-permute-start(f32[3,4,8,128]{3,2,1,0:T(8,128)} %get-tuple-element.98), channel_id=1, source_target_pairs={{8,0},{16,8},{24,16},{0,24},{9,1},{17,9},{25,17},{1,25},{10,2},{18... | collective-permute-start | bytes 147464 | tf_op jit(solution)/shard_map/ppermute | solution.py:358
  39.7 2.0 %copy-start.7 = (f32[2,3,8,128]{3,2,1,0:T(8,128)}, f32[2,3,8,128]{3,2,1,0:T(8,128)S(1)}, u32[]{:S(2)}) copy-start(f32[2,3,8,128]{3,2,1,0:T(8,128)S(1)} %collective-permute-done.11.rest_2_.rest_3_) | copy-start | bytes 73732
  39.7 8.6 %collective-permute-start.14 = (f32[2,3,8,128]{3,2,1,0:T(8,128)}, f32[2,3,8,128]{3,2,1,0:T(8,128)S(1)}, u32[]{:S(2)}, u32[]{:S(2)}) collective-permute-start(f32[2,3,8,128]{3,2,1,0:T(8,128)} %get-tuple-element.99), channel_id=1, source_target_pairs={{0,4},{4,0},{1,5},{5,1},{2,6},{6,2},{3,7},{7,3},{8,12},{12,8},{9,1... | collective-permute-start | bytes 73736 | tf_op jit(solution)/shard_map/ppermute | solution.py:359
  41.7 0.6 copy-start.13
  41.7 0.6 copy-start.17
  46.5 10.5 %collective-permute-start.15 = (f32[3,4,8,128]{3,2,1,0:T(8,128)}, f32[3,4,8,128]{3,2,1,0:T(8,128)S(1)}, u32[]{:S(2)}, u32[]{:S(2)}) collective-permute-start(f32[3,4,8,128]{3,2,1,0:T(8,128)} %get-tuple-element.104), channel_id=1, source_target_pairs={{0,8},{8,16},{16,24},{24,0},{1,9},{9,17},{17,25},{25,1},{2,10},{10... | collective-permute-start | bytes 147464 | tf_op jit(solution)/shard_map/ppermute | solution.py:357
  46.6 10.4 %collective-permute-start.16 = (f32[3,4,8,128]{3,2,1,0:T(8,128)}, f32[3,4,8,128]{3,2,1,0:T(8,128)S(1)}, u32[]{:S(2)}, u32[]{:S(2)}) collective-permute-start(f32[3,4,8,128]{3,2,1,0:T(8,128)} %get-tuple-element.105), channel_id=1, source_target_pairs={{8,0},{16,8},{24,16},{0,24},{9,1},{17,9},{25,17},{1,25},{10,2},{18... | collective-permute-start | bytes 147464 | tf_op jit(solution)/shard_map/ppermute | solution.py:358
  48.3 6.6 %collective-permute-start.17 = (f32[2,3,8,128]{3,2,1,0:T(8,128)}, f32[2,3,8,128]{3,2,1,0:T(8,128)S(1)}, u32[]{:S(2)}, u32[]{:S(2)}) collective-permute-start(f32[2,3,8,128]{3,2,1,0:T(8,128)} %get-tuple-element.106), channel_id=1, source_target_pairs={{0,4},{4,0},{1,5},{5,1},{2,6},{6,2},{3,7},{7,3},{8,12},{12,8},{9,1... | collective-permute-start | bytes 73736 | tf_op jit(solution)/shard_map/ppermute | solution.py:359
  48.4 0.6 copy-start.14
  48.4 0.6 copy-start.18
  53.2 8.7 %collective-permute-start.18 = (f32[3,4,8,128]{3,2,1,0:T(8,128)}, f32[3,4,8,128]{3,2,1,0:T(8,128)S(1)}, u32[]{:S(2)}, u32[]{:S(2)}) collective-permute-start(f32[3,4,8,128]{3,2,1,0:T(8,128)} %get-tuple-element.111), channel_id=1, source_target_pairs={{0,8},{8,16},{16,24},{24,0},{1,9},{9,17},{17,25},{25,1},{2,10},{10... | collective-permute-start | bytes 147464 | tf_op jit(solution)/shard_map/ppermute | solution.py:357
  53.4 8.5 %collective-permute-start.19 = (f32[3,4,8,128]{3,2,1,0:T(8,128)}, f32[3,4,8,128]{3,2,1,0:T(8,128)S(1)}, u32[]{:S(2)}, u32[]{:S(2)}) collective-permute-start(f32[3,4,8,128]{3,2,1,0:T(8,128)} %get-tuple-element.112), channel_id=1, source_target_pairs={{8,0},{16,8},{24,16},{0,24},{9,1},{17,9},{25,17},{1,25},{10,2},{18... | collective-permute-start | bytes 147464 | tf_op jit(solution)/shard_map/ppermute | solution.py:358
  55.0 2.0 %copy-start.9 = (f32[2,3,8,128]{3,2,1,0:T(8,128)}, f32[2,3,8,128]{3,2,1,0:T(8,128)S(1)}, u32[]{:S(2)}) copy-start(f32[2,3,8,128]{3,2,1,0:T(8,128)S(1)} %collective-permute-done.17.rest_2_.rest_3_) | copy-start | bytes 73732
  55.0 6.8 %collective-permute-start.20 = (f32[2,3,8,128]{3,2,1,0:T(8,128)}, f32[2,3,8,128]{3,2,1,0:T(8,128)S(1)}, u32[]{:S(2)}, u32[]{:S(2)}) collective-permute-start(f32[2,3,8,128]{3,2,1,0:T(8,128)} %get-tuple-element.113), channel_id=1, source_target_pairs={{0,4},{4,0},{1,5},{5,1},{2,6},{6,2},{3,7},{7,3},{8,12},{12,8},{9,1... | collective-permute-start | bytes 73736 | tf_op jit(solution)/shard_map/ppermute | solution.py:359
  57.0 0.6 copy-start.15
  57.0 0.7 copy-start.19
  61.9 0.6 copy-start.10
  61.9 0.6 copy-start.20
  61.9 0.6 copy-start.21
  70.6 6.2 %collective-permute-start.21 = (f32[8,8,128]{2,1,0:T(8,128)}, f32[8,8,128]{2,1,0:T(8,128)S(1)}, u32[]{:S(2)}, u32[]{:S(2)}) collective-permute-start(f32[8,8,128]{2,1,0:T(8,128)} %get-tuple-element.118.rest_0_), channel_id=1, source_target_pairs={{0,1},{1,2},{2,3},{3,0},{4,5},{5,6},{6,7},{7,4},{8,9},{9,10},{10,1... | collective-permute-start | bytes 98312 | tf_op jit(solution)/shard_map/ppermute | solution.py:455
  72.2 5.4 %collective-permute-start.22 = (f32[8,8,128]{2,1,0:T(8,128)}, f32[8,8,128]{2,1,0:T(8,128)S(1)}, u32[]{:S(2)}, u32[]{:S(2)}) collective-permute-start(f32[8,8,128]{2,1,0:T(8,128)} %get-tuple-element.118.rest_0_), channel_id=1, source_target_pairs={{0,2},{1,3},{2,0},{3,1},{4,6},{5,7},{6,4},{7,5},{8,10},{9,11},{10,... | collective-permute-start | bytes 98312 | tf_op jit(solution)/shard_map/ppermute | solution.py:455
  74.8 4.1 %collective-permute-start.23 = (f32[8,8,128]{2,1,0:T(8,128)}, f32[8,8,128]{2,1,0:T(8,128)S(1)}, u32[]{:S(2)}, u32[]{:S(2)}) collective-permute-start(f32[8,8,128]{2,1,0:T(8,128)} %get-tuple-element.118.rest_0_), channel_id=1, source_target_pairs={{0,3},{1,0},{2,1},{3,2},{4,7},{5,4},{6,5},{7,6},{8,11},{9,8},{10,9... | collective-permute-start | bytes 98312 | tf_op jit(solution)/shard_map/ppermute | solution.py:455
  76.8 2.1 %copy-start.24 = (f32[8,8,128]{2,1,0:T(8,128)}, f32[8,8,128]{2,1,0:T(8,128)S(1)}, u32[]{:S(2)}) copy-start(f32[8,8,128]{2,1,0:T(8,128)S(1)} %collective-permute-done.21.rest_1_) | copy-start | bytes 98308
  77.6 1.3 %copy-start.25 = (f32[8,8,128]{2,1,0:T(8,128)}, f32[8,8,128]{2,1,0:T(8,128)S(1)}, u32[]{:S(2)}) copy-start(f32[8,8,128]{2,1,0:T(8,128)S(1)} %collective-permute-done.22.rest_2_) | copy-start | bytes 98308
  78.9 0.6 copy-start.26
  (3 other events, 1.8 us)

commit v8 on v6

--- a/solution.py
+++ b/solution.py
@@ -124,22 +124,22 @@
 
 
 def make_section_kernel(chunk, first):
-    def kernel(h_ref, w_ref, c_ref, m_ref, sill_ref, co_ref, xflo_ref, xfhi_ref, yflo_ref, yfhi_ref,
-               *rest):
+    def kernel(h_ref, w_ref, c_ref, m_ref, sill_ref, co_ref, *rest):
         if first:
-            ho_ref, wo_ref, cbo_ref, mo_ref, xf_ref, xl_ref, y_ref = rest
+            xflo_ref, xfhi_ref, yflo_ref, yfhi_ref = rest[:4]
+            ho_ref, wo_ref, cbo_ref, mo_ref, xf_ref, xl_ref, y_ref, nb_ref = rest[4:]
             xslo_ref, xshi_ref, yslo_ref, yshi_ref = xflo_ref, xfhi_ref, yflo_ref, yfhi_ref
+            cylo = [yflo_ref[1, f] for f in (3, 4)]
+            cyhi = [yfhi_ref[0, f] for f in (3, 4)]
         else:
-            xslo_ref, xshi_ref, yslo_ref, yshi_ref = rest[:4]
-            ho_ref, wo_ref, cbo_ref, mo_ref, xf_ref, xl_ref, y_ref = rest[4:]
+            nb_ref, xslo_ref, xshi_ref, yslo_ref, yshi_ref = rest[:5]
+            ho_ref, wo_ref, cbo_ref, mo_ref, xf_ref, xl_ref, y_ref = rest[5:]
         depth = h_ref.shape[0]
         groups = depth // ROWS
         sub, lane = iotas()
         zero = jnp.zeros((ROWS, LANES), f32)
         sylo = [yslo_ref[1, f] for f in range(3)]
         syhi = [yshi_ref[0, f] for f in range(3)]
-        cylo = [yflo_ref[1, f] for f in (3, 4)]
-        cyhi = [yfhi_ref[0, f] for f in (3, 4)]
 
         def group(a, carry):
             y_f, y_l = carry
@@ -149,8 +149,6 @@
                 row = pl.ds(b, ROWS, stride=0)
                 sxlo = [xslo_ref[f, a, row, :] for f in range(3)]
                 sxhi = [xshi_ref[f, a, row, :] for f in range(3)]
-                cxlo = [xflo_ref[f, a, row, :] for f in (3, 4)]
-                cxhi = [xfhi_ref[f, a, row, :] for f in (3, 4)]
                 d = chunk * depth + i
                 heat = h_ref[i]
                 water = w_ref[i]
@@ -159,21 +157,35 @@
                 sill = sill_ref[i].astype(f32)
                 cx = co_ref[0, i]
                 cy = co_ref[1, i]
-                vx = co_ref[2, i]
-                vy = co_ref[3, i]
                 mobile = [heat, water, carbon]
                 q_xm = [x_minus(mobile[f], sxlo[f], b, sub) for f in range(3)]
                 q_xp = [x_plus(mobile[f], sxhi[f], b, sub) for f in range(3)]
                 q_ym = [y_minus(mobile[f], sylo[f], d, lane) for f in range(3)]
                 q_yp = [y_plus(mobile[f], syhi[f], d, lane) for f in range(3)]
-                cx_m = x_minus(cx, cxlo[0], b, sub)
-                cx_p = x_plus(cx, cxhi[0], b, sub)
-                vx_m = x_minus(vx, cxlo[1], b, sub)
-                vx_p = x_plus(vx, cxhi[1], b, sub)
-                cy_m = y_minus(cy, cylo[0], d, lane)
-                cy_p = y_plus(cy, cyhi[0], d, lane)
-                vy_m = y_minus(vy, cylo[1], d, lane)
-                vy_p = y_plus(vy, cyhi[1], d, lane)
+                if first:
+                    cxlo = [xflo_ref[f, a, row, :] for f in (3, 4)]
+                    cxhi = [xfhi_ref[f, a, row, :] for f in (3, 4)]
+                    vx = co_ref[2, i]
+                    vy = co_ref[3, i]
+                    cx_m = x_minus(cx, cxlo[0], b, sub)
+                    cx_p = x_plus(cx, cxhi[0], b, sub)
+                    vx_m = x_minus(vx, cxlo[1], b, sub)
+                    vx_p = x_plus(vx, cxhi[1], b, sub)
+                    cy_m = y_minus(cy, cylo[0], d, lane)
+                    cy_p = y_plus(cy, cyhi[0], d, lane)
+                    vy_m = y_minus(vy, cylo[1], d, lane)
+                    vy_p = y_plus(vy, cyhi[1], d, lane)
+                    fvx_m = 0.5 * (vx_m + vx)
+                    fvx_p = 0.5 * (vx + vx_p)
+                    fvy_m = 0.5 * (vy_m + vy)
+                    fvy_p = 0.5 * (vy + vy_p)
+                    near = (cx_m, cx_p, cy_m, cy_p, fvx_m, fvx_p, fvy_m, fvy_p)
+                    for f, v in enumerate(near):
+                        nb_ref[f, i] = v
+                else:
+                    cx_m, cx_p, cy_m, cy_p, fvx_m, fvx_p, fvy_m, fvy_p = [
+                        nb_ref[f, i] for f in range(8)
+                    ]
                 soft = jnp.exp(-SOFTEN * heat)
                 kx = cx * soft
                 ky = cy * soft
@@ -186,10 +198,6 @@
                 flux_y_lo = 0.5 * (ky_m + ky) * (heat - q_ym[0])
                 flux_y_hi = 0.5 * (ky + ky_p) * (q_yp[0] - heat)
                 diffused = flux_x_hi - flux_x_lo + flux_y_hi - flux_y_lo
-                fvx_m = 0.5 * (vx_m + vx)
-                fvx_p = 0.5 * (vx + vx_p)
-                fvy_m = 0.5 * (vy_m + vy)
-                fvy_p = 0.5 * (vy + vy_p)
                 inflow = []
                 for f in range(3):
                     lo_x = jnp.maximum(fvx_m, 0.0) * q_xm[f] + jnp.minimum(fvx_m, 0.0) * mobile[f]
@@ -406,33 +414,41 @@
         return pl.BlockSpec((depth, ROWS, LANES), lambda i: (k, 0, 0))
 
     halos = [None] * chunks
+    nears = [None] * chunks
+    x3 = full_spec((3, cgroups, ROWS, LANES))
+    y3 = full_spec((2, 3, ROWS, LANES))
+    near_spec = full_spec((8, depth, ROWS, LANES))
     for section_no in range(SECTIONS):
         first = section_no == 0
         for k in range(chunks):
-            x5 = pl.BlockSpec((5, cgroups, ROWS, LANES), lambda i, k=k: (0, k, 0, 0))
-            y5 = full_spec((2, 5, ROWS, LANES))
-            in_specs = [block_spec(k)] * 5 + [
-                pl.BlockSpec((4, depth, ROWS, LANES), lambda i, k=k: (0, k, 0, 0)),
-                x5, x5, y5, y5,
-            ]
-            args = [heat, water, carbon, melt, injection_flags, co, xflo, xfhi, yflo, yfhi]
-            if not first:
-                in_specs += [full_spec((3, cgroups, ROWS, LANES))] * 2
-                in_specs += [full_spec((2, 3, ROWS, LANES))] * 2
-                args += list(halos[k])
-            heat, water, carbon, melt, xf, xl, ys = pl.pallas_call(
+            args = [heat, water, carbon, melt, injection_flags, co]
+            in_specs = [block_spec(k)] * 5
+            out_shape = [sds(shape)] * 4 + [sds((3, cgroups, ROWS, LANES))] * 2
+            out_shape += [sds((2, 3, ROWS, LANES))]
+            out_specs = [block_spec(k)] * 4 + [x3, x3, y3]
+            if first:
+                x5 = pl.BlockSpec((5, cgroups, ROWS, LANES), lambda i, k=k: (0, k, 0, 0))
+                y5 = full_spec((2, 5, ROWS, LANES))
+                in_specs += [pl.BlockSpec((4, depth, ROWS, LANES), lambda i, k=k: (0, k, 0, 0)),
+                             x5, x5, y5, y5]
+                args += [xflo, xfhi, yflo, yfhi]
+                out_shape += [sds((8, depth, ROWS, LANES))]
+                out_specs += [near_spec]
+            else:
+                in_specs += [pl.BlockSpec((2, depth, ROWS, LANES), lambda i, k=k: (0, k, 0, 0)),
+                             near_spec, x3, x3, y3, y3]
+                args += [nears[k]] + list(halos[k])
+            outs = pl.pallas_call(
                 make_section_kernel(k, first),
                 grid=(1,),
-                out_shape=(sds(shape), sds(shape), sds(shape), sds(shape),
-                           sds((3, cgroups, ROWS, LANES)), sds((3, cgroups, ROWS, LANES)),
-                           sds((2, 3, ROWS, LANES))),
+                out_shape=tuple(out_shape),
                 in_specs=in_specs,
-                out_specs=[block_spec(k)] * 4 + [
-                    full_spec((3, cgroups, ROWS, LANES)), full_spec((3, cgroups, ROWS, LANES)),
-                    full_spec((2, 3, ROWS, LANES)),
-                ],
+                out_specs=out_specs,
                 input_output_aliases={0: 0, 1: 1, 2: 2, 3: 3},
             )(*args)
+            heat, water, carbon, melt, xf, xl, ys = outs[:7]
+            if first:
+                nears[k] = outs[7]
             if section_no + 1 < SECTIONS:
                 halos[k] = exchange(xf, xl, ys)
 

time: 81.5 us -> 78.9 us (0.968)
  Pallas kernels: 44 us -> 41.4 us
    pallas_call x8, Pallas kernels: 33.1 us -> 30.6 us  [local(): pl.pallas_call(make_section_kernel(k, first), grid=(1,), out_shape=tuple(...]
  transfers between devices with their start and end apart: 24 -> 24, of which waited for: 5 -> 5; matrix products, arithmetic and copies ran while one was open for 0% -> 0% of each run, Pallas kernels for 31% -> 29%
where the time goes in v8:
time: 78.9 us; the launch traced here: 78.5 us
  Pallas kernels  41.4 us (52%)
  starting transfers between devices  25.9 us (33%)
  waiting for transfers between devices  5.37 us (7%)
  local copies, waits for them, and re-layouts  4.94 us (6%)
  between operations  0.83 us (1%)
    pallas_call x8, Pallas kernels, local(): pl.pallas_call(make_section_kernel(k, first), grid=(1,), out_shape=tuple(...  30.6 us
    ppermute x7, starting transfers between devices, exchange(): xhi = lax.ppermute(xf, 'east', east_bwd)  9.42 us
    ppermute x7, starting transfers between devices, exchange(): ylo = lax.ppermute(ys, 'north', north_fwd)  8.35 us
    ppermute x3, starting transfers between devices, local(): lax.ppermute(red, 'depth', [(i, (i + k) % count) for i in range(count)])  5.4 us
    unnamed x48, local copies, waits for them, and re-layouts  4.94 us
    pallas_call x1, Pallas kernels, local(): pl.pallas_call(prep_kernel, out_shape=(sds(shape), sds(shape), sds(shape)...  4.57 us
    pallas_call x1, Pallas kernels, local(): pl.pallas_call(sweep_kernel, grid=(1,), out_shape=(sds(shape), sds(shape)...  3.87 us
    ppermute x3, waiting for transfers between devices, local(): lax.ppermute(red, 'depth', [(i, (i + k) % count) for i in range(count)])  2.77 us
  transfers between devices with their start and end apart: 24, of which 5 were waited for; matrix products, arithmetic and copies ran while one was open for 0% of the time, Pallas kernels for 29%

profile of v8, /device:TPU:0, one launch (start us, length us, event | category | flops | bytes accessed | tf_op | source)
XLA Modules:
  0.0 78.5 jit_solution(11432280301208476302)
XLA Ops:
  0.6 4.6 %shard_map.120 = (f32[64,8,128]{2,1,0:T(8,128)}, f32[64,8,128]{2,1,0:T(8,128)}, f32[64,8,128]{2,1,0:T(8,128)}, f32[64,8,128]{2,1,0:T(8,128)}, f32[5,64,8,128]{3,...) custom-call(f32[2,12]{1,0:T(2,128)} %lat_ref.1, f32[12]{0:T(128)} %vert_ref.1, ...), custom_call_target="tpu_custom_call" | custom-call | tf_op jit(solution)/shard_map/pallas_call | solution.py:403
  5.2 0.5 collective-permute-start
  5.7 2.0 %collective-permute-start.1 = (f32[5,8,8,128]{3,2,1,0:T(8,128)}, f32[5,8,8,128]{3,2,1,0:T(8,128)S(1)}, u32[]{:S(2)}, u32[]{:S(2)}) collective-permute-start(f32[5,8,8,128]{3,2,1,0:T(8,128)} %get-tuple-element.74), channel_id=1, source_target_pairs={{8,0},{16,8},{24,16},{0,24},{9,1},{17,9},{25,17},{1,25},{10,2},{18... | collective-permute-start | bytes 491528 | tf_op jit(solution)/shard_map/ppermute | solution.py:369
  7.7 2.3 %collective-permute-start.2 = (f32[2,5,8,128]{3,2,1,0:T(8,128)}, f32[2,5,8,128]{3,2,1,0:T(8,128)S(1)}, u32[]{:S(2)}, u32[]{:S(2)}) collective-permute-start(f32[2,5,8,128]{3,2,1,0:T(8,128)} %get-tuple-element.75), channel_id=1, source_target_pairs={{0,4},{4,0},{1,5},{5,1},{2,6},{6,2},{3,7},{7,3},{8,12},{12,8},{9,1... | collective-permute-start | bytes 122888 | tf_op jit(solution)/shard_map/ppermute | solution.py:370
  10.0 2.2 %collective-permute-done.2.rest_2_.rest_3_ = f32[2,5,8,128]{3,2,1,0:T(8,128)S(1)} collective-permute-done((f32[2,5,8,128]{3,2,1,0:T(8,128)}, f32[2,5,8,128]{3,2,1,0:T(8,128)S(1)}, u32[]{:S(2)}, u32[]{:S(2)}) %collective-permute-start.2) | collective-permute-done | bytes 40992 | tf_op jit(solution)/shard_map/ppermute | solution.py:370
  12.2 0.4 collective-permute-done.1.rest_1_
  12.5 0.2 copy-done.2
  12.8 0.1 copy-done
  12.8 0.4 copy-done.1
  13.2 4.5 %shard_map.121 = (f32[64,8,128]{2,1,0:T(8,128)}, f32[64,8,128]{2,1,0:T(8,128)}, f32[64,8,128]{2,1,0:T(8,128)}, f32[64,8,128]{2,1,0:T(8,128)}, f32[3,4,8,128]{3,2...) custom-call(f32[64,8,128]{2,1,0:T(8,128)} %get-tuple-element.68.h_re, ...), custom_call_target="tpu_custom_call", output_to_operand_aliasing={{0}: (0, {}), {1}: (1, {}), {2}: (2, {}), {3}: (3, {})} | custom-call | tf_op jit(solution)/shard_map/pallas_call | solution.py:441
  17.7 0.7 collective-permute-start.3
  18.4 1.3 %collective-permute-start.4 = (f32[3,4,8,128]{3,2,1,0:T(8,128)}, f32[3,4,8,128]{3,2,1,0:T(8,128)S(1)}, u32[]{:S(2)}, u32[]{:S(2)}) collective-permute-start(f32[3,4,8,128]{3,2,1,0:T(8,128)} %get-tuple-element.86), channel_id=1, source_target_pairs={{8,0},{16,8},{24,16},{0,24},{9,1},{17,9},{25,17},{1,25},{10,2},{18... | collective-permute-start | bytes 147464 | tf_op jit(solution)/shard_map/ppermute | solution.py:369
  19.8 1.4 %collective-permute-start.5 = (f32[2,3,8,128]{3,2,1,0:T(8,128)}, f32[2,3,8,128]{3,2,1,0:T(8,128)S(1)}, u32[]{:S(2)}, u32[]{:S(2)}) collective-permute-start(f32[2,3,8,128]{3,2,1,0:T(8,128)} %get-tuple-element.87), channel_id=1, source_target_pairs={{0,4},{4,0},{1,5},{5,1},{2,6},{6,2},{3,7},{7,3},{8,12},{12,8},{9,1... | collective-permute-start | bytes 73736 | tf_op jit(solution)/shard_map/ppermute | solution.py:370
  21.2 4.5 %shard_map.122 = (f32[64,8,128]{2,1,0:T(8,128)}, f32[64,8,128]{2,1,0:T(8,128)}, f32[64,8,128]{2,1,0:T(8,128)}, f32[64,8,128]{2,1,0:T(8,128)}, f32[3,4,8,128]{3,2...) custom-call(f32[64,8,128]{2,1,0:T(8,128)} %get-tuple-element.76.h_re, ...), custom_call_target="tpu_custom_call", output_to_operand_aliasing={{0}: (0, {}), {1}: (1, {}), {2}: (2, {}), {3}: (3, {})} | custom-call | tf_op jit(solution)/shard_map/pallas_call | solution.py:441
  25.7 1.7 %collective-permute-start.7 = (f32[3,4,8,128]{3,2,1,0:T(8,128)}, f32[3,4,8,128]{3,2,1,0:T(8,128)S(1)}, u32[]{:S(2)}, u32[]{:S(2)}) collective-permute-start(f32[3,4,8,128]{3,2,1,0:T(8,128)} %get-tuple-element.94), channel_id=1, source_target_pairs={{8,0},{16,8},{24,16},{0,24},{9,1},{17,9},{25,17},{1,25},{10,2},{18... | collective-permute-start | bytes 147464 | tf_op jit(solution)/shard_map/ppermute | solution.py:369
  27.5 0.6 collective-permute-start.8
  28.1 0.6 copy-done.19
  28.8 3.6 %shard_map.123 = (f32[64,8,128]{2,1,0:T(8,128)}, f32[64,8,128]{2,1,0:T(8,128)}, f32[64,8,128]{2,1,0:T(8,128)}, f32[64,8,128]{2,1,0:T(8,128)}, f32[3,4,8,128]{3,2...) custom-call(f32[64,8,128]{2,1,0:T(8,128)} %get-tuple-element.80.h_re, ...), custom_call_target="tpu_custom_call", output_to_operand_aliasing={{0}: (0, {}), {1}: (1, {}), {2}: (2, {}), {3}: (3, {})} | custom-call | tf_op jit(solution)/shard_map/pallas_call | solution.py:441
  32.3 0.2 collective-permute-start.10
  32.5 0.3 collective-permute-start.9
  32.9 1.4 %collective-permute-start.11 = (f32[2,3,8,128]{3,2,1,0:T(8,128)}, f32[2,3,8,128]{3,2,1,0:T(8,128)S(1)}, u32[]{:S(2)}, u32[]{:S(2)}) collective-permute-start(f32[2,3,8,128]{3,2,1,0:T(8,128)} %get-tuple-element.102), channel_id=1, source_target_pairs={{0,4},{4,0},{1,5},{5,1},{2,6},{6,2},{3,7},{7,3},{8,12},{12,8},{9,1... | collective-permute-start | bytes 73736 | tf_op jit(solution)/shard_map/ppermute | solution.py:370
  34.3 0.6 copy-done.9
  34.9 3.6 %shard_map.124 = (f32[64,8,128]{2,1,0:T(8,128)}, f32[64,8,128]{2,1,0:T(8,128)}, f32[64,8,128]{2,1,0:T(8,128)}, f32[64,8,128]{2,1,0:T(8,128)}, f32[3,4,8,128]{3,2...) custom-call(f32[64,8,128]{2,1,0:T(8,128)} %get-tuple-element.88.h_re, ...), custom_call_target="tpu_custom_call", output_to_operand_aliasing={{0}: (0, {}), {1}: (1, {}), {2}: (2, {}), {3}: (3, {})} | custom-call | tf_op jit(solution)/shard_map/pallas_call | solution.py:441
  38.5 0.9 %collective-permute-start.12 = (f32[3,4,8,128]{3,2,1,0:T(8,128)}, f32[3,4,8,128]{3,2,1,0:T(8,128)S(1)}, u32[]{:S(2)}, u32[]{:S(2)}) collective-permute-start(f32[3,4,8,128]{3,2,1,0:T(8,128)} %get-tuple-element.107), channel_id=1, source_target_pairs={{0,8},{8,16},{16,24},{24,0},{1,9},{9,17},{17,25},{25,1},{2,10},{10... | collective-permute-start | bytes 147464 | tf_op jit(solution)/shard_map/ppermute | solution.py:368
  39.4 0.9 %collective-permute-start.13 = (f32[3,4,8,128]{3,2,1,0:T(8,128)}, f32[3,4,8,128]{3,2,1,0:T(8,128)S(1)}, u32[]{:S(2)}, u32[]{:S(2)}) collective-permute-start(f32[3,4,8,128]{3,2,1,0:T(8,128)} %get-tuple-element.108), channel_id=1, source_target_pairs={{8,0},{16,8},{24,16},{0,24},{9,1},{17,9},{25,17},{1,25},{10,2},{18... | collective-permute-start | bytes 147464 | tf_op jit(solution)/shard_map/ppermute | solution.py:369
  40.3 0.6 collective-permute-start.14
  40.9 0.6 copy-done.10
  41.5 3.6 %shard_map.125 = (f32[64,8,128]{2,1,0:T(8,128)}, f32[64,8,128]{2,1,0:T(8,128)}, f32[64,8,128]{2,1,0:T(8,128)}, f32[64,8,128]{2,1,0:T(8,128)}, f32[3,4,8,128]{3,2...) custom-call(f32[64,8,128]{2,1,0:T(8,128)} %get-tuple-element.96.h_re, ...), custom_call_target="tpu_custom_call", output_to_operand_aliasing={{0}: (0, {}), {1}: (1, {}), {2}: (2, {}), {3}: (3, {})} | custom-call | tf_op jit(solution)/shard_map/pallas_call | solution.py:441
  45.1 0.2 collective-permute-start.15
  45.3 1.6 %collective-permute-start.16 = (f32[3,4,8,128]{3,2,1,0:T(8,128)}, f32[3,4,8,128]{3,2,1,0:T(8,128)S(1)}, u32[]{:S(2)}, u32[]{:S(2)}) collective-permute-start(f32[3,4,8,128]{3,2,1,0:T(8,128)} %get-tuple-element.115), channel_id=1, source_target_pairs={{8,0},{16,8},{24,16},{0,24},{9,1},{17,9},{25,17},{1,25},{10,2},{18... | collective-permute-start | bytes 147464 | tf_op jit(solution)/shard_map/ppermute | solution.py:369
  46.9 1.4 %collective-permute-start.17 = (f32[2,3,8,128]{3,2,1,0:T(8,128)}, f32[2,3,8,128]{3,2,1,0:T(8,128)S(1)}, u32[]{:S(2)}, u32[]{:S(2)}) collective-permute-start(f32[2,3,8,128]{3,2,1,0:T(8,128)} %get-tuple-element.116), channel_id=1, source_target_pairs={{0,4},{4,0},{1,5},{5,1},{2,6},{6,2},{3,7},{7,3},{8,12},{12,8},{9,1... | collective-permute-start | bytes 73736 | tf_op jit(solution)/shard_map/ppermute | solution.py:370
  48.3 0.6 copy-done.12
  48.9 3.6 %shard_map.126 = (f32[64,8,128]{2,1,0:T(8,128)}, f32[64,8,128]{2,1,0:T(8,128)}, f32[64,8,128]{2,1,0:T(8,128)}, f32[64,8,128]{2,1,0:T(8,128)}, f32[3,4,8,128]{3,2...) custom-call(f32[64,8,128]{2,1,0:T(8,128)} %get-tuple-element.103.h_r, ...), custom_call_target="tpu_custom_call", output_to_operand_aliasing={{0}: (0, {}), {1}: (1, {}), {2}: (2, {}), {3}: (3, {})} | custom-call | tf_op jit(solution)/shard_map/pallas_call | solution.py:441
  52.6 1.7 %collective-permute-start.19 = (f32[3,4,8,128]{3,2,1,0:T(8,128)}, f32[3,4,8,128]{3,2,1,0:T(8,128)S(1)}, u32[]{:S(2)}, u32[]{:S(2)}) collective-permute-start(f32[3,4,8,128]{3,2,1,0:T(8,128)} %get-tuple-element.122), channel_id=1, source_target_pairs={{8,0},{16,8},{24,16},{0,24},{9,1},{17,9},{25,17},{1,25},{10,2},{18... | collective-permute-start | bytes 147464 | tf_op jit(solution)/shard_map/ppermute | solution.py:369
  54.3 0.6 collective-permute-start.20
  55.0 0.6 copy-done.11
  55.6 3.6 %shard_map.127 = (f32[64,8,128]{2,1,0:T(8,128)}, f32[64,8,128]{2,1,0:T(8,128)}, f32[64,8,128]{2,1,0:T(8,128)}, f32[64,8,128]{2,1,0:T(8,128)}, f32[3,4,8,128]{3,2...) custom-call(f32[64,8,128]{2,1,0:T(8,128)} %get-tuple-element.110.h_r, ...), custom_call_target="tpu_custom_call", output_to_operand_aliasing={{0}: (0, {}), {1}: (1, {}), {2}: (2, {}), {3}: (3, {})} | custom-call | tf_op jit(solution)/shard_map/pallas_call | solution.py:441
  59.2 0.6 copy-done.7
  59.8 3.6 %shard_map.128 = (f32[64,8,128]{2,1,0:T(8,128)}, f32[64,8,128]{2,1,0:T(8,128)}, f32[64,8,128]{2,1,0:T(8,128)}, f32[64,8,128]{2,1,0:T(8,128)}, f32[3,4,8,128]{3,2...) custom-call(f32[64,8,128]{2,1,0:T(8,128)} %get-tuple-element.117.h_r, ...), custom_call_target="tpu_custom_call", output_to_operand_aliasing={{0}: (0, {}), {1}: (1, {}), {2}: (2, {}), {3}: (3, {})} | custom-call | tf_op jit(solution)/shard_map/pallas_call | solution.py:441
  63.4 3.9 %shard_map.129 = (f32[64,8,128]{2,1,0:T(8,128)}, f32[64,8,128]{2,1,0:T(8,128)}, f32[64,8,128]{2,1,0:T(8,128)}, f32[8,8,128]{2,1,0:T(8,128)}) custom-call(f32[64,8,128]{2,1,0:T(8,128)} %get-tuple-element.124.r_ref, f32[5,64,8,128]{3,2,1,0:T(8,128)} %get-tuple-element.72.co_ref.cz_ref), custom_call_target="tpu_custom_call" | custom-call | tf_op jit(solution)/shard_map/pallas_call | solution.py:455
  67.3 1.5 %collective-permute-start.21 = (f32[8,8,128]{2,1,0:T(8,128)}, f32[8,8,128]{2,1,0:T(8,128)S(1)}, u32[]{:S(2)}, u32[]{:S(2)}) collective-permute-start(f32[8,8,128]{2,1,0:T(8,128)} %get-tuple-element.128.rest_0_), channel_id=1, source_target_pairs={{0,1},{1,2},{2,3},{3,0},{4,5},{5,6},{6,7},{7,4},{8,9},{9,10},{10,1... | collective-permute-start | bytes 98312 | tf_op jit(solution)/shard_map/ppermute | solution.py:467
  68.8 2.6 %collective-permute-start.22 = (f32[8,8,128]{2,1,0:T(8,128)}, f32[8,8,128]{2,1,0:T(8,128)S(1)}, u32[]{:S(2)}, u32[]{:S(2)}) collective-permute-start(f32[8,8,128]{2,1,0:T(8,128)} %get-tuple-element.128.rest_0_), channel_id=1, source_target_pairs={{0,2},{1,3},{2,0},{3,1},{4,6},{5,7},{6,4},{7,5},{8,10},{9,11},{10,... | collective-permute-start | bytes 98312 | tf_op jit(solution)/shard_map/ppermute | solution.py:467
  71.3 1.3 %collective-permute-start.23 = (f32[8,8,128]{2,1,0:T(8,128)}, f32[8,8,128]{2,1,0:T(8,128)S(1)}, u32[]{:S(2)}, u32[]{:S(2)}) collective-permute-start(f32[8,8,128]{2,1,0:T(8,128)} %get-tuple-element.128.rest_0_), channel_id=1, source_target_pairs={{0,3},{1,0},{2,1},{3,2},{4,7},{5,4},{6,5},{7,6},{8,11},{9,8},{10,9... | collective-permute-start | bytes 98312 | tf_op jit(solution)/shard_map/ppermute | solution.py:467
  72.7 1.0 %collective-permute-done.21.rest_1_ = f32[8,8,128]{2,1,0:T(8,128)S(1)} collective-permute-done((f32[8,8,128]{2,1,0:T(8,128)}, f32[8,8,128]{2,1,0:T(8,128)S(1)}, u32[]{:S(2)}, u32[]{:S(2)}) %collective-permute-start.21) | collective-permute-done | bytes 32800 | tf_op jit(solution)/shard_map/ppermute | solution.py:467
  73.7 0.6 collective-permute-done.22.rest_2_
  74.2 1.2 %collective-permute-done.23.rest_3_ = f32[8,8,128]{2,1,0:T(8,128)S(1)} collective-permute-done((f32[8,8,128]{2,1,0:T(8,128)}, f32[8,8,128]{2,1,0:T(8,128)S(1)}, u32[]{:S(2)}, u32[]{:S(2)}) %collective-permute-start.23) | collective-permute-done | bytes 32800 | tf_op jit(solution)/shard_map/ppermute | solution.py:467
  75.5 0.6 copy-done.23
  76.1 2.4 %shard_map.130 = f32[64,8,128]{2,1,0:T(8,128)} custom-call(s32[1]{0:T(128)} %bitcast.rank_ref, f32[64,8,128]{2,1,0:T(8,128)} %get-tuple-element.125.y_ref, f32[64,8,128]{2,1,0:T(8,128)} %get-tuple-element.126.a_ref, f32[64,8,128]{2,1,0:T(8,128)} %get-tuple-element.127.b_ref, f32[8,8,128]{2,1,0:T(8,128)} %get-tuple-element.128.rest_0_, ...), custom_call_target="tpu_custom_call" | custom-call | tf_op jit(solution)/shard_map/pallas_call | solution.py:469
  (59 shorter events, 0.3 us)
Async XLA Ops:
  5.2 7.0 %collective-permute-start = (f32[5,8,8,128]{3,2,1,0:T(8,128)}, f32[5,8,8,128]{3,2,1,0:T(8,128)S(1)}, u32[]{:S(2)}, u32[]{:S(2)}) collective-permute-start(f32[5,8,8,128]{3,2,1,0:T(8,128)} %get-tuple-element.73), channel_id=1, source_target_pairs={{0,8},{8,16},{16,24},{24,0},{1,9},{9,17},{17,25},{25,1},{2,10},{10... | collective-permute-start | bytes 491528 | tf_op jit(solution)/shard_map/ppermute | solution.py:368
  5.7 6.8 %collective-permute-start.1 = (f32[5,8,8,128]{3,2,1,0:T(8,128)}, f32[5,8,8,128]{3,2,1,0:T(8,128)S(1)}, u32[]{:S(2)}, u32[]{:S(2)}) collective-permute-start(f32[5,8,8,128]{3,2,1,0:T(8,128)} %get-tuple-element.74), channel_id=1, source_target_pairs={{8,0},{16,8},{24,16},{0,24},{9,1},{17,9},{25,17},{1,25},{10,2},{18... | collective-permute-start | bytes 491528 | tf_op jit(solution)/shard_map/ppermute | solution.py:369
  7.7 4.5 %collective-permute-start.2 = (f32[2,5,8,128]{3,2,1,0:T(8,128)}, f32[2,5,8,128]{3,2,1,0:T(8,128)S(1)}, u32[]{:S(2)}, u32[]{:S(2)}) collective-permute-start(f32[2,5,8,128]{3,2,1,0:T(8,128)} %get-tuple-element.75), channel_id=1, source_target_pairs={{0,4},{4,0},{1,5},{5,1},{2,6},{6,2},{3,7},{7,3},{8,12},{12,8},{9,1... | collective-permute-start | bytes 122888 | tf_op jit(solution)/shard_map/ppermute | solution.py:370
  12.2 0.6 copy-start.2
  12.2 0.7 copy-start
  12.5 0.7 copy-start.1
  17.7 10.4 %collective-permute-start.3 = (f32[3,4,8,128]{3,2,1,0:T(8,128)}, f32[3,4,8,128]{3,2,1,0:T(8,128)S(1)}, u32[]{:S(2)}, u32[]{:S(2)}) collective-permute-start(f32[3,4,8,128]{3,2,1,0:T(8,128)} %get-tuple-element.85), channel_id=1, source_target_pairs={{0,8},{8,16},{16,24},{24,0},{1,9},{9,17},{17,25},{25,1},{2,10},{10... | collective-permute-start | bytes 147464 | tf_op jit(solution)/shard_map/ppermute | solution.py:368
  18.4 9.7 %collective-permute-start.4 = (f32[3,4,8,128]{3,2,1,0:T(8,128)}, f32[3,4,8,128]{3,2,1,0:T(8,128)S(1)}, u32[]{:S(2)}, u32[]{:S(2)}) collective-permute-start(f32[3,4,8,128]{3,2,1,0:T(8,128)} %get-tuple-element.86), channel_id=1, source_target_pairs={{8,0},{16,8},{24,16},{0,24},{9,1},{17,9},{25,17},{1,25},{10,2},{18... | collective-permute-start | bytes 147464 | tf_op jit(solution)/shard_map/ppermute | solution.py:369
  19.8 7.7 %collective-permute-start.5 = (f32[2,3,8,128]{3,2,1,0:T(8,128)}, f32[2,3,8,128]{3,2,1,0:T(8,128)S(1)}, u32[]{:S(2)}, u32[]{:S(2)}) collective-permute-start(f32[2,3,8,128]{3,2,1,0:T(8,128)} %get-tuple-element.87), channel_id=1, source_target_pairs={{0,4},{4,0},{1,5},{5,1},{2,6},{6,2},{3,7},{7,3},{8,12},{12,8},{9,1... | collective-permute-start | bytes 73736 | tf_op jit(solution)/shard_map/ppermute | solution.py:370
  25.7 8.6 %collective-permute-start.6 = (f32[3,4,8,128]{3,2,1,0:T(8,128)}, f32[3,4,8,128]{3,2,1,0:T(8,128)S(1)}, u32[]{:S(2)}, u32[]{:S(2)}) collective-permute-start(f32[3,4,8,128]{3,2,1,0:T(8,128)} %get-tuple-element.93), channel_id=1, source_target_pairs={{0,8},{8,16},{16,24},{24,0},{1,9},{9,17},{17,25},{25,1},{2,10},{10... | collective-permute-start | bytes 147464 | tf_op jit(solution)/shard_map/ppermute | solution.py:368
  25.7 8.6 %collective-permute-start.7 = (f32[3,4,8,128]{3,2,1,0:T(8,128)}, f32[3,4,8,128]{3,2,1,0:T(8,128)S(1)}, u32[]{:S(2)}, u32[]{:S(2)}) collective-permute-start(f32[3,4,8,128]{3,2,1,0:T(8,128)} %get-tuple-element.94), channel_id=1, source_target_pairs={{8,0},{16,8},{24,16},{0,24},{9,1},{17,9},{25,17},{1,25},{10,2},{18... | collective-permute-start | bytes 147464 | tf_op jit(solution)/shard_map/ppermute | solution.py:369
  27.5 0.7 copy-start.8
  27.5 5.4 %collective-permute-start.8 = (f32[2,3,8,128]{3,2,1,0:T(8,128)}, f32[2,3,8,128]{3,2,1,0:T(8,128)S(1)}, u32[]{:S(2)}, u32[]{:S(2)}) collective-permute-start(f32[2,3,8,128]{3,2,1,0:T(8,128)} %get-tuple-element.95), channel_id=1, source_target_pairs={{0,4},{4,0},{1,5},{5,1},{2,6},{6,2},{3,7},{7,3},{8,12},{12,8},{9,1... | collective-permute-start | bytes 73736 | tf_op jit(solution)/shard_map/ppermute | solution.py:370
  28.1 0.6 copy-start.19
  28.1 0.6 copy-start.20
  32.3 8.6 %collective-permute-start.10 = (f32[3,4,8,128]{3,2,1,0:T(8,128)}, f32[3,4,8,128]{3,2,1,0:T(8,128)S(1)}, u32[]{:S(2)}, u32[]{:S(2)}) collective-permute-start(f32[3,4,8,128]{3,2,1,0:T(8,128)} %get-tuple-element.101), channel_id=1, source_target_pairs={{8,0},{16,8},{24,16},{0,24},{9,1},{17,9},{25,17},{1,25},{10,2},{18... | collective-permute-start | bytes 147464 | tf_op jit(solution)/shard_map/ppermute | solution.py:369
  32.5 8.4 %collective-permute-start.9 = (f32[3,4,8,128]{3,2,1,0:T(8,128)}, f32[3,4,8,128]{3,2,1,0:T(8,128)S(1)}, u32[]{:S(2)}, u32[]{:S(2)}) collective-permute-start(f32[3,4,8,128]{3,2,1,0:T(8,128)} %get-tuple-element.100), channel_id=1, source_target_pairs={{0,8},{8,16},{16,24},{24,0},{1,9},{9,17},{17,25},{25,1},{2,10},{10... | collective-permute-start | bytes 147464 | tf_op jit(solution)/shard_map/ppermute | solution.py:368
  32.9 1.4 %copy-start.3 = (f32[2,3,8,128]{3,2,1,0:T(8,128)}, f32[2,3,8,128]{3,2,1,0:T(8,128)S(1)}, u32[]{:S(2)}) copy-start(f32[2,3,8,128]{3,2,1,0:T(8,128)S(1)} %collective-permute-done.8.rest_3_.rest_4_) | copy-start | bytes 73732
  32.9 7.4 %collective-permute-start.11 = (f32[2,3,8,128]{3,2,1,0:T(8,128)}, f32[2,3,8,128]{3,2,1,0:T(8,128)S(1)}, u32[]{:S(2)}, u32[]{:S(2)}) collective-permute-start(f32[2,3,8,128]{3,2,1,0:T(8,128)} %get-tuple-element.102), channel_id=1, source_target_pairs={{0,4},{4,0},{1,5},{5,1},{2,6},{6,2},{3,7},{7,3},{8,12},{12,8},{9,1... | collective-permute-start | bytes 73736 | tf_op jit(solution)/shard_map/ppermute | solution.py:370
  34.3 0.6 copy-start.9
  34.3 0.6 copy-start.13
  38.5 9.8 %collective-permute-start.12 = (f32[3,4,8,128]{3,2,1,0:T(8,128)}, f32[3,4,8,128]{3,2,1,0:T(8,128)S(1)}, u32[]{:S(2)}, u32[]{:S(2)}) collective-permute-start(f32[3,4,8,128]{3,2,1,0:T(8,128)} %get-tuple-element.107), channel_id=1, source_target_pairs={{0,8},{8,16},{16,24},{24,0},{1,9},{9,17},{17,25},{25,1},{2,10},{10... | collective-permute-start | bytes 147464 | tf_op jit(solution)/shard_map/ppermute | solution.py:368
  39.4 8.9 %collective-permute-start.13 = (f32[3,4,8,128]{3,2,1,0:T(8,128)}, f32[3,4,8,128]{3,2,1,0:T(8,128)S(1)}, u32[]{:S(2)}, u32[]{:S(2)}) collective-permute-start(f32[3,4,8,128]{3,2,1,0:T(8,128)} %get-tuple-element.108), channel_id=1, source_target_pairs={{8,0},{16,8},{24,16},{0,24},{9,1},{17,9},{25,17},{1,25},{10,2},{18... | collective-permute-start | bytes 147464 | tf_op jit(solution)/shard_map/ppermute | solution.py:369
  40.3 0.7 copy-start.4
  40.3 6.6 %collective-permute-start.14 = (f32[2,3,8,128]{3,2,1,0:T(8,128)}, f32[2,3,8,128]{3,2,1,0:T(8,128)S(1)}, u32[]{:S(2)}, u32[]{:S(2)}) collective-permute-start(f32[2,3,8,128]{3,2,1,0:T(8,128)} %get-tuple-element.109), channel_id=1, source_target_pairs={{0,4},{4,0},{1,5},{5,1},{2,6},{6,2},{3,7},{7,3},{8,12},{12,8},{9,1... | collective-permute-start | bytes 73736 | tf_op jit(solution)/shard_map/ppermute | solution.py:370
  40.9 0.6 copy-start.10
  40.9 0.6 copy-start.14
  45.1 9.8 %collective-permute-start.15 = (f32[3,4,8,128]{3,2,1,0:T(8,128)}, f32[3,4,8,128]{3,2,1,0:T(8,128)S(1)}, u32[]{:S(2)}, u32[]{:S(2)}) collective-permute-start(f32[3,4,8,128]{3,2,1,0:T(8,128)} %get-tuple-element.114), channel_id=1, source_target_pairs={{0,8},{8,16},{16,24},{24,0},{1,9},{9,17},{17,25},{25,1},{2,10},{10... | collective-permute-start | bytes 147464 | tf_op jit(solution)/shard_map/ppermute | solution.py:368
  45.3 9.6 %collective-permute-start.16 = (f32[3,4,8,128]{3,2,1,0:T(8,128)}, f32[3,4,8,128]{3,2,1,0:T(8,128)S(1)}, u32[]{:S(2)}, u32[]{:S(2)}) collective-permute-start(f32[3,4,8,128]{3,2,1,0:T(8,128)} %get-tuple-element.115), channel_id=1, source_target_pairs={{8,0},{16,8},{24,16},{0,24},{9,1},{17,9},{25,17},{1,25},{10,2},{18... | collective-permute-start | bytes 147464 | tf_op jit(solution)/shard_map/ppermute | solution.py:369
  46.9 1.4 %copy-start.6 = (f32[2,3,8,128]{3,2,1,0:T(8,128)}, f32[2,3,8,128]{3,2,1,0:T(8,128)S(1)}, u32[]{:S(2)}) copy-start(f32[2,3,8,128]{3,2,1,0:T(8,128)S(1)} %collective-permute-done.14.rest_3_.rest_4_) | copy-start | bytes 73732
  46.9 7.4 %collective-permute-start.17 = (f32[2,3,8,128]{3,2,1,0:T(8,128)}, f32[2,3,8,128]{3,2,1,0:T(8,128)S(1)}, u32[]{:S(2)}, u32[]{:S(2)}) collective-permute-start(f32[2,3,8,128]{3,2,1,0:T(8,128)} %get-tuple-element.116), channel_id=1, source_target_pairs={{0,4},{4,0},{1,5},{5,1},{2,6},{6,2},{3,7},{7,3},{8,12},{12,8},{9,1... | collective-permute-start | bytes 73736 | tf_op jit(solution)/shard_map/ppermute | solution.py:370
  48.3 0.6 copy-start.12
  48.3 0.6 copy-start.16
  52.6 6.6 %collective-permute-start.18 = (f32[3,4,8,128]{3,2,1,0:T(8,128)}, f32[3,4,8,128]{3,2,1,0:T(8,128)S(1)}, u32[]{:S(2)}, u32[]{:S(2)}) collective-permute-start(f32[3,4,8,128]{3,2,1,0:T(8,128)} %get-tuple-element.121), channel_id=1, source_target_pairs={{0,8},{8,16},{16,24},{24,0},{1,9},{9,17},{17,25},{25,1},{2,10},{10... | collective-permute-start | bytes 147464 | tf_op jit(solution)/shard_map/ppermute | solution.py:368
  52.6 6.6 %collective-permute-start.19 = (f32[3,4,8,128]{3,2,1,0:T(8,128)}, f32[3,4,8,128]{3,2,1,0:T(8,128)S(1)}, u32[]{:S(2)}, u32[]{:S(2)}) collective-permute-start(f32[3,4,8,128]{3,2,1,0:T(8,128)} %get-tuple-element.122), channel_id=1, source_target_pairs={{8,0},{16,8},{24,16},{0,24},{9,1},{17,9},{25,17},{1,25},{10,2},{18... | collective-permute-start | bytes 147464 | tf_op jit(solution)/shard_map/ppermute | solution.py:369
  54.3 0.7 copy-start.5
  54.3 4.8 %collective-permute-start.20 = (f32[2,3,8,128]{3,2,1,0:T(8,128)}, f32[2,3,8,128]{3,2,1,0:T(8,128)S(1)}, u32[]{:S(2)}, u32[]{:S(2)}) collective-permute-start(f32[2,3,8,128]{3,2,1,0:T(8,128)} %get-tuple-element.123), channel_id=1, source_target_pairs={{0,4},{4,0},{1,5},{5,1},{2,6},{6,2},{3,7},{7,3},{8,12},{12,8},{9,1... | collective-permute-start | bytes 73736 | tf_op jit(solution)/shard_map/ppermute | solution.py:370
  55.0 0.6 copy-start.11
  55.0 0.6 copy-start.15
  59.2 0.6 copy-start.7
  59.2 0.6 copy-start.17
  59.2 0.6 copy-start.18
  67.3 6.4 %collective-permute-start.21 = (f32[8,8,128]{2,1,0:T(8,128)}, f32[8,8,128]{2,1,0:T(8,128)S(1)}, u32[]{:S(2)}, u32[]{:S(2)}) collective-permute-start(f32[8,8,128]{2,1,0:T(8,128)} %get-tuple-element.128.rest_0_), channel_id=1, source_target_pairs={{0,1},{1,2},{2,3},{3,0},{4,5},{5,6},{6,7},{7,4},{8,9},{9,10},{10,1... | collective-permute-start | bytes 98312 | tf_op jit(solution)/shard_map/ppermute | solution.py:467
  68.8 5.5 %collective-permute-start.22 = (f32[8,8,128]{2,1,0:T(8,128)}, f32[8,8,128]{2,1,0:T(8,128)S(1)}, u32[]{:S(2)}, u32[]{:S(2)}) collective-permute-start(f32[8,8,128]{2,1,0:T(8,128)} %get-tuple-element.128.rest_0_), channel_id=1, source_target_pairs={{0,2},{1,3},{2,0},{3,1},{4,6},{5,7},{6,4},{7,5},{8,10},{9,11},{10,... | collective-permute-start | bytes 98312 | tf_op jit(solution)/shard_map/ppermute | solution.py:467
  71.3 4.1 %collective-permute-start.23 = (f32[8,8,128]{2,1,0:T(8,128)}, f32[8,8,128]{2,1,0:T(8,128)S(1)}, u32[]{:S(2)}, u32[]{:S(2)}) collective-permute-start(f32[8,8,128]{2,1,0:T(8,128)} %get-tuple-element.128.rest_0_), channel_id=1, source_target_pairs={{0,3},{1,0},{2,1},{3,2},{4,7},{5,4},{6,5},{7,6},{8,11},{9,8},{10,9... | collective-permute-start | bytes 98312 | tf_op jit(solution)/shard_map/ppermute | solution.py:467
  73.7 1.8 %copy-start.21 = (f32[8,8,128]{2,1,0:T(8,128)}, f32[8,8,128]{2,1,0:T(8,128)S(1)}, u32[]{:S(2)}) copy-start(f32[8,8,128]{2,1,0:T(8,128)S(1)} %collective-permute-done.21.rest_1_) | copy-start | bytes 98308
  74.2 1.2 %copy-start.22 = (f32[8,8,128]{2,1,0:T(8,128)}, f32[8,8,128]{2,1,0:T(8,128)S(1)}, u32[]{:S(2)}) copy-start(f32[8,8,128]{2,1,0:T(8,128)S(1)} %collective-permute-done.22.rest_2_) | copy-start | bytes 98308
  75.5 0.6 copy-start.23

commit v9 on v8

--- a/solution.py
+++ b/solution.py
@@ -98,6 +98,8 @@
                 hit = layer == l
                 entries = (lat_ref[0, l], lat_ref[1, l], adv_ref[0, l], adv_ref[1, l], vert_ref[l])
                 vals = [jnp.where(hit, entries[k], vals[k]) for k in range(5)]
+            vals[0] = 0.5 * vals[0]
+            vals[1] = 0.5 * vals[1]
             for k in range(5):
                 co_ref[k, d] = vals[k]
             heat, water, carbon = h_ref[d], w_ref[d], c_ref[d]
@@ -193,10 +195,10 @@
                 kx_p = cx_p * jnp.exp(-SOFTEN * q_xp[0])
                 ky_m = cy_m * jnp.exp(-SOFTEN * q_ym[0])
                 ky_p = cy_p * jnp.exp(-SOFTEN * q_yp[0])
-                flux_x_lo = 0.5 * (kx_m + kx) * (heat - q_xm[0])
-                flux_x_hi = 0.5 * (kx + kx_p) * (q_xp[0] - heat)
-                flux_y_lo = 0.5 * (ky_m + ky) * (heat - q_ym[0])
-                flux_y_hi = 0.5 * (ky + ky_p) * (q_yp[0] - heat)
+                flux_x_lo = (kx_m + kx) * (heat - q_xm[0])
+                flux_x_hi = (kx + kx_p) * (q_xp[0] - heat)
+                flux_y_lo = (ky_m + ky) * (heat - q_ym[0])
+                flux_y_hi = (ky + ky_p) * (q_yp[0] - heat)
                 diffused = flux_x_hi - flux_x_lo + flux_y_hi - flux_y_lo
                 inflow = []
                 for f in range(3):

time: 78.9 us -> 79 us (level)
  no operation moved by 1% of the time
where the time goes in v9:
time: 79 us; the launch traced here: 78.6 us
  Pallas kernels  41.6 us (53%)
  starting transfers between devices  25.8 us (33%)
  waiting for transfers between devices  5.37 us (7%)
  local copies, waits for them, and re-layouts  4.94 us (6%)
  between operations  0.83 us (1%)
    pallas_call x8, Pallas kernels, local(): pl.pallas_call(make_section_kernel(k, first), grid=(1,), out_shape=tuple(...  30.7 us
    ppermute x7, starting transfers between devices, exchange(): xhi = lax.ppermute(xf, 'east', east_bwd)  9.42 us
    ppermute x7, starting transfers between devices, exchange(): ylo = lax.ppermute(ys, 'north', north_fwd)  8.36 us
    ppermute x3, starting transfers between devices, local(): lax.ppermute(red, 'depth', [(i, (i + k) % count) for i in range(count)])  5.39 us
    unnamed x48, local copies, waits for them, and re-layouts  4.94 us
    pallas_call x1, Pallas kernels, local(): pl.pallas_call(prep_kernel, out_shape=(sds(shape), sds(shape), sds(shape)...  4.7 us
    pallas_call x1, Pallas kernels, local(): pl.pallas_call(sweep_kernel, grid=(1,), out_shape=(sds(shape), sds(shape)...  3.87 us
    ppermute x3, waiting for transfers between devices, local(): lax.ppermute(red, 'depth', [(i, (i + k) % count) for i in range(count)])  2.77 us
  transfers between devices with their start and end apart: 24, of which 5 were waited for; matrix products, arithmetic and copies ran while one was open for 0% of the time, Pallas kernels for 29%

profile of v9, /device:TPU:0, one launch (start us, length us, event | category | flops | bytes accessed | tf_op | source)
XLA Modules:
  0.0 78.6 jit_solution(14421733977242334770)
XLA Ops:
  0.6 4.7 %shard_map.120 = (f32[64,8,128]{2,1,0:T(8,128)}, f32[64,8,128]{2,1,0:T(8,128)}, f32[64,8,128]{2,1,0:T(8,128)}, f32[64,8,128]{2,1,0:T(8,128)}, f32[5,64,8,128]{3,...) custom-call(f32[2,12]{1,0:T(2,128)} %lat_ref.1, f32[12]{0:T(128)} %vert_ref.1, ...), custom_call_target="tpu_custom_call" | custom-call | tf_op jit(solution)/shard_map/pallas_call | solution.py:405
  5.3 0.5 collective-permute-start
  5.8 2.0 %collective-permute-start.1 = (f32[5,8,8,128]{3,2,1,0:T(8,128)}, f32[5,8,8,128]{3,2,1,0:T(8,128)S(1)}, u32[]{:S(2)}, u32[]{:S(2)}) collective-permute-start(f32[5,8,8,128]{3,2,1,0:T(8,128)} %get-tuple-element.74), channel_id=1, source_target_pairs={{8,0},{16,8},{24,16},{0,24},{9,1},{17,9},{25,17},{1,25},{10,2},{18... | collective-permute-start | bytes 491528 | tf_op jit(solution)/shard_map/ppermute | solution.py:371
  7.8 2.3 %collective-permute-start.2 = (f32[2,5,8,128]{3,2,1,0:T(8,128)}, f32[2,5,8,128]{3,2,1,0:T(8,128)S(1)}, u32[]{:S(2)}, u32[]{:S(2)}) collective-permute-start(f32[2,5,8,128]{3,2,1,0:T(8,128)} %get-tuple-element.75), channel_id=1, source_target_pairs={{0,4},{4,0},{1,5},{5,1},{2,6},{6,2},{3,7},{7,3},{8,12},{12,8},{9,1... | collective-permute-start | bytes 122888 | tf_op jit(solution)/shard_map/ppermute | solution.py:372
  10.1 2.2 %collective-permute-done.2.rest_2_.rest_3_ = f32[2,5,8,128]{3,2,1,0:T(8,128)S(1)} collective-permute-done((f32[2,5,8,128]{3,2,1,0:T(8,128)}, f32[2,5,8,128]{3,2,1,0:T(8,128)S(1)}, u32[]{:S(2)}, u32[]{:S(2)}) %collective-permute-start.2) | collective-permute-done | bytes 40992 | tf_op jit(solution)/shard_map/ppermute | solution.py:372
  12.2 0.4 collective-permute-done.1.rest_1_
  12.6 0.2 copy-done.2
  12.9 0.1 copy-done
  12.9 0.4 copy-done.1
  13.3 4.5 %shard_map.121 = (f32[64,8,128]{2,1,0:T(8,128)}, f32[64,8,128]{2,1,0:T(8,128)}, f32[64,8,128]{2,1,0:T(8,128)}, f32[64,8,128]{2,1,0:T(8,128)}, f32[3,4,8,128]{3,2...) custom-call(f32[64,8,128]{2,1,0:T(8,128)} %get-tuple-element.68.h_re, ...), custom_call_target="tpu_custom_call", output_to_operand_aliasing={{0}: (0, {}), {1}: (1, {}), {2}: (2, {}), {3}: (3, {})} | custom-call | tf_op jit(solution)/shard_map/pallas_call | solution.py:443
  17.8 0.7 collective-permute-start.3
  18.5 1.3 %collective-permute-start.4 = (f32[3,4,8,128]{3,2,1,0:T(8,128)}, f32[3,4,8,128]{3,2,1,0:T(8,128)S(1)}, u32[]{:S(2)}, u32[]{:S(2)}) collective-permute-start(f32[3,4,8,128]{3,2,1,0:T(8,128)} %get-tuple-element.86), channel_id=1, source_target_pairs={{8,0},{16,8},{24,16},{0,24},{9,1},{17,9},{25,17},{1,25},{10,2},{18... | collective-permute-start | bytes 147464 | tf_op jit(solution)/shard_map/ppermute | solution.py:371
  19.9 1.4 %collective-permute-start.5 = (f32[2,3,8,128]{3,2,1,0:T(8,128)}, f32[2,3,8,128]{3,2,1,0:T(8,128)S(1)}, u32[]{:S(2)}, u32[]{:S(2)}) collective-permute-start(f32[2,3,8,128]{3,2,1,0:T(8,128)} %get-tuple-element.87), channel_id=1, source_target_pairs={{0,4},{4,0},{1,5},{5,1},{2,6},{6,2},{3,7},{7,3},{8,12},{12,8},{9,1... | collective-permute-start | bytes 73736 | tf_op jit(solution)/shard_map/ppermute | solution.py:372
  21.3 4.5 %shard_map.122 = (f32[64,8,128]{2,1,0:T(8,128)}, f32[64,8,128]{2,1,0:T(8,128)}, f32[64,8,128]{2,1,0:T(8,128)}, f32[64,8,128]{2,1,0:T(8,128)}, f32[3,4,8,128]{3,2...) custom-call(f32[64,8,128]{2,1,0:T(8,128)} %get-tuple-element.76.h_re, ...), custom_call_target="tpu_custom_call", output_to_operand_aliasing={{0}: (0, {}), {1}: (1, {}), {2}: (2, {}), {3}: (3, {})} | custom-call | tf_op jit(solution)/shard_map/pallas_call | solution.py:443
  25.8 1.7 %collective-permute-start.7 = (f32[3,4,8,128]{3,2,1,0:T(8,128)}, f32[3,4,8,128]{3,2,1,0:T(8,128)S(1)}, u32[]{:S(2)}, u32[]{:S(2)}) collective-permute-start(f32[3,4,8,128]{3,2,1,0:T(8,128)} %get-tuple-element.94), channel_id=1, source_target_pairs={{8,0},{16,8},{24,16},{0,24},{9,1},{17,9},{25,17},{1,25},{10,2},{18... | collective-permute-start | bytes 147464 | tf_op jit(solution)/shard_map/ppermute | solution.py:371
  27.5 0.6 collective-permute-start.8
  28.2 0.6 copy-done.19
  28.8 3.6 %shard_map.123 = (f32[64,8,128]{2,1,0:T(8,128)}, f32[64,8,128]{2,1,0:T(8,128)}, f32[64,8,128]{2,1,0:T(8,128)}, f32[64,8,128]{2,1,0:T(8,128)}, f32[3,4,8,128]{3,2...) custom-call(f32[64,8,128]{2,1,0:T(8,128)} %get-tuple-element.80.h_re, ...), custom_call_target="tpu_custom_call", output_to_operand_aliasing={{0}: (0, {}), {1}: (1, {}), {2}: (2, {}), {3}: (3, {})} | custom-call | tf_op jit(solution)/shard_map/pallas_call | solution.py:443
  32.4 0.2 collective-permute-start.10
  32.6 0.3 collective-permute-start.9
  33.0 1.4 %collective-permute-start.11 = (f32[2,3,8,128]{3,2,1,0:T(8,128)}, f32[2,3,8,128]{3,2,1,0:T(8,128)S(1)}, u32[]{:S(2)}, u32[]{:S(2)}) collective-permute-start(f32[2,3,8,128]{3,2,1,0:T(8,128)} %get-tuple-element.102), channel_id=1, source_target_pairs={{0,4},{4,0},{1,5},{5,1},{2,6},{6,2},{3,7},{7,3},{8,12},{12,8},{9,1... | collective-permute-start | bytes 73736 | tf_op jit(solution)/shard_map/ppermute | solution.py:372
  34.4 0.6 copy-done.9
  35.0 3.6 %shard_map.124 = (f32[64,8,128]{2,1,0:T(8,128)}, f32[64,8,128]{2,1,0:T(8,128)}, f32[64,8,128]{2,1,0:T(8,128)}, f32[64,8,128]{2,1,0:T(8,128)}, f32[3,4,8,128]{3,2...) custom-call(f32[64,8,128]{2,1,0:T(8,128)} %get-tuple-element.88.h_re, ...), custom_call_target="tpu_custom_call", output_to_operand_aliasing={{0}: (0, {}), {1}: (1, {}), {2}: (2, {}), {3}: (3, {})} | custom-call | tf_op jit(solution)/shard_map/pallas_call | solution.py:443
  38.6 0.9 %collective-permute-start.12 = (f32[3,4,8,128]{3,2,1,0:T(8,128)}, f32[3,4,8,128]{3,2,1,0:T(8,128)S(1)}, u32[]{:S(2)}, u32[]{:S(2)}) collective-permute-start(f32[3,4,8,128]{3,2,1,0:T(8,128)} %get-tuple-element.107), channel_id=1, source_target_pairs={{0,8},{8,16},{16,24},{24,0},{1,9},{9,17},{17,25},{25,1},{2,10},{10... | collective-permute-start | bytes 147464 | tf_op jit(solution)/shard_map/ppermute | solution.py:370
  39.5 0.9 %collective-permute-start.13 = (f32[3,4,8,128]{3,2,1,0:T(8,128)}, f32[3,4,8,128]{3,2,1,0:T(8,128)S(1)}, u32[]{:S(2)}, u32[]{:S(2)}) collective-permute-start(f32[3,4,8,128]{3,2,1,0:T(8,128)} %get-tuple-element.108), channel_id=1, source_target_pairs={{8,0},{16,8},{24,16},{0,24},{9,1},{17,9},{25,17},{1,25},{10,2},{18... | collective-permute-start | bytes 147464 | tf_op jit(solution)/shard_map/ppermute | solution.py:371
  40.4 0.6 collective-permute-start.14
  41.1 0.6 copy-done.10
  41.6 3.6 %shard_map.125 = (f32[64,8,128]{2,1,0:T(8,128)}, f32[64,8,128]{2,1,0:T(8,128)}, f32[64,8,128]{2,1,0:T(8,128)}, f32[64,8,128]{2,1,0:T(8,128)}, f32[3,4,8,128]{3,2...) custom-call(f32[64,8,128]{2,1,0:T(8,128)} %get-tuple-element.96.h_re, ...), custom_call_target="tpu_custom_call", output_to_operand_aliasing={{0}: (0, {}), {1}: (1, {}), {2}: (2, {}), {3}: (3, {})} | custom-call | tf_op jit(solution)/shard_map/pallas_call | solution.py:443
  45.2 0.2 collective-permute-start.15
  45.5 1.6 %collective-permute-start.16 = (f32[3,4,8,128]{3,2,1,0:T(8,128)}, f32[3,4,8,128]{3,2,1,0:T(8,128)S(1)}, u32[]{:S(2)}, u32[]{:S(2)}) collective-permute-start(f32[3,4,8,128]{3,2,1,0:T(8,128)} %get-tuple-element.115), channel_id=1, source_target_pairs={{8,0},{16,8},{24,16},{0,24},{9,1},{17,9},{25,17},{1,25},{10,2},{18... | collective-permute-start | bytes 147464 | tf_op jit(solution)/shard_map/ppermute | solution.py:371
  47.0 1.4 %collective-permute-start.17 = (f32[2,3,8,128]{3,2,1,0:T(8,128)}, f32[2,3,8,128]{3,2,1,0:T(8,128)S(1)}, u32[]{:S(2)}, u32[]{:S(2)}) collective-permute-start(f32[2,3,8,128]{3,2,1,0:T(8,128)} %get-tuple-element.116), channel_id=1, source_target_pairs={{0,4},{4,0},{1,5},{5,1},{2,6},{6,2},{3,7},{7,3},{8,12},{12,8},{9,1... | collective-permute-start | bytes 73736 | tf_op jit(solution)/shard_map/ppermute | solution.py:372
  48.4 0.6 copy-done.12
  49.1 3.6 %shard_map.126 = (f32[64,8,128]{2,1,0:T(8,128)}, f32[64,8,128]{2,1,0:T(8,128)}, f32[64,8,128]{2,1,0:T(8,128)}, f32[64,8,128]{2,1,0:T(8,128)}, f32[3,4,8,128]{3,2...) custom-call(f32[64,8,128]{2,1,0:T(8,128)} %get-tuple-element.103.h_r, ...), custom_call_target="tpu_custom_call", output_to_operand_aliasing={{0}: (0, {}), {1}: (1, {}), {2}: (2, {}), {3}: (3, {})} | custom-call | tf_op jit(solution)/shard_map/pallas_call | solution.py:443
  52.7 1.7 %collective-permute-start.19 = (f32[3,4,8,128]{3,2,1,0:T(8,128)}, f32[3,4,8,128]{3,2,1,0:T(8,128)S(1)}, u32[]{:S(2)}, u32[]{:S(2)}) collective-permute-start(f32[3,4,8,128]{3,2,1,0:T(8,128)} %get-tuple-element.122), channel_id=1, source_target_pairs={{8,0},{16,8},{24,16},{0,24},{9,1},{17,9},{25,17},{1,25},{10,2},{18... | collective-permute-start | bytes 147464 | tf_op jit(solution)/shard_map/ppermute | solution.py:371
  54.4 0.6 collective-permute-start.20
  55.1 0.6 copy-done.11
  55.7 3.6 %shard_map.127 = (f32[64,8,128]{2,1,0:T(8,128)}, f32[64,8,128]{2,1,0:T(8,128)}, f32[64,8,128]{2,1,0:T(8,128)}, f32[64,8,128]{2,1,0:T(8,128)}, f32[3,4,8,128]{3,2...) custom-call(f32[64,8,128]{2,1,0:T(8,128)} %get-tuple-element.110.h_r, ...), custom_call_target="tpu_custom_call", output_to_operand_aliasing={{0}: (0, {}), {1}: (1, {}), {2}: (2, {}), {3}: (3, {})} | custom-call | tf_op jit(solution)/shard_map/pallas_call | solution.py:443
  59.4 0.6 copy-done.7
  60.0 3.6 %shard_map.128 = (f32[64,8,128]{2,1,0:T(8,128)}, f32[64,8,128]{2,1,0:T(8,128)}, f32[64,8,128]{2,1,0:T(8,128)}, f32[64,8,128]{2,1,0:T(8,128)}, f32[3,4,8,128]{3,2...) custom-call(f32[64,8,128]{2,1,0:T(8,128)} %get-tuple-element.117.h_r, ...), custom_call_target="tpu_custom_call", output_to_operand_aliasing={{0}: (0, {}), {1}: (1, {}), {2}: (2, {}), {3}: (3, {})} | custom-call | tf_op jit(solution)/shard_map/pallas_call | solution.py:443
  63.6 3.9 %shard_map.129 = (f32[64,8,128]{2,1,0:T(8,128)}, f32[64,8,128]{2,1,0:T(8,128)}, f32[64,8,128]{2,1,0:T(8,128)}, f32[8,8,128]{2,1,0:T(8,128)}) custom-call(f32[64,8,128]{2,1,0:T(8,128)} %get-tuple-element.124.r_ref, f32[5,64,8,128]{3,2,1,0:T(8,128)} %get-tuple-element.72.co_ref.cz_ref), custom_call_target="tpu_custom_call" | custom-call | tf_op jit(solution)/shard_map/pallas_call | solution.py:457
  67.4 1.5 %collective-permute-start.21 = (f32[8,8,128]{2,1,0:T(8,128)}, f32[8,8,128]{2,1,0:T(8,128)S(1)}, u32[]{:S(2)}, u32[]{:S(2)}) collective-permute-start(f32[8,8,128]{2,1,0:T(8,128)} %get-tuple-element.128.rest_0_), channel_id=1, source_target_pairs={{0,1},{1,2},{2,3},{3,0},{4,5},{5,6},{6,7},{7,4},{8,9},{9,10},{10,1... | collective-permute-start | bytes 98312 | tf_op jit(solution)/shard_map/ppermute | solution.py:469
  68.9 2.6 %collective-permute-start.22 = (f32[8,8,128]{2,1,0:T(8,128)}, f32[8,8,128]{2,1,0:T(8,128)S(1)}, u32[]{:S(2)}, u32[]{:S(2)}) collective-permute-start(f32[8,8,128]{2,1,0:T(8,128)} %get-tuple-element.128.rest_0_), channel_id=1, source_target_pairs={{0,2},{1,3},{2,0},{3,1},{4,6},{5,7},{6,4},{7,5},{8,10},{9,11},{10,... | collective-permute-start | bytes 98312 | tf_op jit(solution)/shard_map/ppermute | solution.py:469
  71.5 1.3 %collective-permute-start.23 = (f32[8,8,128]{2,1,0:T(8,128)}, f32[8,8,128]{2,1,0:T(8,128)S(1)}, u32[]{:S(2)}, u32[]{:S(2)}) collective-permute-start(f32[8,8,128]{2,1,0:T(8,128)} %get-tuple-element.128.rest_0_), channel_id=1, source_target_pairs={{0,3},{1,0},{2,1},{3,2},{4,7},{5,4},{6,5},{7,6},{8,11},{9,8},{10,9... | collective-permute-start | bytes 98312 | tf_op jit(solution)/shard_map/ppermute | solution.py:469
  72.8 1.0 %collective-permute-done.21.rest_1_ = f32[8,8,128]{2,1,0:T(8,128)S(1)} collective-permute-done((f32[8,8,128]{2,1,0:T(8,128)}, f32[8,8,128]{2,1,0:T(8,128)S(1)}, u32[]{:S(2)}, u32[]{:S(2)}) %collective-permute-start.21) | collective-permute-done | bytes 32800 | tf_op jit(solution)/shard_map/ppermute | solution.py:469
  73.8 0.6 collective-permute-done.22.rest_2_
  74.4 1.2 %collective-permute-done.23.rest_3_ = f32[8,8,128]{2,1,0:T(8,128)S(1)} collective-permute-done((f32[8,8,128]{2,1,0:T(8,128)}, f32[8,8,128]{2,1,0:T(8,128)S(1)}, u32[]{:S(2)}, u32[]{:S(2)}) %collective-permute-start.23) | collective-permute-done | bytes 32800 | tf_op jit(solution)/shard_map/ppermute | solution.py:469
  75.6 0.6 copy-done.23
  76.2 2.4 %shard_map.130 = f32[64,8,128]{2,1,0:T(8,128)} custom-call(s32[1]{0:T(128)} %bitcast.rank_ref, f32[64,8,128]{2,1,0:T(8,128)} %get-tuple-element.125.y_ref, f32[64,8,128]{2,1,0:T(8,128)} %get-tuple-element.126.a_ref, f32[64,8,128]{2,1,0:T(8,128)} %get-tuple-element.127.b_ref, f32[8,8,128]{2,1,0:T(8,128)} %get-tuple-element.128.rest_0_, ...), custom_call_target="tpu_custom_call" | custom-call | tf_op jit(solution)/shard_map/pallas_call | solution.py:471
  (59 shorter events, 0.3 us)
Async XLA Ops:
  5.3 6.9 %collective-permute-start = (f32[5,8,8,128]{3,2,1,0:T(8,128)}, f32[5,8,8,128]{3,2,1,0:T(8,128)S(1)}, u32[]{:S(2)}, u32[]{:S(2)}) collective-permute-start(f32[5,8,8,128]{3,2,1,0:T(8,128)} %get-tuple-element.73), channel_id=1, source_target_pairs={{0,8},{8,16},{16,24},{24,0},{1,9},{9,17},{17,25},{25,1},{2,10},{10... | collective-permute-start | bytes 491528 | tf_op jit(solution)/shard_map/ppermute | solution.py:370
  5.8 6.8 %collective-permute-start.1 = (f32[5,8,8,128]{3,2,1,0:T(8,128)}, f32[5,8,8,128]{3,2,1,0:T(8,128)S(1)}, u32[]{:S(2)}, u32[]{:S(2)}) collective-permute-start(f32[5,8,8,128]{3,2,1,0:T(8,128)} %get-tuple-element.74), channel_id=1, source_target_pairs={{8,0},{16,8},{24,16},{0,24},{9,1},{17,9},{25,17},{1,25},{10,2},{18... | collective-permute-start | bytes 491528 | tf_op jit(solution)/shard_map/ppermute | solution.py:371
  7.8 4.5 %collective-permute-start.2 = (f32[2,5,8,128]{3,2,1,0:T(8,128)}, f32[2,5,8,128]{3,2,1,0:T(8,128)S(1)}, u32[]{:S(2)}, u32[]{:S(2)}) collective-permute-start(f32[2,5,8,128]{3,2,1,0:T(8,128)} %get-tuple-element.75), channel_id=1, source_target_pairs={{0,4},{4,0},{1,5},{5,1},{2,6},{6,2},{3,7},{7,3},{8,12},{12,8},{9,1... | collective-permute-start | bytes 122888 | tf_op jit(solution)/shard_map/ppermute | solution.py:372
  12.2 0.6 copy-start.2
  12.2 0.7 copy-start
  12.6 0.7 copy-start.1
  17.8 10.4 %collective-permute-start.3 = (f32[3,4,8,128]{3,2,1,0:T(8,128)}, f32[3,4,8,128]{3,2,1,0:T(8,128)S(1)}, u32[]{:S(2)}, u32[]{:S(2)}) collective-permute-start(f32[3,4,8,128]{3,2,1,0:T(8,128)} %get-tuple-element.85), channel_id=1, source_target_pairs={{0,8},{8,16},{16,24},{24,0},{1,9},{9,17},{17,25},{25,1},{2,10},{10... | collective-permute-start | bytes 147464 | tf_op jit(solution)/shard_map/ppermute | solution.py:370
  18.5 9.6 %collective-permute-start.4 = (f32[3,4,8,128]{3,2,1,0:T(8,128)}, f32[3,4,8,128]{3,2,1,0:T(8,128)S(1)}, u32[]{:S(2)}, u32[]{:S(2)}) collective-permute-start(f32[3,4,8,128]{3,2,1,0:T(8,128)} %get-tuple-element.86), channel_id=1, source_target_pairs={{8,0},{16,8},{24,16},{0,24},{9,1},{17,9},{25,17},{1,25},{10,2},{18... | collective-permute-start | bytes 147464 | tf_op jit(solution)/shard_map/ppermute | solution.py:371
  19.9 7.7 %collective-permute-start.5 = (f32[2,3,8,128]{3,2,1,0:T(8,128)}, f32[2,3,8,128]{3,2,1,0:T(8,128)S(1)}, u32[]{:S(2)}, u32[]{:S(2)}) collective-permute-start(f32[2,3,8,128]{3,2,1,0:T(8,128)} %get-tuple-element.87), channel_id=1, source_target_pairs={{0,4},{4,0},{1,5},{5,1},{2,6},{6,2},{3,7},{7,3},{8,12},{12,8},{9,1... | collective-permute-start | bytes 73736 | tf_op jit(solution)/shard_map/ppermute | solution.py:372
  25.8 8.6 %collective-permute-start.6 = (f32[3,4,8,128]{3,2,1,0:T(8,128)}, f32[3,4,8,128]{3,2,1,0:T(8,128)S(1)}, u32[]{:S(2)}, u32[]{:S(2)}) collective-permute-start(f32[3,4,8,128]{3,2,1,0:T(8,128)} %get-tuple-element.93), channel_id=1, source_target_pairs={{0,8},{8,16},{16,24},{24,0},{1,9},{9,17},{17,25},{25,1},{2,10},{10... | collective-permute-start | bytes 147464 | tf_op jit(solution)/shard_map/ppermute | solution.py:370
  25.8 8.6 %collective-permute-start.7 = (f32[3,4,8,128]{3,2,1,0:T(8,128)}, f32[3,4,8,128]{3,2,1,0:T(8,128)S(1)}, u32[]{:S(2)}, u32[]{:S(2)}) collective-permute-start(f32[3,4,8,128]{3,2,1,0:T(8,128)} %get-tuple-element.94), channel_id=1, source_target_pairs={{8,0},{16,8},{24,16},{0,24},{9,1},{17,9},{25,17},{1,25},{10,2},{18... | collective-permute-start | bytes 147464 | tf_op jit(solution)/shard_map/ppermute | solution.py:371
  27.5 0.7 copy-start.8
  27.5 5.4 %collective-permute-start.8 = (f32[2,3,8,128]{3,2,1,0:T(8,128)}, f32[2,3,8,128]{3,2,1,0:T(8,128)S(1)}, u32[]{:S(2)}, u32[]{:S(2)}) collective-permute-start(f32[2,3,8,128]{3,2,1,0:T(8,128)} %get-tuple-element.95), channel_id=1, source_target_pairs={{0,4},{4,0},{1,5},{5,1},{2,6},{6,2},{3,7},{7,3},{8,12},{12,8},{9,1... | collective-permute-start | bytes 73736 | tf_op jit(solution)/shard_map/ppermute | solution.py:372
  28.2 0.6 copy-start.19
  28.2 0.6 copy-start.20
  32.4 8.6 %collective-permute-start.10 = (f32[3,4,8,128]{3,2,1,0:T(8,128)}, f32[3,4,8,128]{3,2,1,0:T(8,128)S(1)}, u32[]{:S(2)}, u32[]{:S(2)}) collective-permute-start(f32[3,4,8,128]{3,2,1,0:T(8,128)} %get-tuple-element.101), channel_id=1, source_target_pairs={{8,0},{16,8},{24,16},{0,24},{9,1},{17,9},{25,17},{1,25},{10,2},{18... | collective-permute-start | bytes 147464 | tf_op jit(solution)/shard_map/ppermute | solution.py:371
  32.6 8.4 %collective-permute-start.9 = (f32[3,4,8,128]{3,2,1,0:T(8,128)}, f32[3,4,8,128]{3,2,1,0:T(8,128)S(1)}, u32[]{:S(2)}, u32[]{:S(2)}) collective-permute-start(f32[3,4,8,128]{3,2,1,0:T(8,128)} %get-tuple-element.100), channel_id=1, source_target_pairs={{0,8},{8,16},{16,24},{24,0},{1,9},{9,17},{17,25},{25,1},{2,10},{10... | collective-permute-start | bytes 147464 | tf_op jit(solution)/shard_map/ppermute | solution.py:370
  33.0 1.4 %copy-start.3 = (f32[2,3,8,128]{3,2,1,0:T(8,128)}, f32[2,3,8,128]{3,2,1,0:T(8,128)S(1)}, u32[]{:S(2)}) copy-start(f32[2,3,8,128]{3,2,1,0:T(8,128)S(1)} %collective-permute-done.8.rest_3_.rest_4_) | copy-start | bytes 73732
  33.0 7.4 %collective-permute-start.11 = (f32[2,3,8,128]{3,2,1,0:T(8,128)}, f32[2,3,8,128]{3,2,1,0:T(8,128)S(1)}, u32[]{:S(2)}, u32[]{:S(2)}) collective-permute-start(f32[2,3,8,128]{3,2,1,0:T(8,128)} %get-tuple-element.102), channel_id=1, source_target_pairs={{0,4},{4,0},{1,5},{5,1},{2,6},{6,2},{3,7},{7,3},{8,12},{12,8},{9,1... | collective-permute-start | bytes 73736 | tf_op jit(solution)/shard_map/ppermute | solution.py:372
  34.4 0.6 copy-start.9
  34.4 0.6 copy-start.13
  38.6 9.8 %collective-permute-start.12 = (f32[3,4,8,128]{3,2,1,0:T(8,128)}, f32[3,4,8,128]{3,2,1,0:T(8,128)S(1)}, u32[]{:S(2)}, u32[]{:S(2)}) collective-permute-start(f32[3,4,8,128]{3,2,1,0:T(8,128)} %get-tuple-element.107), channel_id=1, source_target_pairs={{0,8},{8,16},{16,24},{24,0},{1,9},{9,17},{17,25},{25,1},{2,10},{10... | collective-permute-start | bytes 147464 | tf_op jit(solution)/shard_map/ppermute | solution.py:370
  39.5 8.9 %collective-permute-start.13 = (f32[3,4,8,128]{3,2,1,0:T(8,128)}, f32[3,4,8,128]{3,2,1,0:T(8,128)S(1)}, u32[]{:S(2)}, u32[]{:S(2)}) collective-permute-start(f32[3,4,8,128]{3,2,1,0:T(8,128)} %get-tuple-element.108), channel_id=1, source_target_pairs={{8,0},{16,8},{24,16},{0,24},{9,1},{17,9},{25,17},{1,25},{10,2},{18... | collective-permute-start | bytes 147464 | tf_op jit(solution)/shard_map/ppermute | solution.py:371
  40.4 0.7 copy-start.4
  40.4 6.6 %collective-permute-start.14 = (f32[2,3,8,128]{3,2,1,0:T(8,128)}, f32[2,3,8,128]{3,2,1,0:T(8,128)S(1)}, u32[]{:S(2)}, u32[]{:S(2)}) collective-permute-start(f32[2,3,8,128]{3,2,1,0:T(8,128)} %get-tuple-element.109), channel_id=1, source_target_pairs={{0,4},{4,0},{1,5},{5,1},{2,6},{6,2},{3,7},{7,3},{8,12},{12,8},{9,1... | collective-permute-start | bytes 73736 | tf_op jit(solution)/shard_map/ppermute | solution.py:372
  41.0 0.6 copy-start.10
  41.0 0.6 copy-start.14
  45.2 9.8 %collective-permute-start.15 = (f32[3,4,8,128]{3,2,1,0:T(8,128)}, f32[3,4,8,128]{3,2,1,0:T(8,128)S(1)}, u32[]{:S(2)}, u32[]{:S(2)}) collective-permute-start(f32[3,4,8,128]{3,2,1,0:T(8,128)} %get-tuple-element.114), channel_id=1, source_target_pairs={{0,8},{8,16},{16,24},{24,0},{1,9},{9,17},{17,25},{25,1},{2,10},{10... | collective-permute-start | bytes 147464 | tf_op jit(solution)/shard_map/ppermute | solution.py:370
  45.5 9.6 %collective-permute-start.16 = (f32[3,4,8,128]{3,2,1,0:T(8,128)}, f32[3,4,8,128]{3,2,1,0:T(8,128)S(1)}, u32[]{:S(2)}, u32[]{:S(2)}) collective-permute-start(f32[3,4,8,128]{3,2,1,0:T(8,128)} %get-tuple-element.115), channel_id=1, source_target_pairs={{8,0},{16,8},{24,16},{0,24},{9,1},{17,9},{25,17},{1,25},{10,2},{18... | collective-permute-start | bytes 147464 | tf_op jit(solution)/shard_map/ppermute | solution.py:371
  47.0 1.4 %copy-start.6 = (f32[2,3,8,128]{3,2,1,0:T(8,128)}, f32[2,3,8,128]{3,2,1,0:T(8,128)S(1)}, u32[]{:S(2)}) copy-start(f32[2,3,8,128]{3,2,1,0:T(8,128)S(1)} %collective-permute-done.14.rest_3_.rest_4_) | copy-start | bytes 73732
  47.0 7.4 %collective-permute-start.17 = (f32[2,3,8,128]{3,2,1,0:T(8,128)}, f32[2,3,8,128]{3,2,1,0:T(8,128)S(1)}, u32[]{:S(2)}, u32[]{:S(2)}) collective-permute-start(f32[2,3,8,128]{3,2,1,0:T(8,128)} %get-tuple-element.116), channel_id=1, source_target_pairs={{0,4},{4,0},{1,5},{5,1},{2,6},{6,2},{3,7},{7,3},{8,12},{12,8},{9,1... | collective-permute-start | bytes 73736 | tf_op jit(solution)/shard_map/ppermute | solution.py:372
  48.4 0.6 copy-start.12
  48.4 0.6 copy-start.16
  52.7 6.6 %collective-permute-start.18 = (f32[3,4,8,128]{3,2,1,0:T(8,128)}, f32[3,4,8,128]{3,2,1,0:T(8,128)S(1)}, u32[]{:S(2)}, u32[]{:S(2)}) collective-permute-start(f32[3,4,8,128]{3,2,1,0:T(8,128)} %get-tuple-element.121), channel_id=1, source_target_pairs={{0,8},{8,16},{16,24},{24,0},{1,9},{9,17},{17,25},{25,1},{2,10},{10... | collective-permute-start | bytes 147464 | tf_op jit(solution)/shard_map/ppermute | solution.py:370
  52.7 6.6 %collective-permute-start.19 = (f32[3,4,8,128]{3,2,1,0:T(8,128)}, f32[3,4,8,128]{3,2,1,0:T(8,128)S(1)}, u32[]{:S(2)}, u32[]{:S(2)}) collective-permute-start(f32[3,4,8,128]{3,2,1,0:T(8,128)} %get-tuple-element.122), channel_id=1, source_target_pairs={{8,0},{16,8},{24,16},{0,24},{9,1},{17,9},{25,17},{1,25},{10,2},{18... | collective-permute-start | bytes 147464 | tf_op jit(solution)/shard_map/ppermute | solution.py:371
  54.4 0.7 copy-start.5
  54.4 4.9 %collective-permute-start.20 = (f32[2,3,8,128]{3,2,1,0:T(8,128)}, f32[2,3,8,128]{3,2,1,0:T(8,128)S(1)}, u32[]{:S(2)}, u32[]{:S(2)}) collective-permute-start(f32[2,3,8,128]{3,2,1,0:T(8,128)} %get-tuple-element.123), channel_id=1, source_target_pairs={{0,4},{4,0},{1,5},{5,1},{2,6},{6,2},{3,7},{7,3},{8,12},{12,8},{9,1... | collective-permute-start | bytes 73736 | tf_op jit(solution)/shard_map/ppermute | solution.py:372
  55.1 0.6 copy-start.11
  55.1 0.6 copy-start.15
  59.3 0.6 copy-start.7
  59.3 0.6 copy-start.17
  59.3 0.6 copy-start.18
  67.4 6.4 %collective-permute-start.21 = (f32[8,8,128]{2,1,0:T(8,128)}, f32[8,8,128]{2,1,0:T(8,128)S(1)}, u32[]{:S(2)}, u32[]{:S(2)}) collective-permute-start(f32[8,8,128]{2,1,0:T(8,128)} %get-tuple-element.128.rest_0_), channel_id=1, source_target_pairs={{0,1},{1,2},{2,3},{3,0},{4,5},{5,6},{6,7},{7,4},{8,9},{9,10},{10,1... | collective-permute-start | bytes 98312 | tf_op jit(solution)/shard_map/ppermute | solution.py:469
  68.9 5.5 %collective-permute-start.22 = (f32[8,8,128]{2,1,0:T(8,128)}, f32[8,8,128]{2,1,0:T(8,128)S(1)}, u32[]{:S(2)}, u32[]{:S(2)}) collective-permute-start(f32[8,8,128]{2,1,0:T(8,128)} %get-tuple-element.128.rest_0_), channel_id=1, source_target_pairs={{0,2},{1,3},{2,0},{3,1},{4,6},{5,7},{6,4},{7,5},{8,10},{9,11},{10,... | collective-permute-start | bytes 98312 | tf_op jit(solution)/shard_map/ppermute | solution.py:469
  71.5 4.1 %collective-permute-start.23 = (f32[8,8,128]{2,1,0:T(8,128)}, f32[8,8,128]{2,1,0:T(8,128)S(1)}, u32[]{:S(2)}, u32[]{:S(2)}) collective-permute-start(f32[8,8,128]{2,1,0:T(8,128)} %get-tuple-element.128.rest_0_), channel_id=1, source_target_pairs={{0,3},{1,0},{2,1},{3,2},{4,7},{5,4},{6,5},{7,6},{8,11},{9,8},{10,9... | collective-permute-start | bytes 98312 | tf_op jit(solution)/shard_map/ppermute | solution.py:469
  73.8 1.8 %copy-start.21 = (f32[8,8,128]{2,1,0:T(8,128)}, f32[8,8,128]{2,1,0:T(8,128)S(1)}, u32[]{:S(2)}) copy-start(f32[8,8,128]{2,1,0:T(8,128)S(1)} %collective-permute-done.21.rest_1_) | copy-start | bytes 98308
  74.4 1.3 %copy-start.22 = (f32[8,8,128]{2,1,0:T(8,128)}, f32[8,8,128]{2,1,0:T(8,128)S(1)}, u32[]{:S(2)}) copy-start(f32[8,8,128]{2,1,0:T(8,128)S(1)} %collective-permute-done.22.rest_2_) | copy-start | bytes 98308
  75.6 0.6 copy-start.23

commit v10 on v9

--- a/solution.py
+++ b/solution.py
@@ -80,49 +80,80 @@
     )
 
 
+def lookup_tile(layer, entry, count):
+    val = jnp.zeros(layer.shape, f32)
+    for l in range(count):
+        val = jnp.where(layer == l, entry(l), val)
+    return val
+
+
+def edge_kernel(lat_ref, adv_ref, layer_ref, h_ref, w_ref, c_ref, xf_ref, xl_ref, y_ref):
+    n = layer_ref.shape[0]
+    count = lat_ref.shape[1]
+    lane = lax.broadcasted_iota(jnp.int32, (ROWS, LANES), 1)
+    half_cx = lambda l: 0.5 * lat_ref[0, l]
+    half_cy = lambda l: 0.5 * lat_ref[1, l]
+    vx = lambda l: adv_ref[0, l]
+    vy = lambda l: adv_ref[1, l]
+    for a in range(n // ROWS):
+        planes = pl.ds(a * ROWS, ROWS)
+        for out_ref, row in ((xf_ref, 0), (xl_ref, ROWS - 1)):
+            for f, src_ref in enumerate((h_ref, w_ref, c_ref)):
+                out_ref[f, a] = src_ref[planes, row, :]
+            layer = layer_ref[planes, row, :]
+            out_ref[3, a] = lookup_tile(layer, half_cx, count)
+            out_ref[4, a] = lookup_tile(layer, vx, count)
+    zero = jnp.zeros((ROWS, LANES), f32)
+    izero = jnp.zeros((ROWS, LANES), jnp.int32)
+
+    def plane(d, carry):
+        firsts, lasts, lay_f, lay_l = carry
+        at_d = lane == d
+        firsts = tuple(
+            jnp.where(at_d, pltpu.roll(r[d], d, 1), v) for r, v in zip((h_ref, w_ref, c_ref), firsts)
+        )
+        lasts = tuple(
+            jnp.where(at_d, pltpu.roll(r[d], (d + 1) % LANES, 1), v)
+            for r, v in zip((h_ref, w_ref, c_ref), lasts)
+        )
+        layer = layer_ref[d]
+        lay_f = jnp.where(at_d, pltpu.roll(layer, d, 1), lay_f)
+        lay_l = jnp.where(at_d, pltpu.roll(layer, (d + 1) % LANES, 1), lay_l)
+        return firsts, lasts, lay_f, lay_l
+
+    firsts, lasts, lay_f, lay_l = lax.fori_loop(
+        0, n, plane, ((zero,) * 3, (zero,) * 3, izero, izero)
+    )
+    for side, vals, lay in ((0, firsts, lay_f), (1, lasts, lay_l)):
+        for f in range(3):
+            y_ref[side, f] = vals[f]
+        y_ref[side, 3] = lookup_tile(lay, half_cy, count)
+        y_ref[side, 4] = lookup_tile(lay, vy, count)
+
+
 def prep_kernel(lat_ref, vert_ref, adv_ref, layer_ref, h_ref, w_ref, c_ref, m_ref,
-                ho_ref, wo_ref, cbo_ref, mo_ref, co_ref, xf_ref, xl_ref, y_ref):
-    groups = layer_ref.shape[0] // ROWS
+                ho_ref, wo_ref, cbo_ref, mo_ref, co_ref):
     layers_count = vert_ref.shape[0]
-    sub, lane = iotas()
-    zero = jnp.zeros((ROWS, LANES), f32)
-
-    def group(a, carry):
-        y_f, y_l = carry
-        acc = EdgeAcc(5, y_f, y_l)
-        for b in range(ROWS):
-            d = a * ROWS + b
-            layer = layer_ref[d]
-            vals = [zero] * 5
-            for l in range(layers_count):
-                hit = layer == l
-                entries = (lat_ref[0, l], lat_ref[1, l], adv_ref[0, l], adv_ref[1, l], vert_ref[l])
-                vals = [jnp.where(hit, entries[k], vals[k]) for k in range(5)]
-            vals[0] = 0.5 * vals[0]
-            vals[1] = 0.5 * vals[1]
-            for k in range(5):
-                co_ref[k, d] = vals[k]
-            heat, water, carbon = h_ref[d], w_ref[d], c_ref[d]
-            ho_ref[d] = heat
-            wo_ref[d] = water
-            cbo_ref[d] = carbon
-            mo_ref[d] = m_ref[d]
-            acc.add_y([heat, water, carbon, vals[1], vals[3]], d, lane)
-        planes = pl.ds(a * ROWS, ROWS)
-        sources = ((ho_ref, None), (wo_ref, None), (cbo_ref, None), (co_ref, 0), (co_ref, 2))
-        for f, (out, field) in enumerate(sources):
-            if field is None:
-                xf_ref[f, a] = out[planes, 0, :]
-                xl_ref[f, a] = out[planes, ROWS - 1, :]
-            else:
-                xf_ref[f, a] = out[field, planes, 0, :]
-                xl_ref[f, a] = out[field, planes, ROWS - 1, :]
-        return (tuple(acc.yf), tuple(acc.yl))
-
-    y_f, y_l = lax.fori_loop(0, groups, group, ((zero,) * 5, (zero,) * 5))
-    for f in range(5):
-        y_ref[0, f] = y_f[f]
-        y_ref[1, f] = y_l[f]
+
+    def plane(d, carry):
+        layer = layer_ref[d]
+        zero = jnp.zeros(layer.shape, f32)
+        vals = [zero] * 5
+        for l in range(layers_count):
+            hit = layer == l
+            entries = (lat_ref[0, l], lat_ref[1, l], adv_ref[0, l], adv_ref[1, l], vert_ref[l])
+            vals = [jnp.where(hit, entries[k], vals[k]) for k in range(5)]
+        vals[0] = 0.5 * vals[0]
+        vals[1] = 0.5 * vals[1]
+        for k in range(5):
+            co_ref[k, d] = vals[k]
+        ho_ref[d] = h_ref[d]
+        wo_ref[d] = w_ref[d]
+        cbo_ref[d] = c_ref[d]
+        mo_ref[d] = m_ref[d]
+        return carry
+
+    lax.fori_loop(0, layer_ref.shape[0], plane, 0)
 
 
 def make_section_kernel(chunk, first):
@@ -402,15 +433,20 @@
     cgroups = depth // ROWS
     smem_spec = pl.BlockSpec(memory_space=pltpu.SMEM)
     vspec = pl.BlockSpec(memory_space=pltpu.MemorySpace.VMEM)
-    heat, water, carbon, melt, co, xf0, xl0, y0 = pl.pallas_call(
+    xf0, xl0, y0 = pl.pallas_call(
+        edge_kernel,
+        out_shape=(sds((5, groups, ROWS, LANES)), sds((5, groups, ROWS, LANES)),
+                   sds((2, 5, ROWS, LANES))),
+        in_specs=[smem_spec] * 2 + [vspec] * 4,
+    )(lateral_transmissivity, stratum_advection_offsets, stratum_number_grid,
+      thermal_field, steam_content_grid, carbonic_gas_grid)
+    xflo, xfhi, yflo, yfhi = exchange(xf0, xl0, y0)
+    heat, water, carbon, melt, co = pl.pallas_call(
         prep_kernel,
-        out_shape=(sds(shape), sds(shape), sds(shape), sds(shape), sds((5,) + shape),
-                   sds((5, groups, ROWS, LANES)), sds((5, groups, ROWS, LANES)),
-                   sds((2, 5, ROWS, LANES))),
+        out_shape=(sds(shape), sds(shape), sds(shape), sds(shape), sds((5,) + shape)),
         in_specs=[smem_spec] * 3 + [vspec] * 5,
-    )(lateral_transmissivity, vertical_transmissivity, stratum_advection_offsets, stratum_number_grid, thermal_field, steam_content_grid, carbonic_gas_grid,
-      liquid_fraction)
-    xflo, xfhi, yflo, yfhi = exchange(xf0, xl0, y0)
+    )(lateral_transmissivity, vertical_transmissivity, stratum_advection_offsets,
+      stratum_number_grid, thermal_field, steam_content_grid, carbonic_gas_grid, liquid_fraction)
 
     def block_spec(k):
         return pl.BlockSpec((depth, ROWS, LANES), lambda i: (k, 0, 0))

time: 79 us -> 84 us (1.063)
  Pallas kernels: 41.6 us -> 49.2 us
  waiting for transfers between devices: 5.37 us -> 2.83 us
    pallas_call x0 -> x1, Pallas kernels: none -> 7.97 us  [local(): pl.pallas_call(edge_kernel, out_shape=(sds((5, groups, ROWS, LANES)), sds...]
    ppermute x7, waiting for transfers between devices: 2.2 us -> 0.02 us  [exchange(): ylo = lax.ppermute(ys, 'north', north_fwd)]
  transfers between devices with their start and end apart: 24 -> 24, of which waited for: 5 -> 3; matrix products, arithmetic and copies ran while one was open for 0% -> 0% of each run, Pallas kernels for 29% -> 32%
where the time goes in v10:
time: 84 us; the launch traced here: 83.5 us
  Pallas kernels  49.2 us (59%)
  starting transfers between devices  25.6 us (30%)
  local copies, waits for them, and re-layouts  5.01 us (6%)
  waiting for transfers between devices  2.83 us (3%)
  between operations  0.86 us (1%)
    pallas_call x8, Pallas kernels, local(): pl.pallas_call(make_section_kernel(k, first), grid=(1,), out_shape=tuple(...  30.7 us
    ppermute x7, starting transfers between devices, exchange(): xhi = lax.ppermute(xf, 'east', east_bwd)  9.06 us
    ppermute x7, starting transfers between devices, exchange(): ylo = lax.ppermute(ys, 'north', north_fwd)  8.41 us
    pallas_call x1, Pallas kernels, local(): pl.pallas_call(edge_kernel, out_shape=(sds((5, groups, ROWS, LANES)), sds...  7.97 us
    ppermute x3, starting transfers between devices, local(): lax.ppermute(red, 'depth', [(i, (i + k) % count) for i in range(count)])  5.52 us
    unnamed x48, local copies, waits for them, and re-layouts  5.01 us
    pallas_call x1, Pallas kernels, local(): pl.pallas_call(prep_kernel, out_shape=(sds(shape), sds(shape), sds(shape)...  4.27 us
    pallas_call x1, Pallas kernels, local(): pl.pallas_call(sweep_kernel, grid=(1,), out_shape=(sds(shape), sds(shape)...  3.88 us
  transfers between devices with their start and end apart: 24, of which 3 were waited for; matrix products, arithmetic and copies ran while one was open for 0% of the time, Pallas kernels for 32%

profile of v10, /device:TPU:0, one launch (start us, length us, event | category | flops | bytes accessed | tf_op | source)
XLA Modules:
  0.0 83.5 jit_solution(9174384541256145845)
XLA Ops:
  0.6 8.0 %shard_map.121 = (f32[5,8,8,128]{3,2,1,0:T(8,128)}, f32[5,8,8,128]{3,2,1,0:T(8,128)}, f32[2,5,8,128]{3,2,1,0:T(8,128)}) custom-call(f32[2,12]{1,0:T(2,128)} %lat_ref.3, f32[2,12]{1,0:T(2,128)} %adv_ref.3, s32[64,8,128]{2,1,0:T(8,128)} %layer_ref.3, f32[64,8,128]{2,1,0:T(8,128)} %h_ref.3, f32[64,8,128]{2,1,0:T(8,128)} %w_ref.3, f32[64,8,128]{2,1,0:T(8,128)} %c_ref.3), custom_call_target="tpu_custom_call" | custom-call | tf_op jit(solution)/shard_map/pallas_call | solution.py:436
  8.6 0.5 collective-permute-start
  9.1 1.9 %collective-permute-start.1 = (f32[5,8,8,128]{3,2,1,0:T(8,128)}, f32[5,8,8,128]{3,2,1,0:T(8,128)S(1)}, u32[]{:S(2)}, u32[]{:S(2)}) collective-permute-start(f32[5,8,8,128]{3,2,1,0:T(8,128)} %get-tuple-element.74), channel_id=1, source_target_pairs={{8,0},{16,8},{24,16},{0,24},{9,1},{17,9},{25,17},{1,25},{10,2},{18... | collective-permute-start | bytes 491528 | tf_op jit(solution)/shard_map/ppermute | solution.py:402
  11.0 2.3 %collective-permute-start.2 = (f32[2,5,8,128]{3,2,1,0:T(8,128)}, f32[2,5,8,128]{3,2,1,0:T(8,128)S(1)}, u32[]{:S(2)}, u32[]{:S(2)}) collective-permute-start(f32[2,5,8,128]{3,2,1,0:T(8,128)} %get-tuple-element.75), channel_id=1, source_target_pairs={{0,4},{4,0},{1,5},{5,1},{2,6},{6,2},{3,7},{7,3},{8,12},{12,8},{9,1... | collective-permute-start | bytes 122888 | tf_op jit(solution)/shard_map/ppermute | solution.py:403
  13.3 4.3 %shard_map.120 = (f32[64,8,128]{2,1,0:T(8,128)}, f32[64,8,128]{2,1,0:T(8,128)}, f32[64,8,128]{2,1,0:T(8,128)}, f32[64,8,128]{2,1,0:T(8,128)}, f32[5,64,8,128]{3,2,1,0:T(8,128)}) custom-call(f32[2,12]{1,0:T(2,128)} %lat_ref.3, f32[12]{0:T(128)} %vert_ref.1, f32[2,12]{1,0:T(2,128)} %adv_ref.3, s32[64,8,128]{2,1,0:T(8,128)} %layer_ref.3, f32[64,8,128]{2,1,0:T(8,128)} %h_ref.3, ...), custom_call_target="tpu_custom_call" | custom-call | tf_op jit(solution)/shard_map/pallas_call | solution.py:444
  17.6 0.6 copy-done.2
  18.2 0.1 copy-done
  18.3 0.1 copy-done.1
  18.3 4.5 %shard_map.122 = (f32[64,8,128]{2,1,0:T(8,128)}, f32[64,8,128]{2,1,0:T(8,128)}, f32[64,8,128]{2,1,0:T(8,128)}, f32[64,8,128]{2,1,0:T(8,128)}, f32[3,4,8,128]{3,2...) custom-call(f32[64,8,128]{2,1,0:T(8,128)} %get-tuple-element.68.h_re, ...), custom_call_target="tpu_custom_call", output_to_operand_aliasing={{0}: (0, {}), {1}: (1, {}), {2}: (2, {}), {3}: (3, {})} | custom-call | tf_op jit(solution)/shard_map/pallas_call | solution.py:479
  22.9 1.7 %collective-permute-start.4 = (f32[3,4,8,128]{3,2,1,0:T(8,128)}, f32[3,4,8,128]{3,2,1,0:T(8,128)S(1)}, u32[]{:S(2)}, u32[]{:S(2)}) collective-permute-start(f32[3,4,8,128]{3,2,1,0:T(8,128)} %get-tuple-element.86), channel_id=1, source_target_pairs={{8,0},{16,8},{24,16},{0,24},{9,1},{17,9},{25,17},{1,25},{10,2},{18... | collective-permute-start | bytes 147464 | tf_op jit(solution)/shard_map/ppermute | solution.py:402
  24.6 4.5 %shard_map.123 = (f32[64,8,128]{2,1,0:T(8,128)}, f32[64,8,128]{2,1,0:T(8,128)}, f32[64,8,128]{2,1,0:T(8,128)}, f32[64,8,128]{2,1,0:T(8,128)}, f32[3,4,8,128]{3,2...) custom-call(f32[64,8,128]{2,1,0:T(8,128)} %get-tuple-element.76.h_re, ...), custom_call_target="tpu_custom_call", output_to_operand_aliasing={{0}: (0, {}), {1}: (1, {}), {2}: (2, {}), {3}: (3, {})} | custom-call | tf_op jit(solution)/shard_map/pallas_call | solution.py:479
  29.2 0.1 collective-permute-start.6
  29.2 1.7 %collective-permute-start.7 = (f32[3,4,8,128]{3,2,1,0:T(8,128)}, f32[3,4,8,128]{3,2,1,0:T(8,128)S(1)}, u32[]{:S(2)}, u32[]{:S(2)}) collective-permute-start(f32[3,4,8,128]{3,2,1,0:T(8,128)} %get-tuple-element.94), channel_id=1, source_target_pairs={{8,0},{16,8},{24,16},{0,24},{9,1},{17,9},{25,17},{1,25},{10,2},{18... | collective-permute-start | bytes 147464 | tf_op jit(solution)/shard_map/ppermute | solution.py:402
  30.9 2.0 %collective-permute-start.8 = (f32[2,3,8,128]{3,2,1,0:T(8,128)}, f32[2,3,8,128]{3,2,1,0:T(8,128)S(1)}, u32[]{:S(2)}, u32[]{:S(2)}) collective-permute-start(f32[2,3,8,128]{3,2,1,0:T(8,128)} %get-tuple-element.95), channel_id=1, source_target_pairs={{0,4},{4,0},{1,5},{5,1},{2,6},{6,2},{3,7},{7,3},{8,12},{12,8},{9,1... | collective-permute-start | bytes 73736 | tf_op jit(solution)/shard_map/ppermute | solution.py:403
  33.0 0.6 copy-done.19
  33.6 3.6 %shard_map.124 = (f32[64,8,128]{2,1,0:T(8,128)}, f32[64,8,128]{2,1,0:T(8,128)}, f32[64,8,128]{2,1,0:T(8,128)}, f32[64,8,128]{2,1,0:T(8,128)}, f32[3,4,8,128]{3,2...) custom-call(f32[64,8,128]{2,1,0:T(8,128)} %get-tuple-element.80.h_re, ...), custom_call_target="tpu_custom_call", output_to_operand_aliasing={{0}: (0, {}), {1}: (1, {}), {2}: (2, {}), {3}: (3, {})} | custom-call | tf_op jit(solution)/shard_map/pallas_call | solution.py:479
  37.2 0.5 collective-permute-start.9
  37.7 0.6 copy-done.3
  38.3 0.0 copy-done.9
  38.3 0.0 copy-done.13
  38.4 3.6 %shard_map.125 = (f32[64,8,128]{2,1,0:T(8,128)}, f32[64,8,128]{2,1,0:T(8,128)}, f32[64,8,128]{2,1,0:T(8,128)}, f32[64,8,128]{2,1,0:T(8,128)}, f32[3,4,8,128]{3,2...) custom-call(f32[64,8,128]{2,1,0:T(8,128)} %get-tuple-element.88.h_re, ...), custom_call_target="tpu_custom_call", output_to_operand_aliasing={{0}: (0, {}), {1}: (1, {}), {2}: (2, {}), {3}: (3, {})} | custom-call | tf_op jit(solution)/shard_map/pallas_call | solution.py:479
  42.0 1.4 %collective-permute-start.12 = (f32[3,4,8,128]{3,2,1,0:T(8,128)}, f32[3,4,8,128]{3,2,1,0:T(8,128)S(1)}, u32[]{:S(2)}, u32[]{:S(2)}) collective-permute-start(f32[3,4,8,128]{3,2,1,0:T(8,128)} %get-tuple-element.107), channel_id=1, source_target_pairs={{0,8},{8,16},{16,24},{24,0},{1,9},{9,17},{17,25},{25,1},{2,10},{10... | collective-permute-start | bytes 147464 | tf_op jit(solution)/shard_map/ppermute | solution.py:401
  43.4 0.4 collective-permute-start.13
  43.8 2.0 %collective-permute-start.14 = (f32[2,3,8,128]{3,2,1,0:T(8,128)}, f32[2,3,8,128]{3,2,1,0:T(8,128)S(1)}, u32[]{:S(2)}, u32[]{:S(2)}) collective-permute-start(f32[2,3,8,128]{3,2,1,0:T(8,128)} %get-tuple-element.109), channel_id=1, source_target_pairs={{0,4},{4,0},{1,5},{5,1},{2,6},{6,2},{3,7},{7,3},{8,12},{12,8},{9,1... | collective-permute-start | bytes 73736 | tf_op jit(solution)/shard_map/ppermute | solution.py:403
  45.8 0.6 copy-done.10
  46.4 3.6 %shard_map.126 = (f32[64,8,128]{2,1,0:T(8,128)}, f32[64,8,128]{2,1,0:T(8,128)}, f32[64,8,128]{2,1,0:T(8,128)}, f32[64,8,128]{2,1,0:T(8,128)}, f32[3,4,8,128]{3,2...) custom-call(f32[64,8,128]{2,1,0:T(8,128)} %get-tuple-element.96.h_re, ...), custom_call_target="tpu_custom_call", output_to_operand_aliasing={{0}: (0, {}), {1}: (1, {}), {2}: (2, {}), {3}: (3, {})} | custom-call | tf_op jit(solution)/shard_map/pallas_call | solution.py:479
  50.0 1.7 %collective-permute-start.16 = (f32[3,4,8,128]{3,2,1,0:T(8,128)}, f32[3,4,8,128]{3,2,1,0:T(8,128)S(1)}, u32[]{:S(2)}, u32[]{:S(2)}) collective-permute-start(f32[3,4,8,128]{3,2,1,0:T(8,128)} %get-tuple-element.115), channel_id=1, source_target_pairs={{8,0},{16,8},{24,16},{0,24},{9,1},{17,9},{25,17},{1,25},{10,2},{18... | collective-permute-start | bytes 147464 | tf_op jit(solution)/shard_map/ppermute | solution.py:402
  51.8 0.6 copy-done.6
  52.4 0.0 copy-done.12
  52.4 3.6 %shard_map.127 = (f32[64,8,128]{2,1,0:T(8,128)}, f32[64,8,128]{2,1,0:T(8,128)}, f32[64,8,128]{2,1,0:T(8,128)}, f32[64,8,128]{2,1,0:T(8,128)}, f32[3,4,8,128]{3,2...) custom-call(f32[64,8,128]{2,1,0:T(8,128)} %get-tuple-element.103.h_r, ...), custom_call_target="tpu_custom_call", output_to_operand_aliasing={{0}: (0, {}), {1}: (1, {}), {2}: (2, {}), {3}: (3, {})} | custom-call | tf_op jit(solution)/shard_map/pallas_call | solution.py:479
  56.0 0.2 collective-permute-start.18
  56.2 1.6 %collective-permute-start.19 = (f32[3,4,8,128]{3,2,1,0:T(8,128)}, f32[3,4,8,128]{3,2,1,0:T(8,128)S(1)}, u32[]{:S(2)}, u32[]{:S(2)}) collective-permute-start(f32[3,4,8,128]{3,2,1,0:T(8,128)} %get-tuple-element.122), channel_id=1, source_target_pairs={{8,0},{16,8},{24,16},{0,24},{9,1},{17,9},{25,17},{1,25},{10,2},{18... | collective-permute-start | bytes 147464 | tf_op jit(solution)/shard_map/ppermute | solution.py:402
  57.8 2.0 %collective-permute-start.20 = (f32[2,3,8,128]{3,2,1,0:T(8,128)}, f32[2,3,8,128]{3,2,1,0:T(8,128)S(1)}, u32[]{:S(2)}, u32[]{:S(2)}) collective-permute-start(f32[2,3,8,128]{3,2,1,0:T(8,128)} %get-tuple-element.123), channel_id=1, source_target_pairs={{0,4},{4,0},{1,5},{5,1},{2,6},{6,2},{3,7},{7,3},{8,12},{12,8},{9,1... | collective-permute-start | bytes 73736 | tf_op jit(solution)/shard_map/ppermute | solution.py:403
  59.9 0.6 copy-done.11
  60.5 3.6 %shard_map.128 = (f32[64,8,128]{2,1,0:T(8,128)}, f32[64,8,128]{2,1,0:T(8,128)}, f32[64,8,128]{2,1,0:T(8,128)}, f32[64,8,128]{2,1,0:T(8,128)}, f32[3,4,8,128]{3,2...) custom-call(f32[64,8,128]{2,1,0:T(8,128)} %get-tuple-element.110.h_r, ...), custom_call_target="tpu_custom_call", output_to_operand_aliasing={{0}: (0, {}), {1}: (1, {}), {2}: (2, {}), {3}: (3, {})} | custom-call | tf_op jit(solution)/shard_map/pallas_call | solution.py:479
  64.1 0.6 copy-done.7
  64.7 0.0 copy-done.17
  64.7 0.0 copy-done.18
  64.7 3.6 %shard_map.129 = (f32[64,8,128]{2,1,0:T(8,128)}, f32[64,8,128]{2,1,0:T(8,128)}, f32[64,8,128]{2,1,0:T(8,128)}, f32[64,8,128]{2,1,0:T(8,128)}, f32[3,4,8,128]{3,2...) custom-call(f32[64,8,128]{2,1,0:T(8,128)} %get-tuple-element.117.h_r, ...), custom_call_target="tpu_custom_call", output_to_operand_aliasing={{0}: (0, {}), {1}: (1, {}), {2}: (2, {}), {3}: (3, {})} | custom-call | tf_op jit(solution)/shard_map/pallas_call | solution.py:479
  68.4 3.9 %shard_map.130 = (f32[64,8,128]{2,1,0:T(8,128)}, f32[64,8,128]{2,1,0:T(8,128)}, f32[64,8,128]{2,1,0:T(8,128)}, f32[8,8,128]{2,1,0:T(8,128)}) custom-call(f32[64,8,128]{2,1,0:T(8,128)} %get-tuple-element.124.r_ref, f32[5,64,8,128]{3,2,1,0:T(8,128)} %get-tuple-element.72.co_ref.cz_ref), custom_call_target="tpu_custom_call" | custom-call | tf_op jit(solution)/shard_map/pallas_call | solution.py:493
  72.2 1.6 %collective-permute-start.21 = (f32[8,8,128]{2,1,0:T(8,128)}, f32[8,8,128]{2,1,0:T(8,128)S(1)}, u32[]{:S(2)}, u32[]{:S(2)}) collective-permute-start(f32[8,8,128]{2,1,0:T(8,128)} %get-tuple-element.128.rest_0_), channel_id=1, source_target_pairs={{0,1},{1,2},{2,3},{3,0},{4,5},{5,6},{6,7},{7,4},{8,9},{9,10},{10,1... | collective-permute-start | bytes 98312 | tf_op jit(solution)/shard_map/ppermute | solution.py:505
  73.8 2.6 %collective-permute-start.22 = (f32[8,8,128]{2,1,0:T(8,128)}, f32[8,8,128]{2,1,0:T(8,128)S(1)}, u32[]{:S(2)}, u32[]{:S(2)}) collective-permute-start(f32[8,8,128]{2,1,0:T(8,128)} %get-tuple-element.128.rest_0_), channel_id=1, source_target_pairs={{0,2},{1,3},{2,0},{3,1},{4,6},{5,7},{6,4},{7,5},{8,10},{9,11},{10,... | collective-permute-start | bytes 98312 | tf_op jit(solution)/shard_map/ppermute | solution.py:505
  76.4 1.3 %collective-permute-start.23 = (f32[8,8,128]{2,1,0:T(8,128)}, f32[8,8,128]{2,1,0:T(8,128)S(1)}, u32[]{:S(2)}, u32[]{:S(2)}) collective-permute-start(f32[8,8,128]{2,1,0:T(8,128)} %get-tuple-element.128.rest_0_), channel_id=1, source_target_pairs={{0,3},{1,0},{2,1},{3,2},{4,7},{5,4},{6,5},{7,6},{8,11},{9,8},{10,9... | collective-permute-start | bytes 98312 | tf_op jit(solution)/shard_map/ppermute | solution.py:505
  77.8 0.7 collective-permute-done.21.rest_1_
  78.5 0.8 collective-permute-done.22.rest_2_
  79.2 1.3 %collective-permute-done.23.rest_3_ = f32[8,8,128]{2,1,0:T(8,128)S(1)} collective-permute-done((f32[8,8,128]{2,1,0:T(8,128)}, f32[8,8,128]{2,1,0:T(8,128)S(1)}, u32[]{:S(2)}, u32[]{:S(2)}) %collective-permute-start.23) | collective-permute-done | bytes 32800 | tf_op jit(solution)/shard_map/ppermute | solution.py:505
  80.5 0.6 copy-done.23
  81.1 2.4 %shard_map.131 = f32[64,8,128]{2,1,0:T(8,128)} custom-call(s32[1]{0:T(128)} %bitcast.rank_ref, f32[64,8,128]{2,1,0:T(8,128)} %get-tuple-element.125.y_ref, f32[64,8,128]{2,1,0:T(8,128)} %get-tuple-element.126.a_ref, f32[64,8,128]{2,1,0:T(8,128)} %get-tuple-element.127.b_ref, f32[8,8,128]{2,1,0:T(8,128)} %get-tuple-element.128.rest_0_, ...), custom_call_target="tpu_custom_call" | custom-call | tf_op jit(solution)/shard_map/pallas_call | solution.py:507
  (60 shorter events, 0.3 us)
Async XLA Ops:
  8.6 9.0 %collective-permute-start = (f32[5,8,8,128]{3,2,1,0:T(8,128)}, f32[5,8,8,128]{3,2,1,0:T(8,128)S(1)}, u32[]{:S(2)}, u32[]{:S(2)}) collective-permute-start(f32[5,8,8,128]{3,2,1,0:T(8,128)} %get-tuple-element.73), channel_id=1, source_target_pairs={{0,8},{8,16},{16,24},{24,0},{1,9},{9,17},{17,25},{25,1},{2,10},{10... | collective-permute-start | bytes 491528 | tf_op jit(solution)/shard_map/ppermute | solution.py:401
  9.1 8.6 %collective-permute-start.1 = (f32[5,8,8,128]{3,2,1,0:T(8,128)}, f32[5,8,8,128]{3,2,1,0:T(8,128)S(1)}, u32[]{:S(2)}, u32[]{:S(2)}) collective-permute-start(f32[5,8,8,128]{3,2,1,0:T(8,128)} %get-tuple-element.74), channel_id=1, source_target_pairs={{8,0},{16,8},{24,16},{0,24},{9,1},{17,9},{25,17},{1,25},{10,2},{18... | collective-permute-start | bytes 491528 | tf_op jit(solution)/shard_map/ppermute | solution.py:402
  11.0 6.6 %collective-permute-start.2 = (f32[2,5,8,128]{3,2,1,0:T(8,128)}, f32[2,5,8,128]{3,2,1,0:T(8,128)S(1)}, u32[]{:S(2)}, u32[]{:S(2)}) collective-permute-start(f32[2,5,8,128]{3,2,1,0:T(8,128)} %get-tuple-element.75), channel_id=1, source_target_pairs={{0,4},{4,0},{1,5},{5,1},{2,6},{6,2},{3,7},{7,3},{8,12},{12,8},{9,1... | collective-permute-start | bytes 122888 | tf_op jit(solution)/shard_map/ppermute | solution.py:403
  17.6 0.6 copy-start.2
  17.6 0.7 copy-start
  17.6 0.7 copy-start.1
  22.9 10.1 %collective-permute-start.3 = (f32[3,4,8,128]{3,2,1,0:T(8,128)}, f32[3,4,8,128]{3,2,1,0:T(8,128)S(1)}, u32[]{:S(2)}, u32[]{:S(2)}) collective-permute-start(f32[3,4,8,128]{3,2,1,0:T(8,128)} %get-tuple-element.85), channel_id=1, source_target_pairs={{0,8},{8,16},{16,24},{24,0},{1,9},{9,17},{17,25},{25,1},{2,10},{10... | collective-permute-start | bytes 147464 | tf_op jit(solution)/shard_map/ppermute | solution.py:401
  22.9 10.1 %collective-permute-start.4 = (f32[3,4,8,128]{3,2,1,0:T(8,128)}, f32[3,4,8,128]{3,2,1,0:T(8,128)S(1)}, u32[]{:S(2)}, u32[]{:S(2)}) collective-permute-start(f32[3,4,8,128]{3,2,1,0:T(8,128)} %get-tuple-element.86), channel_id=1, source_target_pairs={{8,0},{16,8},{24,16},{0,24},{9,1},{17,9},{25,17},{1,25},{10,2},{18... | collective-permute-start | bytes 147464 | tf_op jit(solution)/shard_map/ppermute | solution.py:402
  24.6 6.3 %collective-permute-start.5 = (f32[2,3,8,128]{3,2,1,0:T(8,128)}, f32[2,3,8,128]{3,2,1,0:T(8,128)S(1)}, u32[]{:S(2)}, u32[]{:S(2)}) collective-permute-start(f32[2,3,8,128]{3,2,1,0:T(8,128)} %get-tuple-element.87), channel_id=1, source_target_pairs={{0,4},{4,0},{1,5},{5,1},{2,6},{6,2},{3,7},{7,3},{8,12},{12,8},{9,1... | collective-permute-start | bytes 73736 | tf_op jit(solution)/shard_map/ppermute | solution.py:403
  29.2 8.6 %collective-permute-start.6 = (f32[3,4,8,128]{3,2,1,0:T(8,128)}, f32[3,4,8,128]{3,2,1,0:T(8,128)S(1)}, u32[]{:S(2)}, u32[]{:S(2)}) collective-permute-start(f32[3,4,8,128]{3,2,1,0:T(8,128)} %get-tuple-element.93), channel_id=1, source_target_pairs={{0,8},{8,16},{16,24},{24,0},{1,9},{9,17},{17,25},{25,1},{2,10},{10... | collective-permute-start | bytes 147464 | tf_op jit(solution)/shard_map/ppermute | solution.py:401
  29.2 8.5 %collective-permute-start.7 = (f32[3,4,8,128]{3,2,1,0:T(8,128)}, f32[3,4,8,128]{3,2,1,0:T(8,128)S(1)}, u32[]{:S(2)}, u32[]{:S(2)}) collective-permute-start(f32[3,4,8,128]{3,2,1,0:T(8,128)} %get-tuple-element.94), channel_id=1, source_target_pairs={{8,0},{16,8},{24,16},{0,24},{9,1},{17,9},{25,17},{1,25},{10,2},{18... | collective-permute-start | bytes 147464 | tf_op jit(solution)/shard_map/ppermute | solution.py:402
  30.9 2.0 %copy-start.8 = (f32[2,3,8,128]{3,2,1,0:T(8,128)}, f32[2,3,8,128]{3,2,1,0:T(8,128)S(1)}, u32[]{:S(2)}) copy-start(f32[2,3,8,128]{3,2,1,0:T(8,128)S(1)} %collective-permute-done.5.rest_3_.rest_4_) | copy-start | bytes 73732
  30.9 6.8 %collective-permute-start.8 = (f32[2,3,8,128]{3,2,1,0:T(8,128)}, f32[2,3,8,128]{3,2,1,0:T(8,128)S(1)}, u32[]{:S(2)}, u32[]{:S(2)}) collective-permute-start(f32[2,3,8,128]{3,2,1,0:T(8,128)} %get-tuple-element.95), channel_id=1, source_target_pairs={{0,4},{4,0},{1,5},{5,1},{2,6},{6,2},{3,7},{7,3},{8,12},{12,8},{9,1... | collective-permute-start | bytes 73736 | tf_op jit(solution)/shard_map/ppermute | solution.py:403
  32.9 0.6 copy-start.19
  32.9 0.6 copy-start.20
  37.2 8.6 %collective-permute-start.10 = (f32[3,4,8,128]{3,2,1,0:T(8,128)}, f32[3,4,8,128]{3,2,1,0:T(8,128)S(1)}, u32[]{:S(2)}, u32[]{:S(2)}) collective-permute-start(f32[3,4,8,128]{3,2,1,0:T(8,128)} %get-tuple-element.101), channel_id=1, source_target_pairs={{8,0},{16,8},{24,16},{0,24},{9,1},{17,9},{25,17},{1,25},{10,2},{18... | collective-permute-start | bytes 147464 | tf_op jit(solution)/shard_map/ppermute | solution.py:402
  37.2 8.6 %collective-permute-start.9 = (f32[3,4,8,128]{3,2,1,0:T(8,128)}, f32[3,4,8,128]{3,2,1,0:T(8,128)S(1)}, u32[]{:S(2)}, u32[]{:S(2)}) collective-permute-start(f32[3,4,8,128]{3,2,1,0:T(8,128)} %get-tuple-element.100), channel_id=1, source_target_pairs={{0,8},{8,16},{16,24},{24,0},{1,9},{9,17},{17,25},{25,1},{2,10},{10... | collective-permute-start | bytes 147464 | tf_op jit(solution)/shard_map/ppermute | solution.py:401
  37.7 0.6 copy-start.3
  37.7 6.0 %collective-permute-start.11 = (f32[2,3,8,128]{3,2,1,0:T(8,128)}, f32[2,3,8,128]{3,2,1,0:T(8,128)S(1)}, u32[]{:S(2)}, u32[]{:S(2)}) collective-permute-start(f32[2,3,8,128]{3,2,1,0:T(8,128)} %get-tuple-element.102), channel_id=1, source_target_pairs={{0,4},{4,0},{1,5},{5,1},{2,6},{6,2},{3,7},{7,3},{8,12},{12,8},{9,1... | collective-permute-start | bytes 73736 | tf_op jit(solution)/shard_map/ppermute | solution.py:403
  37.7 0.6 copy-start.9
  37.7 0.6 copy-start.13
  42.0 9.8 %collective-permute-start.12 = (f32[3,4,8,128]{3,2,1,0:T(8,128)}, f32[3,4,8,128]{3,2,1,0:T(8,128)S(1)}, u32[]{:S(2)}, u32[]{:S(2)}) collective-permute-start(f32[3,4,8,128]{3,2,1,0:T(8,128)} %get-tuple-element.107), channel_id=1, source_target_pairs={{0,8},{8,16},{16,24},{24,0},{1,9},{9,17},{17,25},{25,1},{2,10},{10... | collective-permute-start | bytes 147464 | tf_op jit(solution)/shard_map/ppermute | solution.py:401
  43.4 8.4 %collective-permute-start.13 = (f32[3,4,8,128]{3,2,1,0:T(8,128)}, f32[3,4,8,128]{3,2,1,0:T(8,128)S(1)}, u32[]{:S(2)}, u32[]{:S(2)}) collective-permute-start(f32[3,4,8,128]{3,2,1,0:T(8,128)} %get-tuple-element.108), channel_id=1, source_target_pairs={{8,0},{16,8},{24,16},{0,24},{9,1},{17,9},{25,17},{1,25},{10,2},{18... | collective-permute-start | bytes 147464 | tf_op jit(solution)/shard_map/ppermute | solution.py:402
  43.7 2.0 %copy-start.4 = (f32[2,3,8,128]{3,2,1,0:T(8,128)}, f32[2,3,8,128]{3,2,1,0:T(8,128)S(1)}, u32[]{:S(2)}) copy-start(f32[2,3,8,128]{3,2,1,0:T(8,128)S(1)} %collective-permute-done.11.rest_3_.rest_4_) | copy-start | bytes 73732
  43.8 8.0 %collective-permute-start.14 = (f32[2,3,8,128]{3,2,1,0:T(8,128)}, f32[2,3,8,128]{3,2,1,0:T(8,128)S(1)}, u32[]{:S(2)}, u32[]{:S(2)}) collective-permute-start(f32[2,3,8,128]{3,2,1,0:T(8,128)} %get-tuple-element.109), channel_id=1, source_target_pairs={{0,4},{4,0},{1,5},{5,1},{2,6},{6,2},{3,7},{7,3},{8,12},{12,8},{9,1... | collective-permute-start | bytes 73736 | tf_op jit(solution)/shard_map/ppermute | solution.py:403
  45.8 0.6 copy-start.10
  45.8 0.6 copy-start.14
  50.0 9.8 %collective-permute-start.15 = (f32[3,4,8,128]{3,2,1,0:T(8,128)}, f32[3,4,8,128]{3,2,1,0:T(8,128)S(1)}, u32[]{:S(2)}, u32[]{:S(2)}) collective-permute-start(f32[3,4,8,128]{3,2,1,0:T(8,128)} %get-tuple-element.114), channel_id=1, source_target_pairs={{0,8},{8,16},{16,24},{24,0},{1,9},{9,17},{17,25},{25,1},{2,10},{10... | collective-permute-start | bytes 147464 | tf_op jit(solution)/shard_map/ppermute | solution.py:401
  50.0 9.8 %collective-permute-start.16 = (f32[3,4,8,128]{3,2,1,0:T(8,128)}, f32[3,4,8,128]{3,2,1,0:T(8,128)S(1)}, u32[]{:S(2)}, u32[]{:S(2)}) collective-permute-start(f32[3,4,8,128]{3,2,1,0:T(8,128)} %get-tuple-element.115), channel_id=1, source_target_pairs={{8,0},{16,8},{24,16},{0,24},{9,1},{17,9},{25,17},{1,25},{10,2},{18... | collective-permute-start | bytes 147464 | tf_op jit(solution)/shard_map/ppermute | solution.py:402
  51.8 0.6 copy-start.6
  51.8 6.0 %collective-permute-start.17 = (f32[2,3,8,128]{3,2,1,0:T(8,128)}, f32[2,3,8,128]{3,2,1,0:T(8,128)S(1)}, u32[]{:S(2)}, u32[]{:S(2)}) collective-permute-start(f32[2,3,8,128]{3,2,1,0:T(8,128)} %get-tuple-element.116), channel_id=1, source_target_pairs={{0,4},{4,0},{1,5},{5,1},{2,6},{6,2},{3,7},{7,3},{8,12},{12,8},{9,1... | collective-permute-start | bytes 73736 | tf_op jit(solution)/shard_map/ppermute | solution.py:403
  51.8 0.6 copy-start.12
  51.8 0.6 copy-start.16
  56.0 8.0 %collective-permute-start.18 = (f32[3,4,8,128]{3,2,1,0:T(8,128)}, f32[3,4,8,128]{3,2,1,0:T(8,128)S(1)}, u32[]{:S(2)}, u32[]{:S(2)}) collective-permute-start(f32[3,4,8,128]{3,2,1,0:T(8,128)} %get-tuple-element.121), channel_id=1, source_target_pairs={{0,8},{8,16},{16,24},{24,0},{1,9},{9,17},{17,25},{25,1},{2,10},{10... | collective-permute-start | bytes 147464 | tf_op jit(solution)/shard_map/ppermute | solution.py:401
  56.2 7.9 %collective-permute-start.19 = (f32[3,4,8,128]{3,2,1,0:T(8,128)}, f32[3,4,8,128]{3,2,1,0:T(8,128)S(1)}, u32[]{:S(2)}, u32[]{:S(2)}) collective-permute-start(f32[3,4,8,128]{3,2,1,0:T(8,128)} %get-tuple-element.122), channel_id=1, source_target_pairs={{8,0},{16,8},{24,16},{0,24},{9,1},{17,9},{25,17},{1,25},{10,2},{18... | collective-permute-start | bytes 147464 | tf_op jit(solution)/shard_map/ppermute | solution.py:402
  57.8 2.0 %copy-start.5 = (f32[2,3,8,128]{3,2,1,0:T(8,128)}, f32[2,3,8,128]{3,2,1,0:T(8,128)S(1)}, u32[]{:S(2)}) copy-start(f32[2,3,8,128]{3,2,1,0:T(8,128)S(1)} %collective-permute-done.17.rest_3_.rest_4_) | copy-start | bytes 73732
  57.8 6.3 %collective-permute-start.20 = (f32[2,3,8,128]{3,2,1,0:T(8,128)}, f32[2,3,8,128]{3,2,1,0:T(8,128)S(1)}, u32[]{:S(2)}, u32[]{:S(2)}) collective-permute-start(f32[2,3,8,128]{3,2,1,0:T(8,128)} %get-tuple-element.123), channel_id=1, source_target_pairs={{0,4},{4,0},{1,5},{5,1},{2,6},{6,2},{3,7},{7,3},{8,12},{12,8},{9,1... | collective-permute-start | bytes 73736 | tf_op jit(solution)/shard_map/ppermute | solution.py:403
  59.8 0.6 copy-start.11
  59.8 0.6 copy-start.15
  64.1 0.6 copy-start.7
  64.1 0.6 copy-start.17
  64.1 0.6 copy-start.18
  72.2 6.2 %collective-permute-start.21 = (f32[8,8,128]{2,1,0:T(8,128)}, f32[8,8,128]{2,1,0:T(8,128)S(1)}, u32[]{:S(2)}, u32[]{:S(2)}) collective-permute-start(f32[8,8,128]{2,1,0:T(8,128)} %get-tuple-element.128.rest_0_), channel_id=1, source_target_pairs={{0,1},{1,2},{2,3},{3,0},{4,5},{5,6},{6,7},{7,4},{8,9},{9,10},{10,1... | collective-permute-start | bytes 98312 | tf_op jit(solution)/shard_map/ppermute | solution.py:505
  73.8 5.4 %collective-permute-start.22 = (f32[8,8,128]{2,1,0:T(8,128)}, f32[8,8,128]{2,1,0:T(8,128)S(1)}, u32[]{:S(2)}, u32[]{:S(2)}) collective-permute-start(f32[8,8,128]{2,1,0:T(8,128)} %get-tuple-element.128.rest_0_), channel_id=1, source_target_pairs={{0,2},{1,3},{2,0},{3,1},{4,6},{5,7},{6,4},{7,5},{8,10},{9,11},{10,... | collective-permute-start | bytes 98312 | tf_op jit(solution)/shard_map/ppermute | solution.py:505
  76.4 4.1 %collective-permute-start.23 = (f32[8,8,128]{2,1,0:T(8,128)}, f32[8,8,128]{2,1,0:T(8,128)S(1)}, u32[]{:S(2)}, u32[]{:S(2)}) collective-permute-start(f32[8,8,128]{2,1,0:T(8,128)} %get-tuple-element.128.rest_0_), channel_id=1, source_target_pairs={{0,3},{1,0},{2,1},{3,2},{4,7},{5,4},{6,5},{7,6},{8,11},{9,8},{10,9... | collective-permute-start | bytes 98312 | tf_op jit(solution)/shard_map/ppermute | solution.py:505
  78.5 2.1 %copy-start.21 = (f32[8,8,128]{2,1,0:T(8,128)}, f32[8,8,128]{2,1,0:T(8,128)S(1)}, u32[]{:S(2)}) copy-start(f32[8,8,128]{2,1,0:T(8,128)S(1)} %collective-permute-done.21.rest_1_) | copy-start | bytes 98308
  79.2 1.3 %copy-start.22 = (f32[8,8,128]{2,1,0:T(8,128)}, f32[8,8,128]{2,1,0:T(8,128)S(1)}, u32[]{:S(2)}) copy-start(f32[8,8,128]{2,1,0:T(8,128)S(1)} %collective-permute-done.22.rest_2_) | copy-start | bytes 98308
  80.5 0.6 copy-start.23

commit v11 on v10

--- a/solution.py
+++ b/solution.py
@@ -106,23 +106,26 @@
     zero = jnp.zeros((ROWS, LANES), f32)
     izero = jnp.zeros((ROWS, LANES), jnp.int32)
 
-    def plane(d, carry):
+    def group(a, carry):
         firsts, lasts, lay_f, lay_l = carry
-        at_d = lane == d
-        firsts = tuple(
-            jnp.where(at_d, pltpu.roll(r[d], d, 1), v) for r, v in zip((h_ref, w_ref, c_ref), firsts)
-        )
-        lasts = tuple(
-            jnp.where(at_d, pltpu.roll(r[d], (d + 1) % LANES, 1), v)
-            for r, v in zip((h_ref, w_ref, c_ref), lasts)
-        )
-        layer = layer_ref[d]
-        lay_f = jnp.where(at_d, pltpu.roll(layer, d, 1), lay_f)
-        lay_l = jnp.where(at_d, pltpu.roll(layer, (d + 1) % LANES, 1), lay_l)
+        for b in range(ROWS):
+            d = a * ROWS + b
+            at_d = lane == d
+            srcs = (h_ref[d], w_ref[d], c_ref[d])
+            firsts = tuple(
+                jnp.where(at_d, pltpu.roll(v, d, 1), acc) for v, acc in zip(srcs, firsts)
+            )
+            lasts = tuple(
+                jnp.where(at_d, pltpu.roll(v, (d + 1) % LANES, 1), acc)
+                for v, acc in zip(srcs, lasts)
+            )
+            layer = layer_ref[d]
+            lay_f = jnp.where(at_d, pltpu.roll(layer, d, 1), lay_f)
+            lay_l = jnp.where(at_d, pltpu.roll(layer, (d + 1) % LANES, 1), lay_l)
         return firsts, lasts, lay_f, lay_l
 
     firsts, lasts, lay_f, lay_l = lax.fori_loop(
-        0, n, plane, ((zero,) * 3, (zero,) * 3, izero, izero)
+        0, n // ROWS, group, ((zero,) * 3, (zero,) * 3, izero, izero)
     )
     for side, vals, lay in ((0, firsts, lay_f), (1, lasts, lay_l)):
         for f in range(3):

time: 84 us -> 80 us (0.952)
  Pallas kernels: 49.2 us -> 45.3 us
    pallas_call x1, Pallas kernels: 7.97 us -> 4.02 us  [local(): pl.pallas_call(edge_kernel, out_shape=(sds((5, groups, ROWS, LANES)), sds...]
  transfers between devices with their start and end apart: 24 -> 24, of which waited for: 3 -> 3; matrix products, arithmetic and copies ran while one was open for 0% -> 0% of each run, Pallas kernels for 32% -> 34%
where the time goes in v11:
time: 80 us; the launch traced here: 79.6 us
  Pallas kernels  45.3 us (57%)
  starting transfers between devices  25.6 us (32%)
  local copies, waits for them, and re-layouts  5.01 us (6%)
  waiting for transfers between devices  2.83 us (4%)
  between operations  0.86 us (1%)
    pallas_call x8, Pallas kernels, local(): pl.pallas_call(make_section_kernel(k, first), grid=(1,), out_shape=tuple(...  30.7 us
    ppermute x7, starting transfers between devices, exchange(): xhi = lax.ppermute(xf, 'east', east_bwd)  9.06 us
    ppermute x7, starting transfers between devices, exchange(): ylo = lax.ppermute(ys, 'north', north_fwd)  8.41 us
    ppermute x3, starting transfers between devices, local(): lax.ppermute(red, 'depth', [(i, (i + k) % count) for i in range(count)])  5.52 us
    unnamed x48, local copies, waits for them, and re-layouts  5.01 us
    pallas_call x1, Pallas kernels, local(): pl.pallas_call(prep_kernel, out_shape=(sds(shape), sds(shape), sds(shape)...  4.27 us
    pallas_call x1, Pallas kernels, local(): pl.pallas_call(edge_kernel, out_shape=(sds((5, groups, ROWS, LANES)), sds...  4.02 us
    pallas_call x1, Pallas kernels, local(): pl.pallas_call(sweep_kernel, grid=(1,), out_shape=(sds(shape), sds(shape)...  3.88 us
  transfers between devices with their start and end apart: 24, of which 3 were waited for; matrix products, arithmetic and copies ran while one was open for 0% of the time, Pallas kernels for 34%

profile of v11, /device:TPU:0, one launch (start us, length us, event | category | flops | bytes accessed | tf_op | source)
XLA Modules:
  0.0 79.6 jit_solution(14874977494972691022)
XLA Ops:
  0.6 4.0 %shard_map.121 = (f32[5,8,8,128]{3,2,1,0:T(8,128)}, f32[5,8,8,128]{3,2,1,0:T(8,128)}, f32[2,5,8,128]{3,2,1,0:T(8,128)}) custom-call(f32[2,12]{1,0:T(2,128)} %lat_ref.3, f32[2,12]{1,0:T(2,128)} %adv_ref.3, s32[64,8,128]{2,1,0:T(8,128)} %layer_ref.3, f32[64,8,128]{2,1,0:T(8,128)} %h_ref.3, f32[64,8,128]{2,1,0:T(8,128)} %w_ref.3, f32[64,8,128]{2,1,0:T(8,128)} %c_ref.3), custom_call_target="tpu_custom_call" | custom-call | tf_op jit(solution)/shard_map/pallas_call | solution.py:439
  4.7 0.5 collective-permute-start
  5.1 1.9 %collective-permute-start.1 = (f32[5,8,8,128]{3,2,1,0:T(8,128)}, f32[5,8,8,128]{3,2,1,0:T(8,128)S(1)}, u32[]{:S(2)}, u32[]{:S(2)}) collective-permute-start(f32[5,8,8,128]{3,2,1,0:T(8,128)} %get-tuple-element.74), channel_id=1, source_target_pairs={{8,0},{16,8},{24,16},{0,24},{9,1},{17,9},{25,17},{1,25},{10,2},{18... | collective-permute-start | bytes 491528 | tf_op jit(solution)/shard_map/ppermute | solution.py:405
  7.0 2.3 %collective-permute-start.2 = (f32[2,5,8,128]{3,2,1,0:T(8,128)}, f32[2,5,8,128]{3,2,1,0:T(8,128)S(1)}, u32[]{:S(2)}, u32[]{:S(2)}) collective-permute-start(f32[2,5,8,128]{3,2,1,0:T(8,128)} %get-tuple-element.75), channel_id=1, source_target_pairs={{0,4},{4,0},{1,5},{5,1},{2,6},{6,2},{3,7},{7,3},{8,12},{12,8},{9,1... | collective-permute-start | bytes 122888 | tf_op jit(solution)/shard_map/ppermute | solution.py:406
  9.4 4.3 %shard_map.120 = (f32[64,8,128]{2,1,0:T(8,128)}, f32[64,8,128]{2,1,0:T(8,128)}, f32[64,8,128]{2,1,0:T(8,128)}, f32[64,8,128]{2,1,0:T(8,128)}, f32[5,64,8,128]{3,2,1,0:T(8,128)}) custom-call(f32[2,12]{1,0:T(2,128)} %lat_ref.3, f32[12]{0:T(128)} %vert_ref.1, f32[2,12]{1,0:T(2,128)} %adv_ref.3, s32[64,8,128]{2,1,0:T(8,128)} %layer_ref.3, f32[64,8,128]{2,1,0:T(8,128)} %h_ref.3, ...), custom_call_target="tpu_custom_call" | custom-call | tf_op jit(solution)/shard_map/pallas_call | solution.py:447
  13.7 0.6 copy-done.2
  14.3 0.1 copy-done
  14.3 0.1 copy-done.1
  14.4 4.5 %shard_map.122 = (f32[64,8,128]{2,1,0:T(8,128)}, f32[64,8,128]{2,1,0:T(8,128)}, f32[64,8,128]{2,1,0:T(8,128)}, f32[64,8,128]{2,1,0:T(8,128)}, f32[3,4,8,128]{3,2...) custom-call(f32[64,8,128]{2,1,0:T(8,128)} %get-tuple-element.68.h_re, ...), custom_call_target="tpu_custom_call", output_to_operand_aliasing={{0}: (0, {}), {1}: (1, {}), {2}: (2, {}), {3}: (3, {})} | custom-call | tf_op jit(solution)/shard_map/pallas_call | solution.py:482
  18.9 1.7 %collective-permute-start.4 = (f32[3,4,8,128]{3,2,1,0:T(8,128)}, f32[3,4,8,128]{3,2,1,0:T(8,128)S(1)}, u32[]{:S(2)}, u32[]{:S(2)}) collective-permute-start(f32[3,4,8,128]{3,2,1,0:T(8,128)} %get-tuple-element.86), channel_id=1, source_target_pairs={{8,0},{16,8},{24,16},{0,24},{9,1},{17,9},{25,17},{1,25},{10,2},{18... | collective-permute-start | bytes 147464 | tf_op jit(solution)/shard_map/ppermute | solution.py:405
  20.7 4.5 %shard_map.123 = (f32[64,8,128]{2,1,0:T(8,128)}, f32[64,8,128]{2,1,0:T(8,128)}, f32[64,8,128]{2,1,0:T(8,128)}, f32[64,8,128]{2,1,0:T(8,128)}, f32[3,4,8,128]{3,2...) custom-call(f32[64,8,128]{2,1,0:T(8,128)} %get-tuple-element.76.h_re, ...), custom_call_target="tpu_custom_call", output_to_operand_aliasing={{0}: (0, {}), {1}: (1, {}), {2}: (2, {}), {3}: (3, {})} | custom-call | tf_op jit(solution)/shard_map/pallas_call | solution.py:482
  25.2 0.1 collective-permute-start.6
  25.3 1.7 %collective-permute-start.7 = (f32[3,4,8,128]{3,2,1,0:T(8,128)}, f32[3,4,8,128]{3,2,1,0:T(8,128)S(1)}, u32[]{:S(2)}, u32[]{:S(2)}) collective-permute-start(f32[3,4,8,128]{3,2,1,0:T(8,128)} %get-tuple-element.94), channel_id=1, source_target_pairs={{8,0},{16,8},{24,16},{0,24},{9,1},{17,9},{25,17},{1,25},{10,2},{18... | collective-permute-start | bytes 147464 | tf_op jit(solution)/shard_map/ppermute | solution.py:405
  27.0 2.0 %collective-permute-start.8 = (f32[2,3,8,128]{3,2,1,0:T(8,128)}, f32[2,3,8,128]{3,2,1,0:T(8,128)S(1)}, u32[]{:S(2)}, u32[]{:S(2)}) collective-permute-start(f32[2,3,8,128]{3,2,1,0:T(8,128)} %get-tuple-element.95), channel_id=1, source_target_pairs={{0,4},{4,0},{1,5},{5,1},{2,6},{6,2},{3,7},{7,3},{8,12},{12,8},{9,1... | collective-permute-start | bytes 73736 | tf_op jit(solution)/shard_map/ppermute | solution.py:406
  29.0 0.6 copy-done.19
  29.6 0.0 copy-done.20
  29.6 3.6 %shard_map.124 = (f32[64,8,128]{2,1,0:T(8,128)}, f32[64,8,128]{2,1,0:T(8,128)}, f32[64,8,128]{2,1,0:T(8,128)}, f32[64,8,128]{2,1,0:T(8,128)}, f32[3,4,8,128]{3,2...) custom-call(f32[64,8,128]{2,1,0:T(8,128)} %get-tuple-element.80.h_re, ...), custom_call_target="tpu_custom_call", output_to_operand_aliasing={{0}: (0, {}), {1}: (1, {}), {2}: (2, {}), {3}: (3, {})} | custom-call | tf_op jit(solution)/shard_map/pallas_call | solution.py:482
  33.2 0.5 collective-permute-start.9
  33.8 0.6 copy-done.3
  34.3 0.0 copy-done.9
  34.4 0.0 copy-done.13
  34.4 3.6 %shard_map.125 = (f32[64,8,128]{2,1,0:T(8,128)}, f32[64,8,128]{2,1,0:T(8,128)}, f32[64,8,128]{2,1,0:T(8,128)}, f32[64,8,128]{2,1,0:T(8,128)}, f32[3,4,8,128]{3,2...) custom-call(f32[64,8,128]{2,1,0:T(8,128)} %get-tuple-element.88.h_re, ...), custom_call_target="tpu_custom_call", output_to_operand_aliasing={{0}: (0, {}), {1}: (1, {}), {2}: (2, {}), {3}: (3, {})} | custom-call | tf_op jit(solution)/shard_map/pallas_call | solution.py:482
  38.0 1.4 %collective-permute-start.12 = (f32[3,4,8,128]{3,2,1,0:T(8,128)}, f32[3,4,8,128]{3,2,1,0:T(8,128)S(1)}, u32[]{:S(2)}, u32[]{:S(2)}) collective-permute-start(f32[3,4,8,128]{3,2,1,0:T(8,128)} %get-tuple-element.107), channel_id=1, source_target_pairs={{0,8},{8,16},{16,24},{24,0},{1,9},{9,17},{17,25},{25,1},{2,10},{10... | collective-permute-start | bytes 147464 | tf_op jit(solution)/shard_map/ppermute | solution.py:404
  39.4 0.4 collective-permute-start.13
  39.8 2.0 %collective-permute-start.14 = (f32[2,3,8,128]{3,2,1,0:T(8,128)}, f32[2,3,8,128]{3,2,1,0:T(8,128)S(1)}, u32[]{:S(2)}, u32[]{:S(2)}) collective-permute-start(f32[2,3,8,128]{3,2,1,0:T(8,128)} %get-tuple-element.109), channel_id=1, source_target_pairs={{0,4},{4,0},{1,5},{5,1},{2,6},{6,2},{3,7},{7,3},{8,12},{12,8},{9,1... | collective-permute-start | bytes 73736 | tf_op jit(solution)/shard_map/ppermute | solution.py:406
  41.8 0.6 copy-done.10
  42.5 3.6 %shard_map.126 = (f32[64,8,128]{2,1,0:T(8,128)}, f32[64,8,128]{2,1,0:T(8,128)}, f32[64,8,128]{2,1,0:T(8,128)}, f32[64,8,128]{2,1,0:T(8,128)}, f32[3,4,8,128]{3,2...) custom-call(f32[64,8,128]{2,1,0:T(8,128)} %get-tuple-element.96.h_re, ...), custom_call_target="tpu_custom_call", output_to_operand_aliasing={{0}: (0, {}), {1}: (1, {}), {2}: (2, {}), {3}: (3, {})} | custom-call | tf_op jit(solution)/shard_map/pallas_call | solution.py:482
  46.1 1.7 %collective-permute-start.16 = (f32[3,4,8,128]{3,2,1,0:T(8,128)}, f32[3,4,8,128]{3,2,1,0:T(8,128)S(1)}, u32[]{:S(2)}, u32[]{:S(2)}) collective-permute-start(f32[3,4,8,128]{3,2,1,0:T(8,128)} %get-tuple-element.115), channel_id=1, source_target_pairs={{8,0},{16,8},{24,16},{0,24},{9,1},{17,9},{25,17},{1,25},{10,2},{18... | collective-permute-start | bytes 147464 | tf_op jit(solution)/shard_map/ppermute | solution.py:405
  47.9 0.6 copy-done.6
  48.4 0.0 copy-done.12
  48.5 3.6 %shard_map.127 = (f32[64,8,128]{2,1,0:T(8,128)}, f32[64,8,128]{2,1,0:T(8,128)}, f32[64,8,128]{2,1,0:T(8,128)}, f32[64,8,128]{2,1,0:T(8,128)}, f32[3,4,8,128]{3,2...) custom-call(f32[64,8,128]{2,1,0:T(8,128)} %get-tuple-element.103.h_r, ...), custom_call_target="tpu_custom_call", output_to_operand_aliasing={{0}: (0, {}), {1}: (1, {}), {2}: (2, {}), {3}: (3, {})} | custom-call | tf_op jit(solution)/shard_map/pallas_call | solution.py:482
  52.1 0.2 collective-permute-start.18
  52.3 1.6 %collective-permute-start.19 = (f32[3,4,8,128]{3,2,1,0:T(8,128)}, f32[3,4,8,128]{3,2,1,0:T(8,128)S(1)}, u32[]{:S(2)}, u32[]{:S(2)}) collective-permute-start(f32[3,4,8,128]{3,2,1,0:T(8,128)} %get-tuple-element.122), channel_id=1, source_target_pairs={{8,0},{16,8},{24,16},{0,24},{9,1},{17,9},{25,17},{1,25},{10,2},{18... | collective-permute-start | bytes 147464 | tf_op jit(solution)/shard_map/ppermute | solution.py:405
  53.9 2.0 %collective-permute-start.20 = (f32[2,3,8,128]{3,2,1,0:T(8,128)}, f32[2,3,8,128]{3,2,1,0:T(8,128)S(1)}, u32[]{:S(2)}, u32[]{:S(2)}) collective-permute-start(f32[2,3,8,128]{3,2,1,0:T(8,128)} %get-tuple-element.123), channel_id=1, source_target_pairs={{0,4},{4,0},{1,5},{5,1},{2,6},{6,2},{3,7},{7,3},{8,12},{12,8},{9,1... | collective-permute-start | bytes 73736 | tf_op jit(solution)/shard_map/ppermute | solution.py:406
  55.9 0.6 copy-done.11
  56.5 3.6 %shard_map.128 = (f32[64,8,128]{2,1,0:T(8,128)}, f32[64,8,128]{2,1,0:T(8,128)}, f32[64,8,128]{2,1,0:T(8,128)}, f32[64,8,128]{2,1,0:T(8,128)}, f32[3,4,8,128]{3,2...) custom-call(f32[64,8,128]{2,1,0:T(8,128)} %get-tuple-element.110.h_r, ...), custom_call_target="tpu_custom_call", output_to_operand_aliasing={{0}: (0, {}), {1}: (1, {}), {2}: (2, {}), {3}: (3, {})} | custom-call | tf_op jit(solution)/shard_map/pallas_call | solution.py:482
  60.2 0.6 copy-done.7
  60.7 0.0 copy-done.17
  60.8 3.6 %shard_map.129 = (f32[64,8,128]{2,1,0:T(8,128)}, f32[64,8,128]{2,1,0:T(8,128)}, f32[64,8,128]{2,1,0:T(8,128)}, f32[64,8,128]{2,1,0:T(8,128)}, f32[3,4,8,128]{3,2...) custom-call(f32[64,8,128]{2,1,0:T(8,128)} %get-tuple-element.117.h_r, ...), custom_call_target="tpu_custom_call", output_to_operand_aliasing={{0}: (0, {}), {1}: (1, {}), {2}: (2, {}), {3}: (3, {})} | custom-call | tf_op jit(solution)/shard_map/pallas_call | solution.py:482
  64.4 3.9 %shard_map.130 = (f32[64,8,128]{2,1,0:T(8,128)}, f32[64,8,128]{2,1,0:T(8,128)}, f32[64,8,128]{2,1,0:T(8,128)}, f32[8,8,128]{2,1,0:T(8,128)}) custom-call(f32[64,8,128]{2,1,0:T(8,128)} %get-tuple-element.124.r_ref, f32[5,64,8,128]{3,2,1,0:T(8,128)} %get-tuple-element.72.co_ref.cz_ref), custom_call_target="tpu_custom_call" | custom-call | tf_op jit(solution)/shard_map/pallas_call | solution.py:496
  68.3 1.6 %collective-permute-start.21 = (f32[8,8,128]{2,1,0:T(8,128)}, f32[8,8,128]{2,1,0:T(8,128)S(1)}, u32[]{:S(2)}, u32[]{:S(2)}) collective-permute-start(f32[8,8,128]{2,1,0:T(8,128)} %get-tuple-element.128.rest_0_), channel_id=1, source_target_pairs={{0,1},{1,2},{2,3},{3,0},{4,5},{5,6},{6,7},{7,4},{8,9},{9,10},{10,1... | collective-permute-start | bytes 98312 | tf_op jit(solution)/shard_map/ppermute | solution.py:508
  69.9 2.6 %collective-permute-start.22 = (f32[8,8,128]{2,1,0:T(8,128)}, f32[8,8,128]{2,1,0:T(8,128)S(1)}, u32[]{:S(2)}, u32[]{:S(2)}) collective-permute-start(f32[8,8,128]{2,1,0:T(8,128)} %get-tuple-element.128.rest_0_), channel_id=1, source_target_pairs={{0,2},{1,3},{2,0},{3,1},{4,6},{5,7},{6,4},{7,5},{8,10},{9,11},{10,... | collective-permute-start | bytes 98312 | tf_op jit(solution)/shard_map/ppermute | solution.py:508
  72.5 1.3 %collective-permute-start.23 = (f32[8,8,128]{2,1,0:T(8,128)}, f32[8,8,128]{2,1,0:T(8,128)S(1)}, u32[]{:S(2)}, u32[]{:S(2)}) collective-permute-start(f32[8,8,128]{2,1,0:T(8,128)} %get-tuple-element.128.rest_0_), channel_id=1, source_target_pairs={{0,3},{1,0},{2,1},{3,2},{4,7},{5,4},{6,5},{7,6},{8,11},{9,8},{10,9... | collective-permute-start | bytes 98312 | tf_op jit(solution)/shard_map/ppermute | solution.py:508
  73.8 0.7 collective-permute-done.21.rest_1_
  74.5 0.8 collective-permute-done.22.rest_2_
  75.3 1.3 %collective-permute-done.23.rest_3_ = f32[8,8,128]{2,1,0:T(8,128)S(1)} collective-permute-done((f32[8,8,128]{2,1,0:T(8,128)}, f32[8,8,128]{2,1,0:T(8,128)S(1)}, u32[]{:S(2)}, u32[]{:S(2)}) %collective-permute-start.23) | collective-permute-done | bytes 32800 | tf_op jit(solution)/shard_map/ppermute | solution.py:508
  76.6 0.6 copy-done.23
  77.2 2.4 %shard_map.131 = f32[64,8,128]{2,1,0:T(8,128)} custom-call(s32[1]{0:T(128)} %bitcast.rank_ref, f32[64,8,128]{2,1,0:T(8,128)} %get-tuple-element.125.y_ref, f32[64,8,128]{2,1,0:T(8,128)} %get-tuple-element.126.a_ref, f32[64,8,128]{2,1,0:T(8,128)} %get-tuple-element.127.b_ref, f32[8,8,128]{2,1,0:T(8,128)} %get-tuple-element.128.rest_0_, ...), custom_call_target="tpu_custom_call" | custom-call | tf_op jit(solution)/shard_map/pallas_call | solution.py:510
  (60 shorter events, 0.3 us)
Async XLA Ops:
  4.7 9.0 %collective-permute-start = (f32[5,8,8,128]{3,2,1,0:T(8,128)}, f32[5,8,8,128]{3,2,1,0:T(8,128)S(1)}, u32[]{:S(2)}, u32[]{:S(2)}) collective-permute-start(f32[5,8,8,128]{3,2,1,0:T(8,128)} %get-tuple-element.73), channel_id=1, source_target_pairs={{0,8},{8,16},{16,24},{24,0},{1,9},{9,17},{17,25},{25,1},{2,10},{10... | collective-permute-start | bytes 491528 | tf_op jit(solution)/shard_map/ppermute | solution.py:404
  5.1 8.6 %collective-permute-start.1 = (f32[5,8,8,128]{3,2,1,0:T(8,128)}, f32[5,8,8,128]{3,2,1,0:T(8,128)S(1)}, u32[]{:S(2)}, u32[]{:S(2)}) collective-permute-start(f32[5,8,8,128]{3,2,1,0:T(8,128)} %get-tuple-element.74), channel_id=1, source_target_pairs={{8,0},{16,8},{24,16},{0,24},{9,1},{17,9},{25,17},{1,25},{10,2},{18... | collective-permute-start | bytes 491528 | tf_op jit(solution)/shard_map/ppermute | solution.py:405
  7.0 6.6 %collective-permute-start.2 = (f32[2,5,8,128]{3,2,1,0:T(8,128)}, f32[2,5,8,128]{3,2,1,0:T(8,128)S(1)}, u32[]{:S(2)}, u32[]{:S(2)}) collective-permute-start(f32[2,5,8,128]{3,2,1,0:T(8,128)} %get-tuple-element.75), channel_id=1, source_target_pairs={{0,4},{4,0},{1,5},{5,1},{2,6},{6,2},{3,7},{7,3},{8,12},{12,8},{9,1... | collective-permute-start | bytes 122888 | tf_op jit(solution)/shard_map/ppermute | solution.py:406
  13.6 0.6 copy-start.2
  13.7 0.7 copy-start
  13.7 0.7 copy-start.1
  18.9 10.1 %collective-permute-start.3 = (f32[3,4,8,128]{3,2,1,0:T(8,128)}, f32[3,4,8,128]{3,2,1,0:T(8,128)S(1)}, u32[]{:S(2)}, u32[]{:S(2)}) collective-permute-start(f32[3,4,8,128]{3,2,1,0:T(8,128)} %get-tuple-element.85), channel_id=1, source_target_pairs={{0,8},{8,16},{16,24},{24,0},{1,9},{9,17},{17,25},{25,1},{2,10},{10... | collective-permute-start | bytes 147464 | tf_op jit(solution)/shard_map/ppermute | solution.py:404
  18.9 10.1 %collective-permute-start.4 = (f32[3,4,8,128]{3,2,1,0:T(8,128)}, f32[3,4,8,128]{3,2,1,0:T(8,128)S(1)}, u32[]{:S(2)}, u32[]{:S(2)}) collective-permute-start(f32[3,4,8,128]{3,2,1,0:T(8,128)} %get-tuple-element.86), channel_id=1, source_target_pairs={{8,0},{16,8},{24,16},{0,24},{9,1},{17,9},{25,17},{1,25},{10,2},{18... | collective-permute-start | bytes 147464 | tf_op jit(solution)/shard_map/ppermute | solution.py:405
  20.7 6.3 %collective-permute-start.5 = (f32[2,3,8,128]{3,2,1,0:T(8,128)}, f32[2,3,8,128]{3,2,1,0:T(8,128)S(1)}, u32[]{:S(2)}, u32[]{:S(2)}) collective-permute-start(f32[2,3,8,128]{3,2,1,0:T(8,128)} %get-tuple-element.87), channel_id=1, source_target_pairs={{0,4},{4,0},{1,5},{5,1},{2,6},{6,2},{3,7},{7,3},{8,12},{12,8},{9,1... | collective-permute-start | bytes 73736 | tf_op jit(solution)/shard_map/ppermute | solution.py:406
  25.2 8.6 %collective-permute-start.6 = (f32[3,4,8,128]{3,2,1,0:T(8,128)}, f32[3,4,8,128]{3,2,1,0:T(8,128)S(1)}, u32[]{:S(2)}, u32[]{:S(2)}) collective-permute-start(f32[3,4,8,128]{3,2,1,0:T(8,128)} %get-tuple-element.93), channel_id=1, source_target_pairs={{0,8},{8,16},{16,24},{24,0},{1,9},{9,17},{17,25},{25,1},{2,10},{10... | collective-permute-start | bytes 147464 | tf_op jit(solution)/shard_map/ppermute | solution.py:404
  25.3 8.5 %collective-permute-start.7 = (f32[3,4,8,128]{3,2,1,0:T(8,128)}, f32[3,4,8,128]{3,2,1,0:T(8,128)S(1)}, u32[]{:S(2)}, u32[]{:S(2)}) collective-permute-start(f32[3,4,8,128]{3,2,1,0:T(8,128)} %get-tuple-element.94), channel_id=1, source_target_pairs={{8,0},{16,8},{24,16},{0,24},{9,1},{17,9},{25,17},{1,25},{10,2},{18... | collective-permute-start | bytes 147464 | tf_op jit(solution)/shard_map/ppermute | solution.py:405
  27.0 2.0 %copy-start.8 = (f32[2,3,8,128]{3,2,1,0:T(8,128)}, f32[2,3,8,128]{3,2,1,0:T(8,128)S(1)}, u32[]{:S(2)}) copy-start(f32[2,3,8,128]{3,2,1,0:T(8,128)S(1)} %collective-permute-done.5.rest_3_.rest_4_) | copy-start | bytes 73732
  27.0 6.8 %collective-permute-start.8 = (f32[2,3,8,128]{3,2,1,0:T(8,128)}, f32[2,3,8,128]{3,2,1,0:T(8,128)S(1)}, u32[]{:S(2)}, u32[]{:S(2)}) collective-permute-start(f32[2,3,8,128]{3,2,1,0:T(8,128)} %get-tuple-element.95), channel_id=1, source_target_pairs={{0,4},{4,0},{1,5},{5,1},{2,6},{6,2},{3,7},{7,3},{8,12},{12,8},{9,1... | collective-permute-start | bytes 73736 | tf_op jit(solution)/shard_map/ppermute | solution.py:406
  29.0 0.6 copy-start.19
  29.0 0.6 copy-start.20
  33.2 8.6 %collective-permute-start.10 = (f32[3,4,8,128]{3,2,1,0:T(8,128)}, f32[3,4,8,128]{3,2,1,0:T(8,128)S(1)}, u32[]{:S(2)}, u32[]{:S(2)}) collective-permute-start(f32[3,4,8,128]{3,2,1,0:T(8,128)} %get-tuple-element.101), channel_id=1, source_target_pairs={{8,0},{16,8},{24,16},{0,24},{9,1},{17,9},{25,17},{1,25},{10,2},{18... | collective-permute-start | bytes 147464 | tf_op jit(solution)/shard_map/ppermute | solution.py:405
  33.2 8.6 %collective-permute-start.9 = (f32[3,4,8,128]{3,2,1,0:T(8,128)}, f32[3,4,8,128]{3,2,1,0:T(8,128)S(1)}, u32[]{:S(2)}, u32[]{:S(2)}) collective-permute-start(f32[3,4,8,128]{3,2,1,0:T(8,128)} %get-tuple-element.100), channel_id=1, source_target_pairs={{0,8},{8,16},{16,24},{24,0},{1,9},{9,17},{17,25},{25,1},{2,10},{10... | collective-permute-start | bytes 147464 | tf_op jit(solution)/shard_map/ppermute | solution.py:404
  33.7 0.6 copy-start.3
  33.7 6.0 %collective-permute-start.11 = (f32[2,3,8,128]{3,2,1,0:T(8,128)}, f32[2,3,8,128]{3,2,1,0:T(8,128)S(1)}, u32[]{:S(2)}, u32[]{:S(2)}) collective-permute-start(f32[2,3,8,128]{3,2,1,0:T(8,128)} %get-tuple-element.102), channel_id=1, source_target_pairs={{0,4},{4,0},{1,5},{5,1},{2,6},{6,2},{3,7},{7,3},{8,12},{12,8},{9,1... | collective-permute-start | bytes 73736 | tf_op jit(solution)/shard_map/ppermute | solution.py:406
  33.8 0.6 copy-start.9
  33.8 0.6 copy-start.13
  38.0 9.8 %collective-permute-start.12 = (f32[3,4,8,128]{3,2,1,0:T(8,128)}, f32[3,4,8,128]{3,2,1,0:T(8,128)S(1)}, u32[]{:S(2)}, u32[]{:S(2)}) collective-permute-start(f32[3,4,8,128]{3,2,1,0:T(8,128)} %get-tuple-element.107), channel_id=1, source_target_pairs={{0,8},{8,16},{16,24},{24,0},{1,9},{9,17},{17,25},{25,1},{2,10},{10... | collective-permute-start | bytes 147464 | tf_op jit(solution)/shard_map/ppermute | solution.py:404
  39.4 8.4 %collective-permute-start.13 = (f32[3,4,8,128]{3,2,1,0:T(8,128)}, f32[3,4,8,128]{3,2,1,0:T(8,128)S(1)}, u32[]{:S(2)}, u32[]{:S(2)}) collective-permute-start(f32[3,4,8,128]{3,2,1,0:T(8,128)} %get-tuple-element.108), channel_id=1, source_target_pairs={{8,0},{16,8},{24,16},{0,24},{9,1},{17,9},{25,17},{1,25},{10,2},{18... | collective-permute-start | bytes 147464 | tf_op jit(solution)/shard_map/ppermute | solution.py:405
  39.8 2.0 %copy-start.4 = (f32[2,3,8,128]{3,2,1,0:T(8,128)}, f32[2,3,8,128]{3,2,1,0:T(8,128)S(1)}, u32[]{:S(2)}) copy-start(f32[2,3,8,128]{3,2,1,0:T(8,128)S(1)} %collective-permute-done.11.rest_3_.rest_4_) | copy-start | bytes 73732
  39.8 8.0 %collective-permute-start.14 = (f32[2,3,8,128]{3,2,1,0:T(8,128)}, f32[2,3,8,128]{3,2,1,0:T(8,128)S(1)}, u32[]{:S(2)}, u32[]{:S(2)}) collective-permute-start(f32[2,3,8,128]{3,2,1,0:T(8,128)} %get-tuple-element.109), channel_id=1, source_target_pairs={{0,4},{4,0},{1,5},{5,1},{2,6},{6,2},{3,7},{7,3},{8,12},{12,8},{9,1... | collective-permute-start | bytes 73736 | tf_op jit(solution)/shard_map/ppermute | solution.py:406
  41.8 0.6 copy-start.10
  41.8 0.6 copy-start.14
  46.1 9.8 %collective-permute-start.15 = (f32[3,4,8,128]{3,2,1,0:T(8,128)}, f32[3,4,8,128]{3,2,1,0:T(8,128)S(1)}, u32[]{:S(2)}, u32[]{:S(2)}) collective-permute-start(f32[3,4,8,128]{3,2,1,0:T(8,128)} %get-tuple-element.114), channel_id=1, source_target_pairs={{0,8},{8,16},{16,24},{24,0},{1,9},{9,17},{17,25},{25,1},{2,10},{10... | collective-permute-start | bytes 147464 | tf_op jit(solution)/shard_map/ppermute | solution.py:404
  46.1 9.8 %collective-permute-start.16 = (f32[3,4,8,128]{3,2,1,0:T(8,128)}, f32[3,4,8,128]{3,2,1,0:T(8,128)S(1)}, u32[]{:S(2)}, u32[]{:S(2)}) collective-permute-start(f32[3,4,8,128]{3,2,1,0:T(8,128)} %get-tuple-element.115), channel_id=1, source_target_pairs={{8,0},{16,8},{24,16},{0,24},{9,1},{17,9},{25,17},{1,25},{10,2},{18... | collective-permute-start | bytes 147464 | tf_op jit(solution)/shard_map/ppermute | solution.py:405
  47.8 0.6 copy-start.6
  47.8 6.0 %collective-permute-start.17 = (f32[2,3,8,128]{3,2,1,0:T(8,128)}, f32[2,3,8,128]{3,2,1,0:T(8,128)S(1)}, u32[]{:S(2)}, u32[]{:S(2)}) collective-permute-start(f32[2,3,8,128]{3,2,1,0:T(8,128)} %get-tuple-element.116), channel_id=1, source_target_pairs={{0,4},{4,0},{1,5},{5,1},{2,6},{6,2},{3,7},{7,3},{8,12},{12,8},{9,1... | collective-permute-start | bytes 73736 | tf_op jit(solution)/shard_map/ppermute | solution.py:406
  47.8 0.6 copy-start.12
  47.9 0.6 copy-start.16
  52.1 8.0 %collective-permute-start.18 = (f32[3,4,8,128]{3,2,1,0:T(8,128)}, f32[3,4,8,128]{3,2,1,0:T(8,128)S(1)}, u32[]{:S(2)}, u32[]{:S(2)}) collective-permute-start(f32[3,4,8,128]{3,2,1,0:T(8,128)} %get-tuple-element.121), channel_id=1, source_target_pairs={{0,8},{8,16},{16,24},{24,0},{1,9},{9,17},{17,25},{25,1},{2,10},{10... | collective-permute-start | bytes 147464 | tf_op jit(solution)/shard_map/ppermute | solution.py:404
  52.3 7.9 %collective-permute-start.19 = (f32[3,4,8,128]{3,2,1,0:T(8,128)}, f32[3,4,8,128]{3,2,1,0:T(8,128)S(1)}, u32[]{:S(2)}, u32[]{:S(2)}) collective-permute-start(f32[3,4,8,128]{3,2,1,0:T(8,128)} %get-tuple-element.122), channel_id=1, source_target_pairs={{8,0},{16,8},{24,16},{0,24},{9,1},{17,9},{25,17},{1,25},{10,2},{18... | collective-permute-start | bytes 147464 | tf_op jit(solution)/shard_map/ppermute | solution.py:405
  53.9 2.0 %copy-start.5 = (f32[2,3,8,128]{3,2,1,0:T(8,128)}, f32[2,3,8,128]{3,2,1,0:T(8,128)S(1)}, u32[]{:S(2)}) copy-start(f32[2,3,8,128]{3,2,1,0:T(8,128)S(1)} %collective-permute-done.17.rest_3_.rest_4_) | copy-start | bytes 73732
  53.9 6.3 %collective-permute-start.20 = (f32[2,3,8,128]{3,2,1,0:T(8,128)}, f32[2,3,8,128]{3,2,1,0:T(8,128)S(1)}, u32[]{:S(2)}, u32[]{:S(2)}) collective-permute-start(f32[2,3,8,128]{3,2,1,0:T(8,128)} %get-tuple-element.123), channel_id=1, source_target_pairs={{0,4},{4,0},{1,5},{5,1},{2,6},{6,2},{3,7},{7,3},{8,12},{12,8},{9,1... | collective-permute-start | bytes 73736 | tf_op jit(solution)/shard_map/ppermute | solution.py:406
  55.9 0.6 copy-start.11
  55.9 0.6 copy-start.15
  60.1 0.6 copy-start.7
  60.1 0.6 copy-start.17
  60.2 0.6 copy-start.18
  68.3 6.2 %collective-permute-start.21 = (f32[8,8,128]{2,1,0:T(8,128)}, f32[8,8,128]{2,1,0:T(8,128)S(1)}, u32[]{:S(2)}, u32[]{:S(2)}) collective-permute-start(f32[8,8,128]{2,1,0:T(8,128)} %get-tuple-element.128.rest_0_), channel_id=1, source_target_pairs={{0,1},{1,2},{2,3},{3,0},{4,5},{5,6},{6,7},{7,4},{8,9},{9,10},{10,1... | collective-permute-start | bytes 98312 | tf_op jit(solution)/shard_map/ppermute | solution.py:508
  69.9 5.4 %collective-permute-start.22 = (f32[8,8,128]{2,1,0:T(8,128)}, f32[8,8,128]{2,1,0:T(8,128)S(1)}, u32[]{:S(2)}, u32[]{:S(2)}) collective-permute-start(f32[8,8,128]{2,1,0:T(8,128)} %get-tuple-element.128.rest_0_), channel_id=1, source_target_pairs={{0,2},{1,3},{2,0},{3,1},{4,6},{5,7},{6,4},{7,5},{8,10},{9,11},{10,... | collective-permute-start | bytes 98312 | tf_op jit(solution)/shard_map/ppermute | solution.py:508
  72.5 4.1 %collective-permute-start.23 = (f32[8,8,128]{2,1,0:T(8,128)}, f32[8,8,128]{2,1,0:T(8,128)S(1)}, u32[]{:S(2)}, u32[]{:S(2)}) collective-permute-start(f32[8,8,128]{2,1,0:T(8,128)} %get-tuple-element.128.rest_0_), channel_id=1, source_target_pairs={{0,3},{1,0},{2,1},{3,2},{4,7},{5,4},{6,5},{7,6},{8,11},{9,8},{10,9... | collective-permute-start | bytes 98312 | tf_op jit(solution)/shard_map/ppermute | solution.py:508
  74.5 2.1 %copy-start.21 = (f32[8,8,128]{2,1,0:T(8,128)}, f32[8,8,128]{2,1,0:T(8,128)S(1)}, u32[]{:S(2)}) copy-start(f32[8,8,128]{2,1,0:T(8,128)S(1)} %collective-permute-done.21.rest_1_) | copy-start | bytes 98308
  75.3 1.3 %copy-start.22 = (f32[8,8,128]{2,1,0:T(8,128)}, f32[8,8,128]{2,1,0:T(8,128)S(1)}, u32[]{:S(2)}) copy-start(f32[8,8,128]{2,1,0:T(8,128)S(1)} %collective-permute-done.22.rest_2_) | copy-start | bytes 98308
  76.6 0.6 copy-start.23

commit v12 on v8

--- a/solution.py
+++ b/solution.py
@@ -21,7 +21,7 @@
 LATENT = 0.3
 
 ROWS = 8
-CHUNKS = 2
+CHUNKS = 4
 LANES = 128
 f32 = jnp.float32
 

time: 78.9 us -> 106 us (1.34)
  starting transfers between devices: 25.9 us -> 42.9 us
  Pallas kernels: 41.4 us -> 53.5 us
  local copies, waits for them, and re-layouts: 4.94 us -> 2.66 us
    pallas_call x8 -> x16, Pallas kernels: 30.6 us -> 42.7 us  [local(): pl.pallas_call(make_section_kernel(k, first), grid=(1,), out_shape=tuple(...]
    ppermute x7 -> x13, starting transfers between devices: 9.42 us -> 19.4 us  [exchange(): xhi = lax.ppermute(xf, 'east', east_bwd)]
    ppermute x7 -> x13, starting transfers between devices: 8.35 us -> 15.1 us  [exchange(): ylo = lax.ppermute(ys, 'north', north_fwd)]
    unnamed x48 -> x120, local copies, waits for them, and re-layouts: 4.94 us -> 2.66 us
    ppermute x7 -> x13, starting transfers between devices: 2.75 us -> 3.31 us  [exchange(): xlo = lax.ppermute(xl, 'east', east_fwd)]
    ppermute x7 -> x13, waiting for transfers between devices: 2.2 us -> 2.22 us  [exchange(): ylo = lax.ppermute(ys, 'north', north_fwd)]
  transfers between devices with their start and end apart: 24 -> 42, of which waited for: 5 -> 5; matrix products, arithmetic and copies ran while one was open for 0% -> 0% of each run, Pallas kernels for 29% -> 35%
where the time goes in v12:
time: 106 us
  Pallas kernels  53.5 us (50%)
  starting transfers between devices  42.9 us (40%)
  waiting for transfers between devices  5.42 us (5%)
  local copies, waits for them, and re-layouts  2.66 us (3%)
  between operations  1.36 us (1%)
    pallas_call x16, Pallas kernels, local(): pl.pallas_call(make_section_kernel(k, first), grid=(1,), out_shape=tuple(...  42.7 us
    ppermute x13, starting transfers between devices, exchange(): xhi = lax.ppermute(xf, 'east', east_bwd)  19.4 us
    ppermute x13, starting transfers between devices, exchange(): ylo = lax.ppermute(ys, 'north', north_fwd)  15.1 us
    ppermute x3, starting transfers between devices, local(): lax.ppermute(red, 'depth', [(i, (i + k) % count) for i in range(count)])  5.11 us
    pallas_call x1, Pallas kernels, local(): pl.pallas_call(prep_kernel, out_shape=(sds(shape), sds(shape), sds(shape)...  4.57 us
    pallas_call x1, Pallas kernels, local(): pl.pallas_call(sweep_kernel, grid=(1,), out_shape=(sds(shape), sds(shape)...  3.84 us
    ppermute x13, starting transfers between devices, exchange(): xlo = lax.ppermute(xl, 'east', east_fwd)  3.31 us
    ppermute x3, waiting for transfers between devices, local(): lax.ppermute(red, 'depth', [(i, (i + k) % count) for i in range(count)])  2.77 us
  transfers between devices with their start and end apart: 42, of which 5 were waited for; matrix products, arithmetic and copies ran while one was open for 0% of the time, Pallas kernels for 35%

profile of v12, /device:TPU:0, one launch (start us, length us, event | category | flops | bytes accessed | tf_op | source)
XLA Modules:
  0.0 105.9 jit_solution(16689957473974511745)
XLA Ops:
  0.6 4.6 %shard_map.120 = (f32[64,8,128]{2,1,0:T(8,128)}, f32[64,8,128]{2,1,0:T(8,128)}, f32[64,8,128]{2,1,0:T(8,128)}, f32[64,8,128]{2,1,0:T(8,128)}, f32[5,64,8,128]{3,...) custom-call(f32[2,12]{1,0:T(2,128)} %lat_ref.1, f32[12]{0:T(128)} %vert_ref.1, ...), custom_call_target="tpu_custom_call" | custom-call | tf_op jit(solution)/shard_map/pallas_call | solution.py:403
  5.7 2.0 %collective-permute-start.1 = (f32[5,8,8,128]{3,2,1,0:T(8,128)}, f32[5,8,8,128]{3,2,1,0:T(8,128)S(1)}, u32[]{:S(2)}, u32[]{:S(2)}) collective-permute-start(f32[5,8,8,128]{3,2,1,0:T(8,128)} %get-tuple-element.126), channel_id=1, source_target_pairs={{8,0},{16,8},{24,16},{0,24},{9,1},{17,9},{25,17},{1,25},{10,2},{18... | collective-permute-start | bytes 491528 | tf_op jit(solution)/shard_map/ppermute | solution.py:369
  7.7 2.3 %collective-permute-start.2 = (f32[2,5,8,128]{3,2,1,0:T(8,128)}, f32[2,5,8,128]{3,2,1,0:T(8,128)S(1)}, u32[]{:S(2)}, u32[]{:S(2)}) collective-permute-start(f32[2,5,8,128]{3,2,1,0:T(8,128)} %get-tuple-element.127), channel_id=1, source_target_pairs={{0,4},{4,0},{1,5},{5,1},{2,6},{6,2},{3,7},{7,3},{8,12},{12,8},{9,1... | collective-permute-start | bytes 122888 | tf_op jit(solution)/shard_map/ppermute | solution.py:370
  10.0 2.2 %collective-permute-done.2.rest_2_.rest_3_ = f32[2,5,8,128]{3,2,1,0:T(8,128)S(1)} collective-permute-done((f32[2,5,8,128]{3,2,1,0:T(8,128)}, f32[2,5,8,128]{3,2,1,0:T(8,128)S(1)}, u32[]{:S(2)}, u32[]{:S(2)}) %collective-permute-start.2) | collective-permute-done | bytes 40992 | tf_op jit(solution)/shard_map/ppermute | solution.py:370
  13.2 3.0 %shard_map.121 = (f32[64,8,128]{2,1,0:T(8,128)}, f32[64,8,128]{2,1,0:T(8,128)}, f32[64,8,128]{2,1,0:T(8,128)}, f32[64,8,128]{2,1,0:T(8,128)}, f32[3,2,8,128]{3,2...) custom-call(f32[64,8,128]{2,1,0:T(8,128)} %get-tuple-element.120.h_r, ...), custom_call_target="tpu_custom_call", output_to_operand_aliasing={{0}: (0, {}), {1}: (1, {}), {2}: (2, {}), {3}: (3, {})} | custom-call | tf_op jit(solution)/shard_map/pallas_call | solution.py:441
  16.9 1.3 %collective-permute-start.4 = (f32[3,2,8,128]{3,2,1,0:T(8,128)}, f32[3,2,8,128]{3,2,1,0:T(8,128)S(1)}, u32[]{:S(2)}, u32[]{:S(2)}) collective-permute-start(f32[3,2,8,128]{3,2,1,0:T(8,128)} %get-tuple-element.146), channel_id=1, source_target_pairs={{8,0},{16,8},{24,16},{0,24},{9,1},{17,9},{25,17},{1,25},{10,2},{18... | collective-permute-start | bytes 73736 | tf_op jit(solution)/shard_map/ppermute | solution.py:369
  18.2 1.4 %collective-permute-start.5 = (f32[2,3,8,128]{3,2,1,0:T(8,128)}, f32[2,3,8,128]{3,2,1,0:T(8,128)S(1)}, u32[]{:S(2)}, u32[]{:S(2)}) collective-permute-start(f32[2,3,8,128]{3,2,1,0:T(8,128)} %get-tuple-element.147), channel_id=1, source_target_pairs={{0,4},{4,0},{1,5},{5,1},{2,6},{6,2},{3,7},{7,3},{8,12},{12,8},{9,1... | collective-permute-start | bytes 73736 | tf_op jit(solution)/shard_map/ppermute | solution.py:370
  19.6 3.0 %shard_map.122 = (f32[64,8,128]{2,1,0:T(8,128)}, f32[64,8,128]{2,1,0:T(8,128)}, f32[64,8,128]{2,1,0:T(8,128)}, f32[64,8,128]{2,1,0:T(8,128)}, f32[3,2,8,128]{3,2...) custom-call(f32[64,8,128]{2,1,0:T(8,128)} %get-tuple-element.128.h_r, ...), custom_call_target="tpu_custom_call", output_to_operand_aliasing={{0}: (0, {}), {1}: (1, {}), {2}: (2, {}), {3}: (3, {})} | custom-call | tf_op jit(solution)/shard_map/pallas_call | solution.py:441
  22.7 1.7 %collective-permute-start.7 = (f32[3,2,8,128]{3,2,1,0:T(8,128)}, f32[3,2,8,128]{3,2,1,0:T(8,128)S(1)}, u32[]{:S(2)}, u32[]{:S(2)}) collective-permute-start(f32[3,2,8,128]{3,2,1,0:T(8,128)} %get-tuple-element.154), channel_id=1, source_target_pairs={{8,0},{16,8},{24,16},{0,24},{9,1},{17,9},{25,17},{1,25},{10,2},{18... | collective-permute-start | bytes 73736 | tf_op jit(solution)/shard_map/ppermute | solution.py:369
  25.0 3.0 %shard_map.123 = (f32[64,8,128]{2,1,0:T(8,128)}, f32[64,8,128]{2,1,0:T(8,128)}, f32[64,8,128]{2,1,0:T(8,128)}, f32[64,8,128]{2,1,0:T(8,128)}, f32[3,2,8,128]{3,2...) custom-call(f32[64,8,128]{2,1,0:T(8,128)} %get-tuple-element.132.h_r, ...), custom_call_target="tpu_custom_call", output_to_operand_aliasing={{0}: (0, {}), {1}: (1, {}), {2}: (2, {}), {3}: (3, {})} | custom-call | tf_op jit(solution)/shard_map/pallas_call | solution.py:441
  28.0 3.0 %shard_map.124 = (f32[64,8,128]{2,1,0:T(8,128)}, f32[64,8,128]{2,1,0:T(8,128)}, f32[64,8,128]{2,1,0:T(8,128)}, f32[64,8,128]{2,1,0:T(8,128)}, f32[3,2,8,128]{3,2...) custom-call(f32[64,8,128]{2,1,0:T(8,128)} %get-tuple-element.136.h_r, ...), custom_call_target="tpu_custom_call", output_to_operand_aliasing={{0}: (0, {}), {1}: (1, {}), {2}: (2, {}), {3}: (3, {})} | custom-call | tf_op jit(solution)/shard_map/pallas_call | solution.py:441
  31.3 1.3 %collective-permute-start.11 = (f32[2,3,8,128]{3,2,1,0:T(8,128)S(1)}, f32[2,3,8,128]{3,2,1,0:T(8,128)S(1)}, u32[]{:S(2)}, u32[]{:S(2)}) collective-permute-start(f32[2,3,8,128]{3,2,1,0:T(8,128)S(1)} %copy-done.52), channel_id=1, source_target_pairs={{0,4},{4,0},{1,5},{5,1},{2,6},{6,2},{3,7},{7,3},{8,12},{12,8},{9,1... | collective-permute-start | bytes 73736 | tf_op jit(solution)/shard_map/ppermute | solution.py:370
  32.8 1.4 %collective-permute-start.12 = (f32[3,2,8,128]{3,2,1,0:T(8,128)}, f32[3,2,8,128]{3,2,1,0:T(8,128)S(1)}, u32[]{:S(2)}, u32[]{:S(2)}) collective-permute-start(f32[3,2,8,128]{3,2,1,0:T(8,128)} %get-tuple-element.169), channel_id=1, source_target_pairs={{0,8},{8,16},{16,24},{24,0},{1,9},{9,17},{17,25},{25,1},{2,10},{10... | collective-permute-start | bytes 73736 | tf_op jit(solution)/shard_map/ppermute | solution.py:368
  34.6 2.6 %shard_map.125 = (f32[64,8,128]{2,1,0:T(8,128)}, f32[64,8,128]{2,1,0:T(8,128)}, f32[64,8,128]{2,1,0:T(8,128)}, f32[64,8,128]{2,1,0:T(8,128)}, f32[3,2,8,128]{3,2...) custom-call(f32[64,8,128]{2,1,0:T(8,128)} %get-tuple-element.140.h_r, ...), custom_call_target="tpu_custom_call", output_to_operand_aliasing={{0}: (0, {}), {1}: (1, {}), {2}: (2, {}), {3}: (3, {})} | custom-call | tf_op jit(solution)/shard_map/pallas_call | solution.py:441
  37.2 2.6 %shard_map.126 = (f32[64,8,128]{2,1,0:T(8,128)}, f32[64,8,128]{2,1,0:T(8,128)}, f32[64,8,128]{2,1,0:T(8,128)}, f32[64,8,128]{2,1,0:T(8,128)}, f32[3,2,8,128]{3,2...) custom-call(f32[64,8,128]{2,1,0:T(8,128)} %get-tuple-element.148.h_r, ...), custom_call_target="tpu_custom_call", output_to_operand_aliasing={{0}: (0, {}), {1}: (1, {}), {2}: (2, {}), {3}: (3, {})} | custom-call | tf_op jit(solution)/shard_map/pallas_call | solution.py:441
  39.8 0.9 collective-permute-start.14
  41.0 1.6 %collective-permute-start.16 = (f32[3,2,8,128]{3,2,1,0:T(8,128)S(1)}, f32[3,2,8,128]{3,2,1,0:T(8,128)S(1)}, u32[]{:S(2)}, u32[]{:S(2)}) collective-permute-start(f32[3,2,8,128]{3,2,1,0:T(8,128)S(1)} %copy-done.54), channel_id=1, source_target_pairs={{8,0},{16,8},{24,16},{0,24},{9,1},{17,9},{25,17},{1,25},{10,2},{18... | collective-permute-start | bytes 73736 | tf_op jit(solution)/shard_map/ppermute | solution.py:369
  42.7 1.2 %collective-permute-start.17 = (f32[2,3,8,128]{3,2,1,0:T(8,128)S(1)}, f32[2,3,8,128]{3,2,1,0:T(8,128)S(1)}, u32[]{:S(2)}, u32[]{:S(2)}) collective-permute-start(f32[2,3,8,128]{3,2,1,0:T(8,128)S(1)} %copy-done.50), channel_id=1, source_target_pairs={{0,4},{4,0},{1,5},{5,1},{2,6},{6,2},{3,7},{7,3},{8,12},{12,8},{9,1... | collective-permute-start | bytes 73736 | tf_op jit(solution)/shard_map/ppermute | solution.py:370
  43.9 2.6 %shard_map.127 = (f32[64,8,128]{2,1,0:T(8,128)}, f32[64,8,128]{2,1,0:T(8,128)}, f32[64,8,128]{2,1,0:T(8,128)}, f32[64,8,128]{2,1,0:T(8,128)}, f32[3,2,8,128]{3,2...) custom-call(f32[64,8,128]{2,1,0:T(8,128)} %get-tuple-element.156.h_r, ...), custom_call_target="tpu_custom_call", output_to_operand_aliasing={{0}: (0, {}), {1}: (1, {}), {2}: (2, {}), {3}: (3, {})} | custom-call | tf_op jit(solution)/shard_map/pallas_call | solution.py:441
  46.5 1.8 %collective-permute-start.19 = (f32[3,2,8,128]{3,2,1,0:T(8,128)S(1)}, f32[3,2,8,128]{3,2,1,0:T(8,128)S(1)}, u32[]{:S(2)}, u32[]{:S(2)}) collective-permute-start(f32[3,2,8,128]{3,2,1,0:T(8,128)S(1)} %copy-done.46), channel_id=1, source_target_pairs={{8,0},{16,8},{24,16},{0,24},{9,1},{17,9},{25,17},{1,25},{10,2},{18... | collective-permute-start | bytes 73736 | tf_op jit(solution)/shard_map/ppermute | solution.py:369
  48.3 1.0 collective-permute-start.20
  49.3 1.7 %collective-permute-start.22 = (f32[3,2,8,128]{3,2,1,0:T(8,128)}, f32[3,2,8,128]{3,2,1,0:T(8,128)S(1)}, u32[]{:S(2)}, u32[]{:S(2)}) collective-permute-start(f32[3,2,8,128]{3,2,1,0:T(8,128)} %get-tuple-element.191), channel_id=1, source_target_pairs={{8,0},{16,8},{24,16},{0,24},{9,1},{17,9},{25,17},{1,25},{10,2},{18... | collective-permute-start | bytes 73736 | tf_op jit(solution)/shard_map/ppermute | solution.py:369
  51.0 1.1 %collective-permute-start.23 = (f32[2,3,8,128]{3,2,1,0:T(8,128)}, f32[2,3,8,128]{3,2,1,0:T(8,128)S(1)}, u32[]{:S(2)}, u32[]{:S(2)}) collective-permute-start(f32[2,3,8,128]{3,2,1,0:T(8,128)} %get-tuple-element.192), channel_id=1, source_target_pairs={{0,4},{4,0},{1,5},{5,1},{2,6},{6,2},{3,7},{7,3},{8,12},{12,8},{9,1... | collective-permute-start | bytes 73736 | tf_op jit(solution)/shard_map/ppermute | solution.py:370
  52.2 2.6 %shard_map.128 = (f32[64,8,128]{2,1,0:T(8,128)}, f32[64,8,128]{2,1,0:T(8,128)}, f32[64,8,128]{2,1,0:T(8,128)}, f32[64,8,128]{2,1,0:T(8,128)}, f32[3,2,8,128]{3,2...) custom-call(f32[64,8,128]{2,1,0:T(8,128)} %get-tuple-element.164.h_r, ...), custom_call_target="tpu_custom_call", output_to_operand_aliasing={{0}: (0, {}), {1}: (1, {}), {2}: (2, {}), {3}: (3, {})} | custom-call | tf_op jit(solution)/shard_map/pallas_call | solution.py:441
  54.8 2.6 %shard_map.129 = (f32[64,8,128]{2,1,0:T(8,128)}, f32[64,8,128]{2,1,0:T(8,128)}, f32[64,8,128]{2,1,0:T(8,128)}, f32[64,8,128]{2,1,0:T(8,128)}, f32[3,2,8,128]{3,2...) custom-call(f32[64,8,128]{2,1,0:T(8,128)} %get-tuple-element.172.h_r, ...), custom_call_target="tpu_custom_call", output_to_operand_aliasing={{0}: (0, {}), {1}: (1, {}), {2}: (2, {}), {3}: (3, {})} | custom-call | tf_op jit(solution)/shard_map/pallas_call | solution.py:441
  57.5 1.8 %collective-permute-start.25 = (f32[3,2,8,128]{3,2,1,0:T(8,128)S(1)}, f32[3,2,8,128]{3,2,1,0:T(8,128)S(1)}, u32[]{:S(2)}, u32[]{:S(2)}) collective-permute-start(f32[3,2,8,128]{3,2,1,0:T(8,128)S(1)} %copy-done.53), channel_id=1, source_target_pairs={{8,0},{16,8},{24,16},{0,24},{9,1},{17,9},{25,17},{1,25},{10,2},{18... | collective-permute-start | bytes 73736 | tf_op jit(solution)/shard_map/ppermute | solution.py:369
  59.3 1.0 collective-permute-start.26
  60.3 1.7 %collective-permute-start.28 = (f32[3,2,8,128]{3,2,1,0:T(8,128)}, f32[3,2,8,128]{3,2,1,0:T(8,128)S(1)}, u32[]{:S(2)}, u32[]{:S(2)}) collective-permute-start(f32[3,2,8,128]{3,2,1,0:T(8,128)} %get-tuple-element.205), channel_id=1, source_target_pairs={{8,0},{16,8},{24,16},{0,24},{9,1},{17,9},{25,17},{1,25},{10,2},{18... | collective-permute-start | bytes 73736 | tf_op jit(solution)/shard_map/ppermute | solution.py:369
  62.0 2.6 %shard_map.130 = (f32[64,8,128]{2,1,0:T(8,128)}, f32[64,8,128]{2,1,0:T(8,128)}, f32[64,8,128]{2,1,0:T(8,128)}, f32[64,8,128]{2,1,0:T(8,128)}, f32[3,2,8,128]{3,2...) custom-call(f32[64,8,128]{2,1,0:T(8,128)} %get-tuple-element.179.h_r, ...), custom_call_target="tpu_custom_call", output_to_operand_aliasing={{0}: (0, {}), {1}: (1, {}), {2}: (2, {}), {3}: (3, {})} | custom-call | tf_op jit(solution)/shard_map/pallas_call | solution.py:441
  64.6 2.6 %shard_map.131 = (f32[64,8,128]{2,1,0:T(8,128)}, f32[64,8,128]{2,1,0:T(8,128)}, f32[64,8,128]{2,1,0:T(8,128)}, f32[64,8,128]{2,1,0:T(8,128)}, f32[3,2,8,128]{3,2...) custom-call(f32[64,8,128]{2,1,0:T(8,128)} %get-tuple-element.186.h_r, ...), custom_call_target="tpu_custom_call", output_to_operand_aliasing={{0}: (0, {}), {1}: (1, {}), {2}: (2, {}), {3}: (3, {})} | custom-call | tf_op jit(solution)/shard_map/pallas_call | solution.py:441
  67.2 1.2 %collective-permute-start.29 = (f32[2,3,8,128]{3,2,1,0:T(8,128)S(1)}, f32[2,3,8,128]{3,2,1,0:T(8,128)S(1)}, u32[]{:S(2)}, u32[]{:S(2)}) collective-permute-start(f32[2,3,8,128]{3,2,1,0:T(8,128)S(1)} %copy-done.47), channel_id=1, source_target_pairs={{0,4},{4,0},{1,5},{5,1},{2,6},{6,2},{3,7},{7,3},{8,12},{12,8},{9,1... | collective-permute-start | bytes 73736 | tf_op jit(solution)/shard_map/ppermute | solution.py:370
  68.5 1.8 %collective-permute-start.31 = (f32[3,2,8,128]{3,2,1,0:T(8,128)S(1)}, f32[3,2,8,128]{3,2,1,0:T(8,128)S(1)}, u32[]{:S(2)}, u32[]{:S(2)}) collective-permute-start(f32[3,2,8,128]{3,2,1,0:T(8,128)S(1)} %copy-done.55), channel_id=1, source_target_pairs={{8,0},{16,8},{24,16},{0,24},{9,1},{17,9},{25,17},{1,25},{10,2},{18... | collective-permute-start | bytes 73736 | tf_op jit(solution)/shard_map/ppermute | solution.py:369
  70.3 1.0 collective-permute-start.32
  71.3 2.6 %shard_map.132 = (f32[64,8,128]{2,1,0:T(8,128)}, f32[64,8,128]{2,1,0:T(8,128)}, f32[64,8,128]{2,1,0:T(8,128)}, f32[64,8,128]{2,1,0:T(8,128)}, f32[3,2,8,128]{3,2...) custom-call(f32[64,8,128]{2,1,0:T(8,128)} %get-tuple-element.193.h_r, ...), custom_call_target="tpu_custom_call", output_to_operand_aliasing={{0}: (0, {}), {1}: (1, {}), {2}: (2, {}), {3}: (3, {})} | custom-call | tf_op jit(solution)/shard_map/pallas_call | solution.py:441
  73.9 1.8 %collective-permute-start.34 = (f32[3,2,8,128]{3,2,1,0:T(8,128)S(1)}, f32[3,2,8,128]{3,2,1,0:T(8,128)S(1)}, u32[]{:S(2)}, u32[]{:S(2)}) collective-permute-start(f32[3,2,8,128]{3,2,1,0:T(8,128)S(1)} %copy-done.43), channel_id=1, source_target_pairs={{8,0},{16,8},{24,16},{0,24},{9,1},{17,9},{25,17},{1,25},{10,2},{18... | collective-permute-start | bytes 73736 | tf_op jit(solution)/shard_map/ppermute | solution.py:369
  75.7 1.2 %collective-permute-start.35 = (f32[2,3,8,128]{3,2,1,0:T(8,128)S(1)}, f32[2,3,8,128]{3,2,1,0:T(8,128)S(1)}, u32[]{:S(2)}, u32[]{:S(2)}) collective-permute-start(f32[2,3,8,128]{3,2,1,0:T(8,128)S(1)} %copy-done.42), channel_id=1, source_target_pairs={{0,4},{4,0},{1,5},{5,1},{2,6},{6,2},{3,7},{7,3},{8,12},{12,8},{9,1... | collective-permute-start | bytes 73736 | tf_op jit(solution)/shard_map/ppermute | solution.py:370
  76.9 1.7 %collective-permute-start.37 = (f32[3,2,8,128]{3,2,1,0:T(8,128)}, f32[3,2,8,128]{3,2,1,0:T(8,128)S(1)}, u32[]{:S(2)}, u32[]{:S(2)}) collective-permute-start(f32[3,2,8,128]{3,2,1,0:T(8,128)} %get-tuple-element.226), channel_id=1, source_target_pairs={{8,0},{16,8},{24,16},{0,24},{9,1},{17,9},{25,17},{1,25},{10,2},{18... | collective-permute-start | bytes 73736 | tf_op jit(solution)/shard_map/ppermute | solution.py:369
  79.6 2.6 %shard_map.133 = (f32[64,8,128]{2,1,0:T(8,128)}, f32[64,8,128]{2,1,0:T(8,128)}, f32[64,8,128]{2,1,0:T(8,128)}, f32[64,8,128]{2,1,0:T(8,128)}, f32[3,2,8,128]{3,2...) custom-call(f32[64,8,128]{2,1,0:T(8,128)} %get-tuple-element.200.h_r, ...), custom_call_target="tpu_custom_call", output_to_operand_aliasing={{0}: (0, {}), {1}: (1, {}), {2}: (2, {}), {3}: (3, {})} | custom-call | tf_op jit(solution)/shard_map/pallas_call | solution.py:441
  82.2 2.6 %shard_map.134 = (f32[64,8,128]{2,1,0:T(8,128)}, f32[64,8,128]{2,1,0:T(8,128)}, f32[64,8,128]{2,1,0:T(8,128)}, f32[64,8,128]{2,1,0:T(8,128)}, f32[3,2,8,128]{3,2...) custom-call(f32[64,8,128]{2,1,0:T(8,128)} %get-tuple-element.207.h_r, ...), custom_call_target="tpu_custom_call", output_to_operand_aliasing={{0}: (0, {}), {1}: (1, {}), {2}: (2, {}), {3}: (3, {})} | custom-call | tf_op jit(solution)/shard_map/pallas_call | solution.py:441
  85.4 2.6 %shard_map.135 = (f32[64,8,128]{2,1,0:T(8,128)}, f32[64,8,128]{2,1,0:T(8,128)}, f32[64,8,128]{2,1,0:T(8,128)}, f32[64,8,128]{2,1,0:T(8,128)}, f32[3,2,8,128]{3,2...) custom-call(f32[64,8,128]{2,1,0:T(8,128)} %get-tuple-element.214.h_r, ...), custom_call_target="tpu_custom_call", output_to_operand_aliasing={{0}: (0, {}), {1}: (1, {}), {2}: (2, {}), {3}: (3, {})} | custom-call | tf_op jit(solution)/shard_map/pallas_call | solution.py:441
  88.6 2.6 %shard_map.136 = (f32[64,8,128]{2,1,0:T(8,128)}, f32[64,8,128]{2,1,0:T(8,128)}, f32[64,8,128]{2,1,0:T(8,128)}, f32[64,8,128]{2,1,0:T(8,128)}, f32[3,2,8,128]{3,2...) custom-call(f32[64,8,128]{2,1,0:T(8,128)} %get-tuple-element.221.h_r, ...), custom_call_target="tpu_custom_call", output_to_operand_aliasing={{0}: (0, {}), {1}: (1, {}), {2}: (2, {}), {3}: (3, {})} | custom-call | tf_op jit(solution)/shard_map/pallas_call | solution.py:441
  91.1 3.8 %shard_map.137 = (f32[64,8,128]{2,1,0:T(8,128)}, f32[64,8,128]{2,1,0:T(8,128)}, f32[64,8,128]{2,1,0:T(8,128)}, f32[8,8,128]{2,1,0:T(8,128)}) custom-call(f32[64,8,128]{2,1,0:T(8,128)} %get-tuple-element.228.r_ref, f32[5,64,8,128]{3,2,1,0:T(8,128)} %get-tuple-element.124.co_ref.cz_ref), custom_call_target="tpu_custom_call" | custom-call | tf_op jit(solution)/shard_map/pallas_call | solution.py:455
  95.0 1.2 %collective-permute-start.39 = (f32[8,8,128]{2,1,0:T(8,128)}, f32[8,8,128]{2,1,0:T(8,128)S(1)}, u32[]{:S(2)}, u32[]{:S(2)}) collective-permute-start(f32[8,8,128]{2,1,0:T(8,128)} %get-tuple-element.232.rest_0_), channel_id=1, source_target_pairs={{0,1},{1,2},{2,3},{3,0},{4,5},{5,6},{6,7},{7,4},{8,9},{9,10},{10,1... | collective-permute-start | bytes 98312 | tf_op jit(solution)/shard_map/ppermute | solution.py:467
  96.1 2.6 %collective-permute-start.40 = (f32[8,8,128]{2,1,0:T(8,128)}, f32[8,8,128]{2,1,0:T(8,128)S(1)}, u32[]{:S(2)}, u32[]{:S(2)}) collective-permute-start(f32[8,8,128]{2,1,0:T(8,128)} %get-tuple-element.232.rest_0_), channel_id=1, source_target_pairs={{0,2},{1,3},{2,0},{3,1},{4,6},{5,7},{6,4},{7,5},{8,10},{9,11},{10,... | collective-permute-start | bytes 98312 | tf_op jit(solution)/shard_map/ppermute | solution.py:467
  98.7 1.3 %collective-permute-start.41 = (f32[8,8,128]{2,1,0:T(8,128)}, f32[8,8,128]{2,1,0:T(8,128)S(1)}, u32[]{:S(2)}, u32[]{:S(2)}) collective-permute-start(f32[8,8,128]{2,1,0:T(8,128)} %get-tuple-element.232.rest_0_), channel_id=1, source_target_pairs={{0,3},{1,0},{2,1},{3,2},{4,7},{5,4},{6,5},{7,6},{8,11},{9,8},{10,9... | collective-permute-start | bytes 98312 | tf_op jit(solution)/shard_map/ppermute | solution.py:467
  100.1 1.2 %collective-permute-done.39.rest_1_ = f32[8,8,128]{2,1,0:T(8,128)S(1)} collective-permute-done((f32[8,8,128]{2,1,0:T(8,128)}, f32[8,8,128]{2,1,0:T(8,128)S(1)}, u32[]{:S(2)}, u32[]{:S(2)}) %collective-permute-start.39) | collective-permute-done | bytes 32800 | tf_op jit(solution)/shard_map/ppermute | solution.py:467
  101.6 1.2 %collective-permute-done.41.rest_3_ = f32[8,8,128]{2,1,0:T(8,128)S(1)} collective-permute-done((f32[8,8,128]{2,1,0:T(8,128)}, f32[8,8,128]{2,1,0:T(8,128)S(1)}, u32[]{:S(2)}, u32[]{:S(2)}) %collective-permute-start.41) | collective-permute-done | bytes 32800 | tf_op jit(solution)/shard_map/ppermute | solution.py:467
  103.5 2.4 %shard_map.138 = f32[64,8,128]{2,1,0:T(8,128)} custom-call(s32[1]{0:T(128)} %bitcast.rank_ref, f32[64,8,128]{2,1,0:T(8,128)} %get-tuple-element.229.y_ref, f32[64,8,128]{2,1,0:T(8,128)} %get-tuple-element.230.a_ref, f32[64,8,128]{2,1,0:T(8,128)} %get-tuple-element.231.b_ref, f32[8,8,128]{2,1,0:T(8,128)} %get-tuple-element.232.rest_0_, ...), custom_call_target="tpu_custom_call" | custom-call | tf_op jit(solution)/shard_map/pallas_call | solution.py:469
  (175 shorter events, 7.5 us)
Async XLA Ops:
  5.2 7.0 %collective-permute-start = (f32[5,8,8,128]{3,2,1,0:T(8,128)}, f32[5,8,8,128]{3,2,1,0:T(8,128)S(1)}, u32[]{:S(2)}, u32[]{:S(2)}) collective-permute-start(f32[5,8,8,128]{3,2,1,0:T(8,128)} %get-tuple-element.125), channel_id=1, source_target_pairs={{0,8},{8,16},{16,24},{24,0},{1,9},{9,17},{17,25},{25,1},{2,10},{10... | collective-permute-start | bytes 491528 | tf_op jit(solution)/shard_map/ppermute | solution.py:368
  5.7 6.8 %collective-permute-start.1 = (f32[5,8,8,128]{3,2,1,0:T(8,128)}, f32[5,8,8,128]{3,2,1,0:T(8,128)S(1)}, u32[]{:S(2)}, u32[]{:S(2)}) collective-permute-start(f32[5,8,8,128]{3,2,1,0:T(8,128)} %get-tuple-element.126), channel_id=1, source_target_pairs={{8,0},{16,8},{24,16},{0,24},{9,1},{17,9},{25,17},{1,25},{10,2},{18... | collective-permute-start | bytes 491528 | tf_op jit(solution)/shard_map/ppermute | solution.py:369
  7.7 4.5 %collective-permute-start.2 = (f32[2,5,8,128]{3,2,1,0:T(8,128)}, f32[2,5,8,128]{3,2,1,0:T(8,128)S(1)}, u32[]{:S(2)}, u32[]{:S(2)}) collective-permute-start(f32[2,5,8,128]{3,2,1,0:T(8,128)} %get-tuple-element.127), channel_id=1, source_target_pairs={{0,4},{4,0},{1,5},{5,1},{2,6},{6,2},{3,7},{7,3},{8,12},{12,8},{9,1... | collective-permute-start | bytes 122888 | tf_op jit(solution)/shard_map/ppermute | solution.py:370
  16.2 8.2 %collective-permute-start.3 = (f32[3,2,8,128]{3,2,1,0:T(8,128)}, f32[3,2,8,128]{3,2,1,0:T(8,128)S(1)}, u32[]{:S(2)}, u32[]{:S(2)}) collective-permute-start(f32[3,2,8,128]{3,2,1,0:T(8,128)} %get-tuple-element.145), channel_id=1, source_target_pairs={{0,8},{8,16},{16,24},{24,0},{1,9},{9,17},{17,25},{25,1},{2,10},{10... | collective-permute-start | bytes 73736 | tf_op jit(solution)/shard_map/ppermute | solution.py:368
  16.9 14.1 %collective-permute-start.4 = (f32[3,2,8,128]{3,2,1,0:T(8,128)}, f32[3,2,8,128]{3,2,1,0:T(8,128)S(1)}, u32[]{:S(2)}, u32[]{:S(2)}) collective-permute-start(f32[3,2,8,128]{3,2,1,0:T(8,128)} %get-tuple-element.146), channel_id=1, source_target_pairs={{8,0},{16,8},{24,16},{0,24},{9,1},{17,9},{25,17},{1,25},{10,2},{18... | collective-permute-start | bytes 73736 | tf_op jit(solution)/shard_map/ppermute | solution.py:369
  18.2 13.0 %collective-permute-start.5 = (f32[2,3,8,128]{3,2,1,0:T(8,128)}, f32[2,3,8,128]{3,2,1,0:T(8,128)S(1)}, u32[]{:S(2)}, u32[]{:S(2)}) collective-permute-start(f32[2,3,8,128]{3,2,1,0:T(8,128)} %get-tuple-element.147), channel_id=1, source_target_pairs={{0,4},{4,0},{1,5},{5,1},{2,6},{6,2},{3,7},{7,3},{8,12},{12,8},{9,1... | collective-permute-start | bytes 73736 | tf_op jit(solution)/shard_map/ppermute | solution.py:370
  22.6 10.0 %collective-permute-start.6 = (f32[3,2,8,128]{3,2,1,0:T(8,128)}, f32[3,2,8,128]{3,2,1,0:T(8,128)S(1)}, u32[]{:S(2)}, u32[]{:S(2)}) collective-permute-start(f32[3,2,8,128]{3,2,1,0:T(8,128)} %get-tuple-element.153), channel_id=1, source_target_pairs={{0,8},{8,16},{16,24},{24,0},{1,9},{9,17},{17,25},{25,1},{2,10},{10... | collective-permute-start | bytes 73736 | tf_op jit(solution)/shard_map/ppermute | solution.py:368
  22.7 10.2 %collective-permute-start.7 = (f32[3,2,8,128]{3,2,1,0:T(8,128)}, f32[3,2,8,128]{3,2,1,0:T(8,128)S(1)}, u32[]{:S(2)}, u32[]{:S(2)}) collective-permute-start(f32[3,2,8,128]{3,2,1,0:T(8,128)} %get-tuple-element.154), channel_id=1, source_target_pairs={{8,0},{16,8},{24,16},{0,24},{9,1},{17,9},{25,17},{1,25},{10,2},{18... | collective-permute-start | bytes 73736 | tf_op jit(solution)/shard_map/ppermute | solution.py:369
  24.4 9.9 %collective-permute-start.8 = (f32[2,3,8,128]{3,2,1,0:T(8,128)}, f32[2,3,8,128]{3,2,1,0:T(8,128)S(1)}, u32[]{:S(2)}, u32[]{:S(2)}) collective-permute-start(f32[2,3,8,128]{3,2,1,0:T(8,128)} %get-tuple-element.155), channel_id=1, source_target_pairs={{0,4},{4,0},{1,5},{5,1},{2,6},{6,2},{3,7},{7,3},{8,12},{12,8},{9,1... | collective-permute-start | bytes 73736 | tf_op jit(solution)/shard_map/ppermute | solution.py:370
  31.0 8.8 %collective-permute-start.10 = (f32[3,2,8,128]{3,2,1,0:T(8,128)S(1)}, f32[3,2,8,128]{3,2,1,0:T(8,128)S(1)}, u32[]{:S(2)}, u32[]{:S(2)}) collective-permute-start(f32[3,2,8,128]{3,2,1,0:T(8,128)S(1)} %copy-done.56), channel_id=1, source_target_pairs={{8,0},{16,8},{24,16},{0,24},{9,1},{17,9},{25,17},{1,25},{10,2},{18... | collective-permute-start | bytes 73736 | tf_op jit(solution)/shard_map/ppermute | solution.py:369
  31.3 9.5 %collective-permute-start.11 = (f32[2,3,8,128]{3,2,1,0:T(8,128)S(1)}, f32[2,3,8,128]{3,2,1,0:T(8,128)S(1)}, u32[]{:S(2)}, u32[]{:S(2)}) collective-permute-start(f32[2,3,8,128]{3,2,1,0:T(8,128)S(1)} %copy-done.52), channel_id=1, source_target_pairs={{0,4},{4,0},{1,5},{5,1},{2,6},{6,2},{3,7},{7,3},{8,12},{12,8},{9,1... | collective-permute-start | bytes 73736 | tf_op jit(solution)/shard_map/ppermute | solution.py:370
  32.6 8.4 %collective-permute-start.9 = (f32[3,2,8,128]{3,2,1,0:T(8,128)S(1)}, f32[3,2,8,128]{3,2,1,0:T(8,128)S(1)}, u32[]{:S(2)}, u32[]{:S(2)}) collective-permute-start(f32[3,2,8,128]{3,2,1,0:T(8,128)S(1)} %copy-done.48), channel_id=1, source_target_pairs={{0,8},{8,16},{16,24},{24,0},{1,9},{9,17},{17,25},{25,1},{2,10},{10... | collective-permute-start | bytes 73736 | tf_op jit(solution)/shard_map/ppermute | solution.py:368
  32.8 9.8 %collective-permute-start.12 = (f32[3,2,8,128]{3,2,1,0:T(8,128)}, f32[3,2,8,128]{3,2,1,0:T(8,128)S(1)}, u32[]{:S(2)}, u32[]{:S(2)}) collective-permute-start(f32[3,2,8,128]{3,2,1,0:T(8,128)} %get-tuple-element.169), channel_id=1, source_target_pairs={{0,8},{8,16},{16,24},{24,0},{1,9},{9,17},{17,25},{25,1},{2,10},{10... | collective-permute-start | bytes 73736 | tf_op jit(solution)/shard_map/ppermute | solution.py:368
  34.3 9.6 %collective-permute-start.13 = (f32[3,2,8,128]{3,2,1,0:T(8,128)}, f32[3,2,8,128]{3,2,1,0:T(8,128)S(1)}, u32[]{:S(2)}, u32[]{:S(2)}) collective-permute-start(f32[3,2,8,128]{3,2,1,0:T(8,128)} %get-tuple-element.170), channel_id=1, source_target_pairs={{8,0},{16,8},{24,16},{0,24},{9,1},{17,9},{25,17},{1,25},{10,2},{18... | collective-permute-start | bytes 73736 | tf_op jit(solution)/shard_map/ppermute | solution.py:369
  39.8 6.7 %collective-permute-start.14 = (f32[2,3,8,128]{3,2,1,0:T(8,128)S(1)}, f32[2,3,8,128]{3,2,1,0:T(8,128)S(1)}, u32[]{:S(2)}, u32[]{:S(2)}) collective-permute-start(f32[2,3,8,128]{3,2,1,0:T(8,128)S(1)} %copy-done.45), channel_id=1, source_target_pairs={{0,4},{4,0},{1,5},{5,1},{2,6},{6,2},{3,7},{7,3},{8,12},{12,8},{9,1... | collective-permute-start | bytes 73736 | tf_op jit(solution)/shard_map/ppermute | solution.py:370
  40.8 7.5 %collective-permute-start.15 = (f32[3,2,8,128]{3,2,1,0:T(8,128)S(1)}, f32[3,2,8,128]{3,2,1,0:T(8,128)S(1)}, u32[]{:S(2)}, u32[]{:S(2)}) collective-permute-start(f32[3,2,8,128]{3,2,1,0:T(8,128)S(1)} %copy-done.58), channel_id=1, source_target_pairs={{0,8},{8,16},{16,24},{24,0},{1,9},{9,17},{17,25},{25,1},{2,10},{10... | collective-permute-start | bytes 73736 | tf_op jit(solution)/shard_map/ppermute | solution.py:368
  41.0 8.2 %collective-permute-start.16 = (f32[3,2,8,128]{3,2,1,0:T(8,128)S(1)}, f32[3,2,8,128]{3,2,1,0:T(8,128)S(1)}, u32[]{:S(2)}, u32[]{:S(2)}) collective-permute-start(f32[3,2,8,128]{3,2,1,0:T(8,128)S(1)} %copy-done.54), channel_id=1, source_target_pairs={{8,0},{16,8},{24,16},{0,24},{9,1},{17,9},{25,17},{1,25},{10,2},{18... | collective-permute-start | bytes 73736 | tf_op jit(solution)/shard_map/ppermute | solution.py:369
  42.7 6.6 %collective-permute-start.17 = (f32[2,3,8,128]{3,2,1,0:T(8,128)S(1)}, f32[2,3,8,128]{3,2,1,0:T(8,128)S(1)}, u32[]{:S(2)}, u32[]{:S(2)}) collective-permute-start(f32[2,3,8,128]{3,2,1,0:T(8,128)S(1)} %copy-done.50), channel_id=1, source_target_pairs={{0,4},{4,0},{1,5},{5,1},{2,6},{6,2},{3,7},{7,3},{8,12},{12,8},{9,1... | collective-permute-start | bytes 73736 | tf_op jit(solution)/shard_map/ppermute | solution.py:370
  43.9 7.2 %collective-permute-start.18 = (f32[3,2,8,128]{3,2,1,0:T(8,128)}, f32[3,2,8,128]{3,2,1,0:T(8,128)S(1)}, u32[]{:S(2)}, u32[]{:S(2)}) collective-permute-start(f32[3,2,8,128]{3,2,1,0:T(8,128)} %get-tuple-element.183), channel_id=1, source_target_pairs={{0,8},{8,16},{16,24},{24,0},{1,9},{9,17},{17,25},{25,1},{2,10},{10... | collective-permute-start | bytes 73736 | tf_op jit(solution)/shard_map/ppermute | solution.py:368
  46.5 5.6 %copy-start.6 = (f32[2,3,8,128]{3,2,1,0:T(8,128)}, f32[2,3,8,128]{3,2,1,0:T(8,128)S(1)}, u32[]{:S(2)}) copy-start(f32[2,3,8,128]{3,2,1,0:T(8,128)S(1)} %collective-permute-done.14.rest_3_.rest_4_) | copy-start | bytes 73732
  46.5 10.8 %collective-permute-start.19 = (f32[3,2,8,128]{3,2,1,0:T(8,128)S(1)}, f32[3,2,8,128]{3,2,1,0:T(8,128)S(1)}, u32[]{:S(2)}, u32[]{:S(2)}) collective-permute-start(f32[3,2,8,128]{3,2,1,0:T(8,128)S(1)} %copy-done.46), channel_id=1, source_target_pairs={{8,0},{16,8},{24,16},{0,24},{9,1},{17,9},{25,17},{1,25},{10,2},{18... | collective-permute-start | bytes 73736 | tf_op jit(solution)/shard_map/ppermute | solution.py:369
  48.3 6.4 %copy-start.31 = (f32[3,2,8,128]{3,2,1,0:T(8,128)}, f32[3,2,8,128]{3,2,1,0:T(8,128)S(1)}, u32[]{:S(2)}) copy-start(f32[3,2,8,128]{3,2,1,0:T(8,128)S(1)} %collective-permute-done.15.rest_1_) | copy-start | bytes 73732
  48.3 9.1 %collective-permute-start.20 = (f32[2,3,8,128]{3,2,1,0:T(8,128)S(1)}, f32[2,3,8,128]{3,2,1,0:T(8,128)S(1)}, u32[]{:S(2)}, u32[]{:S(2)}) collective-permute-start(f32[2,3,8,128]{3,2,1,0:T(8,128)S(1)} %copy-done.44), channel_id=1, source_target_pairs={{0,4},{4,0},{1,5},{5,1},{2,6},{6,2},{3,7},{7,3},{8,12},{12,8},{9,1... | collective-permute-start | bytes 73736 | tf_op jit(solution)/shard_map/ppermute | solution.py:370
  49.3 5.5 %copy-start.39 = (f32[3,2,8,128]{3,2,1,0:T(8,128)}, f32[3,2,8,128]{3,2,1,0:T(8,128)S(1)}, u32[]{:S(2)}) copy-start(f32[3,2,8,128]{3,2,1,0:T(8,128)S(1)} %collective-permute-done.16.rest_2_) | copy-start | bytes 73732
  49.3 10.0 %collective-permute-start.21 = (f32[3,2,8,128]{3,2,1,0:T(8,128)}, f32[3,2,8,128]{3,2,1,0:T(8,128)S(1)}, u32[]{:S(2)}, u32[]{:S(2)}) collective-permute-start(f32[3,2,8,128]{3,2,1,0:T(8,128)} %get-tuple-element.190), channel_id=1, source_target_pairs={{0,8},{8,16},{16,24},{24,0},{1,9},{9,17},{17,25},{25,1},{2,10},{10... | collective-permute-start | bytes 73736 | tf_op jit(solution)/shard_map/ppermute | solution.py:368
  49.3 10.9 %collective-permute-start.22 = (f32[3,2,8,128]{3,2,1,0:T(8,128)}, f32[3,2,8,128]{3,2,1,0:T(8,128)S(1)}, u32[]{:S(2)}, u32[]{:S(2)}) collective-permute-start(f32[3,2,8,128]{3,2,1,0:T(8,128)} %get-tuple-element.191), channel_id=1, source_target_pairs={{8,0},{16,8},{24,16},{0,24},{9,1},{17,9},{25,17},{1,25},{10,2},{18... | collective-permute-start | bytes 73736 | tf_op jit(solution)/shard_map/ppermute | solution.py:369
  51.0 9.2 %collective-permute-start.23 = (f32[2,3,8,128]{3,2,1,0:T(8,128)}, f32[2,3,8,128]{3,2,1,0:T(8,128)S(1)}, u32[]{:S(2)}, u32[]{:S(2)}) collective-permute-start(f32[2,3,8,128]{3,2,1,0:T(8,128)} %get-tuple-element.192), channel_id=1, source_target_pairs={{0,4},{4,0},{1,5},{5,1},{2,6},{6,2},{3,7},{7,3},{8,12},{12,8},{9,1... | collective-permute-start | bytes 73736 | tf_op jit(solution)/shard_map/ppermute | solution.py:370
  57.4 9.8 %collective-permute-start.24 = (f32[3,2,8,128]{3,2,1,0:T(8,128)S(1)}, f32[3,2,8,128]{3,2,1,0:T(8,128)S(1)}, u32[]{:S(2)}, u32[]{:S(2)}) collective-permute-start(f32[3,2,8,128]{3,2,1,0:T(8,128)S(1)} %copy-done.57), channel_id=1, source_target_pairs={{0,8},{8,16},{16,24},{24,0},{1,9},{9,17},{17,25},{25,1},{2,10},{10... | collective-permute-start | bytes 73736 | tf_op jit(solution)/shard_map/ppermute | solution.py:368
  57.5 10.9 %collective-permute-start.25 = (f32[3,2,8,128]{3,2,1,0:T(8,128)S(1)}, f32[3,2,8,128]{3,2,1,0:T(8,128)S(1)}, u32[]{:S(2)}, u32[]{:S(2)}) collective-permute-start(f32[3,2,8,128]{3,2,1,0:T(8,128)S(1)} %copy-done.53), channel_id=1, source_target_pairs={{8,0},{16,8},{24,16},{0,24},{9,1},{17,9},{25,17},{1,25},{10,2},{18... | collective-permute-start | bytes 73736 | tf_op jit(solution)/shard_map/ppermute | solution.py:369
  59.3 9.2 %collective-permute-start.26 = (f32[2,3,8,128]{3,2,1,0:T(8,128)S(1)}, f32[2,3,8,128]{3,2,1,0:T(8,128)S(1)}, u32[]{:S(2)}, u32[]{:S(2)}) collective-permute-start(f32[2,3,8,128]{3,2,1,0:T(8,128)S(1)} %copy-done.49), channel_id=1, source_target_pairs={{0,4},{4,0},{1,5},{5,1},{2,6},{6,2},{3,7},{7,3},{8,12},{12,8},{9,1... | collective-permute-start | bytes 73736 | tf_op jit(solution)/shard_map/ppermute | solution.py:370
  60.2 10.0 %collective-permute-start.27 = (f32[3,2,8,128]{3,2,1,0:T(8,128)}, f32[3,2,8,128]{3,2,1,0:T(8,128)S(1)}, u32[]{:S(2)}, u32[]{:S(2)}) collective-permute-start(f32[3,2,8,128]{3,2,1,0:T(8,128)} %get-tuple-element.204), channel_id=1, source_target_pairs={{0,8},{8,16},{16,24},{24,0},{1,9},{9,17},{17,25},{25,1},{2,10},{10... | collective-permute-start | bytes 73736 | tf_op jit(solution)/shard_map/ppermute | solution.py:368
  60.3 11.0 %collective-permute-start.28 = (f32[3,2,8,128]{3,2,1,0:T(8,128)}, f32[3,2,8,128]{3,2,1,0:T(8,128)S(1)}, u32[]{:S(2)}, u32[]{:S(2)}) collective-permute-start(f32[3,2,8,128]{3,2,1,0:T(8,128)} %get-tuple-element.205), channel_id=1, source_target_pairs={{8,0},{16,8},{24,16},{0,24},{9,1},{17,9},{25,17},{1,25},{10,2},{18... | collective-permute-start | bytes 73736 | tf_op jit(solution)/shard_map/ppermute | solution.py:369
  64.6 5.7 %copy-start.51 = (f32[2,3,8,128]{3,2,1,0:T(8,128)S(1)}, f32[2,3,8,128]{3,2,1,0:T(8,128)}, u32[]{:S(2)}) copy-start(f32[2,3,8,128]{3,2,1,0:T(8,128)} %get-tuple-element.213) | copy-start | bytes 73732
  67.2 6.7 %collective-permute-start.29 = (f32[2,3,8,128]{3,2,1,0:T(8,128)S(1)}, f32[2,3,8,128]{3,2,1,0:T(8,128)S(1)}, u32[]{:S(2)}, u32[]{:S(2)}) collective-permute-start(f32[2,3,8,128]{3,2,1,0:T(8,128)S(1)} %copy-done.47), channel_id=1, source_target_pairs={{0,4},{4,0},{1,5},{5,1},{2,6},{6,2},{3,7},{7,3},{8,12},{12,8},{9,1... | collective-permute-start | bytes 73736 | tf_op jit(solution)/shard_map/ppermute | solution.py:370
  68.4 7.3 %collective-permute-start.30 = (f32[3,2,8,128]{3,2,1,0:T(8,128)S(1)}, f32[3,2,8,128]{3,2,1,0:T(8,128)S(1)}, u32[]{:S(2)}, u32[]{:S(2)}) collective-permute-start(f32[3,2,8,128]{3,2,1,0:T(8,128)S(1)} %copy-done.59), channel_id=1, source_target_pairs={{0,8},{8,16},{16,24},{24,0},{1,9},{9,17},{17,25},{25,1},{2,10},{10... | collective-permute-start | bytes 73736 | tf_op jit(solution)/shard_map/ppermute | solution.py:368
  68.5 8.4 %collective-permute-start.31 = (f32[3,2,8,128]{3,2,1,0:T(8,128)S(1)}, f32[3,2,8,128]{3,2,1,0:T(8,128)S(1)}, u32[]{:S(2)}, u32[]{:S(2)}) collective-permute-start(f32[3,2,8,128]{3,2,1,0:T(8,128)S(1)} %copy-done.55), channel_id=1, source_target_pairs={{8,0},{16,8},{24,16},{0,24},{9,1},{17,9},{25,17},{1,25},{10,2},{18... | collective-permute-start | bytes 73736 | tf_op jit(solution)/shard_map/ppermute | solution.py:369
  70.3 6.6 %collective-permute-start.32 = (f32[2,3,8,128]{3,2,1,0:T(8,128)S(1)}, f32[2,3,8,128]{3,2,1,0:T(8,128)S(1)}, u32[]{:S(2)}, u32[]{:S(2)}) collective-permute-start(f32[2,3,8,128]{3,2,1,0:T(8,128)S(1)} %copy-done.51), channel_id=1, source_target_pairs={{0,4},{4,0},{1,5},{5,1},{2,6},{6,2},{3,7},{7,3},{8,12},{12,8},{9,1... | collective-permute-start | bytes 73736 | tf_op jit(solution)/shard_map/ppermute | solution.py:370
  71.3 7.4 %collective-permute-start.33 = (f32[3,2,8,128]{3,2,1,0:T(8,128)}, f32[3,2,8,128]{3,2,1,0:T(8,128)S(1)}, u32[]{:S(2)}, u32[]{:S(2)}) collective-permute-start(f32[3,2,8,128]{3,2,1,0:T(8,128)} %get-tuple-element.218), channel_id=1, source_target_pairs={{0,8},{8,16},{16,24},{24,0},{1,9},{9,17},{17,25},{25,1},{2,10},{10... | collective-permute-start | bytes 73736 | tf_op jit(solution)/shard_map/ppermute | solution.py:368
  73.9 5.6 %copy-start.7 = (f32[2,3,8,128]{3,2,1,0:T(8,128)}, f32[2,3,8,128]{3,2,1,0:T(8,128)S(1)}, u32[]{:S(2)}) copy-start(f32[2,3,8,128]{3,2,1,0:T(8,128)S(1)} %collective-permute-done.29.rest_3_.rest_4_) | copy-start | bytes 73732
  73.9 10.8 %collective-permute-start.34 = (f32[3,2,8,128]{3,2,1,0:T(8,128)S(1)}, f32[3,2,8,128]{3,2,1,0:T(8,128)S(1)}, u32[]{:S(2)}, u32[]{:S(2)}) collective-permute-start(f32[3,2,8,128]{3,2,1,0:T(8,128)S(1)} %copy-done.43), channel_id=1, source_target_pairs={{8,0},{16,8},{24,16},{0,24},{9,1},{17,9},{25,17},{1,25},{10,2},{18... | collective-permute-start | bytes 73736 | tf_op jit(solution)/shard_map/ppermute | solution.py:369
  75.7 6.4 %copy-start.30 = (f32[3,2,8,128]{3,2,1,0:T(8,128)}, f32[3,2,8,128]{3,2,1,0:T(8,128)S(1)}, u32[]{:S(2)}) copy-start(f32[3,2,8,128]{3,2,1,0:T(8,128)S(1)} %collective-permute-done.30.rest_1_) | copy-start | bytes 73732
  75.7 9.0 %collective-permute-start.35 = (f32[2,3,8,128]{3,2,1,0:T(8,128)S(1)}, f32[2,3,8,128]{3,2,1,0:T(8,128)S(1)}, u32[]{:S(2)}, u32[]{:S(2)}) collective-permute-start(f32[2,3,8,128]{3,2,1,0:T(8,128)S(1)} %copy-done.42), channel_id=1, source_target_pairs={{0,4},{4,0},{1,5},{5,1},{2,6},{6,2},{3,7},{7,3},{8,12},{12,8},{9,1... | collective-permute-start | bytes 73736 | tf_op jit(solution)/shard_map/ppermute | solution.py:370
  76.9 11.1 %collective-permute-start.36 = (f32[3,2,8,128]{3,2,1,0:T(8,128)}, f32[3,2,8,128]{3,2,1,0:T(8,128)S(1)}, u32[]{:S(2)}, u32[]{:S(2)}) collective-permute-start(f32[3,2,8,128]{3,2,1,0:T(8,128)} %get-tuple-element.225), channel_id=1, source_target_pairs={{0,8},{8,16},{16,24},{24,0},{1,9},{9,17},{17,25},{25,1},{2,10},{10... | collective-permute-start | bytes 73736 | tf_op jit(solution)/shard_map/ppermute | solution.py:368
  76.9 11.0 %collective-permute-start.37 = (f32[3,2,8,128]{3,2,1,0:T(8,128)}, f32[3,2,8,128]{3,2,1,0:T(8,128)S(1)}, u32[]{:S(2)}, u32[]{:S(2)}) collective-permute-start(f32[3,2,8,128]{3,2,1,0:T(8,128)} %get-tuple-element.226), channel_id=1, source_target_pairs={{8,0},{16,8},{24,16},{0,24},{9,1},{17,9},{25,17},{1,25},{10,2},{18... | collective-permute-start | bytes 73736 | tf_op jit(solution)/shard_map/ppermute | solution.py:369
  78.6 9.3 %collective-permute-start.38 = (f32[2,3,8,128]{3,2,1,0:T(8,128)}, f32[2,3,8,128]{3,2,1,0:T(8,128)S(1)}, u32[]{:S(2)}, u32[]{:S(2)}) collective-permute-start(f32[2,3,8,128]{3,2,1,0:T(8,128)} %get-tuple-element.227), channel_id=1, source_target_pairs={{0,4},{4,0},{1,5},{5,1},{2,6},{6,2},{3,7},{7,3},{8,12},{12,8},{9,1... | collective-permute-start | bytes 73736 | tf_op jit(solution)/shard_map/ppermute | solution.py:370
  95.0 6.3 %collective-permute-start.39 = (f32[8,8,128]{2,1,0:T(8,128)}, f32[8,8,128]{2,1,0:T(8,128)S(1)}, u32[]{:S(2)}, u32[]{:S(2)}) collective-permute-start(f32[8,8,128]{2,1,0:T(8,128)} %get-tuple-element.232.rest_0_), channel_id=1, source_target_pairs={{0,1},{1,2},{2,3},{3,0},{4,5},{5,6},{6,7},{7,4},{8,9},{9,10},{10,1... | collective-permute-start | bytes 98312 | tf_op jit(solution)/shard_map/ppermute | solution.py:467
  96.1 5.5 %collective-permute-start.40 = (f32[8,8,128]{2,1,0:T(8,128)}, f32[8,8,128]{2,1,0:T(8,128)S(1)}, u32[]{:S(2)}, u32[]{:S(2)}) collective-permute-start(f32[8,8,128]{2,1,0:T(8,128)} %get-tuple-element.232.rest_0_), channel_id=1, source_target_pairs={{0,2},{1,3},{2,0},{3,1},{4,6},{5,7},{6,4},{7,5},{8,10},{9,11},{10,... | collective-permute-start | bytes 98312 | tf_op jit(solution)/shard_map/ppermute | solution.py:467
  98.7 4.1 %collective-permute-start.41 = (f32[8,8,128]{2,1,0:T(8,128)}, f32[8,8,128]{2,1,0:T(8,128)S(1)}, u32[]{:S(2)}, u32[]{:S(2)}) collective-permute-start(f32[8,8,128]{2,1,0:T(8,128)} %get-tuple-element.232.rest_0_), channel_id=1, source_target_pairs={{0,3},{1,0},{2,1},{3,2},{4,7},{5,4},{6,5},{7,6},{8,11},{9,8},{10,9... | collective-permute-start | bytes 98312 | tf_op jit(solution)/shard_map/ppermute | solution.py:467
  (54 other events, 170.1 us)

commit v13 on v8

--- a/solution.py
+++ b/solution.py
@@ -123,11 +123,13 @@
         y_ref[1, f] = y_l[f]
 
 
-def make_section_kernel(chunk, first):
+def make_section_kernel(chunk, first, last):
     def kernel(h_ref, w_ref, c_ref, m_ref, sill_ref, co_ref, *rest):
+        if last:
+            rest = rest + (None, None, None)
         if first:
             xflo_ref, xfhi_ref, yflo_ref, yfhi_ref = rest[:4]
-            ho_ref, wo_ref, cbo_ref, mo_ref, xf_ref, xl_ref, y_ref, nb_ref = rest[4:]
+            ho_ref, wo_ref, cbo_ref, mo_ref, nb_ref, xf_ref, xl_ref, y_ref = rest[4:]
             xslo_ref, xshi_ref, yslo_ref, yshi_ref = xflo_ref, xfhi_ref, yflo_ref, yfhi_ref
             cylo = [yflo_ref[1, f] for f in (3, 4)]
             cyhi = [yfhi_ref[0, f] for f in (3, 4)]
@@ -217,17 +219,20 @@
                 wo_ref[i] = water_two
                 cbo_ref[i] = carbon_two
                 mo_ref[i] = melt_two
-                acc.add_y([heat_three, water_two, carbon_two], d, lane)
-            planes = pl.ds(a * ROWS, ROWS)
-            for f, out in enumerate((ho_ref, wo_ref, cbo_ref)):
-                xf_ref[f, a] = out[planes, 0, :]
-                xl_ref[f, a] = out[planes, ROWS - 1, :]
+                if not last:
+                    acc.add_y([heat_three, water_two, carbon_two], d, lane)
+            if not last:
+                planes = pl.ds(a * ROWS, ROWS)
+                for f, out in enumerate((ho_ref, wo_ref, cbo_ref)):
+                    xf_ref[f, a] = out[planes, 0, :]
+                    xl_ref[f, a] = out[planes, ROWS - 1, :]
             return (tuple(acc.yf), tuple(acc.yl))
 
         y_f, y_l = lax.fori_loop(0, groups, group, ((zero,) * 3, (zero,) * 3))
-        for f in range(3):
-            y_ref[0, f] = y_f[f]
-            y_ref[1, f] = y_l[f]
+        if not last:
+            for f in range(3):
+                y_ref[0, f] = y_f[f]
+                y_ref[1, f] = y_l[f]
 
     return kernel
 
@@ -421,11 +426,11 @@
     for section_no in range(SECTIONS):
         first = section_no == 0
         for k in range(chunks):
+            last = section_no + 1 == SECTIONS
             args = [heat, water, carbon, melt, injection_flags, co]
             in_specs = [block_spec(k)] * 5
-            out_shape = [sds(shape)] * 4 + [sds((3, cgroups, ROWS, LANES))] * 2
-            out_shape += [sds((2, 3, ROWS, LANES))]
-            out_specs = [block_spec(k)] * 4 + [x3, x3, y3]
+            out_shape = [sds(shape)] * 4
+            out_specs = [block_spec(k)] * 4
             if first:
                 x5 = pl.BlockSpec((5, cgroups, ROWS, LANES), lambda i, k=k: (0, k, 0, 0))
                 y5 = full_spec((2, 5, ROWS, LANES))
@@ -438,19 +443,23 @@
                 in_specs += [pl.BlockSpec((2, depth, ROWS, LANES), lambda i, k=k: (0, k, 0, 0)),
                              near_spec, x3, x3, y3, y3]
                 args += [nears[k]] + list(halos[k])
+            if not last:
+                out_shape += [sds((3, cgroups, ROWS, LANES))] * 2 + [sds((2, 3, ROWS, LANES))]
+                out_specs += [x3, x3, y3]
             outs = pl.pallas_call(
-                make_section_kernel(k, first),
+                make_section_kernel(k, first, last),
                 grid=(1,),
                 out_shape=tuple(out_shape),
                 in_specs=in_specs,
                 out_specs=out_specs,
                 input_output_aliases={0: 0, 1: 1, 2: 2, 3: 3},
             )(*args)
-            heat, water, carbon, melt, xf, xl, ys = outs[:7]
+            heat, water, carbon, melt = outs[:4]
+            rest = list(outs[4:])
             if first:
-                nears[k] = outs[7]
-            if section_no + 1 < SECTIONS:
-                halos[k] = exchange(xf, xl, ys)
+                nears[k] = rest.pop(0)
+            if not last:
+                halos[k] = exchange(*rest)
 
     y, a, b, red = pl.pallas_call(
         sweep_kernel,

time: 78.9 us -> 78 us (0.989)
  Pallas kernels: 41.4 us -> 40.5 us
    pallas_call x8, Pallas kernels: 30.6 us -> 29.7 us  [local(): pl.pallas_call(make_section_kernel(k, first, last), grid=(1,), out_shape=...]
  transfers between devices with their start and end apart: 24 -> 24, of which waited for: 5 -> 5; matrix products, arithmetic and copies ran while one was open for 0% -> 0% of each run, Pallas kernels for 29% -> 28%
where the time goes in v13:
time: 78 us; the launch traced here: 77.6 us
  Pallas kernels  40.5 us (52%)
  starting transfers between devices  25.9 us (33%)
  waiting for transfers between devices  5.37 us (7%)
  local copies, waits for them, and re-layouts  4.95 us (6%)
  between operations  0.83 us (1%)
    pallas_call x8, Pallas kernels, local(): pl.pallas_call(make_section_kernel(k, first, last), grid=(1,), out_shape=...  29.7 us
    ppermute x7, starting transfers between devices, exchange(): xhi = lax.ppermute(xf, 'east', east_bwd)  9.42 us
    ppermute x7, starting transfers between devices, exchange(): ylo = lax.ppermute(ys, 'north', north_fwd)  8.35 us
    ppermute x3, starting transfers between devices, local(): lax.ppermute(red, 'depth', [(i, (i + k) % count) for i in range(count)])  5.4 us
    unnamed x48, local copies, waits for them, and re-layouts  4.95 us
    pallas_call x1, Pallas kernels, local(): pl.pallas_call(prep_kernel, out_shape=(sds(shape), sds(shape), sds(shape)...  4.57 us
    pallas_call x1, Pallas kernels, local(): pl.pallas_call(sweep_kernel, grid=(1,), out_shape=(sds(shape), sds(shape)...  3.87 us
    ppermute x3, waiting for transfers between devices, local(): lax.ppermute(red, 'depth', [(i, (i + k) % count) for i in range(count)])  2.77 us
  transfers between devices with their start and end apart: 24, of which 5 were waited for; matrix products, arithmetic and copies ran while one was open for 0% of the time, Pallas kernels for 28%

profile of v13, /device:TPU:0, one launch (start us, length us, event | category | flops | bytes accessed | tf_op | source)
XLA Modules:
  0.0 77.6 jit_solution(4210358893472801090)
XLA Ops:
  0.6 4.6 %shard_map.120 = (f32[64,8,128]{2,1,0:T(8,128)}, f32[64,8,128]{2,1,0:T(8,128)}, f32[64,8,128]{2,1,0:T(8,128)}, f32[64,8,128]{2,1,0:T(8,128)}, f32[5,64,8,128]{3,...) custom-call(f32[2,12]{1,0:T(2,128)} %lat_ref.1, f32[12]{0:T(128)} %vert_ref.1, ...), custom_call_target="tpu_custom_call" | custom-call | tf_op jit(solution)/shard_map/pallas_call | solution.py:408
  5.2 0.5 collective-permute-start
  5.7 2.0 %collective-permute-start.1 = (f32[5,8,8,128]{3,2,1,0:T(8,128)}, f32[5,8,8,128]{3,2,1,0:T(8,128)S(1)}, u32[]{:S(2)}, u32[]{:S(2)}) collective-permute-start(f32[5,8,8,128]{3,2,1,0:T(8,128)} %get-tuple-element.74), channel_id=1, source_target_pairs={{8,0},{16,8},{24,16},{0,24},{9,1},{17,9},{25,17},{1,25},{10,2},{18... | collective-permute-start | bytes 491528 | tf_op jit(solution)/shard_map/ppermute | solution.py:374
  7.7 2.3 %collective-permute-start.2 = (f32[2,5,8,128]{3,2,1,0:T(8,128)}, f32[2,5,8,128]{3,2,1,0:T(8,128)S(1)}, u32[]{:S(2)}, u32[]{:S(2)}) collective-permute-start(f32[2,5,8,128]{3,2,1,0:T(8,128)} %get-tuple-element.75), channel_id=1, source_target_pairs={{0,4},{4,0},{1,5},{5,1},{2,6},{6,2},{3,7},{7,3},{8,12},{12,8},{9,1... | collective-permute-start | bytes 122888 | tf_op jit(solution)/shard_map/ppermute | solution.py:375
  10.0 2.2 %collective-permute-done.2.rest_2_.rest_3_ = f32[2,5,8,128]{3,2,1,0:T(8,128)S(1)} collective-permute-done((f32[2,5,8,128]{3,2,1,0:T(8,128)}, f32[2,5,8,128]{3,2,1,0:T(8,128)S(1)}, u32[]{:S(2)}, u32[]{:S(2)}) %collective-permute-start.2) | collective-permute-done | bytes 40992 | tf_op jit(solution)/shard_map/ppermute | solution.py:375
  12.2 0.4 collective-permute-done.1.rest_1_
  12.5 0.2 copy-done.2
  12.8 0.1 copy-done
  12.8 0.4 copy-done.1
  13.2 4.5 %shard_map.121 = (f32[64,8,128]{2,1,0:T(8,128)}, f32[64,8,128]{2,1,0:T(8,128)}, f32[64,8,128]{2,1,0:T(8,128)}, f32[64,8,128]{2,1,0:T(8,128)}, f32[8,32,8,128]{3,...) custom-call(f32[64,8,128]{2,1,0:T(8,128)} %get-tuple-element.68.h_re, ...), custom_call_target="tpu_custom_call", output_to_operand_aliasing={{0}: (0, {}), {1}: (1, {}), {2}: (2, {}), {3}: (3, {})} | custom-call | tf_op jit(solution)/shard_map/pallas_call | solution.py:449
  17.7 0.7 collective-permute-start.3
  18.4 1.3 %collective-permute-start.4 = (f32[3,4,8,128]{3,2,1,0:T(8,128)}, f32[3,4,8,128]{3,2,1,0:T(8,128)S(1)}, u32[]{:S(2)}, u32[]{:S(2)}) collective-permute-start(f32[3,4,8,128]{3,2,1,0:T(8,128)} %get-tuple-element.86), channel_id=1, source_target_pairs={{8,0},{16,8},{24,16},{0,24},{9,1},{17,9},{25,17},{1,25},{10,2},{18... | collective-permute-start | bytes 147464 | tf_op jit(solution)/shard_map/ppermute | solution.py:374
  19.8 1.4 %collective-permute-start.5 = (f32[2,3,8,128]{3,2,1,0:T(8,128)}, f32[2,3,8,128]{3,2,1,0:T(8,128)S(1)}, u32[]{:S(2)}, u32[]{:S(2)}) collective-permute-start(f32[2,3,8,128]{3,2,1,0:T(8,128)} %get-tuple-element.87), channel_id=1, source_target_pairs={{0,4},{4,0},{1,5},{5,1},{2,6},{6,2},{3,7},{7,3},{8,12},{12,8},{9,1... | collective-permute-start | bytes 73736 | tf_op jit(solution)/shard_map/ppermute | solution.py:375
  21.2 4.5 %shard_map.122 = (f32[64,8,128]{2,1,0:T(8,128)}, f32[64,8,128]{2,1,0:T(8,128)}, f32[64,8,128]{2,1,0:T(8,128)}, f32[64,8,128]{2,1,0:T(8,128)}, f32[8,32,8,128]{3,...) custom-call(f32[64,8,128]{2,1,0:T(8,128)} %get-tuple-element.76.h_re, ...), custom_call_target="tpu_custom_call", output_to_operand_aliasing={{0}: (0, {}), {1}: (1, {}), {2}: (2, {}), {3}: (3, {})} | custom-call | tf_op jit(solution)/shard_map/pallas_call | solution.py:449
  25.7 1.7 %collective-permute-start.7 = (f32[3,4,8,128]{3,2,1,0:T(8,128)}, f32[3,4,8,128]{3,2,1,0:T(8,128)S(1)}, u32[]{:S(2)}, u32[]{:S(2)}) collective-permute-start(f32[3,4,8,128]{3,2,1,0:T(8,128)} %get-tuple-element.94), channel_id=1, source_target_pairs={{8,0},{16,8},{24,16},{0,24},{9,1},{17,9},{25,17},{1,25},{10,2},{18... | collective-permute-start | bytes 147464 | tf_op jit(solution)/shard_map/ppermute | solution.py:374
  27.5 0.6 collective-permute-start.8
  28.1 0.6 copy-done.17
  28.7 3.6 %shard_map.123 = (f32[64,8,128]{2,1,0:T(8,128)}, f32[64,8,128]{2,1,0:T(8,128)}, f32[64,8,128]{2,1,0:T(8,128)}, f32[64,8,128]{2,1,0:T(8,128)}, f32[3,4,8,128]{3,2...) custom-call(f32[64,8,128]{2,1,0:T(8,128)} %get-tuple-element.80.h_re, ...), custom_call_target="tpu_custom_call", output_to_operand_aliasing={{0}: (0, {}), {1}: (1, {}), {2}: (2, {}), {3}: (3, {})} | custom-call | tf_op jit(solution)/shard_map/pallas_call | solution.py:449
  32.3 0.2 collective-permute-start.10
  32.5 0.3 collective-permute-start.9
  32.9 1.4 %collective-permute-start.11 = (f32[2,3,8,128]{3,2,1,0:T(8,128)}, f32[2,3,8,128]{3,2,1,0:T(8,128)S(1)}, u32[]{:S(2)}, u32[]{:S(2)}) collective-permute-start(f32[2,3,8,128]{3,2,1,0:T(8,128)} %get-tuple-element.102), channel_id=1, source_target_pairs={{0,4},{4,0},{1,5},{5,1},{2,6},{6,2},{3,7},{7,3},{8,12},{12,8},{9,1... | collective-permute-start | bytes 73736 | tf_op jit(solution)/shard_map/ppermute | solution.py:375
  34.3 0.6 copy-done.9
  34.9 3.6 %shard_map.124 = (f32[64,8,128]{2,1,0:T(8,128)}, f32[64,8,128]{2,1,0:T(8,128)}, f32[64,8,128]{2,1,0:T(8,128)}, f32[64,8,128]{2,1,0:T(8,128)}, f32[3,4,8,128]{3,2...) custom-call(f32[64,8,128]{2,1,0:T(8,128)} %get-tuple-element.88.h_re, ...), custom_call_target="tpu_custom_call", output_to_operand_aliasing={{0}: (0, {}), {1}: (1, {}), {2}: (2, {}), {3}: (3, {})} | custom-call | tf_op jit(solution)/shard_map/pallas_call | solution.py:449
  38.5 0.9 %collective-permute-start.12 = (f32[3,4,8,128]{3,2,1,0:T(8,128)}, f32[3,4,8,128]{3,2,1,0:T(8,128)S(1)}, u32[]{:S(2)}, u32[]{:S(2)}) collective-permute-start(f32[3,4,8,128]{3,2,1,0:T(8,128)} %get-tuple-element.107), channel_id=1, source_target_pairs={{0,8},{8,16},{16,24},{24,0},{1,9},{9,17},{17,25},{25,1},{2,10},{10... | collective-permute-start | bytes 147464 | tf_op jit(solution)/shard_map/ppermute | solution.py:373
  39.4 0.9 %collective-permute-start.13 = (f32[3,4,8,128]{3,2,1,0:T(8,128)}, f32[3,4,8,128]{3,2,1,0:T(8,128)S(1)}, u32[]{:S(2)}, u32[]{:S(2)}) collective-permute-start(f32[3,4,8,128]{3,2,1,0:T(8,128)} %get-tuple-element.108), channel_id=1, source_target_pairs={{8,0},{16,8},{24,16},{0,24},{9,1},{17,9},{25,17},{1,25},{10,2},{18... | collective-permute-start | bytes 147464 | tf_op jit(solution)/shard_map/ppermute | solution.py:374
  40.3 0.6 collective-permute-start.14
  40.9 0.6 copy-done.10
  41.5 3.6 %shard_map.125 = (f32[64,8,128]{2,1,0:T(8,128)}, f32[64,8,128]{2,1,0:T(8,128)}, f32[64,8,128]{2,1,0:T(8,128)}, f32[64,8,128]{2,1,0:T(8,128)}, f32[3,4,8,128]{3,2...) custom-call(f32[64,8,128]{2,1,0:T(8,128)} %get-tuple-element.96.h_re, ...), custom_call_target="tpu_custom_call", output_to_operand_aliasing={{0}: (0, {}), {1}: (1, {}), {2}: (2, {}), {3}: (3, {})} | custom-call | tf_op jit(solution)/shard_map/pallas_call | solution.py:449
  45.1 0.2 collective-permute-start.15
  45.3 1.6 %collective-permute-start.16 = (f32[3,4,8,128]{3,2,1,0:T(8,128)}, f32[3,4,8,128]{3,2,1,0:T(8,128)S(1)}, u32[]{:S(2)}, u32[]{:S(2)}) collective-permute-start(f32[3,4,8,128]{3,2,1,0:T(8,128)} %get-tuple-element.115), channel_id=1, source_target_pairs={{8,0},{16,8},{24,16},{0,24},{9,1},{17,9},{25,17},{1,25},{10,2},{18... | collective-permute-start | bytes 147464 | tf_op jit(solution)/shard_map/ppermute | solution.py:374
  46.9 1.4 %collective-permute-start.17 = (f32[2,3,8,128]{3,2,1,0:T(8,128)}, f32[2,3,8,128]{3,2,1,0:T(8,128)S(1)}, u32[]{:S(2)}, u32[]{:S(2)}) collective-permute-start(f32[2,3,8,128]{3,2,1,0:T(8,128)} %get-tuple-element.116), channel_id=1, source_target_pairs={{0,4},{4,0},{1,5},{5,1},{2,6},{6,2},{3,7},{7,3},{8,12},{12,8},{9,1... | collective-permute-start | bytes 73736 | tf_op jit(solution)/shard_map/ppermute | solution.py:375
  48.3 0.6 copy-done.11
  48.9 3.6 %shard_map.126 = (f32[64,8,128]{2,1,0:T(8,128)}, f32[64,8,128]{2,1,0:T(8,128)}, f32[64,8,128]{2,1,0:T(8,128)}, f32[64,8,128]{2,1,0:T(8,128)}, f32[3,4,8,128]{3,2...) custom-call(f32[64,8,128]{2,1,0:T(8,128)} %get-tuple-element.103.h_r, ...), custom_call_target="tpu_custom_call", output_to_operand_aliasing={{0}: (0, {}), {1}: (1, {}), {2}: (2, {}), {3}: (3, {})} | custom-call | tf_op jit(solution)/shard_map/pallas_call | solution.py:449
  52.6 1.7 %collective-permute-start.19 = (f32[3,4,8,128]{3,2,1,0:T(8,128)}, f32[3,4,8,128]{3,2,1,0:T(8,128)S(1)}, u32[]{:S(2)}, u32[]{:S(2)}) collective-permute-start(f32[3,4,8,128]{3,2,1,0:T(8,128)} %get-tuple-element.122), channel_id=1, source_target_pairs={{8,0},{16,8},{24,16},{0,24},{9,1},{17,9},{25,17},{1,25},{10,2},{18... | collective-permute-start | bytes 147464 | tf_op jit(solution)/shard_map/ppermute | solution.py:374
  54.3 0.6 collective-permute-start.20
  55.0 0.6 copy-done.14
  55.6 3.2 %shard_map.127 = (f32[64,8,128]{2,1,0:T(8,128)}, f32[64,8,128]{2,1,0:T(8,128)}, f32[64,8,128]{2,1,0:T(8,128)}, f32[64,8,128]{2,1,0:T(8,128)}) custom-call(f32[64,8,128]{2,1,0:T(8,128)} %get-tuple-element.110.h_ref, f32[64,8,128]{2,1,0:T(8,128)} %get-tuple-element.111.w_ref, ...), custom_call_target="tpu_custom_call", output_to_operand_aliasing={{0}: (0, {}), {1}: (1, {}), {2}: (2, {}), {3}: (3, {})} | custom-call | tf_op jit(solution)/shard_map/pallas_call | solution.py:449
  58.8 0.5 copy-done.8
  59.4 3.2 %shard_map.128 = (f32[64,8,128]{2,1,0:T(8,128)}, f32[64,8,128]{2,1,0:T(8,128)}, f32[64,8,128]{2,1,0:T(8,128)}, f32[64,8,128]{2,1,0:T(8,128)}) custom-call(f32[64,8,128]{2,1,0:T(8,128)} %get-tuple-element.117.h_ref, f32[64,8,128]{2,1,0:T(8,128)} %get-tuple-element.118.w_ref, ...), custom_call_target="tpu_custom_call", output_to_operand_aliasing={{0}: (0, {}), {1}: (1, {}), {2}: (2, {}), {3}: (3, {})} | custom-call | tf_op jit(solution)/shard_map/pallas_call | solution.py:449
  62.6 3.9 %shard_map.129 = (f32[64,8,128]{2,1,0:T(8,128)}, f32[64,8,128]{2,1,0:T(8,128)}, f32[64,8,128]{2,1,0:T(8,128)}, f32[8,8,128]{2,1,0:T(8,128)}) custom-call(f32[64,8,128]{2,1,0:T(8,128)} %get-tuple-element.124.r_ref, f32[5,64,8,128]{3,2,1,0:T(8,128)} %get-tuple-element.72.co_ref.cz_ref), custom_call_target="tpu_custom_call" | custom-call | tf_op jit(solution)/shard_map/pallas_call | solution.py:464
  66.4 1.5 %collective-permute-start.21 = (f32[8,8,128]{2,1,0:T(8,128)}, f32[8,8,128]{2,1,0:T(8,128)S(1)}, u32[]{:S(2)}, u32[]{:S(2)}) collective-permute-start(f32[8,8,128]{2,1,0:T(8,128)} %get-tuple-element.128.rest_0_), channel_id=1, source_target_pairs={{0,1},{1,2},{2,3},{3,0},{4,5},{5,6},{6,7},{7,4},{8,9},{9,10},{10,1... | collective-permute-start | bytes 98312 | tf_op jit(solution)/shard_map/ppermute | solution.py:476
  67.9 2.6 %collective-permute-start.22 = (f32[8,8,128]{2,1,0:T(8,128)}, f32[8,8,128]{2,1,0:T(8,128)S(1)}, u32[]{:S(2)}, u32[]{:S(2)}) collective-permute-start(f32[8,8,128]{2,1,0:T(8,128)} %get-tuple-element.128.rest_0_), channel_id=1, source_target_pairs={{0,2},{1,3},{2,0},{3,1},{4,6},{5,7},{6,4},{7,5},{8,10},{9,11},{10,... | collective-permute-start | bytes 98312 | tf_op jit(solution)/shard_map/ppermute | solution.py:476
  70.5 1.3 %collective-permute-start.23 = (f32[8,8,128]{2,1,0:T(8,128)}, f32[8,8,128]{2,1,0:T(8,128)S(1)}, u32[]{:S(2)}, u32[]{:S(2)}) collective-permute-start(f32[8,8,128]{2,1,0:T(8,128)} %get-tuple-element.128.rest_0_), channel_id=1, source_target_pairs={{0,3},{1,0},{2,1},{3,2},{4,7},{5,4},{6,5},{7,6},{8,11},{9,8},{10,9... | collective-permute-start | bytes 98312 | tf_op jit(solution)/shard_map/ppermute | solution.py:476
  71.8 1.0 %collective-permute-done.21.rest_1_ = f32[8,8,128]{2,1,0:T(8,128)S(1)} collective-permute-done((f32[8,8,128]{2,1,0:T(8,128)}, f32[8,8,128]{2,1,0:T(8,128)S(1)}, u32[]{:S(2)}, u32[]{:S(2)}) %collective-permute-start.21) | collective-permute-done | bytes 32800 | tf_op jit(solution)/shard_map/ppermute | solution.py:476
  72.8 0.6 collective-permute-done.22.rest_2_
  73.4 1.2 %collective-permute-done.23.rest_3_ = f32[8,8,128]{2,1,0:T(8,128)S(1)} collective-permute-done((f32[8,8,128]{2,1,0:T(8,128)}, f32[8,8,128]{2,1,0:T(8,128)S(1)}, u32[]{:S(2)}, u32[]{:S(2)}) %collective-permute-start.23) | collective-permute-done | bytes 32800 | tf_op jit(solution)/shard_map/ppermute | solution.py:476
  74.6 0.6 copy-done.23
  75.2 2.4 %shard_map.130 = f32[64,8,128]{2,1,0:T(8,128)} custom-call(s32[1]{0:T(128)} %bitcast.rank_ref, f32[64,8,128]{2,1,0:T(8,128)} %get-tuple-element.125.y_ref, f32[64,8,128]{2,1,0:T(8,128)} %get-tuple-element.126.a_ref, f32[64,8,128]{2,1,0:T(8,128)} %get-tuple-element.127.b_ref, f32[8,8,128]{2,1,0:T(8,128)} %get-tuple-element.128.rest_0_, ...), custom_call_target="tpu_custom_call" | custom-call | tf_op jit(solution)/shard_map/pallas_call | solution.py:478
  (59 shorter events, 0.4 us)
Async XLA Ops:
  5.2 7.0 %collective-permute-start = (f32[5,8,8,128]{3,2,1,0:T(8,128)}, f32[5,8,8,128]{3,2,1,0:T(8,128)S(1)}, u32[]{:S(2)}, u32[]{:S(2)}) collective-permute-start(f32[5,8,8,128]{3,2,1,0:T(8,128)} %get-tuple-element.73), channel_id=1, source_target_pairs={{0,8},{8,16},{16,24},{24,0},{1,9},{9,17},{17,25},{25,1},{2,10},{10... | collective-permute-start | bytes 491528 | tf_op jit(solution)/shard_map/ppermute | solution.py:373
  5.7 6.8 %collective-permute-start.1 = (f32[5,8,8,128]{3,2,1,0:T(8,128)}, f32[5,8,8,128]{3,2,1,0:T(8,128)S(1)}, u32[]{:S(2)}, u32[]{:S(2)}) collective-permute-start(f32[5,8,8,128]{3,2,1,0:T(8,128)} %get-tuple-element.74), channel_id=1, source_target_pairs={{8,0},{16,8},{24,16},{0,24},{9,1},{17,9},{25,17},{1,25},{10,2},{18... | collective-permute-start | bytes 491528 | tf_op jit(solution)/shard_map/ppermute | solution.py:374
  7.7 4.5 %collective-permute-start.2 = (f32[2,5,8,128]{3,2,1,0:T(8,128)}, f32[2,5,8,128]{3,2,1,0:T(8,128)S(1)}, u32[]{:S(2)}, u32[]{:S(2)}) collective-permute-start(f32[2,5,8,128]{3,2,1,0:T(8,128)} %get-tuple-element.75), channel_id=1, source_target_pairs={{0,4},{4,0},{1,5},{5,1},{2,6},{6,2},{3,7},{7,3},{8,12},{12,8},{9,1... | collective-permute-start | bytes 122888 | tf_op jit(solution)/shard_map/ppermute | solution.py:375
  12.2 0.6 copy-start.2
  12.2 0.7 copy-start
  12.5 0.7 copy-start.1
  17.7 10.4 %collective-permute-start.3 = (f32[3,4,8,128]{3,2,1,0:T(8,128)}, f32[3,4,8,128]{3,2,1,0:T(8,128)S(1)}, u32[]{:S(2)}, u32[]{:S(2)}) collective-permute-start(f32[3,4,8,128]{3,2,1,0:T(8,128)} %get-tuple-element.85), channel_id=1, source_target_pairs={{0,8},{8,16},{16,24},{24,0},{1,9},{9,17},{17,25},{25,1},{2,10},{10... | collective-permute-start | bytes 147464 | tf_op jit(solution)/shard_map/ppermute | solution.py:373
  18.4 9.7 %collective-permute-start.4 = (f32[3,4,8,128]{3,2,1,0:T(8,128)}, f32[3,4,8,128]{3,2,1,0:T(8,128)S(1)}, u32[]{:S(2)}, u32[]{:S(2)}) collective-permute-start(f32[3,4,8,128]{3,2,1,0:T(8,128)} %get-tuple-element.86), channel_id=1, source_target_pairs={{8,0},{16,8},{24,16},{0,24},{9,1},{17,9},{25,17},{1,25},{10,2},{18... | collective-permute-start | bytes 147464 | tf_op jit(solution)/shard_map/ppermute | solution.py:374
  19.8 7.7 %collective-permute-start.5 = (f32[2,3,8,128]{3,2,1,0:T(8,128)}, f32[2,3,8,128]{3,2,1,0:T(8,128)S(1)}, u32[]{:S(2)}, u32[]{:S(2)}) collective-permute-start(f32[2,3,8,128]{3,2,1,0:T(8,128)} %get-tuple-element.87), channel_id=1, source_target_pairs={{0,4},{4,0},{1,5},{5,1},{2,6},{6,2},{3,7},{7,3},{8,12},{12,8},{9,1... | collective-permute-start | bytes 73736 | tf_op jit(solution)/shard_map/ppermute | solution.py:375
  25.7 8.6 %collective-permute-start.6 = (f32[3,4,8,128]{3,2,1,0:T(8,128)}, f32[3,4,8,128]{3,2,1,0:T(8,128)S(1)}, u32[]{:S(2)}, u32[]{:S(2)}) collective-permute-start(f32[3,4,8,128]{3,2,1,0:T(8,128)} %get-tuple-element.93), channel_id=1, source_target_pairs={{0,8},{8,16},{16,24},{24,0},{1,9},{9,17},{17,25},{25,1},{2,10},{10... | collective-permute-start | bytes 147464 | tf_op jit(solution)/shard_map/ppermute | solution.py:373
  25.7 8.6 %collective-permute-start.7 = (f32[3,4,8,128]{3,2,1,0:T(8,128)}, f32[3,4,8,128]{3,2,1,0:T(8,128)S(1)}, u32[]{:S(2)}, u32[]{:S(2)}) collective-permute-start(f32[3,4,8,128]{3,2,1,0:T(8,128)} %get-tuple-element.94), channel_id=1, source_target_pairs={{8,0},{16,8},{24,16},{0,24},{9,1},{17,9},{25,17},{1,25},{10,2},{18... | collective-permute-start | bytes 147464 | tf_op jit(solution)/shard_map/ppermute | solution.py:374
  27.5 0.7 copy-start.7
  27.5 5.4 %collective-permute-start.8 = (f32[2,3,8,128]{3,2,1,0:T(8,128)}, f32[2,3,8,128]{3,2,1,0:T(8,128)S(1)}, u32[]{:S(2)}, u32[]{:S(2)}) collective-permute-start(f32[2,3,8,128]{3,2,1,0:T(8,128)} %get-tuple-element.95), channel_id=1, source_target_pairs={{0,4},{4,0},{1,5},{5,1},{2,6},{6,2},{3,7},{7,3},{8,12},{12,8},{9,1... | collective-permute-start | bytes 73736 | tf_op jit(solution)/shard_map/ppermute | solution.py:375
  28.1 0.6 copy-start.17
  28.1 0.6 copy-start.18
  32.3 8.6 %collective-permute-start.10 = (f32[3,4,8,128]{3,2,1,0:T(8,128)}, f32[3,4,8,128]{3,2,1,0:T(8,128)S(1)}, u32[]{:S(2)}, u32[]{:S(2)}) collective-permute-start(f32[3,4,8,128]{3,2,1,0:T(8,128)} %get-tuple-element.101), channel_id=1, source_target_pairs={{8,0},{16,8},{24,16},{0,24},{9,1},{17,9},{25,17},{1,25},{10,2},{18... | collective-permute-start | bytes 147464 | tf_op jit(solution)/shard_map/ppermute | solution.py:374
  32.5 8.4 %collective-permute-start.9 = (f32[3,4,8,128]{3,2,1,0:T(8,128)}, f32[3,4,8,128]{3,2,1,0:T(8,128)S(1)}, u32[]{:S(2)}, u32[]{:S(2)}) collective-permute-start(f32[3,4,8,128]{3,2,1,0:T(8,128)} %get-tuple-element.100), channel_id=1, source_target_pairs={{0,8},{8,16},{16,24},{24,0},{1,9},{9,17},{17,25},{25,1},{2,10},{10... | collective-permute-start | bytes 147464 | tf_op jit(solution)/shard_map/ppermute | solution.py:373
  32.9 1.4 %copy-start.3 = (f32[2,3,8,128]{3,2,1,0:T(8,128)}, f32[2,3,8,128]{3,2,1,0:T(8,128)S(1)}, u32[]{:S(2)}) copy-start(f32[2,3,8,128]{3,2,1,0:T(8,128)S(1)} %collective-permute-done.8.rest_3_.rest_4_) | copy-start | bytes 73732
  32.9 7.4 %collective-permute-start.11 = (f32[2,3,8,128]{3,2,1,0:T(8,128)}, f32[2,3,8,128]{3,2,1,0:T(8,128)S(1)}, u32[]{:S(2)}, u32[]{:S(2)}) collective-permute-start(f32[2,3,8,128]{3,2,1,0:T(8,128)} %get-tuple-element.102), channel_id=1, source_target_pairs={{0,4},{4,0},{1,5},{5,1},{2,6},{6,2},{3,7},{7,3},{8,12},{12,8},{9,1... | collective-permute-start | bytes 73736 | tf_op jit(solution)/shard_map/ppermute | solution.py:375
  34.3 0.6 copy-start.9
  34.3 0.6 copy-start.12
  38.5 9.8 %collective-permute-start.12 = (f32[3,4,8,128]{3,2,1,0:T(8,128)}, f32[3,4,8,128]{3,2,1,0:T(8,128)S(1)}, u32[]{:S(2)}, u32[]{:S(2)}) collective-permute-start(f32[3,4,8,128]{3,2,1,0:T(8,128)} %get-tuple-element.107), channel_id=1, source_target_pairs={{0,8},{8,16},{16,24},{24,0},{1,9},{9,17},{17,25},{25,1},{2,10},{10... | collective-permute-start | bytes 147464 | tf_op jit(solution)/shard_map/ppermute | solution.py:373
  39.4 8.9 %collective-permute-start.13 = (f32[3,4,8,128]{3,2,1,0:T(8,128)}, f32[3,4,8,128]{3,2,1,0:T(8,128)S(1)}, u32[]{:S(2)}, u32[]{:S(2)}) collective-permute-start(f32[3,4,8,128]{3,2,1,0:T(8,128)} %get-tuple-element.108), channel_id=1, source_target_pairs={{8,0},{16,8},{24,16},{0,24},{9,1},{17,9},{25,17},{1,25},{10,2},{18... | collective-permute-start | bytes 147464 | tf_op jit(solution)/shard_map/ppermute | solution.py:374
  40.3 0.7 copy-start.4
  40.3 6.6 %collective-permute-start.14 = (f32[2,3,8,128]{3,2,1,0:T(8,128)}, f32[2,3,8,128]{3,2,1,0:T(8,128)S(1)}, u32[]{:S(2)}, u32[]{:S(2)}) collective-permute-start(f32[2,3,8,128]{3,2,1,0:T(8,128)} %get-tuple-element.109), channel_id=1, source_target_pairs={{0,4},{4,0},{1,5},{5,1},{2,6},{6,2},{3,7},{7,3},{8,12},{12,8},{9,1... | collective-permute-start | bytes 73736 | tf_op jit(solution)/shard_map/ppermute | solution.py:375
  40.9 0.6 copy-start.10
  40.9 0.6 copy-start.13
  45.1 9.8 %collective-permute-start.15 = (f32[3,4,8,128]{3,2,1,0:T(8,128)}, f32[3,4,8,128]{3,2,1,0:T(8,128)S(1)}, u32[]{:S(2)}, u32[]{:S(2)}) collective-permute-start(f32[3,4,8,128]{3,2,1,0:T(8,128)} %get-tuple-element.114), channel_id=1, source_target_pairs={{0,8},{8,16},{16,24},{24,0},{1,9},{9,17},{17,25},{25,1},{2,10},{10... | collective-permute-start | bytes 147464 | tf_op jit(solution)/shard_map/ppermute | solution.py:373
  45.3 9.6 %collective-permute-start.16 = (f32[3,4,8,128]{3,2,1,0:T(8,128)}, f32[3,4,8,128]{3,2,1,0:T(8,128)S(1)}, u32[]{:S(2)}, u32[]{:S(2)}) collective-permute-start(f32[3,4,8,128]{3,2,1,0:T(8,128)} %get-tuple-element.115), channel_id=1, source_target_pairs={{8,0},{16,8},{24,16},{0,24},{9,1},{17,9},{25,17},{1,25},{10,2},{18... | collective-permute-start | bytes 147464 | tf_op jit(solution)/shard_map/ppermute | solution.py:374
  46.9 1.4 %copy-start.5 = (f32[2,3,8,128]{3,2,1,0:T(8,128)}, f32[2,3,8,128]{3,2,1,0:T(8,128)S(1)}, u32[]{:S(2)}) copy-start(f32[2,3,8,128]{3,2,1,0:T(8,128)S(1)} %collective-permute-done.14.rest_3_.rest_4_) | copy-start | bytes 73732
  46.9 7.4 %collective-permute-start.17 = (f32[2,3,8,128]{3,2,1,0:T(8,128)}, f32[2,3,8,128]{3,2,1,0:T(8,128)S(1)}, u32[]{:S(2)}, u32[]{:S(2)}) collective-permute-start(f32[2,3,8,128]{3,2,1,0:T(8,128)} %get-tuple-element.116), channel_id=1, source_target_pairs={{0,4},{4,0},{1,5},{5,1},{2,6},{6,2},{3,7},{7,3},{8,12},{12,8},{9,1... | collective-permute-start | bytes 73736 | tf_op jit(solution)/shard_map/ppermute | solution.py:375
  48.3 0.6 copy-start.11
  48.3 0.6 copy-start.15
  52.5 6.2 %collective-permute-start.18 = (f32[3,4,8,128]{3,2,1,0:T(8,128)}, f32[3,4,8,128]{3,2,1,0:T(8,128)S(1)}, u32[]{:S(2)}, u32[]{:S(2)}) collective-permute-start(f32[3,4,8,128]{3,2,1,0:T(8,128)} %get-tuple-element.121), channel_id=1, source_target_pairs={{0,8},{8,16},{16,24},{24,0},{1,9},{9,17},{17,25},{25,1},{2,10},{10... | collective-permute-start | bytes 147464 | tf_op jit(solution)/shard_map/ppermute | solution.py:373
  52.6 6.2 %collective-permute-start.19 = (f32[3,4,8,128]{3,2,1,0:T(8,128)}, f32[3,4,8,128]{3,2,1,0:T(8,128)S(1)}, u32[]{:S(2)}, u32[]{:S(2)}) collective-permute-start(f32[3,4,8,128]{3,2,1,0:T(8,128)} %get-tuple-element.122), channel_id=1, source_target_pairs={{8,0},{16,8},{24,16},{0,24},{9,1},{17,9},{25,17},{1,25},{10,2},{18... | collective-permute-start | bytes 147464 | tf_op jit(solution)/shard_map/ppermute | solution.py:374
  54.3 0.7 copy-start.6
  54.3 4.4 %collective-permute-start.20 = (f32[2,3,8,128]{3,2,1,0:T(8,128)}, f32[2,3,8,128]{3,2,1,0:T(8,128)S(1)}, u32[]{:S(2)}, u32[]{:S(2)}) collective-permute-start(f32[2,3,8,128]{3,2,1,0:T(8,128)} %get-tuple-element.123), channel_id=1, source_target_pairs={{0,4},{4,0},{1,5},{5,1},{2,6},{6,2},{3,7},{7,3},{8,12},{12,8},{9,1... | collective-permute-start | bytes 73736 | tf_op jit(solution)/shard_map/ppermute | solution.py:375
  54.9 0.6 copy-start.14
  55.0 0.6 copy-start.16
  58.7 0.6 copy-start.8
  58.8 0.6 copy-start.19
  58.8 0.6 copy-start.20
  66.4 6.4 %collective-permute-start.21 = (f32[8,8,128]{2,1,0:T(8,128)}, f32[8,8,128]{2,1,0:T(8,128)S(1)}, u32[]{:S(2)}, u32[]{:S(2)}) collective-permute-start(f32[8,8,128]{2,1,0:T(8,128)} %get-tuple-element.128.rest_0_), channel_id=1, source_target_pairs={{0,1},{1,2},{2,3},{3,0},{4,5},{5,6},{6,7},{7,4},{8,9},{9,10},{10,1... | collective-permute-start | bytes 98312 | tf_op jit(solution)/shard_map/ppermute | solution.py:476
  67.9 5.5 %collective-permute-start.22 = (f32[8,8,128]{2,1,0:T(8,128)}, f32[8,8,128]{2,1,0:T(8,128)S(1)}, u32[]{:S(2)}, u32[]{:S(2)}) collective-permute-start(f32[8,8,128]{2,1,0:T(8,128)} %get-tuple-element.128.rest_0_), channel_id=1, source_target_pairs={{0,2},{1,3},{2,0},{3,1},{4,6},{5,7},{6,4},{7,5},{8,10},{9,11},{10,... | collective-permute-start | bytes 98312 | tf_op jit(solution)/shard_map/ppermute | solution.py:476
  70.5 4.1 %collective-permute-start.23 = (f32[8,8,128]{2,1,0:T(8,128)}, f32[8,8,128]{2,1,0:T(8,128)S(1)}, u32[]{:S(2)}, u32[]{:S(2)}) collective-permute-start(f32[8,8,128]{2,1,0:T(8,128)} %get-tuple-element.128.rest_0_), channel_id=1, source_target_pairs={{0,3},{1,0},{2,1},{3,2},{4,7},{5,4},{6,5},{7,6},{8,11},{9,8},{10,9... | collective-permute-start | bytes 98312 | tf_op jit(solution)/shard_map/ppermute | solution.py:476
  72.8 1.8 %copy-start.21 = (f32[8,8,128]{2,1,0:T(8,128)}, f32[8,8,128]{2,1,0:T(8,128)S(1)}, u32[]{:S(2)}) copy-start(f32[8,8,128]{2,1,0:T(8,128)S(1)} %collective-permute-done.21.rest_1_) | copy-start | bytes 98308
  73.4 1.2 %copy-start.22 = (f32[8,8,128]{2,1,0:T(8,128)}, f32[8,8,128]{2,1,0:T(8,128)S(1)}, u32[]{:S(2)}) copy-start(f32[8,8,128]{2,1,0:T(8,128)S(1)} %collective-permute-done.22.rest_2_) | copy-start | bytes 98308
  74.6 0.6 copy-start.23

commit v14 on v13

--- a/solution.py
+++ b/solution.py
@@ -246,7 +246,7 @@
         c_s[i] = cz_ref[0, i] * jnp.exp(-SOFTEN * r_ref[i])
         return carry
 
-    lax.fori_loop(0, n, conduct, 0)
+    lax.fori_loop(0, n, conduct, 0, unroll=8)
 
     def forward(i, carry):
         g_prev, vy_prev, va_prev = carry
@@ -360,7 +360,7 @@
         t_ref[i] = y_ref[i] + a_ref[i] * first + b_ref[i] * last
         return carry
 
-    lax.fori_loop(0, y_ref.shape[0], combine, 0)
+    lax.fori_loop(0, y_ref.shape[0], combine, 0, unroll=8)
 
 
 def sds(shape):

time: 78 us -> 77.1 us (0.988)
  Pallas kernels: 40.5 us -> 39.6 us
  transfers between devices with their start and end apart: 24 -> 24, of which waited for: 5 -> 5; matrix products, arithmetic and copies ran while one was open for 0% -> 0% of each run, Pallas kernels for 28% -> 29%
where the time goes in v14:
time: 77.1 us; the launch traced here: 76.7 us
  Pallas kernels  39.6 us (51%)
  starting transfers between devices  25.9 us (34%)
  waiting for transfers between devices  5.37 us (7%)
  local copies, waits for them, and re-layouts  4.95 us (6%)
  between operations  0.83 us (1%)
    pallas_call x8, Pallas kernels, local(): pl.pallas_call(make_section_kernel(k, first, last), grid=(1,), out_shape=...  29.7 us
    ppermute x7, starting transfers between devices, exchange(): xhi = lax.ppermute(xf, 'east', east_bwd)  9.42 us
    ppermute x7, starting transfers between devices, exchange(): ylo = lax.ppermute(ys, 'north', north_fwd)  8.35 us
    ppermute x3, starting transfers between devices, local(): lax.ppermute(red, 'depth', [(i, (i + k) % count) for i in range(count)])  5.4 us
    unnamed x48, local copies, waits for them, and re-layouts  4.95 us
    pallas_call x1, Pallas kernels, local(): pl.pallas_call(prep_kernel, out_shape=(sds(shape), sds(shape), sds(shape)...  4.57 us
    pallas_call x1, Pallas kernels, local(): pl.pallas_call(sweep_kernel, grid=(1,), out_shape=(sds(shape), sds(shape)...  3.34 us
    ppermute x3, waiting for transfers between devices, local(): lax.ppermute(red, 'depth', [(i, (i + k) % count) for i in range(count)])  2.77 us
  transfers between devices with their start and end apart: 24, of which 5 were waited for; matrix products, arithmetic and copies ran while one was open for 0% of the time, Pallas kernels for 29%

profile of v14, /device:TPU:0, one launch (start us, length us, event | category | flops | bytes accessed | tf_op | source)
XLA Modules:
  0.0 76.7 jit_solution(16495748034915425848)
XLA Ops:
  0.6 4.6 %shard_map.120 = (f32[64,8,128]{2,1,0:T(8,128)}, f32[64,8,128]{2,1,0:T(8,128)}, f32[64,8,128]{2,1,0:T(8,128)}, f32[64,8,128]{2,1,0:T(8,128)}, f32[5,64,8,128]{3,...) custom-call(f32[2,12]{1,0:T(2,128)} %lat_ref.1, f32[12]{0:T(128)} %vert_ref.1, ...), custom_call_target="tpu_custom_call" | custom-call | tf_op jit(solution)/shard_map/pallas_call | solution.py:408
  5.2 0.5 collective-permute-start
  5.7 2.0 %collective-permute-start.1 = (f32[5,8,8,128]{3,2,1,0:T(8,128)}, f32[5,8,8,128]{3,2,1,0:T(8,128)S(1)}, u32[]{:S(2)}, u32[]{:S(2)}) collective-permute-start(f32[5,8,8,128]{3,2,1,0:T(8,128)} %get-tuple-element.74), channel_id=1, source_target_pairs={{8,0},{16,8},{24,16},{0,24},{9,1},{17,9},{25,17},{1,25},{10,2},{18... | collective-permute-start | bytes 491528 | tf_op jit(solution)/shard_map/ppermute | solution.py:374
  7.7 2.3 %collective-permute-start.2 = (f32[2,5,8,128]{3,2,1,0:T(8,128)}, f32[2,5,8,128]{3,2,1,0:T(8,128)S(1)}, u32[]{:S(2)}, u32[]{:S(2)}) collective-permute-start(f32[2,5,8,128]{3,2,1,0:T(8,128)} %get-tuple-element.75), channel_id=1, source_target_pairs={{0,4},{4,0},{1,5},{5,1},{2,6},{6,2},{3,7},{7,3},{8,12},{12,8},{9,1... | collective-permute-start | bytes 122888 | tf_op jit(solution)/shard_map/ppermute | solution.py:375
  10.0 2.2 %collective-permute-done.2.rest_2_.rest_3_ = f32[2,5,8,128]{3,2,1,0:T(8,128)S(1)} collective-permute-done((f32[2,5,8,128]{3,2,1,0:T(8,128)}, f32[2,5,8,128]{3,2,1,0:T(8,128)S(1)}, u32[]{:S(2)}, u32[]{:S(2)}) %collective-permute-start.2) | collective-permute-done | bytes 40992 | tf_op jit(solution)/shard_map/ppermute | solution.py:375
  12.2 0.4 collective-permute-done.1.rest_1_
  12.5 0.2 copy-done.2
  12.8 0.1 copy-done
  12.8 0.4 copy-done.1
  13.2 4.5 %shard_map.121 = (f32[64,8,128]{2,1,0:T(8,128)}, f32[64,8,128]{2,1,0:T(8,128)}, f32[64,8,128]{2,1,0:T(8,128)}, f32[64,8,128]{2,1,0:T(8,128)}, f32[8,32,8,128]{3,...) custom-call(f32[64,8,128]{2,1,0:T(8,128)} %get-tuple-element.68.h_re, ...), custom_call_target="tpu_custom_call", output_to_operand_aliasing={{0}: (0, {}), {1}: (1, {}), {2}: (2, {}), {3}: (3, {})} | custom-call | tf_op jit(solution)/shard_map/pallas_call | solution.py:449
  17.7 0.7 collective-permute-start.3
  18.4 1.3 %collective-permute-start.4 = (f32[3,4,8,128]{3,2,1,0:T(8,128)}, f32[3,4,8,128]{3,2,1,0:T(8,128)S(1)}, u32[]{:S(2)}, u32[]{:S(2)}) collective-permute-start(f32[3,4,8,128]{3,2,1,0:T(8,128)} %get-tuple-element.86), channel_id=1, source_target_pairs={{8,0},{16,8},{24,16},{0,24},{9,1},{17,9},{25,17},{1,25},{10,2},{18... | collective-permute-start | bytes 147464 | tf_op jit(solution)/shard_map/ppermute | solution.py:374
  19.8 1.4 %collective-permute-start.5 = (f32[2,3,8,128]{3,2,1,0:T(8,128)}, f32[2,3,8,128]{3,2,1,0:T(8,128)S(1)}, u32[]{:S(2)}, u32[]{:S(2)}) collective-permute-start(f32[2,3,8,128]{3,2,1,0:T(8,128)} %get-tuple-element.87), channel_id=1, source_target_pairs={{0,4},{4,0},{1,5},{5,1},{2,6},{6,2},{3,7},{7,3},{8,12},{12,8},{9,1... | collective-permute-start | bytes 73736 | tf_op jit(solution)/shard_map/ppermute | solution.py:375
  21.2 4.5 %shard_map.122 = (f32[64,8,128]{2,1,0:T(8,128)}, f32[64,8,128]{2,1,0:T(8,128)}, f32[64,8,128]{2,1,0:T(8,128)}, f32[64,8,128]{2,1,0:T(8,128)}, f32[8,32,8,128]{3,...) custom-call(f32[64,8,128]{2,1,0:T(8,128)} %get-tuple-element.76.h_re, ...), custom_call_target="tpu_custom_call", output_to_operand_aliasing={{0}: (0, {}), {1}: (1, {}), {2}: (2, {}), {3}: (3, {})} | custom-call | tf_op jit(solution)/shard_map/pallas_call | solution.py:449
  25.7 1.7 %collective-permute-start.7 = (f32[3,4,8,128]{3,2,1,0:T(8,128)}, f32[3,4,8,128]{3,2,1,0:T(8,128)S(1)}, u32[]{:S(2)}, u32[]{:S(2)}) collective-permute-start(f32[3,4,8,128]{3,2,1,0:T(8,128)} %get-tuple-element.94), channel_id=1, source_target_pairs={{8,0},{16,8},{24,16},{0,24},{9,1},{17,9},{25,17},{1,25},{10,2},{18... | collective-permute-start | bytes 147464 | tf_op jit(solution)/shard_map/ppermute | solution.py:374
  27.5 0.6 collective-permute-start.8
  28.1 0.6 copy-done.17
  28.7 3.6 %shard_map.123 = (f32[64,8,128]{2,1,0:T(8,128)}, f32[64,8,128]{2,1,0:T(8,128)}, f32[64,8,128]{2,1,0:T(8,128)}, f32[64,8,128]{2,1,0:T(8,128)}, f32[3,4,8,128]{3,2...) custom-call(f32[64,8,128]{2,1,0:T(8,128)} %get-tuple-element.80.h_re, ...), custom_call_target="tpu_custom_call", output_to_operand_aliasing={{0}: (0, {}), {1}: (1, {}), {2}: (2, {}), {3}: (3, {})} | custom-call | tf_op jit(solution)/shard_map/pallas_call | solution.py:449
  32.3 0.2 collective-permute-start.10
  32.5 0.3 collective-permute-start.9
  32.9 1.4 %collective-permute-start.11 = (f32[2,3,8,128]{3,2,1,0:T(8,128)}, f32[2,3,8,128]{3,2,1,0:T(8,128)S(1)}, u32[]{:S(2)}, u32[]{:S(2)}) collective-permute-start(f32[2,3,8,128]{3,2,1,0:T(8,128)} %get-tuple-element.102), channel_id=1, source_target_pairs={{0,4},{4,0},{1,5},{5,1},{2,6},{6,2},{3,7},{7,3},{8,12},{12,8},{9,1... | collective-permute-start | bytes 73736 | tf_op jit(solution)/shard_map/ppermute | solution.py:375
  34.3 0.6 copy-done.9
  34.9 3.6 %shard_map.124 = (f32[64,8,128]{2,1,0:T(8,128)}, f32[64,8,128]{2,1,0:T(8,128)}, f32[64,8,128]{2,1,0:T(8,128)}, f32[64,8,128]{2,1,0:T(8,128)}, f32[3,4,8,128]{3,2...) custom-call(f32[64,8,128]{2,1,0:T(8,128)} %get-tuple-element.88.h_re, ...), custom_call_target="tpu_custom_call", output_to_operand_aliasing={{0}: (0, {}), {1}: (1, {}), {2}: (2, {}), {3}: (3, {})} | custom-call | tf_op jit(solution)/shard_map/pallas_call | solution.py:449
  38.5 0.9 %collective-permute-start.12 = (f32[3,4,8,128]{3,2,1,0:T(8,128)}, f32[3,4,8,128]{3,2,1,0:T(8,128)S(1)}, u32[]{:S(2)}, u32[]{:S(2)}) collective-permute-start(f32[3,4,8,128]{3,2,1,0:T(8,128)} %get-tuple-element.107), channel_id=1, source_target_pairs={{0,8},{8,16},{16,24},{24,0},{1,9},{9,17},{17,25},{25,1},{2,10},{10... | collective-permute-start | bytes 147464 | tf_op jit(solution)/shard_map/ppermute | solution.py:373
  39.4 0.9 %collective-permute-start.13 = (f32[3,4,8,128]{3,2,1,0:T(8,128)}, f32[3,4,8,128]{3,2,1,0:T(8,128)S(1)}, u32[]{:S(2)}, u32[]{:S(2)}) collective-permute-start(f32[3,4,8,128]{3,2,1,0:T(8,128)} %get-tuple-element.108), channel_id=1, source_target_pairs={{8,0},{16,8},{24,16},{0,24},{9,1},{17,9},{25,17},{1,25},{10,2},{18... | collective-permute-start | bytes 147464 | tf_op jit(solution)/shard_map/ppermute | solution.py:374
  40.3 0.6 collective-permute-start.14
  40.9 0.6 copy-done.10
  41.5 3.6 %shard_map.125 = (f32[64,8,128]{2,1,0:T(8,128)}, f32[64,8,128]{2,1,0:T(8,128)}, f32[64,8,128]{2,1,0:T(8,128)}, f32[64,8,128]{2,1,0:T(8,128)}, f32[3,4,8,128]{3,2...) custom-call(f32[64,8,128]{2,1,0:T(8,128)} %get-tuple-element.96.h_re, ...), custom_call_target="tpu_custom_call", output_to_operand_aliasing={{0}: (0, {}), {1}: (1, {}), {2}: (2, {}), {3}: (3, {})} | custom-call | tf_op jit(solution)/shard_map/pallas_call | solution.py:449
  45.1 0.2 collective-permute-start.15
  45.3 1.6 %collective-permute-start.16 = (f32[3,4,8,128]{3,2,1,0:T(8,128)}, f32[3,4,8,128]{3,2,1,0:T(8,128)S(1)}, u32[]{:S(2)}, u32[]{:S(2)}) collective-permute-start(f32[3,4,8,128]{3,2,1,0:T(8,128)} %get-tuple-element.115), channel_id=1, source_target_pairs={{8,0},{16,8},{24,16},{0,24},{9,1},{17,9},{25,17},{1,25},{10,2},{18... | collective-permute-start | bytes 147464 | tf_op jit(solution)/shard_map/ppermute | solution.py:374
  46.9 1.4 %collective-permute-start.17 = (f32[2,3,8,128]{3,2,1,0:T(8,128)}, f32[2,3,8,128]{3,2,1,0:T(8,128)S(1)}, u32[]{:S(2)}, u32[]{:S(2)}) collective-permute-start(f32[2,3,8,128]{3,2,1,0:T(8,128)} %get-tuple-element.116), channel_id=1, source_target_pairs={{0,4},{4,0},{1,5},{5,1},{2,6},{6,2},{3,7},{7,3},{8,12},{12,8},{9,1... | collective-permute-start | bytes 73736 | tf_op jit(solution)/shard_map/ppermute | solution.py:375
  48.3 0.6 copy-done.11
  48.9 3.6 %shard_map.126 = (f32[64,8,128]{2,1,0:T(8,128)}, f32[64,8,128]{2,1,0:T(8,128)}, f32[64,8,128]{2,1,0:T(8,128)}, f32[64,8,128]{2,1,0:T(8,128)}, f32[3,4,8,128]{3,2...) custom-call(f32[64,8,128]{2,1,0:T(8,128)} %get-tuple-element.103.h_r, ...), custom_call_target="tpu_custom_call", output_to_operand_aliasing={{0}: (0, {}), {1}: (1, {}), {2}: (2, {}), {3}: (3, {})} | custom-call | tf_op jit(solution)/shard_map/pallas_call | solution.py:449
  52.6 1.7 %collective-permute-start.19 = (f32[3,4,8,128]{3,2,1,0:T(8,128)}, f32[3,4,8,128]{3,2,1,0:T(8,128)S(1)}, u32[]{:S(2)}, u32[]{:S(2)}) collective-permute-start(f32[3,4,8,128]{3,2,1,0:T(8,128)} %get-tuple-element.122), channel_id=1, source_target_pairs={{8,0},{16,8},{24,16},{0,24},{9,1},{17,9},{25,17},{1,25},{10,2},{18... | collective-permute-start | bytes 147464 | tf_op jit(solution)/shard_map/ppermute | solution.py:374
  54.3 0.6 collective-permute-start.20
  55.0 0.6 copy-done.14
  55.6 3.2 %shard_map.127 = (f32[64,8,128]{2,1,0:T(8,128)}, f32[64,8,128]{2,1,0:T(8,128)}, f32[64,8,128]{2,1,0:T(8,128)}, f32[64,8,128]{2,1,0:T(8,128)}) custom-call(f32[64,8,128]{2,1,0:T(8,128)} %get-tuple-element.110.h_ref, f32[64,8,128]{2,1,0:T(8,128)} %get-tuple-element.111.w_ref, ...), custom_call_target="tpu_custom_call", output_to_operand_aliasing={{0}: (0, {}), {1}: (1, {}), {2}: (2, {}), {3}: (3, {})} | custom-call | tf_op jit(solution)/shard_map/pallas_call | solution.py:449
  58.8 0.5 copy-done.8
  59.4 3.2 %shard_map.128 = (f32[64,8,128]{2,1,0:T(8,128)}, f32[64,8,128]{2,1,0:T(8,128)}, f32[64,8,128]{2,1,0:T(8,128)}, f32[64,8,128]{2,1,0:T(8,128)}) custom-call(f32[64,8,128]{2,1,0:T(8,128)} %get-tuple-element.117.h_ref, f32[64,8,128]{2,1,0:T(8,128)} %get-tuple-element.118.w_ref, ...), custom_call_target="tpu_custom_call", output_to_operand_aliasing={{0}: (0, {}), {1}: (1, {}), {2}: (2, {}), {3}: (3, {})} | custom-call | tf_op jit(solution)/shard_map/pallas_call | solution.py:449
  62.6 3.3 %shard_map.129 = (f32[64,8,128]{2,1,0:T(8,128)}, f32[64,8,128]{2,1,0:T(8,128)}, f32[64,8,128]{2,1,0:T(8,128)}, f32[8,8,128]{2,1,0:T(8,128)}) custom-call(f32[64,8,128]{2,1,0:T(8,128)} %get-tuple-element.124.r_ref, f32[5,64,8,128]{3,2,1,0:T(8,128)} %get-tuple-element.72.co_ref.cz_ref), custom_call_target="tpu_custom_call" | custom-call | tf_op jit(solution)/shard_map/pallas_call | solution.py:464
  65.9 1.5 %collective-permute-start.21 = (f32[8,8,128]{2,1,0:T(8,128)}, f32[8,8,128]{2,1,0:T(8,128)S(1)}, u32[]{:S(2)}, u32[]{:S(2)}) collective-permute-start(f32[8,8,128]{2,1,0:T(8,128)} %get-tuple-element.128.rest_0_), channel_id=1, source_target_pairs={{0,1},{1,2},{2,3},{3,0},{4,5},{5,6},{6,7},{7,4},{8,9},{9,10},{10,1... | collective-permute-start | bytes 98312 | tf_op jit(solution)/shard_map/ppermute | solution.py:476
  67.4 2.6 %collective-permute-start.22 = (f32[8,8,128]{2,1,0:T(8,128)}, f32[8,8,128]{2,1,0:T(8,128)S(1)}, u32[]{:S(2)}, u32[]{:S(2)}) collective-permute-start(f32[8,8,128]{2,1,0:T(8,128)} %get-tuple-element.128.rest_0_), channel_id=1, source_target_pairs={{0,2},{1,3},{2,0},{3,1},{4,6},{5,7},{6,4},{7,5},{8,10},{9,11},{10,... | collective-permute-start | bytes 98312 | tf_op jit(solution)/shard_map/ppermute | solution.py:476
  70.0 1.3 %collective-permute-start.23 = (f32[8,8,128]{2,1,0:T(8,128)}, f32[8,8,128]{2,1,0:T(8,128)S(1)}, u32[]{:S(2)}, u32[]{:S(2)}) collective-permute-start(f32[8,8,128]{2,1,0:T(8,128)} %get-tuple-element.128.rest_0_), channel_id=1, source_target_pairs={{0,3},{1,0},{2,1},{3,2},{4,7},{5,4},{6,5},{7,6},{8,11},{9,8},{10,9... | collective-permute-start | bytes 98312 | tf_op jit(solution)/shard_map/ppermute | solution.py:476
  71.3 1.0 %collective-permute-done.21.rest_1_ = f32[8,8,128]{2,1,0:T(8,128)S(1)} collective-permute-done((f32[8,8,128]{2,1,0:T(8,128)}, f32[8,8,128]{2,1,0:T(8,128)S(1)}, u32[]{:S(2)}, u32[]{:S(2)}) %collective-permute-start.21) | collective-permute-done | bytes 32800 | tf_op jit(solution)/shard_map/ppermute | solution.py:476
  72.3 0.6 collective-permute-done.22.rest_2_
  72.8 1.2 %collective-permute-done.23.rest_3_ = f32[8,8,128]{2,1,0:T(8,128)S(1)} collective-permute-done((f32[8,8,128]{2,1,0:T(8,128)}, f32[8,8,128]{2,1,0:T(8,128)S(1)}, u32[]{:S(2)}, u32[]{:S(2)}) %collective-permute-start.23) | collective-permute-done | bytes 32800 | tf_op jit(solution)/shard_map/ppermute | solution.py:476
  74.1 0.6 copy-done.23
  74.7 2.0 %shard_map.130 = f32[64,8,128]{2,1,0:T(8,128)} custom-call(s32[1]{0:T(128)} %bitcast.rank_ref, f32[64,8,128]{2,1,0:T(8,128)} %get-tuple-element.125.y_ref, f32[64,8,128]{2,1,0:T(8,128)} %get-tuple-element.126.a_ref, f32[64,8,128]{2,1,0:T(8,128)} %get-tuple-element.127.b_ref, f32[8,8,128]{2,1,0:T(8,128)} %get-tuple-element.128.rest_0_, ...), custom_call_target="tpu_custom_call" | custom-call | tf_op jit(solution)/shard_map/pallas_call | solution.py:478
  (59 shorter events, 0.4 us)
Async XLA Ops:
  5.2 7.0 %collective-permute-start = (f32[5,8,8,128]{3,2,1,0:T(8,128)}, f32[5,8,8,128]{3,2,1,0:T(8,128)S(1)}, u32[]{:S(2)}, u32[]{:S(2)}) collective-permute-start(f32[5,8,8,128]{3,2,1,0:T(8,128)} %get-tuple-element.73), channel_id=1, source_target_pairs={{0,8},{8,16},{16,24},{24,0},{1,9},{9,17},{17,25},{25,1},{2,10},{10... | collective-permute-start | bytes 491528 | tf_op jit(solution)/shard_map/ppermute | solution.py:373
  5.7 6.8 %collective-permute-start.1 = (f32[5,8,8,128]{3,2,1,0:T(8,128)}, f32[5,8,8,128]{3,2,1,0:T(8,128)S(1)}, u32[]{:S(2)}, u32[]{:S(2)}) collective-permute-start(f32[5,8,8,128]{3,2,1,0:T(8,128)} %get-tuple-element.74), channel_id=1, source_target_pairs={{8,0},{16,8},{24,16},{0,24},{9,1},{17,9},{25,17},{1,25},{10,2},{18... | collective-permute-start | bytes 491528 | tf_op jit(solution)/shard_map/ppermute | solution.py:374
  7.7 4.5 %collective-permute-start.2 = (f32[2,5,8,128]{3,2,1,0:T(8,128)}, f32[2,5,8,128]{3,2,1,0:T(8,128)S(1)}, u32[]{:S(2)}, u32[]{:S(2)}) collective-permute-start(f32[2,5,8,128]{3,2,1,0:T(8,128)} %get-tuple-element.75), channel_id=1, source_target_pairs={{0,4},{4,0},{1,5},{5,1},{2,6},{6,2},{3,7},{7,3},{8,12},{12,8},{9,1... | collective-permute-start | bytes 122888 | tf_op jit(solution)/shard_map/ppermute | solution.py:375
  12.2 0.6 copy-start.2
  12.2 0.7 copy-start
  12.5 0.7 copy-start.1
  17.7 10.4 %collective-permute-start.3 = (f32[3,4,8,128]{3,2,1,0:T(8,128)}, f32[3,4,8,128]{3,2,1,0:T(8,128)S(1)}, u32[]{:S(2)}, u32[]{:S(2)}) collective-permute-start(f32[3,4,8,128]{3,2,1,0:T(8,128)} %get-tuple-element.85), channel_id=1, source_target_pairs={{0,8},{8,16},{16,24},{24,0},{1,9},{9,17},{17,25},{25,1},{2,10},{10... | collective-permute-start | bytes 147464 | tf_op jit(solution)/shard_map/ppermute | solution.py:373
  18.4 9.7 %collective-permute-start.4 = (f32[3,4,8,128]{3,2,1,0:T(8,128)}, f32[3,4,8,128]{3,2,1,0:T(8,128)S(1)}, u32[]{:S(2)}, u32[]{:S(2)}) collective-permute-start(f32[3,4,8,128]{3,2,1,0:T(8,128)} %get-tuple-element.86), channel_id=1, source_target_pairs={{8,0},{16,8},{24,16},{0,24},{9,1},{17,9},{25,17},{1,25},{10,2},{18... | collective-permute-start | bytes 147464 | tf_op jit(solution)/shard_map/ppermute | solution.py:374
  19.8 7.7 %collective-permute-start.5 = (f32[2,3,8,128]{3,2,1,0:T(8,128)}, f32[2,3,8,128]{3,2,1,0:T(8,128)S(1)}, u32[]{:S(2)}, u32[]{:S(2)}) collective-permute-start(f32[2,3,8,128]{3,2,1,0:T(8,128)} %get-tuple-element.87), channel_id=1, source_target_pairs={{0,4},{4,0},{1,5},{5,1},{2,6},{6,2},{3,7},{7,3},{8,12},{12,8},{9,1... | collective-permute-start | bytes 73736 | tf_op jit(solution)/shard_map/ppermute | solution.py:375
  25.7 8.6 %collective-permute-start.6 = (f32[3,4,8,128]{3,2,1,0:T(8,128)}, f32[3,4,8,128]{3,2,1,0:T(8,128)S(1)}, u32[]{:S(2)}, u32[]{:S(2)}) collective-permute-start(f32[3,4,8,128]{3,2,1,0:T(8,128)} %get-tuple-element.93), channel_id=1, source_target_pairs={{0,8},{8,16},{16,24},{24,0},{1,9},{9,17},{17,25},{25,1},{2,10},{10... | collective-permute-start | bytes 147464 | tf_op jit(solution)/shard_map/ppermute | solution.py:373
  25.7 8.6 %collective-permute-start.7 = (f32[3,4,8,128]{3,2,1,0:T(8,128)}, f32[3,4,8,128]{3,2,1,0:T(8,128)S(1)}, u32[]{:S(2)}, u32[]{:S(2)}) collective-permute-start(f32[3,4,8,128]{3,2,1,0:T(8,128)} %get-tuple-element.94), channel_id=1, source_target_pairs={{8,0},{16,8},{24,16},{0,24},{9,1},{17,9},{25,17},{1,25},{10,2},{18... | collective-permute-start | bytes 147464 | tf_op jit(solution)/shard_map/ppermute | solution.py:374
  27.5 0.7 copy-start.7
  27.5 5.4 %collective-permute-start.8 = (f32[2,3,8,128]{3,2,1,0:T(8,128)}, f32[2,3,8,128]{3,2,1,0:T(8,128)S(1)}, u32[]{:S(2)}, u32[]{:S(2)}) collective-permute-start(f32[2,3,8,128]{3,2,1,0:T(8,128)} %get-tuple-element.95), channel_id=1, source_target_pairs={{0,4},{4,0},{1,5},{5,1},{2,6},{6,2},{3,7},{7,3},{8,12},{12,8},{9,1... | collective-permute-start | bytes 73736 | tf_op jit(solution)/shard_map/ppermute | solution.py:375
  28.1 0.6 copy-start.17
  28.1 0.6 copy-start.18
  32.3 8.6 %collective-permute-start.10 = (f32[3,4,8,128]{3,2,1,0:T(8,128)}, f32[3,4,8,128]{3,2,1,0:T(8,128)S(1)}, u32[]{:S(2)}, u32[]{:S(2)}) collective-permute-start(f32[3,4,8,128]{3,2,1,0:T(8,128)} %get-tuple-element.101), channel_id=1, source_target_pairs={{8,0},{16,8},{24,16},{0,24},{9,1},{17,9},{25,17},{1,25},{10,2},{18... | collective-permute-start | bytes 147464 | tf_op jit(solution)/shard_map/ppermute | solution.py:374
  32.5 8.4 %collective-permute-start.9 = (f32[3,4,8,128]{3,2,1,0:T(8,128)}, f32[3,4,8,128]{3,2,1,0:T(8,128)S(1)}, u32[]{:S(2)}, u32[]{:S(2)}) collective-permute-start(f32[3,4,8,128]{3,2,1,0:T(8,128)} %get-tuple-element.100), channel_id=1, source_target_pairs={{0,8},{8,16},{16,24},{24,0},{1,9},{9,17},{17,25},{25,1},{2,10},{10... | collective-permute-start | bytes 147464 | tf_op jit(solution)/shard_map/ppermute | solution.py:373
  32.9 1.4 %copy-start.3 = (f32[2,3,8,128]{3,2,1,0:T(8,128)}, f32[2,3,8,128]{3,2,1,0:T(8,128)S(1)}, u32[]{:S(2)}) copy-start(f32[2,3,8,128]{3,2,1,0:T(8,128)S(1)} %collective-permute-done.8.rest_3_.rest_4_) | copy-start | bytes 73732
  32.9 7.4 %collective-permute-start.11 = (f32[2,3,8,128]{3,2,1,0:T(8,128)}, f32[2,3,8,128]{3,2,1,0:T(8,128)S(1)}, u32[]{:S(2)}, u32[]{:S(2)}) collective-permute-start(f32[2,3,8,128]{3,2,1,0:T(8,128)} %get-tuple-element.102), channel_id=1, source_target_pairs={{0,4},{4,0},{1,5},{5,1},{2,6},{6,2},{3,7},{7,3},{8,12},{12,8},{9,1... | collective-permute-start | bytes 73736 | tf_op jit(solution)/shard_map/ppermute | solution.py:375
  34.3 0.6 copy-start.9
  34.3 0.6 copy-start.12
  38.5 9.8 %collective-permute-start.12 = (f32[3,4,8,128]{3,2,1,0:T(8,128)}, f32[3,4,8,128]{3,2,1,0:T(8,128)S(1)}, u32[]{:S(2)}, u32[]{:S(2)}) collective-permute-start(f32[3,4,8,128]{3,2,1,0:T(8,128)} %get-tuple-element.107), channel_id=1, source_target_pairs={{0,8},{8,16},{16,24},{24,0},{1,9},{9,17},{17,25},{25,1},{2,10},{10... | collective-permute-start | bytes 147464 | tf_op jit(solution)/shard_map/ppermute | solution.py:373
  39.4 8.9 %collective-permute-start.13 = (f32[3,4,8,128]{3,2,1,0:T(8,128)}, f32[3,4,8,128]{3,2,1,0:T(8,128)S(1)}, u32[]{:S(2)}, u32[]{:S(2)}) collective-permute-start(f32[3,4,8,128]{3,2,1,0:T(8,128)} %get-tuple-element.108), channel_id=1, source_target_pairs={{8,0},{16,8},{24,16},{0,24},{9,1},{17,9},{25,17},{1,25},{10,2},{18... | collective-permute-start | bytes 147464 | tf_op jit(solution)/shard_map/ppermute | solution.py:374
  40.3 0.7 copy-start.4
  40.3 6.6 %collective-permute-start.14 = (f32[2,3,8,128]{3,2,1,0:T(8,128)}, f32[2,3,8,128]{3,2,1,0:T(8,128)S(1)}, u32[]{:S(2)}, u32[]{:S(2)}) collective-permute-start(f32[2,3,8,128]{3,2,1,0:T(8,128)} %get-tuple-element.109), channel_id=1, source_target_pairs={{0,4},{4,0},{1,5},{5,1},{2,6},{6,2},{3,7},{7,3},{8,12},{12,8},{9,1... | collective-permute-start | bytes 73736 | tf_op jit(solution)/shard_map/ppermute | solution.py:375
  40.9 0.6 copy-start.10
  40.9 0.6 copy-start.13
  45.1 9.8 %collective-permute-start.15 = (f32[3,4,8,128]{3,2,1,0:T(8,128)}, f32[3,4,8,128]{3,2,1,0:T(8,128)S(1)}, u32[]{:S(2)}, u32[]{:S(2)}) collective-permute-start(f32[3,4,8,128]{3,2,1,0:T(8,128)} %get-tuple-element.114), channel_id=1, source_target_pairs={{0,8},{8,16},{16,24},{24,0},{1,9},{9,17},{17,25},{25,1},{2,10},{10... | collective-permute-start | bytes 147464 | tf_op jit(solution)/shard_map/ppermute | solution.py:373
  45.3 9.6 %collective-permute-start.16 = (f32[3,4,8,128]{3,2,1,0:T(8,128)}, f32[3,4,8,128]{3,2,1,0:T(8,128)S(1)}, u32[]{:S(2)}, u32[]{:S(2)}) collective-permute-start(f32[3,4,8,128]{3,2,1,0:T(8,128)} %get-tuple-element.115), channel_id=1, source_target_pairs={{8,0},{16,8},{24,16},{0,24},{9,1},{17,9},{25,17},{1,25},{10,2},{18... | collective-permute-start | bytes 147464 | tf_op jit(solution)/shard_map/ppermute | solution.py:374
  46.9 1.4 %copy-start.5 = (f32[2,3,8,128]{3,2,1,0:T(8,128)}, f32[2,3,8,128]{3,2,1,0:T(8,128)S(1)}, u32[]{:S(2)}) copy-start(f32[2,3,8,128]{3,2,1,0:T(8,128)S(1)} %collective-permute-done.14.rest_3_.rest_4_) | copy-start | bytes 73732
  46.9 7.4 %collective-permute-start.17 = (f32[2,3,8,128]{3,2,1,0:T(8,128)}, f32[2,3,8,128]{3,2,1,0:T(8,128)S(1)}, u32[]{:S(2)}, u32[]{:S(2)}) collective-permute-start(f32[2,3,8,128]{3,2,1,0:T(8,128)} %get-tuple-element.116), channel_id=1, source_target_pairs={{0,4},{4,0},{1,5},{5,1},{2,6},{6,2},{3,7},{7,3},{8,12},{12,8},{9,1... | collective-permute-start | bytes 73736 | tf_op jit(solution)/shard_map/ppermute | solution.py:375
  48.3 0.6 copy-start.11
  48.3 0.6 copy-start.15
  52.5 6.2 %collective-permute-start.18 = (f32[3,4,8,128]{3,2,1,0:T(8,128)}, f32[3,4,8,128]{3,2,1,0:T(8,128)S(1)}, u32[]{:S(2)}, u32[]{:S(2)}) collective-permute-start(f32[3,4,8,128]{3,2,1,0:T(8,128)} %get-tuple-element.121), channel_id=1, source_target_pairs={{0,8},{8,16},{16,24},{24,0},{1,9},{9,17},{17,25},{25,1},{2,10},{10... | collective-permute-start | bytes 147464 | tf_op jit(solution)/shard_map/ppermute | solution.py:373
  52.6 6.2 %collective-permute-start.19 = (f32[3,4,8,128]{3,2,1,0:T(8,128)}, f32[3,4,8,128]{3,2,1,0:T(8,128)S(1)}, u32[]{:S(2)}, u32[]{:S(2)}) collective-permute-start(f32[3,4,8,128]{3,2,1,0:T(8,128)} %get-tuple-element.122), channel_id=1, source_target_pairs={{8,0},{16,8},{24,16},{0,24},{9,1},{17,9},{25,17},{1,25},{10,2},{18... | collective-permute-start | bytes 147464 | tf_op jit(solution)/shard_map/ppermute | solution.py:374
  54.3 0.7 copy-start.6
  54.3 4.4 %collective-permute-start.20 = (f32[2,3,8,128]{3,2,1,0:T(8,128)}, f32[2,3,8,128]{3,2,1,0:T(8,128)S(1)}, u32[]{:S(2)}, u32[]{:S(2)}) collective-permute-start(f32[2,3,8,128]{3,2,1,0:T(8,128)} %get-tuple-element.123), channel_id=1, source_target_pairs={{0,4},{4,0},{1,5},{5,1},{2,6},{6,2},{3,7},{7,3},{8,12},{12,8},{9,1... | collective-permute-start | bytes 73736 | tf_op jit(solution)/shard_map/ppermute | solution.py:375
  54.9 0.6 copy-start.14
  55.0 0.6 copy-start.16
  58.7 0.6 copy-start.8
  58.8 0.6 copy-start.19
  58.8 0.6 copy-start.20
  65.9 6.4 %collective-permute-start.21 = (f32[8,8,128]{2,1,0:T(8,128)}, f32[8,8,128]{2,1,0:T(8,128)S(1)}, u32[]{:S(2)}, u32[]{:S(2)}) collective-permute-start(f32[8,8,128]{2,1,0:T(8,128)} %get-tuple-element.128.rest_0_), channel_id=1, source_target_pairs={{0,1},{1,2},{2,3},{3,0},{4,5},{5,6},{6,7},{7,4},{8,9},{9,10},{10,1... | collective-permute-start | bytes 98312 | tf_op jit(solution)/shard_map/ppermute | solution.py:476
  67.4 5.5 %collective-permute-start.22 = (f32[8,8,128]{2,1,0:T(8,128)}, f32[8,8,128]{2,1,0:T(8,128)S(1)}, u32[]{:S(2)}, u32[]{:S(2)}) collective-permute-start(f32[8,8,128]{2,1,0:T(8,128)} %get-tuple-element.128.rest_0_), channel_id=1, source_target_pairs={{0,2},{1,3},{2,0},{3,1},{4,6},{5,7},{6,4},{7,5},{8,10},{9,11},{10,... | collective-permute-start | bytes 98312 | tf_op jit(solution)/shard_map/ppermute | solution.py:476
  70.0 4.1 %collective-permute-start.23 = (f32[8,8,128]{2,1,0:T(8,128)}, f32[8,8,128]{2,1,0:T(8,128)S(1)}, u32[]{:S(2)}, u32[]{:S(2)}) collective-permute-start(f32[8,8,128]{2,1,0:T(8,128)} %get-tuple-element.128.rest_0_), channel_id=1, source_target_pairs={{0,3},{1,0},{2,1},{3,2},{4,7},{5,4},{6,5},{7,6},{8,11},{9,8},{10,9... | collective-permute-start | bytes 98312 | tf_op jit(solution)/shard_map/ppermute | solution.py:476
  72.3 1.8 %copy-start.21 = (f32[8,8,128]{2,1,0:T(8,128)}, f32[8,8,128]{2,1,0:T(8,128)S(1)}, u32[]{:S(2)}) copy-start(f32[8,8,128]{2,1,0:T(8,128)S(1)} %collective-permute-done.21.rest_1_) | copy-start | bytes 98308
  72.8 1.2 %copy-start.22 = (f32[8,8,128]{2,1,0:T(8,128)}, f32[8,8,128]{2,1,0:T(8,128)S(1)}, u32[]{:S(2)}) copy-start(f32[8,8,128]{2,1,0:T(8,128)S(1)} %collective-permute-done.22.rest_2_) | copy-start | bytes 98308
  74.1 0.6 copy-start.23

commit v15 on v14

--- a/solution.py
+++ b/solution.py
@@ -261,7 +261,7 @@
         va_s[i] = va
         return g, vy, va
 
-    lax.fori_loop(1, n - 1, forward, (zero, zero, one))
+    lax.fori_loop(1, n - 1, forward, (zero, zero, one), unroll=2)
 
     def backward(k, carry):
         i = n - 2 - k
@@ -275,7 +275,7 @@
         b_ref[i] = b
         return y, a, b
 
-    lax.fori_loop(0, n - 2, backward, (zero, zero, one))
+    lax.fori_loop(0, n - 2, backward, (zero, zero, one), unroll=2)
     y_ref[0] = zero
     a_ref[0] = one
     b_ref[0] = zero

time: 77.1 us -> 76.9 us (level)
  no operation moved by 1% of the time
where the time goes in v15:
time: 76.9 us; the launch traced here: 76.5 us
  Pallas kernels  39.4 us (51%)
  starting transfers between devices  25.9 us (34%)
  waiting for transfers between devices  5.37 us (7%)
  local copies, waits for them, and re-layouts  4.95 us (6%)
  between operations  0.83 us (1%)
    pallas_call x8, Pallas kernels, local(): pl.pallas_call(make_section_kernel(k, first, last), grid=(1,), out_shape=...  29.7 us
    ppermute x7, starting transfers between devices, exchange(): xhi = lax.ppermute(xf, 'east', east_bwd)  9.42 us
    ppermute x7, starting transfers between devices, exchange(): ylo = lax.ppermute(ys, 'north', north_fwd)  8.35 us
    ppermute x3, starting transfers between devices, local(): lax.ppermute(red, 'depth', [(i, (i + k) % count) for i in range(count)])  5.4 us
    unnamed x48, local copies, waits for them, and re-layouts  4.95 us
    pallas_call x1, Pallas kernels, local(): pl.pallas_call(prep_kernel, out_shape=(sds(shape), sds(shape), sds(shape)...  4.57 us
    pallas_call x1, Pallas kernels, local(): pl.pallas_call(sweep_kernel, grid=(1,), out_shape=(sds(shape), sds(shape)...  3.08 us
    ppermute x3, waiting for transfers between devices, local(): lax.ppermute(red, 'depth', [(i, (i + k) % count) for i in range(count)])  2.77 us
  transfers between devices with their start and end apart: 24, of which 5 were waited for; matrix products, arithmetic and copies ran while one was open for 0% of the time, Pallas kernels for 29%

profile of v15, /device:TPU:0, one launch (start us, length us, event | category | flops | bytes accessed | tf_op | source)
XLA Modules:
  0.0 76.5 jit_solution(4729975686329643223)
XLA Ops:
  0.6 4.6 %shard_map.120 = (f32[64,8,128]{2,1,0:T(8,128)}, f32[64,8,128]{2,1,0:T(8,128)}, f32[64,8,128]{2,1,0:T(8,128)}, f32[64,8,128]{2,1,0:T(8,128)}, f32[5,64,8,128]{3,...) custom-call(f32[2,12]{1,0:T(2,128)} %lat_ref.1, f32[12]{0:T(128)} %vert_ref.1, ...), custom_call_target="tpu_custom_call" | custom-call | tf_op jit(solution)/shard_map/pallas_call | solution.py:408
  5.2 0.5 collective-permute-start
  5.7 2.0 %collective-permute-start.1 = (f32[5,8,8,128]{3,2,1,0:T(8,128)}, f32[5,8,8,128]{3,2,1,0:T(8,128)S(1)}, u32[]{:S(2)}, u32[]{:S(2)}) collective-permute-start(f32[5,8,8,128]{3,2,1,0:T(8,128)} %get-tuple-element.74), channel_id=1, source_target_pairs={{8,0},{16,8},{24,16},{0,24},{9,1},{17,9},{25,17},{1,25},{10,2},{18... | collective-permute-start | bytes 491528 | tf_op jit(solution)/shard_map/ppermute | solution.py:374
  7.7 2.3 %collective-permute-start.2 = (f32[2,5,8,128]{3,2,1,0:T(8,128)}, f32[2,5,8,128]{3,2,1,0:T(8,128)S(1)}, u32[]{:S(2)}, u32[]{:S(2)}) collective-permute-start(f32[2,5,8,128]{3,2,1,0:T(8,128)} %get-tuple-element.75), channel_id=1, source_target_pairs={{0,4},{4,0},{1,5},{5,1},{2,6},{6,2},{3,7},{7,3},{8,12},{12,8},{9,1... | collective-permute-start | bytes 122888 | tf_op jit(solution)/shard_map/ppermute | solution.py:375
  10.0 2.2 %collective-permute-done.2.rest_2_.rest_3_ = f32[2,5,8,128]{3,2,1,0:T(8,128)S(1)} collective-permute-done((f32[2,5,8,128]{3,2,1,0:T(8,128)}, f32[2,5,8,128]{3,2,1,0:T(8,128)S(1)}, u32[]{:S(2)}, u32[]{:S(2)}) %collective-permute-start.2) | collective-permute-done | bytes 40992 | tf_op jit(solution)/shard_map/ppermute | solution.py:375
  12.2 0.4 collective-permute-done.1.rest_1_
  12.5 0.2 copy-done.2
  12.8 0.1 copy-done
  12.8 0.4 copy-done.1
  13.2 4.5 %shard_map.121 = (f32[64,8,128]{2,1,0:T(8,128)}, f32[64,8,128]{2,1,0:T(8,128)}, f32[64,8,128]{2,1,0:T(8,128)}, f32[64,8,128]{2,1,0:T(8,128)}, f32[8,32,8,128]{3,...) custom-call(f32[64,8,128]{2,1,0:T(8,128)} %get-tuple-element.68.h_re, ...), custom_call_target="tpu_custom_call", output_to_operand_aliasing={{0}: (0, {}), {1}: (1, {}), {2}: (2, {}), {3}: (3, {})} | custom-call | tf_op jit(solution)/shard_map/pallas_call | solution.py:449
  17.7 0.7 collective-permute-start.3
  18.4 1.3 %collective-permute-start.4 = (f32[3,4,8,128]{3,2,1,0:T(8,128)}, f32[3,4,8,128]{3,2,1,0:T(8,128)S(1)}, u32[]{:S(2)}, u32[]{:S(2)}) collective-permute-start(f32[3,4,8,128]{3,2,1,0:T(8,128)} %get-tuple-element.86), channel_id=1, source_target_pairs={{8,0},{16,8},{24,16},{0,24},{9,1},{17,9},{25,17},{1,25},{10,2},{18... | collective-permute-start | bytes 147464 | tf_op jit(solution)/shard_map/ppermute | solution.py:374
  19.8 1.4 %collective-permute-start.5 = (f32[2,3,8,128]{3,2,1,0:T(8,128)}, f32[2,3,8,128]{3,2,1,0:T(8,128)S(1)}, u32[]{:S(2)}, u32[]{:S(2)}) collective-permute-start(f32[2,3,8,128]{3,2,1,0:T(8,128)} %get-tuple-element.87), channel_id=1, source_target_pairs={{0,4},{4,0},{1,5},{5,1},{2,6},{6,2},{3,7},{7,3},{8,12},{12,8},{9,1... | collective-permute-start | bytes 73736 | tf_op jit(solution)/shard_map/ppermute | solution.py:375
  21.2 4.5 %shard_map.122 = (f32[64,8,128]{2,1,0:T(8,128)}, f32[64,8,128]{2,1,0:T(8,128)}, f32[64,8,128]{2,1,0:T(8,128)}, f32[64,8,128]{2,1,0:T(8,128)}, f32[8,32,8,128]{3,...) custom-call(f32[64,8,128]{2,1,0:T(8,128)} %get-tuple-element.76.h_re, ...), custom_call_target="tpu_custom_call", output_to_operand_aliasing={{0}: (0, {}), {1}: (1, {}), {2}: (2, {}), {3}: (3, {})} | custom-call | tf_op jit(solution)/shard_map/pallas_call | solution.py:449
  25.7 1.7 %collective-permute-start.7 = (f32[3,4,8,128]{3,2,1,0:T(8,128)}, f32[3,4,8,128]{3,2,1,0:T(8,128)S(1)}, u32[]{:S(2)}, u32[]{:S(2)}) collective-permute-start(f32[3,4,8,128]{3,2,1,0:T(8,128)} %get-tuple-element.94), channel_id=1, source_target_pairs={{8,0},{16,8},{24,16},{0,24},{9,1},{17,9},{25,17},{1,25},{10,2},{18... | collective-permute-start | bytes 147464 | tf_op jit(solution)/shard_map/ppermute | solution.py:374
  27.5 0.6 collective-permute-start.8
  28.1 0.6 copy-done.17
  28.7 3.6 %shard_map.123 = (f32[64,8,128]{2,1,0:T(8,128)}, f32[64,8,128]{2,1,0:T(8,128)}, f32[64,8,128]{2,1,0:T(8,128)}, f32[64,8,128]{2,1,0:T(8,128)}, f32[3,4,8,128]{3,2...) custom-call(f32[64,8,128]{2,1,0:T(8,128)} %get-tuple-element.80.h_re, ...), custom_call_target="tpu_custom_call", output_to_operand_aliasing={{0}: (0, {}), {1}: (1, {}), {2}: (2, {}), {3}: (3, {})} | custom-call | tf_op jit(solution)/shard_map/pallas_call | solution.py:449
  32.3 0.2 collective-permute-start.10
  32.5 0.3 collective-permute-start.9
  32.9 1.4 %collective-permute-start.11 = (f32[2,3,8,128]{3,2,1,0:T(8,128)}, f32[2,3,8,128]{3,2,1,0:T(8,128)S(1)}, u32[]{:S(2)}, u32[]{:S(2)}) collective-permute-start(f32[2,3,8,128]{3,2,1,0:T(8,128)} %get-tuple-element.102), channel_id=1, source_target_pairs={{0,4},{4,0},{1,5},{5,1},{2,6},{6,2},{3,7},{7,3},{8,12},{12,8},{9,1... | collective-permute-start | bytes 73736 | tf_op jit(solution)/shard_map/ppermute | solution.py:375
  34.3 0.6 copy-done.9
  34.9 3.6 %shard_map.124 = (f32[64,8,128]{2,1,0:T(8,128)}, f32[64,8,128]{2,1,0:T(8,128)}, f32[64,8,128]{2,1,0:T(8,128)}, f32[64,8,128]{2,1,0:T(8,128)}, f32[3,4,8,128]{3,2...) custom-call(f32[64,8,128]{2,1,0:T(8,128)} %get-tuple-element.88.h_re, ...), custom_call_target="tpu_custom_call", output_to_operand_aliasing={{0}: (0, {}), {1}: (1, {}), {2}: (2, {}), {3}: (3, {})} | custom-call | tf_op jit(solution)/shard_map/pallas_call | solution.py:449
  38.5 0.9 %collective-permute-start.12 = (f32[3,4,8,128]{3,2,1,0:T(8,128)}, f32[3,4,8,128]{3,2,1,0:T(8,128)S(1)}, u32[]{:S(2)}, u32[]{:S(2)}) collective-permute-start(f32[3,4,8,128]{3,2,1,0:T(8,128)} %get-tuple-element.107), channel_id=1, source_target_pairs={{0,8},{8,16},{16,24},{24,0},{1,9},{9,17},{17,25},{25,1},{2,10},{10... | collective-permute-start | bytes 147464 | tf_op jit(solution)/shard_map/ppermute | solution.py:373
  39.4 0.9 %collective-permute-start.13 = (f32[3,4,8,128]{3,2,1,0:T(8,128)}, f32[3,4,8,128]{3,2,1,0:T(8,128)S(1)}, u32[]{:S(2)}, u32[]{:S(2)}) collective-permute-start(f32[3,4,8,128]{3,2,1,0:T(8,128)} %get-tuple-element.108), channel_id=1, source_target_pairs={{8,0},{16,8},{24,16},{0,24},{9,1},{17,9},{25,17},{1,25},{10,2},{18... | collective-permute-start | bytes 147464 | tf_op jit(solution)/shard_map/ppermute | solution.py:374
  40.3 0.6 collective-permute-start.14
  40.9 0.6 copy-done.10
  41.5 3.6 %shard_map.125 = (f32[64,8,128]{2,1,0:T(8,128)}, f32[64,8,128]{2,1,0:T(8,128)}, f32[64,8,128]{2,1,0:T(8,128)}, f32[64,8,128]{2,1,0:T(8,128)}, f32[3,4,8,128]{3,2...) custom-call(f32[64,8,128]{2,1,0:T(8,128)} %get-tuple-element.96.h_re, ...), custom_call_target="tpu_custom_call", output_to_operand_aliasing={{0}: (0, {}), {1}: (1, {}), {2}: (2, {}), {3}: (3, {})} | custom-call | tf_op jit(solution)/shard_map/pallas_call | solution.py:449
  45.1 0.2 collective-permute-start.15
  45.3 1.6 %collective-permute-start.16 = (f32[3,4,8,128]{3,2,1,0:T(8,128)}, f32[3,4,8,128]{3,2,1,0:T(8,128)S(1)}, u32[]{:S(2)}, u32[]{:S(2)}) collective-permute-start(f32[3,4,8,128]{3,2,1,0:T(8,128)} %get-tuple-element.115), channel_id=1, source_target_pairs={{8,0},{16,8},{24,16},{0,24},{9,1},{17,9},{25,17},{1,25},{10,2},{18... | collective-permute-start | bytes 147464 | tf_op jit(solution)/shard_map/ppermute | solution.py:374
  46.9 1.4 %collective-permute-start.17 = (f32[2,3,8,128]{3,2,1,0:T(8,128)}, f32[2,3,8,128]{3,2,1,0:T(8,128)S(1)}, u32[]{:S(2)}, u32[]{:S(2)}) collective-permute-start(f32[2,3,8,128]{3,2,1,0:T(8,128)} %get-tuple-element.116), channel_id=1, source_target_pairs={{0,4},{4,0},{1,5},{5,1},{2,6},{6,2},{3,7},{7,3},{8,12},{12,8},{9,1... | collective-permute-start | bytes 73736 | tf_op jit(solution)/shard_map/ppermute | solution.py:375
  48.3 0.6 copy-done.11
  48.9 3.6 %shard_map.126 = (f32[64,8,128]{2,1,0:T(8,128)}, f32[64,8,128]{2,1,0:T(8,128)}, f32[64,8,128]{2,1,0:T(8,128)}, f32[64,8,128]{2,1,0:T(8,128)}, f32[3,4,8,128]{3,2...) custom-call(f32[64,8,128]{2,1,0:T(8,128)} %get-tuple-element.103.h_r, ...), custom_call_target="tpu_custom_call", output_to_operand_aliasing={{0}: (0, {}), {1}: (1, {}), {2}: (2, {}), {3}: (3, {})} | custom-call | tf_op jit(solution)/shard_map/pallas_call | solution.py:449
  52.6 1.7 %collective-permute-start.19 = (f32[3,4,8,128]{3,2,1,0:T(8,128)}, f32[3,4,8,128]{3,2,1,0:T(8,128)S(1)}, u32[]{:S(2)}, u32[]{:S(2)}) collective-permute-start(f32[3,4,8,128]{3,2,1,0:T(8,128)} %get-tuple-element.122), channel_id=1, source_target_pairs={{8,0},{16,8},{24,16},{0,24},{9,1},{17,9},{25,17},{1,25},{10,2},{18... | collective-permute-start | bytes 147464 | tf_op jit(solution)/shard_map/ppermute | solution.py:374
  54.3 0.6 collective-permute-start.20
  55.0 0.6 copy-done.14
  55.6 3.2 %shard_map.127 = (f32[64,8,128]{2,1,0:T(8,128)}, f32[64,8,128]{2,1,0:T(8,128)}, f32[64,8,128]{2,1,0:T(8,128)}, f32[64,8,128]{2,1,0:T(8,128)}) custom-call(f32[64,8,128]{2,1,0:T(8,128)} %get-tuple-element.110.h_ref, f32[64,8,128]{2,1,0:T(8,128)} %get-tuple-element.111.w_ref, ...), custom_call_target="tpu_custom_call", output_to_operand_aliasing={{0}: (0, {}), {1}: (1, {}), {2}: (2, {}), {3}: (3, {})} | custom-call | tf_op jit(solution)/shard_map/pallas_call | solution.py:449
  58.8 0.5 copy-done.8
  59.4 3.2 %shard_map.128 = (f32[64,8,128]{2,1,0:T(8,128)}, f32[64,8,128]{2,1,0:T(8,128)}, f32[64,8,128]{2,1,0:T(8,128)}, f32[64,8,128]{2,1,0:T(8,128)}) custom-call(f32[64,8,128]{2,1,0:T(8,128)} %get-tuple-element.117.h_ref, f32[64,8,128]{2,1,0:T(8,128)} %get-tuple-element.118.w_ref, ...), custom_call_target="tpu_custom_call", output_to_operand_aliasing={{0}: (0, {}), {1}: (1, {}), {2}: (2, {}), {3}: (3, {})} | custom-call | tf_op jit(solution)/shard_map/pallas_call | solution.py:449
  62.6 3.1 %shard_map.129 = (f32[64,8,128]{2,1,0:T(8,128)}, f32[64,8,128]{2,1,0:T(8,128)}, f32[64,8,128]{2,1,0:T(8,128)}, f32[8,8,128]{2,1,0:T(8,128)}) custom-call(f32[64,8,128]{2,1,0:T(8,128)} %get-tuple-element.124.r_ref, f32[5,64,8,128]{3,2,1,0:T(8,128)} %get-tuple-element.72.co_ref.cz_ref), custom_call_target="tpu_custom_call" | custom-call | tf_op jit(solution)/shard_map/pallas_call | solution.py:464
  65.7 1.5 %collective-permute-start.21 = (f32[8,8,128]{2,1,0:T(8,128)}, f32[8,8,128]{2,1,0:T(8,128)S(1)}, u32[]{:S(2)}, u32[]{:S(2)}) collective-permute-start(f32[8,8,128]{2,1,0:T(8,128)} %get-tuple-element.128.rest_0_), channel_id=1, source_target_pairs={{0,1},{1,2},{2,3},{3,0},{4,5},{5,6},{6,7},{7,4},{8,9},{9,10},{10,1... | collective-permute-start | bytes 98312 | tf_op jit(solution)/shard_map/ppermute | solution.py:476
  67.1 2.6 %collective-permute-start.22 = (f32[8,8,128]{2,1,0:T(8,128)}, f32[8,8,128]{2,1,0:T(8,128)S(1)}, u32[]{:S(2)}, u32[]{:S(2)}) collective-permute-start(f32[8,8,128]{2,1,0:T(8,128)} %get-tuple-element.128.rest_0_), channel_id=1, source_target_pairs={{0,2},{1,3},{2,0},{3,1},{4,6},{5,7},{6,4},{7,5},{8,10},{9,11},{10,... | collective-permute-start | bytes 98312 | tf_op jit(solution)/shard_map/ppermute | solution.py:476
  69.7 1.3 %collective-permute-start.23 = (f32[8,8,128]{2,1,0:T(8,128)}, f32[8,8,128]{2,1,0:T(8,128)S(1)}, u32[]{:S(2)}, u32[]{:S(2)}) collective-permute-start(f32[8,8,128]{2,1,0:T(8,128)} %get-tuple-element.128.rest_0_), channel_id=1, source_target_pairs={{0,3},{1,0},{2,1},{3,2},{4,7},{5,4},{6,5},{7,6},{8,11},{9,8},{10,9... | collective-permute-start | bytes 98312 | tf_op jit(solution)/shard_map/ppermute | solution.py:476
  71.1 1.0 %collective-permute-done.21.rest_1_ = f32[8,8,128]{2,1,0:T(8,128)S(1)} collective-permute-done((f32[8,8,128]{2,1,0:T(8,128)}, f32[8,8,128]{2,1,0:T(8,128)S(1)}, u32[]{:S(2)}, u32[]{:S(2)}) %collective-permute-start.21) | collective-permute-done | bytes 32800 | tf_op jit(solution)/shard_map/ppermute | solution.py:476
  72.0 0.6 collective-permute-done.22.rest_2_
  72.6 1.2 %collective-permute-done.23.rest_3_ = f32[8,8,128]{2,1,0:T(8,128)S(1)} collective-permute-done((f32[8,8,128]{2,1,0:T(8,128)}, f32[8,8,128]{2,1,0:T(8,128)S(1)}, u32[]{:S(2)}, u32[]{:S(2)}) %collective-permute-start.23) | collective-permute-done | bytes 32800 | tf_op jit(solution)/shard_map/ppermute | solution.py:476
  73.8 0.6 copy-done.23
  74.4 2.0 %shard_map.130 = f32[64,8,128]{2,1,0:T(8,128)} custom-call(s32[1]{0:T(128)} %bitcast.rank_ref, f32[64,8,128]{2,1,0:T(8,128)} %get-tuple-element.125.y_ref, f32[64,8,128]{2,1,0:T(8,128)} %get-tuple-element.126.a_ref, f32[64,8,128]{2,1,0:T(8,128)} %get-tuple-element.127.b_ref, f32[8,8,128]{2,1,0:T(8,128)} %get-tuple-element.128.rest_0_, ...), custom_call_target="tpu_custom_call" | custom-call | tf_op jit(solution)/shard_map/pallas_call | solution.py:478
  (59 shorter events, 0.4 us)
Async XLA Ops:
  5.2 7.0 %collective-permute-start = (f32[5,8,8,128]{3,2,1,0:T(8,128)}, f32[5,8,8,128]{3,2,1,0:T(8,128)S(1)}, u32[]{:S(2)}, u32[]{:S(2)}) collective-permute-start(f32[5,8,8,128]{3,2,1,0:T(8,128)} %get-tuple-element.73), channel_id=1, source_target_pairs={{0,8},{8,16},{16,24},{24,0},{1,9},{9,17},{17,25},{25,1},{2,10},{10... | collective-permute-start | bytes 491528 | tf_op jit(solution)/shard_map/ppermute | solution.py:373
  5.7 6.8 %collective-permute-start.1 = (f32[5,8,8,128]{3,2,1,0:T(8,128)}, f32[5,8,8,128]{3,2,1,0:T(8,128)S(1)}, u32[]{:S(2)}, u32[]{:S(2)}) collective-permute-start(f32[5,8,8,128]{3,2,1,0:T(8,128)} %get-tuple-element.74), channel_id=1, source_target_pairs={{8,0},{16,8},{24,16},{0,24},{9,1},{17,9},{25,17},{1,25},{10,2},{18... | collective-permute-start | bytes 491528 | tf_op jit(solution)/shard_map/ppermute | solution.py:374
  7.7 4.5 %collective-permute-start.2 = (f32[2,5,8,128]{3,2,1,0:T(8,128)}, f32[2,5,8,128]{3,2,1,0:T(8,128)S(1)}, u32[]{:S(2)}, u32[]{:S(2)}) collective-permute-start(f32[2,5,8,128]{3,2,1,0:T(8,128)} %get-tuple-element.75), channel_id=1, source_target_pairs={{0,4},{4,0},{1,5},{5,1},{2,6},{6,2},{3,7},{7,3},{8,12},{12,8},{9,1... | collective-permute-start | bytes 122888 | tf_op jit(solution)/shard_map/ppermute | solution.py:375
  12.2 0.6 copy-start.2
  12.2 0.7 copy-start
  12.5 0.7 copy-start.1
  17.7 10.4 %collective-permute-start.3 = (f32[3,4,8,128]{3,2,1,0:T(8,128)}, f32[3,4,8,128]{3,2,1,0:T(8,128)S(1)}, u32[]{:S(2)}, u32[]{:S(2)}) collective-permute-start(f32[3,4,8,128]{3,2,1,0:T(8,128)} %get-tuple-element.85), channel_id=1, source_target_pairs={{0,8},{8,16},{16,24},{24,0},{1,9},{9,17},{17,25},{25,1},{2,10},{10... | collective-permute-start | bytes 147464 | tf_op jit(solution)/shard_map/ppermute | solution.py:373
  18.4 9.7 %collective-permute-start.4 = (f32[3,4,8,128]{3,2,1,0:T(8,128)}, f32[3,4,8,128]{3,2,1,0:T(8,128)S(1)}, u32[]{:S(2)}, u32[]{:S(2)}) collective-permute-start(f32[3,4,8,128]{3,2,1,0:T(8,128)} %get-tuple-element.86), channel_id=1, source_target_pairs={{8,0},{16,8},{24,16},{0,24},{9,1},{17,9},{25,17},{1,25},{10,2},{18... | collective-permute-start | bytes 147464 | tf_op jit(solution)/shard_map/ppermute | solution.py:374
  19.8 7.7 %collective-permute-start.5 = (f32[2,3,8,128]{3,2,1,0:T(8,128)}, f32[2,3,8,128]{3,2,1,0:T(8,128)S(1)}, u32[]{:S(2)}, u32[]{:S(2)}) collective-permute-start(f32[2,3,8,128]{3,2,1,0:T(8,128)} %get-tuple-element.87), channel_id=1, source_target_pairs={{0,4},{4,0},{1,5},{5,1},{2,6},{6,2},{3,7},{7,3},{8,12},{12,8},{9,1... | collective-permute-start | bytes 73736 | tf_op jit(solution)/shard_map/ppermute | solution.py:375
  25.7 8.6 %collective-permute-start.6 = (f32[3,4,8,128]{3,2,1,0:T(8,128)}, f32[3,4,8,128]{3,2,1,0:T(8,128)S(1)}, u32[]{:S(2)}, u32[]{:S(2)}) collective-permute-start(f32[3,4,8,128]{3,2,1,0:T(8,128)} %get-tuple-element.93), channel_id=1, source_target_pairs={{0,8},{8,16},{16,24},{24,0},{1,9},{9,17},{17,25},{25,1},{2,10},{10... | collective-permute-start | bytes 147464 | tf_op jit(solution)/shard_map/ppermute | solution.py:373
  25.7 8.6 %collective-permute-start.7 = (f32[3,4,8,128]{3,2,1,0:T(8,128)}, f32[3,4,8,128]{3,2,1,0:T(8,128)S(1)}, u32[]{:S(2)}, u32[]{:S(2)}) collective-permute-start(f32[3,4,8,128]{3,2,1,0:T(8,128)} %get-tuple-element.94), channel_id=1, source_target_pairs={{8,0},{16,8},{24,16},{0,24},{9,1},{17,9},{25,17},{1,25},{10,2},{18... | collective-permute-start | bytes 147464 | tf_op jit(solution)/shard_map/ppermute | solution.py:374
  27.5 0.7 copy-start.7
  27.5 5.4 %collective-permute-start.8 = (f32[2,3,8,128]{3,2,1,0:T(8,128)}, f32[2,3,8,128]{3,2,1,0:T(8,128)S(1)}, u32[]{:S(2)}, u32[]{:S(2)}) collective-permute-start(f32[2,3,8,128]{3,2,1,0:T(8,128)} %get-tuple-element.95), channel_id=1, source_target_pairs={{0,4},{4,0},{1,5},{5,1},{2,6},{6,2},{3,7},{7,3},{8,12},{12,8},{9,1... | collective-permute-start | bytes 73736 | tf_op jit(solution)/shard_map/ppermute | solution.py:375
  28.1 0.6 copy-start.17
  28.1 0.6 copy-start.18
  32.3 8.6 %collective-permute-start.10 = (f32[3,4,8,128]{3,2,1,0:T(8,128)}, f32[3,4,8,128]{3,2,1,0:T(8,128)S(1)}, u32[]{:S(2)}, u32[]{:S(2)}) collective-permute-start(f32[3,4,8,128]{3,2,1,0:T(8,128)} %get-tuple-element.101), channel_id=1, source_target_pairs={{8,0},{16,8},{24,16},{0,24},{9,1},{17,9},{25,17},{1,25},{10,2},{18... | collective-permute-start | bytes 147464 | tf_op jit(solution)/shard_map/ppermute | solution.py:374
  32.5 8.4 %collective-permute-start.9 = (f32[3,4,8,128]{3,2,1,0:T(8,128)}, f32[3,4,8,128]{3,2,1,0:T(8,128)S(1)}, u32[]{:S(2)}, u32[]{:S(2)}) collective-permute-start(f32[3,4,8,128]{3,2,1,0:T(8,128)} %get-tuple-element.100), channel_id=1, source_target_pairs={{0,8},{8,16},{16,24},{24,0},{1,9},{9,17},{17,25},{25,1},{2,10},{10... | collective-permute-start | bytes 147464 | tf_op jit(solution)/shard_map/ppermute | solution.py:373
  32.9 1.4 %copy-start.3 = (f32[2,3,8,128]{3,2,1,0:T(8,128)}, f32[2,3,8,128]{3,2,1,0:T(8,128)S(1)}, u32[]{:S(2)}) copy-start(f32[2,3,8,128]{3,2,1,0:T(8,128)S(1)} %collective-permute-done.8.rest_3_.rest_4_) | copy-start | bytes 73732
  32.9 7.4 %collective-permute-start.11 = (f32[2,3,8,128]{3,2,1,0:T(8,128)}, f32[2,3,8,128]{3,2,1,0:T(8,128)S(1)}, u32[]{:S(2)}, u32[]{:S(2)}) collective-permute-start(f32[2,3,8,128]{3,2,1,0:T(8,128)} %get-tuple-element.102), channel_id=1, source_target_pairs={{0,4},{4,0},{1,5},{5,1},{2,6},{6,2},{3,7},{7,3},{8,12},{12,8},{9,1... | collective-permute-start | bytes 73736 | tf_op jit(solution)/shard_map/ppermute | solution.py:375
  34.3 0.6 copy-start.9
  34.3 0.6 copy-start.12
  38.5 9.8 %collective-permute-start.12 = (f32[3,4,8,128]{3,2,1,0:T(8,128)}, f32[3,4,8,128]{3,2,1,0:T(8,128)S(1)}, u32[]{:S(2)}, u32[]{:S(2)}) collective-permute-start(f32[3,4,8,128]{3,2,1,0:T(8,128)} %get-tuple-element.107), channel_id=1, source_target_pairs={{0,8},{8,16},{16,24},{24,0},{1,9},{9,17},{17,25},{25,1},{2,10},{10... | collective-permute-start | bytes 147464 | tf_op jit(solution)/shard_map/ppermute | solution.py:373
  39.4 8.9 %collective-permute-start.13 = (f32[3,4,8,128]{3,2,1,0:T(8,128)}, f32[3,4,8,128]{3,2,1,0:T(8,128)S(1)}, u32[]{:S(2)}, u32[]{:S(2)}) collective-permute-start(f32[3,4,8,128]{3,2,1,0:T(8,128)} %get-tuple-element.108), channel_id=1, source_target_pairs={{8,0},{16,8},{24,16},{0,24},{9,1},{17,9},{25,17},{1,25},{10,2},{18... | collective-permute-start | bytes 147464 | tf_op jit(solution)/shard_map/ppermute | solution.py:374
  40.3 0.7 copy-start.4
  40.3 6.6 %collective-permute-start.14 = (f32[2,3,8,128]{3,2,1,0:T(8,128)}, f32[2,3,8,128]{3,2,1,0:T(8,128)S(1)}, u32[]{:S(2)}, u32[]{:S(2)}) collective-permute-start(f32[2,3,8,128]{3,2,1,0:T(8,128)} %get-tuple-element.109), channel_id=1, source_target_pairs={{0,4},{4,0},{1,5},{5,1},{2,6},{6,2},{3,7},{7,3},{8,12},{12,8},{9,1... | collective-permute-start | bytes 73736 | tf_op jit(solution)/shard_map/ppermute | solution.py:375
  40.9 0.6 copy-start.10
  40.9 0.6 copy-start.13
  45.1 9.8 %collective-permute-start.15 = (f32[3,4,8,128]{3,2,1,0:T(8,128)}, f32[3,4,8,128]{3,2,1,0:T(8,128)S(1)}, u32[]{:S(2)}, u32[]{:S(2)}) collective-permute-start(f32[3,4,8,128]{3,2,1,0:T(8,128)} %get-tuple-element.114), channel_id=1, source_target_pairs={{0,8},{8,16},{16,24},{24,0},{1,9},{9,17},{17,25},{25,1},{2,10},{10... | collective-permute-start | bytes 147464 | tf_op jit(solution)/shard_map/ppermute | solution.py:373
  45.3 9.6 %collective-permute-start.16 = (f32[3,4,8,128]{3,2,1,0:T(8,128)}, f32[3,4,8,128]{3,2,1,0:T(8,128)S(1)}, u32[]{:S(2)}, u32[]{:S(2)}) collective-permute-start(f32[3,4,8,128]{3,2,1,0:T(8,128)} %get-tuple-element.115), channel_id=1, source_target_pairs={{8,0},{16,8},{24,16},{0,24},{9,1},{17,9},{25,17},{1,25},{10,2},{18... | collective-permute-start | bytes 147464 | tf_op jit(solution)/shard_map/ppermute | solution.py:374
  46.9 1.4 %copy-start.5 = (f32[2,3,8,128]{3,2,1,0:T(8,128)}, f32[2,3,8,128]{3,2,1,0:T(8,128)S(1)}, u32[]{:S(2)}) copy-start(f32[2,3,8,128]{3,2,1,0:T(8,128)S(1)} %collective-permute-done.14.rest_3_.rest_4_) | copy-start | bytes 73732
  46.9 7.4 %collective-permute-start.17 = (f32[2,3,8,128]{3,2,1,0:T(8,128)}, f32[2,3,8,128]{3,2,1,0:T(8,128)S(1)}, u32[]{:S(2)}, u32[]{:S(2)}) collective-permute-start(f32[2,3,8,128]{3,2,1,0:T(8,128)} %get-tuple-element.116), channel_id=1, source_target_pairs={{0,4},{4,0},{1,5},{5,1},{2,6},{6,2},{3,7},{7,3},{8,12},{12,8},{9,1... | collective-permute-start | bytes 73736 | tf_op jit(solution)/shard_map/ppermute | solution.py:375
  48.3 0.6 copy-start.11
  48.3 0.6 copy-start.15
  52.5 6.2 %collective-permute-start.18 = (f32[3,4,8,128]{3,2,1,0:T(8,128)}, f32[3,4,8,128]{3,2,1,0:T(8,128)S(1)}, u32[]{:S(2)}, u32[]{:S(2)}) collective-permute-start(f32[3,4,8,128]{3,2,1,0:T(8,128)} %get-tuple-element.121), channel_id=1, source_target_pairs={{0,8},{8,16},{16,24},{24,0},{1,9},{9,17},{17,25},{25,1},{2,10},{10... | collective-permute-start | bytes 147464 | tf_op jit(solution)/shard_map/ppermute | solution.py:373
  52.6 6.2 %collective-permute-start.19 = (f32[3,4,8,128]{3,2,1,0:T(8,128)}, f32[3,4,8,128]{3,2,1,0:T(8,128)S(1)}, u32[]{:S(2)}, u32[]{:S(2)}) collective-permute-start(f32[3,4,8,128]{3,2,1,0:T(8,128)} %get-tuple-element.122), channel_id=1, source_target_pairs={{8,0},{16,8},{24,16},{0,24},{9,1},{17,9},{25,17},{1,25},{10,2},{18... | collective-permute-start | bytes 147464 | tf_op jit(solution)/shard_map/ppermute | solution.py:374
  54.3 0.7 copy-start.6
  54.3 4.4 %collective-permute-start.20 = (f32[2,3,8,128]{3,2,1,0:T(8,128)}, f32[2,3,8,128]{3,2,1,0:T(8,128)S(1)}, u32[]{:S(2)}, u32[]{:S(2)}) collective-permute-start(f32[2,3,8,128]{3,2,1,0:T(8,128)} %get-tuple-element.123), channel_id=1, source_target_pairs={{0,4},{4,0},{1,5},{5,1},{2,6},{6,2},{3,7},{7,3},{8,12},{12,8},{9,1... | collective-permute-start | bytes 73736 | tf_op jit(solution)/shard_map/ppermute | solution.py:375
  54.9 0.6 copy-start.14
  55.0 0.6 copy-start.16
  58.7 0.6 copy-start.8
  58.8 0.6 copy-start.19
  58.8 0.6 copy-start.20
  65.7 6.4 %collective-permute-start.21 = (f32[8,8,128]{2,1,0:T(8,128)}, f32[8,8,128]{2,1,0:T(8,128)S(1)}, u32[]{:S(2)}, u32[]{:S(2)}) collective-permute-start(f32[8,8,128]{2,1,0:T(8,128)} %get-tuple-element.128.rest_0_), channel_id=1, source_target_pairs={{0,1},{1,2},{2,3},{3,0},{4,5},{5,6},{6,7},{7,4},{8,9},{9,10},{10,1... | collective-permute-start | bytes 98312 | tf_op jit(solution)/shard_map/ppermute | solution.py:476
  67.1 5.5 %collective-permute-start.22 = (f32[8,8,128]{2,1,0:T(8,128)}, f32[8,8,128]{2,1,0:T(8,128)S(1)}, u32[]{:S(2)}, u32[]{:S(2)}) collective-permute-start(f32[8,8,128]{2,1,0:T(8,128)} %get-tuple-element.128.rest_0_), channel_id=1, source_target_pairs={{0,2},{1,3},{2,0},{3,1},{4,6},{5,7},{6,4},{7,5},{8,10},{9,11},{10,... | collective-permute-start | bytes 98312 | tf_op jit(solution)/shard_map/ppermute | solution.py:476
  69.7 4.1 %collective-permute-start.23 = (f32[8,8,128]{2,1,0:T(8,128)}, f32[8,8,128]{2,1,0:T(8,128)S(1)}, u32[]{:S(2)}, u32[]{:S(2)}) collective-permute-start(f32[8,8,128]{2,1,0:T(8,128)} %get-tuple-element.128.rest_0_), channel_id=1, source_target_pairs={{0,3},{1,0},{2,1},{3,2},{4,7},{5,4},{6,5},{7,6},{8,11},{9,8},{10,9... | collective-permute-start | bytes 98312 | tf_op jit(solution)/shard_map/ppermute | solution.py:476
  72.0 1.8 %copy-start.21 = (f32[8,8,128]{2,1,0:T(8,128)}, f32[8,8,128]{2,1,0:T(8,128)S(1)}, u32[]{:S(2)}) copy-start(f32[8,8,128]{2,1,0:T(8,128)S(1)} %collective-permute-done.21.rest_1_) | copy-start | bytes 98308
  72.6 1.2 %copy-start.22 = (f32[8,8,128]{2,1,0:T(8,128)}, f32[8,8,128]{2,1,0:T(8,128)S(1)}, u32[]{:S(2)}) copy-start(f32[8,8,128]{2,1,0:T(8,128)S(1)} %collective-permute-done.22.rest_2_) | copy-start | bytes 98308
  73.8 0.6 copy-start.23

commit v16 on v15

--- a/solution.py
+++ b/solution.py
@@ -228,7 +228,7 @@
                     xl_ref[f, a] = out[planes, ROWS - 1, :]
             return (tuple(acc.yf), tuple(acc.yl))
 
-        y_f, y_l = lax.fori_loop(0, groups, group, ((zero,) * 3, (zero,) * 3))
+        y_f, y_l = lax.fori_loop(0, groups, group, ((zero,) * 3, (zero,) * 3), unroll=2)
         if not last:
             for f in range(3):
                 y_ref[0, f] = y_f[f]

time: 76.9 us -> 82.1 us (1.068)
  Pallas kernels: 39.4 us -> 44.6 us
    pallas_call x8, Pallas kernels: 29.7 us -> 35 us  [local(): pl.pallas_call(make_section_kernel(k, first, last), grid=(1,), out_shape=...]
  transfers between devices with their start and end apart: 24 -> 24, of which waited for: 5 -> 5; matrix products, arithmetic and copies ran while one was open for 0% -> 0% of each run, Pallas kernels for 29% -> 32%
where the time goes in v16:
time: 82.1 us; the launch traced here: 81.7 us
  Pallas kernels  44.6 us (54%)
  starting transfers between devices  25.9 us (32%)
  waiting for transfers between devices  5.37 us (7%)
  local copies, waits for them, and re-layouts  4.95 us (6%)
  between operations  0.83 us (1%)
    pallas_call x8, Pallas kernels, local(): pl.pallas_call(make_section_kernel(k, first, last), grid=(1,), out_shape=...  35 us
    ppermute x7, starting transfers between devices, exchange(): xhi = lax.ppermute(xf, 'east', east_bwd)  9.4 us
    ppermute x7, starting transfers between devices, exchange(): ylo = lax.ppermute(ys, 'north', north_fwd)  8.38 us
    ppermute x3, starting transfers between devices, local(): lax.ppermute(red, 'depth', [(i, (i + k) % count) for i in range(count)])  5.36 us
    unnamed x48, local copies, waits for them, and re-layouts  4.95 us
    pallas_call x1, Pallas kernels, local(): pl.pallas_call(prep_kernel, out_shape=(sds(shape), sds(shape), sds(shape)...  4.57 us
    pallas_call x1, Pallas kernels, local(): pl.pallas_call(sweep_kernel, grid=(1,), out_shape=(sds(shape), sds(shape)...  3.08 us
    ppermute x3, waiting for transfers between devices, local(): lax.ppermute(red, 'depth', [(i, (i + k) % count) for i in range(count)])  2.77 us
  transfers between devices with their start and end apart: 24, of which 5 were waited for; matrix products, arithmetic and copies ran while one was open for 0% of the time, Pallas kernels for 32%

profile of v16, /device:TPU:0, one launch (start us, length us, event | category | flops | bytes accessed | tf_op | source)
XLA Modules:
  0.0 81.7 jit_solution(3546322107385904943)
XLA Ops:
  0.6 4.6 %shard_map.120 = (f32[64,8,128]{2,1,0:T(8,128)}, f32[64,8,128]{2,1,0:T(8,128)}, f32[64,8,128]{2,1,0:T(8,128)}, f32[64,8,128]{2,1,0:T(8,128)}, f32[5,64,8,128]{3,...) custom-call(f32[2,12]{1,0:T(2,128)} %lat_ref.1, f32[12]{0:T(128)} %vert_ref.1, ...), custom_call_target="tpu_custom_call" | custom-call | tf_op jit(solution)/shard_map/pallas_call | solution.py:408
  5.2 0.5 collective-permute-start
  5.7 2.0 %collective-permute-start.1 = (f32[5,8,8,128]{3,2,1,0:T(8,128)}, f32[5,8,8,128]{3,2,1,0:T(8,128)S(1)}, u32[]{:S(2)}, u32[]{:S(2)}) collective-permute-start(f32[5,8,8,128]{3,2,1,0:T(8,128)} %get-tuple-element.74), channel_id=1, source_target_pairs={{8,0},{16,8},{24,16},{0,24},{9,1},{17,9},{25,17},{1,25},{10,2},{18... | collective-permute-start | bytes 491528 | tf_op jit(solution)/shard_map/ppermute | solution.py:374
  7.7 2.3 %collective-permute-start.2 = (f32[2,5,8,128]{3,2,1,0:T(8,128)}, f32[2,5,8,128]{3,2,1,0:T(8,128)S(1)}, u32[]{:S(2)}, u32[]{:S(2)}) collective-permute-start(f32[2,5,8,128]{3,2,1,0:T(8,128)} %get-tuple-element.75), channel_id=1, source_target_pairs={{0,4},{4,0},{1,5},{5,1},{2,6},{6,2},{3,7},{7,3},{8,12},{12,8},{9,1... | collective-permute-start | bytes 122888 | tf_op jit(solution)/shard_map/ppermute | solution.py:375
  10.0 2.2 %collective-permute-done.2.rest_2_.rest_3_ = f32[2,5,8,128]{3,2,1,0:T(8,128)S(1)} collective-permute-done((f32[2,5,8,128]{3,2,1,0:T(8,128)}, f32[2,5,8,128]{3,2,1,0:T(8,128)S(1)}, u32[]{:S(2)}, u32[]{:S(2)}) %collective-permute-start.2) | collective-permute-done | bytes 40992 | tf_op jit(solution)/shard_map/ppermute | solution.py:375
  12.2 0.4 collective-permute-done.1.rest_1_
  12.5 0.2 copy-done.2
  12.8 0.1 copy-done
  12.8 0.4 copy-done.1
  13.2 5.6 %shard_map.121 = (f32[64,8,128]{2,1,0:T(8,128)}, f32[64,8,128]{2,1,0:T(8,128)}, f32[64,8,128]{2,1,0:T(8,128)}, f32[64,8,128]{2,1,0:T(8,128)}, f32[8,32,8,128]{3,...) custom-call(f32[64,8,128]{2,1,0:T(8,128)} %get-tuple-element.68.h_re, ...), custom_call_target="tpu_custom_call", output_to_operand_aliasing={{0}: (0, {}), {1}: (1, {}), {2}: (2, {}), {3}: (3, {})} | custom-call | tf_op jit(solution)/shard_map/pallas_call | solution.py:449
  18.8 0.8 collective-permute-start.3
  19.5 1.3 %collective-permute-start.4 = (f32[3,4,8,128]{3,2,1,0:T(8,128)}, f32[3,4,8,128]{3,2,1,0:T(8,128)S(1)}, u32[]{:S(2)}, u32[]{:S(2)}) collective-permute-start(f32[3,4,8,128]{3,2,1,0:T(8,128)} %get-tuple-element.86), channel_id=1, source_target_pairs={{8,0},{16,8},{24,16},{0,24},{9,1},{17,9},{25,17},{1,25},{10,2},{18... | collective-permute-start | bytes 147464 | tf_op jit(solution)/shard_map/ppermute | solution.py:374
  20.9 1.4 %collective-permute-start.5 = (f32[2,3,8,128]{3,2,1,0:T(8,128)}, f32[2,3,8,128]{3,2,1,0:T(8,128)S(1)}, u32[]{:S(2)}, u32[]{:S(2)}) collective-permute-start(f32[2,3,8,128]{3,2,1,0:T(8,128)} %get-tuple-element.87), channel_id=1, source_target_pairs={{0,4},{4,0},{1,5},{5,1},{2,6},{6,2},{3,7},{7,3},{8,12},{12,8},{9,1... | collective-permute-start | bytes 73736 | tf_op jit(solution)/shard_map/ppermute | solution.py:375
  22.3 5.6 %shard_map.122 = (f32[64,8,128]{2,1,0:T(8,128)}, f32[64,8,128]{2,1,0:T(8,128)}, f32[64,8,128]{2,1,0:T(8,128)}, f32[64,8,128]{2,1,0:T(8,128)}, f32[8,32,8,128]{3,...) custom-call(f32[64,8,128]{2,1,0:T(8,128)} %get-tuple-element.76.h_re, ...), custom_call_target="tpu_custom_call", output_to_operand_aliasing={{0}: (0, {}), {1}: (1, {}), {2}: (2, {}), {3}: (3, {})} | custom-call | tf_op jit(solution)/shard_map/pallas_call | solution.py:449
  27.9 1.7 %collective-permute-start.7 = (f32[3,4,8,128]{3,2,1,0:T(8,128)}, f32[3,4,8,128]{3,2,1,0:T(8,128)S(1)}, u32[]{:S(2)}, u32[]{:S(2)}) collective-permute-start(f32[3,4,8,128]{3,2,1,0:T(8,128)} %get-tuple-element.94), channel_id=1, source_target_pairs={{8,0},{16,8},{24,16},{0,24},{9,1},{17,9},{25,17},{1,25},{10,2},{18... | collective-permute-start | bytes 147464 | tf_op jit(solution)/shard_map/ppermute | solution.py:374
  29.6 0.7 collective-permute-start.8
  30.3 0.6 copy-done.17
  30.9 4.4 %shard_map.123 = (f32[64,8,128]{2,1,0:T(8,128)}, f32[64,8,128]{2,1,0:T(8,128)}, f32[64,8,128]{2,1,0:T(8,128)}, f32[64,8,128]{2,1,0:T(8,128)}, f32[3,4,8,128]{3,2...) custom-call(f32[64,8,128]{2,1,0:T(8,128)} %get-tuple-element.80.h_re, ...), custom_call_target="tpu_custom_call", output_to_operand_aliasing={{0}: (0, {}), {1}: (1, {}), {2}: (2, {}), {3}: (3, {})} | custom-call | tf_op jit(solution)/shard_map/pallas_call | solution.py:449
  35.3 0.2 collective-permute-start.10
  35.5 0.4 collective-permute-start.9
  35.9 1.4 %collective-permute-start.11 = (f32[2,3,8,128]{3,2,1,0:T(8,128)}, f32[2,3,8,128]{3,2,1,0:T(8,128)S(1)}, u32[]{:S(2)}, u32[]{:S(2)}) collective-permute-start(f32[2,3,8,128]{3,2,1,0:T(8,128)} %get-tuple-element.102), channel_id=1, source_target_pairs={{0,4},{4,0},{1,5},{5,1},{2,6},{6,2},{3,7},{7,3},{8,12},{12,8},{9,1... | collective-permute-start | bytes 73736 | tf_op jit(solution)/shard_map/ppermute | solution.py:375
  37.3 0.6 copy-done.9
  37.9 4.4 %shard_map.124 = (f32[64,8,128]{2,1,0:T(8,128)}, f32[64,8,128]{2,1,0:T(8,128)}, f32[64,8,128]{2,1,0:T(8,128)}, f32[64,8,128]{2,1,0:T(8,128)}, f32[3,4,8,128]{3,2...) custom-call(f32[64,8,128]{2,1,0:T(8,128)} %get-tuple-element.88.h_re, ...), custom_call_target="tpu_custom_call", output_to_operand_aliasing={{0}: (0, {}), {1}: (1, {}), {2}: (2, {}), {3}: (3, {})} | custom-call | tf_op jit(solution)/shard_map/pallas_call | solution.py:449
  42.3 0.9 %collective-permute-start.12 = (f32[3,4,8,128]{3,2,1,0:T(8,128)}, f32[3,4,8,128]{3,2,1,0:T(8,128)S(1)}, u32[]{:S(2)}, u32[]{:S(2)}) collective-permute-start(f32[3,4,8,128]{3,2,1,0:T(8,128)} %get-tuple-element.107), channel_id=1, source_target_pairs={{0,8},{8,16},{16,24},{24,0},{1,9},{9,17},{17,25},{25,1},{2,10},{10... | collective-permute-start | bytes 147464 | tf_op jit(solution)/shard_map/ppermute | solution.py:373
  43.2 0.9 %collective-permute-start.13 = (f32[3,4,8,128]{3,2,1,0:T(8,128)}, f32[3,4,8,128]{3,2,1,0:T(8,128)S(1)}, u32[]{:S(2)}, u32[]{:S(2)}) collective-permute-start(f32[3,4,8,128]{3,2,1,0:T(8,128)} %get-tuple-element.108), channel_id=1, source_target_pairs={{8,0},{16,8},{24,16},{0,24},{9,1},{17,9},{25,17},{1,25},{10,2},{18... | collective-permute-start | bytes 147464 | tf_op jit(solution)/shard_map/ppermute | solution.py:374
  44.0 0.7 collective-permute-start.14
  44.7 0.6 copy-done.10
  45.3 4.4 %shard_map.125 = (f32[64,8,128]{2,1,0:T(8,128)}, f32[64,8,128]{2,1,0:T(8,128)}, f32[64,8,128]{2,1,0:T(8,128)}, f32[64,8,128]{2,1,0:T(8,128)}, f32[3,4,8,128]{3,2...) custom-call(f32[64,8,128]{2,1,0:T(8,128)} %get-tuple-element.96.h_re, ...), custom_call_target="tpu_custom_call", output_to_operand_aliasing={{0}: (0, {}), {1}: (1, {}), {2}: (2, {}), {3}: (3, {})} | custom-call | tf_op jit(solution)/shard_map/pallas_call | solution.py:449
  49.8 0.2 collective-permute-start.15
  49.9 1.6 %collective-permute-start.16 = (f32[3,4,8,128]{3,2,1,0:T(8,128)}, f32[3,4,8,128]{3,2,1,0:T(8,128)S(1)}, u32[]{:S(2)}, u32[]{:S(2)}) collective-permute-start(f32[3,4,8,128]{3,2,1,0:T(8,128)} %get-tuple-element.115), channel_id=1, source_target_pairs={{8,0},{16,8},{24,16},{0,24},{9,1},{17,9},{25,17},{1,25},{10,2},{18... | collective-permute-start | bytes 147464 | tf_op jit(solution)/shard_map/ppermute | solution.py:374
  51.5 1.4 %collective-permute-start.17 = (f32[2,3,8,128]{3,2,1,0:T(8,128)}, f32[2,3,8,128]{3,2,1,0:T(8,128)S(1)}, u32[]{:S(2)}, u32[]{:S(2)}) collective-permute-start(f32[2,3,8,128]{3,2,1,0:T(8,128)} %get-tuple-element.116), channel_id=1, source_target_pairs={{0,4},{4,0},{1,5},{5,1},{2,6},{6,2},{3,7},{7,3},{8,12},{12,8},{9,1... | collective-permute-start | bytes 73736 | tf_op jit(solution)/shard_map/ppermute | solution.py:375
  52.9 0.6 copy-done.11
  53.5 4.4 %shard_map.126 = (f32[64,8,128]{2,1,0:T(8,128)}, f32[64,8,128]{2,1,0:T(8,128)}, f32[64,8,128]{2,1,0:T(8,128)}, f32[64,8,128]{2,1,0:T(8,128)}, f32[3,4,8,128]{3,2...) custom-call(f32[64,8,128]{2,1,0:T(8,128)} %get-tuple-element.103.h_r, ...), custom_call_target="tpu_custom_call", output_to_operand_aliasing={{0}: (0, {}), {1}: (1, {}), {2}: (2, {}), {3}: (3, {})} | custom-call | tf_op jit(solution)/shard_map/pallas_call | solution.py:449
  58.0 1.7 %collective-permute-start.19 = (f32[3,4,8,128]{3,2,1,0:T(8,128)}, f32[3,4,8,128]{3,2,1,0:T(8,128)S(1)}, u32[]{:S(2)}, u32[]{:S(2)}) collective-permute-start(f32[3,4,8,128]{3,2,1,0:T(8,128)} %get-tuple-element.122), channel_id=1, source_target_pairs={{8,0},{16,8},{24,16},{0,24},{9,1},{17,9},{25,17},{1,25},{10,2},{18... | collective-permute-start | bytes 147464 | tf_op jit(solution)/shard_map/ppermute | solution.py:374
  59.7 0.7 collective-permute-start.20
  60.4 0.6 copy-done.14
  61.0 3.1 %shard_map.127 = (f32[64,8,128]{2,1,0:T(8,128)}, f32[64,8,128]{2,1,0:T(8,128)}, f32[64,8,128]{2,1,0:T(8,128)}, f32[64,8,128]{2,1,0:T(8,128)}) custom-call(f32[64,8,128]{2,1,0:T(8,128)} %get-tuple-element.110.h_ref, f32[64,8,128]{2,1,0:T(8,128)} %get-tuple-element.111.w_ref, ...), custom_call_target="tpu_custom_call", output_to_operand_aliasing={{0}: (0, {}), {1}: (1, {}), {2}: (2, {}), {3}: (3, {})} | custom-call | tf_op jit(solution)/shard_map/pallas_call | solution.py:449
  64.1 0.5 copy-done.8
  64.7 3.1 %shard_map.128 = (f32[64,8,128]{2,1,0:T(8,128)}, f32[64,8,128]{2,1,0:T(8,128)}, f32[64,8,128]{2,1,0:T(8,128)}, f32[64,8,128]{2,1,0:T(8,128)}) custom-call(f32[64,8,128]{2,1,0:T(8,128)} %get-tuple-element.117.h_ref, f32[64,8,128]{2,1,0:T(8,128)} %get-tuple-element.118.w_ref, ...), custom_call_target="tpu_custom_call", output_to_operand_aliasing={{0}: (0, {}), {1}: (1, {}), {2}: (2, {}), {3}: (3, {})} | custom-call | tf_op jit(solution)/shard_map/pallas_call | solution.py:449
  67.8 3.1 %shard_map.129 = (f32[64,8,128]{2,1,0:T(8,128)}, f32[64,8,128]{2,1,0:T(8,128)}, f32[64,8,128]{2,1,0:T(8,128)}, f32[8,8,128]{2,1,0:T(8,128)}) custom-call(f32[64,8,128]{2,1,0:T(8,128)} %get-tuple-element.124.r_ref, f32[5,64,8,128]{3,2,1,0:T(8,128)} %get-tuple-element.72.co_ref.cz_ref), custom_call_target="tpu_custom_call" | custom-call | tf_op jit(solution)/shard_map/pallas_call | solution.py:464
  70.9 1.4 %collective-permute-start.21 = (f32[8,8,128]{2,1,0:T(8,128)}, f32[8,8,128]{2,1,0:T(8,128)S(1)}, u32[]{:S(2)}, u32[]{:S(2)}) collective-permute-start(f32[8,8,128]{2,1,0:T(8,128)} %get-tuple-element.128.rest_0_), channel_id=1, source_target_pairs={{0,1},{1,2},{2,3},{3,0},{4,5},{5,6},{6,7},{7,4},{8,9},{9,10},{10,1... | collective-permute-start | bytes 98312 | tf_op jit(solution)/shard_map/ppermute | solution.py:476
  72.3 2.6 %collective-permute-start.22 = (f32[8,8,128]{2,1,0:T(8,128)}, f32[8,8,128]{2,1,0:T(8,128)S(1)}, u32[]{:S(2)}, u32[]{:S(2)}) collective-permute-start(f32[8,8,128]{2,1,0:T(8,128)} %get-tuple-element.128.rest_0_), channel_id=1, source_target_pairs={{0,2},{1,3},{2,0},{3,1},{4,6},{5,7},{6,4},{7,5},{8,10},{9,11},{10,... | collective-permute-start | bytes 98312 | tf_op jit(solution)/shard_map/ppermute | solution.py:476
  74.9 1.3 %collective-permute-start.23 = (f32[8,8,128]{2,1,0:T(8,128)}, f32[8,8,128]{2,1,0:T(8,128)S(1)}, u32[]{:S(2)}, u32[]{:S(2)}) collective-permute-start(f32[8,8,128]{2,1,0:T(8,128)} %get-tuple-element.128.rest_0_), channel_id=1, source_target_pairs={{0,3},{1,0},{2,1},{3,2},{4,7},{5,4},{6,5},{7,6},{8,11},{9,8},{10,9... | collective-permute-start | bytes 98312 | tf_op jit(solution)/shard_map/ppermute | solution.py:476
  76.3 1.0 %collective-permute-done.21.rest_1_ = f32[8,8,128]{2,1,0:T(8,128)S(1)} collective-permute-done((f32[8,8,128]{2,1,0:T(8,128)}, f32[8,8,128]{2,1,0:T(8,128)S(1)}, u32[]{:S(2)}, u32[]{:S(2)}) %collective-permute-start.21) | collective-permute-done | bytes 32800 | tf_op jit(solution)/shard_map/ppermute | solution.py:476
  77.3 0.5 collective-permute-done.22.rest_2_
  77.8 1.3 %collective-permute-done.23.rest_3_ = f32[8,8,128]{2,1,0:T(8,128)S(1)} collective-permute-done((f32[8,8,128]{2,1,0:T(8,128)}, f32[8,8,128]{2,1,0:T(8,128)S(1)}, u32[]{:S(2)}, u32[]{:S(2)}) %collective-permute-start.23) | collective-permute-done | bytes 32800 | tf_op jit(solution)/shard_map/ppermute | solution.py:476
  79.1 0.6 copy-done.23
  79.7 2.0 %shard_map.130 = f32[64,8,128]{2,1,0:T(8,128)} custom-call(s32[1]{0:T(128)} %bitcast.rank_ref, f32[64,8,128]{2,1,0:T(8,128)} %get-tuple-element.125.y_ref, f32[64,8,128]{2,1,0:T(8,128)} %get-tuple-element.126.a_ref, f32[64,8,128]{2,1,0:T(8,128)} %get-tuple-element.127.b_ref, f32[8,8,128]{2,1,0:T(8,128)} %get-tuple-element.128.rest_0_, ...), custom_call_target="tpu_custom_call" | custom-call | tf_op jit(solution)/shard_map/pallas_call | solution.py:478
  (59 shorter events, 0.3 us)
Async XLA Ops:
  5.2 7.0 %collective-permute-start = (f32[5,8,8,128]{3,2,1,0:T(8,128)}, f32[5,8,8,128]{3,2,1,0:T(8,128)S(1)}, u32[]{:S(2)}, u32[]{:S(2)}) collective-permute-start(f32[5,8,8,128]{3,2,1,0:T(8,128)} %get-tuple-element.73), channel_id=1, source_target_pairs={{0,8},{8,16},{16,24},{24,0},{1,9},{9,17},{17,25},{25,1},{2,10},{10... | collective-permute-start | bytes 491528 | tf_op jit(solution)/shard_map/ppermute | solution.py:373
  5.7 6.8 %collective-permute-start.1 = (f32[5,8,8,128]{3,2,1,0:T(8,128)}, f32[5,8,8,128]{3,2,1,0:T(8,128)S(1)}, u32[]{:S(2)}, u32[]{:S(2)}) collective-permute-start(f32[5,8,8,128]{3,2,1,0:T(8,128)} %get-tuple-element.74), channel_id=1, source_target_pairs={{8,0},{16,8},{24,16},{0,24},{9,1},{17,9},{25,17},{1,25},{10,2},{18... | collective-permute-start | bytes 491528 | tf_op jit(solution)/shard_map/ppermute | solution.py:374
  7.7 4.5 %collective-permute-start.2 = (f32[2,5,8,128]{3,2,1,0:T(8,128)}, f32[2,5,8,128]{3,2,1,0:T(8,128)S(1)}, u32[]{:S(2)}, u32[]{:S(2)}) collective-permute-start(f32[2,5,8,128]{3,2,1,0:T(8,128)} %get-tuple-element.75), channel_id=1, source_target_pairs={{0,4},{4,0},{1,5},{5,1},{2,6},{6,2},{3,7},{7,3},{8,12},{12,8},{9,1... | collective-permute-start | bytes 122888 | tf_op jit(solution)/shard_map/ppermute | solution.py:375
  12.2 0.6 copy-start.2
  12.2 0.7 copy-start
  12.5 0.7 copy-start.1
  18.8 11.5 %collective-permute-start.3 = (f32[3,4,8,128]{3,2,1,0:T(8,128)}, f32[3,4,8,128]{3,2,1,0:T(8,128)S(1)}, u32[]{:S(2)}, u32[]{:S(2)}) collective-permute-start(f32[3,4,8,128]{3,2,1,0:T(8,128)} %get-tuple-element.85), channel_id=1, source_target_pairs={{0,8},{8,16},{16,24},{24,0},{1,9},{9,17},{17,25},{25,1},{2,10},{10... | collective-permute-start | bytes 147464 | tf_op jit(solution)/shard_map/ppermute | solution.py:373
  19.5 10.7 %collective-permute-start.4 = (f32[3,4,8,128]{3,2,1,0:T(8,128)}, f32[3,4,8,128]{3,2,1,0:T(8,128)S(1)}, u32[]{:S(2)}, u32[]{:S(2)}) collective-permute-start(f32[3,4,8,128]{3,2,1,0:T(8,128)} %get-tuple-element.86), channel_id=1, source_target_pairs={{8,0},{16,8},{24,16},{0,24},{9,1},{17,9},{25,17},{1,25},{10,2},{18... | collective-permute-start | bytes 147464 | tf_op jit(solution)/shard_map/ppermute | solution.py:374
  20.9 8.7 %collective-permute-start.5 = (f32[2,3,8,128]{3,2,1,0:T(8,128)}, f32[2,3,8,128]{3,2,1,0:T(8,128)S(1)}, u32[]{:S(2)}, u32[]{:S(2)}) collective-permute-start(f32[2,3,8,128]{3,2,1,0:T(8,128)} %get-tuple-element.87), channel_id=1, source_target_pairs={{0,4},{4,0},{1,5},{5,1},{2,6},{6,2},{3,7},{7,3},{8,12},{12,8},{9,1... | collective-permute-start | bytes 73736 | tf_op jit(solution)/shard_map/ppermute | solution.py:375
  27.8 9.4 %collective-permute-start.6 = (f32[3,4,8,128]{3,2,1,0:T(8,128)}, f32[3,4,8,128]{3,2,1,0:T(8,128)S(1)}, u32[]{:S(2)}, u32[]{:S(2)}) collective-permute-start(f32[3,4,8,128]{3,2,1,0:T(8,128)} %get-tuple-element.93), channel_id=1, source_target_pairs={{0,8},{8,16},{16,24},{24,0},{1,9},{9,17},{17,25},{25,1},{2,10},{10... | collective-permute-start | bytes 147464 | tf_op jit(solution)/shard_map/ppermute | solution.py:373
  27.9 9.4 %collective-permute-start.7 = (f32[3,4,8,128]{3,2,1,0:T(8,128)}, f32[3,4,8,128]{3,2,1,0:T(8,128)S(1)}, u32[]{:S(2)}, u32[]{:S(2)}) collective-permute-start(f32[3,4,8,128]{3,2,1,0:T(8,128)} %get-tuple-element.94), channel_id=1, source_target_pairs={{8,0},{16,8},{24,16},{0,24},{9,1},{17,9},{25,17},{1,25},{10,2},{18... | collective-permute-start | bytes 147464 | tf_op jit(solution)/shard_map/ppermute | solution.py:374
  29.6 0.7 copy-start.7
  29.6 6.3 %collective-permute-start.8 = (f32[2,3,8,128]{3,2,1,0:T(8,128)}, f32[2,3,8,128]{3,2,1,0:T(8,128)S(1)}, u32[]{:S(2)}, u32[]{:S(2)}) collective-permute-start(f32[2,3,8,128]{3,2,1,0:T(8,128)} %get-tuple-element.95), channel_id=1, source_target_pairs={{0,4},{4,0},{1,5},{5,1},{2,6},{6,2},{3,7},{7,3},{8,12},{12,8},{9,1... | collective-permute-start | bytes 73736 | tf_op jit(solution)/shard_map/ppermute | solution.py:375
  30.3 0.6 copy-start.17
  30.3 0.6 copy-start.18
  35.3 9.4 %collective-permute-start.10 = (f32[3,4,8,128]{3,2,1,0:T(8,128)}, f32[3,4,8,128]{3,2,1,0:T(8,128)S(1)}, u32[]{:S(2)}, u32[]{:S(2)}) collective-permute-start(f32[3,4,8,128]{3,2,1,0:T(8,128)} %get-tuple-element.101), channel_id=1, source_target_pairs={{8,0},{16,8},{24,16},{0,24},{9,1},{17,9},{25,17},{1,25},{10,2},{18... | collective-permute-start | bytes 147464 | tf_op jit(solution)/shard_map/ppermute | solution.py:374
  35.5 9.2 %collective-permute-start.9 = (f32[3,4,8,128]{3,2,1,0:T(8,128)}, f32[3,4,8,128]{3,2,1,0:T(8,128)S(1)}, u32[]{:S(2)}, u32[]{:S(2)}) collective-permute-start(f32[3,4,8,128]{3,2,1,0:T(8,128)} %get-tuple-element.100), channel_id=1, source_target_pairs={{0,8},{8,16},{16,24},{24,0},{1,9},{9,17},{17,25},{25,1},{2,10},{10... | collective-permute-start | bytes 147464 | tf_op jit(solution)/shard_map/ppermute | solution.py:373
  35.9 1.4 %copy-start.3 = (f32[2,3,8,128]{3,2,1,0:T(8,128)}, f32[2,3,8,128]{3,2,1,0:T(8,128)S(1)}, u32[]{:S(2)}) copy-start(f32[2,3,8,128]{3,2,1,0:T(8,128)S(1)} %collective-permute-done.8.rest_3_.rest_4_) | copy-start | bytes 73732
  35.9 8.2 %collective-permute-start.11 = (f32[2,3,8,128]{3,2,1,0:T(8,128)}, f32[2,3,8,128]{3,2,1,0:T(8,128)S(1)}, u32[]{:S(2)}, u32[]{:S(2)}) collective-permute-start(f32[2,3,8,128]{3,2,1,0:T(8,128)} %get-tuple-element.102), channel_id=1, source_target_pairs={{0,4},{4,0},{1,5},{5,1},{2,6},{6,2},{3,7},{7,3},{8,12},{12,8},{9,1... | collective-permute-start | bytes 73736 | tf_op jit(solution)/shard_map/ppermute | solution.py:375
  37.2 0.6 copy-start.9
  37.2 0.6 copy-start.12
  42.3 10.6 %collective-permute-start.12 = (f32[3,4,8,128]{3,2,1,0:T(8,128)}, f32[3,4,8,128]{3,2,1,0:T(8,128)S(1)}, u32[]{:S(2)}, u32[]{:S(2)}) collective-permute-start(f32[3,4,8,128]{3,2,1,0:T(8,128)} %get-tuple-element.107), channel_id=1, source_target_pairs={{0,8},{8,16},{16,24},{24,0},{1,9},{9,17},{17,25},{25,1},{2,10},{10... | collective-permute-start | bytes 147464 | tf_op jit(solution)/shard_map/ppermute | solution.py:373
  43.2 9.7 %collective-permute-start.13 = (f32[3,4,8,128]{3,2,1,0:T(8,128)}, f32[3,4,8,128]{3,2,1,0:T(8,128)S(1)}, u32[]{:S(2)}, u32[]{:S(2)}) collective-permute-start(f32[3,4,8,128]{3,2,1,0:T(8,128)} %get-tuple-element.108), channel_id=1, source_target_pairs={{8,0},{16,8},{24,16},{0,24},{9,1},{17,9},{25,17},{1,25},{10,2},{18... | collective-permute-start | bytes 147464 | tf_op jit(solution)/shard_map/ppermute | solution.py:374
  44.0 0.7 copy-start.4
  44.0 7.5 %collective-permute-start.14 = (f32[2,3,8,128]{3,2,1,0:T(8,128)}, f32[2,3,8,128]{3,2,1,0:T(8,128)S(1)}, u32[]{:S(2)}, u32[]{:S(2)}) collective-permute-start(f32[2,3,8,128]{3,2,1,0:T(8,128)} %get-tuple-element.109), channel_id=1, source_target_pairs={{0,4},{4,0},{1,5},{5,1},{2,6},{6,2},{3,7},{7,3},{8,12},{12,8},{9,1... | collective-permute-start | bytes 73736 | tf_op jit(solution)/shard_map/ppermute | solution.py:375
  44.7 0.6 copy-start.10
  44.7 0.6 copy-start.13
  49.8 10.6 %collective-permute-start.15 = (f32[3,4,8,128]{3,2,1,0:T(8,128)}, f32[3,4,8,128]{3,2,1,0:T(8,128)S(1)}, u32[]{:S(2)}, u32[]{:S(2)}) collective-permute-start(f32[3,4,8,128]{3,2,1,0:T(8,128)} %get-tuple-element.114), channel_id=1, source_target_pairs={{0,8},{8,16},{16,24},{24,0},{1,9},{9,17},{17,25},{25,1},{2,10},{10... | collective-permute-start | bytes 147464 | tf_op jit(solution)/shard_map/ppermute | solution.py:373
  49.9 10.4 %collective-permute-start.16 = (f32[3,4,8,128]{3,2,1,0:T(8,128)}, f32[3,4,8,128]{3,2,1,0:T(8,128)S(1)}, u32[]{:S(2)}, u32[]{:S(2)}) collective-permute-start(f32[3,4,8,128]{3,2,1,0:T(8,128)} %get-tuple-element.115), channel_id=1, source_target_pairs={{8,0},{16,8},{24,16},{0,24},{9,1},{17,9},{25,17},{1,25},{10,2},{18... | collective-permute-start | bytes 147464 | tf_op jit(solution)/shard_map/ppermute | solution.py:374
  51.5 1.4 %copy-start.5 = (f32[2,3,8,128]{3,2,1,0:T(8,128)}, f32[2,3,8,128]{3,2,1,0:T(8,128)S(1)}, u32[]{:S(2)}) copy-start(f32[2,3,8,128]{3,2,1,0:T(8,128)S(1)} %collective-permute-done.14.rest_3_.rest_4_) | copy-start | bytes 73732
  51.5 8.2 %collective-permute-start.17 = (f32[2,3,8,128]{3,2,1,0:T(8,128)}, f32[2,3,8,128]{3,2,1,0:T(8,128)S(1)}, u32[]{:S(2)}, u32[]{:S(2)}) collective-permute-start(f32[2,3,8,128]{3,2,1,0:T(8,128)} %get-tuple-element.116), channel_id=1, source_target_pairs={{0,4},{4,0},{1,5},{5,1},{2,6},{6,2},{3,7},{7,3},{8,12},{12,8},{9,1... | collective-permute-start | bytes 73736 | tf_op jit(solution)/shard_map/ppermute | solution.py:375
  52.9 0.6 copy-start.11
  52.9 0.6 copy-start.15
  57.9 6.2 %collective-permute-start.18 = (f32[3,4,8,128]{3,2,1,0:T(8,128)}, f32[3,4,8,128]{3,2,1,0:T(8,128)S(1)}, u32[]{:S(2)}, u32[]{:S(2)}) collective-permute-start(f32[3,4,8,128]{3,2,1,0:T(8,128)} %get-tuple-element.121), channel_id=1, source_target_pairs={{0,8},{8,16},{16,24},{24,0},{1,9},{9,17},{17,25},{25,1},{2,10},{10... | collective-permute-start | bytes 147464 | tf_op jit(solution)/shard_map/ppermute | solution.py:373
  58.0 6.2 %collective-permute-start.19 = (f32[3,4,8,128]{3,2,1,0:T(8,128)}, f32[3,4,8,128]{3,2,1,0:T(8,128)S(1)}, u32[]{:S(2)}, u32[]{:S(2)}) collective-permute-start(f32[3,4,8,128]{3,2,1,0:T(8,128)} %get-tuple-element.122), channel_id=1, source_target_pairs={{8,0},{16,8},{24,16},{0,24},{9,1},{17,9},{25,17},{1,25},{10,2},{18... | collective-permute-start | bytes 147464 | tf_op jit(solution)/shard_map/ppermute | solution.py:374
  59.7 0.7 copy-start.6
  59.7 4.4 %collective-permute-start.20 = (f32[2,3,8,128]{3,2,1,0:T(8,128)}, f32[2,3,8,128]{3,2,1,0:T(8,128)S(1)}, u32[]{:S(2)}, u32[]{:S(2)}) collective-permute-start(f32[2,3,8,128]{3,2,1,0:T(8,128)} %get-tuple-element.123), channel_id=1, source_target_pairs={{0,4},{4,0},{1,5},{5,1},{2,6},{6,2},{3,7},{7,3},{8,12},{12,8},{9,1... | collective-permute-start | bytes 73736 | tf_op jit(solution)/shard_map/ppermute | solution.py:375
  60.4 0.6 copy-start.14
  60.4 0.6 copy-start.16
  64.1 0.6 copy-start.8
  64.1 0.6 copy-start.19
  64.1 0.6 copy-start.20
  70.9 6.4 %collective-permute-start.21 = (f32[8,8,128]{2,1,0:T(8,128)}, f32[8,8,128]{2,1,0:T(8,128)S(1)}, u32[]{:S(2)}, u32[]{:S(2)}) collective-permute-start(f32[8,8,128]{2,1,0:T(8,128)} %get-tuple-element.128.rest_0_), channel_id=1, source_target_pairs={{0,1},{1,2},{2,3},{3,0},{4,5},{5,6},{6,7},{7,4},{8,9},{9,10},{10,1... | collective-permute-start | bytes 98312 | tf_op jit(solution)/shard_map/ppermute | solution.py:476
  72.3 5.5 %collective-permute-start.22 = (f32[8,8,128]{2,1,0:T(8,128)}, f32[8,8,128]{2,1,0:T(8,128)S(1)}, u32[]{:S(2)}, u32[]{:S(2)}) collective-permute-start(f32[8,8,128]{2,1,0:T(8,128)} %get-tuple-element.128.rest_0_), channel_id=1, source_target_pairs={{0,2},{1,3},{2,0},{3,1},{4,6},{5,7},{6,4},{7,5},{8,10},{9,11},{10,... | collective-permute-start | bytes 98312 | tf_op jit(solution)/shard_map/ppermute | solution.py:476
  74.9 4.1 %collective-permute-start.23 = (f32[8,8,128]{2,1,0:T(8,128)}, f32[8,8,128]{2,1,0:T(8,128)S(1)}, u32[]{:S(2)}, u32[]{:S(2)}) collective-permute-start(f32[8,8,128]{2,1,0:T(8,128)} %get-tuple-element.128.rest_0_), channel_id=1, source_target_pairs={{0,3},{1,0},{2,1},{3,2},{4,7},{5,4},{6,5},{7,6},{8,11},{9,8},{10,9... | collective-permute-start | bytes 98312 | tf_op jit(solution)/shard_map/ppermute | solution.py:476
  77.3 1.8 %copy-start.21 = (f32[8,8,128]{2,1,0:T(8,128)}, f32[8,8,128]{2,1,0:T(8,128)S(1)}, u32[]{:S(2)}) copy-start(f32[8,8,128]{2,1,0:T(8,128)S(1)} %collective-permute-done.21.rest_1_) | copy-start | bytes 98308
  77.8 1.3 %copy-start.22 = (f32[8,8,128]{2,1,0:T(8,128)}, f32[8,8,128]{2,1,0:T(8,128)S(1)}, u32[]{:S(2)}) copy-start(f32[8,8,128]{2,1,0:T(8,128)S(1)} %collective-permute-done.22.rest_2_) | copy-start | bytes 98308
  79.1 0.6 copy-start.23
